TPU v7x, 512 devices: a whole 4x4x16 slice. The times are simulated.
512 devices in a mesh: acq: 16 (over y_lo, x, core), pulse: 32 (over y_hi, z).
Axes of the slice: x: 4, y: 4 (y_hi: 2, y_lo: 2; y = y_hi * 2 + y_lo), z: 16, core: 2. Of those that a mesh axis runs over, the one named last changes fastest.
Arguments:
- raw_echo: bfloat16 [16, 2, 8192, 1535], P('acq', None, 'pulse'), may hold values from -6 to 6
- chirp_phase: float32 [1024], replicated, may hold values from -3.140625 to 3.140625
- pulse_counts: int32 [16], P('acq'), may hold values from 4096 to 8192, as said below
- azimuth_rate: float32 [512], P('pulse'), may hold values from 0.25 to 1
- partner_bits: int32 [16, 2], P('acq'), may hold values from 0 to 3, as said below
Outputs:
- interfere_real: float32 [16, 2, 128, 512], P('acq', None, 'pulse')
- interfere_imag: float32 [16, 2, 128, 512], P('acq', None, 'pulse')
Inputs may be any that keep to these rules, and one draw needn't show every extreme that they name: `pulse_counts`: at least half of 8192; some acquisition records all 8192 pulses and some exactly half. `partner_bits`: the two bits of a row differ.
All inputs are finite; a program needn't handle non-finite values.
Results may differ from a plain program's by a relative error of at most 0.0065.
Values may be sent and summed in bfloat16 or wider, within the bound.
No kernel may reach another device: no remote copies, remote signals or barrier semaphores. Data moves between devices by JAX's collectives and lax.ppermute only.
A program may use at most 64 MiB of HBM per device.

v0:
```python
import math

import jax
import jax.numpy as jnp
from jax import lax
from jax.sharding import PartitionSpec as P

RNG = 512
TAPS = 1024
LOOK_RNG = 4
LOOK_AZ = 16


def partner_2(shard, axis, bit):
    return lax.ppermute(shard, axis, [(i, i ^ 1 << bit) for i in range(lax.axis_size(axis))])


def part_tables(length, inverse):
    steps = jnp.arange(length, dtype=jnp.int32)
    angle = 2.0 * jnp.pi * (steps[:, None] * steps[None, :] % length).astype(jnp.float32) / length
    cosine = jnp.cos(angle)
    sine = jnp.sin(angle)
    if inverse:
        sine = -sine
    return jnp.stack([jnp.stack([cosine, -sine]), jnp.stack([sine, cosine])])


def complex_product(left_re, left_im, right_re, right_im):
    return (left_re * right_re - left_im * right_im, left_re * right_im + left_im * right_re)


def compress(echoes, toeplitz, first_pulse, live_pulses, block_cols, window):
    pulse_rows = echoes.shape[1]
    parts_re = []
    parts_im = []
    for start in range(0, RNG, block_cols):
        segment = echoes[:, :, start : start + window]
        stacked = jnp.concatenate([segment[0], segment[1]], axis=1)
        result = lax.dot_general(
            toeplitz, stacked, (((1,), (1,)), ((), ())), preferred_element_type=jnp.float32
        )
        parts_re.append(result[:block_cols])
        parts_im.append(result[block_cols:])
    joined = jnp.stack([jnp.concatenate(parts_re, axis=0), jnp.concatenate(parts_im, axis=0)])
    pulse_ids = first_pulse + jnp.arange(pulse_rows, dtype=jnp.int32)
    keep = (pulse_ids < live_pulses).astype(jnp.float32)
    return (joined * keep[None, None, :]).astype(jnp.bfloat16)


def azimuth(turned, azimuth_rate):
    columns = turned.shape[1]
    length = turned.shape[2]
    outer_len = 64
    inner_len = length // outer_len
    highest = lax.Precision.HIGHEST
    signal = turned.astype(jnp.float32).reshape(2, columns, outer_len, inner_len)
    section_one = jnp.einsum(
        "pcab,pqak->qckb", signal, part_tables(outer_len, False), precision=highest
    )
    outer_ids = jnp.arange(outer_len, dtype=jnp.int32)
    inner_ids = jnp.arange(inner_len, dtype=jnp.int32)
    twist = (
        2.0
        * jnp.pi
        * (outer_ids[:, None] * inner_ids[None, :] % length).astype(jnp.float32)
        / length
    )
    twist_cos = jnp.cos(twist)
    twist_sin = jnp.sin(twist)
    turned_re, turned_im = complex_product(section_one[0], section_one[1], twist_cos, -twist_sin)
    spectrum = jnp.einsum(
        "pckb,pqbm->qckm",
        jnp.stack([turned_re, turned_im]),
        part_tables(inner_len, False),
        precision=highest,
    )
    freq_index = outer_ids[:, None] + outer_len * inner_ids[None, :]
    signed = jnp.where(freq_index < length // 2, freq_index, freq_index - length).astype(
        jnp.float32
    )
    quad = signed * signed / length
    phase = (jnp.pi * azimuth_rate)[:, None, None] * quad[None, :, :]
    filt_re, filt_im = complex_product(spectrum[0], spectrum[1], jnp.cos(phase), -jnp.sin(phase))
    back_one = jnp.einsum(
        "pckm,pqmb->qckb",
        jnp.stack([filt_re, filt_im]),
        part_tables(inner_len, True),
        precision=highest,
    )
    undo_re, undo_im = complex_product(back_one[0], back_one[1], twist_cos, twist_sin)
    restored = jnp.einsum(
        "pckb,pqka->qcab",
        jnp.stack([undo_re, undo_im]),
        part_tables(outer_len, True),
        precision=highest,
    )
    return (restored / length).reshape(2, columns, length)


def multilook(values):
    columns = values.shape[0]
    pulse_len = values.shape[1]
    shaped = values.reshape(columns // LOOK_RNG, LOOK_RNG, pulse_len // LOOK_AZ, LOOK_AZ)
    return jnp.mean(shaped, axis=(1, 3))


def cross_looks(own_block, partner):
    own_f = own_block.astype(jnp.float32)
    other_f = partner.astype(jnp.float32)
    prod_re = own_f[0] * other_f[0] + own_f[1] * other_f[1]
    prod_im = own_f[1] * other_f[0] - own_f[0] * other_f[1]
    return jnp.stack([multilook(prod_re), multilook(prod_im)])


def per_device(raw_echo, chirp_phase, pulse_counts, azimuth_rate, partner_bits):
    echoes = raw_echo[0]
    pulses_dev = echoes.shape[1]
    block_cols = min(256, RNG)
    window = block_cols + TAPS - 1
    amplitude = 2.0 / math.sqrt(TAPS)
    table_re = (amplitude * jnp.cos(chirp_phase)).astype(jnp.bfloat16)
    table_im = (amplitude * jnp.sin(chirp_phase)).astype(jnp.bfloat16)
    padding = jnp.zeros((block_cols,), jnp.bfloat16)
    band_re = jnp.tile(jnp.concatenate([table_re, padding]), block_cols)[
        : block_cols * window
    ].reshape(block_cols, window)
    band_im = jnp.tile(jnp.concatenate([table_im, padding]), block_cols)[
        : block_cols * window
    ].reshape(block_cols, window)
    toeplitz = jnp.concatenate(
        [jnp.concatenate([band_re, band_im], axis=1), jnp.concatenate([-band_im, band_re], axis=1)],
        axis=0,
    )
    live_pulses = pulse_counts[0]
    first_pulse = lax.axis_index("pulse") * pulses_dev
    compressed = compress(echoes, toeplitz, first_pulse, live_pulses, block_cols, window)
    turned = lax.all_to_all(compressed, "pulse", split_axis=1, concat_axis=2, tiled=True)
    focused = azimuth(turned, azimuth_rate).astype(jnp.bfloat16)
    chosen = partner_bits[0]
    bit_count = lax.axis_size("acq").bit_length() - 1
    arrived = [partner_2(focused, "acq", which) for which in range(bit_count)]
    results = []
    for slot in range(2):
        partner = arrived[0]
        for which in range(1, bit_count):
            partner = jnp.where(chosen[slot] == which, arrived[which], partner)
        results.append(cross_looks(focused, partner))
    interfere_real = jnp.stack([item[0] for item in results])[None]
    interfere_imag = jnp.stack([item[1] for item in results])[None]
    return (interfere_real, interfere_imag)


def solution(mesh):
    in_specs = (P("acq", None, "pulse", None), P(), P("acq"), P("pulse"), P("acq", None))
    out_specs = (P("acq", None, "pulse", None), P("acq", None, "pulse", None))
    return jax.shard_map(
        per_device, mesh=mesh, in_specs=in_specs, out_specs=out_specs, check_vma=False
    )
```

profile of v0, /device:TPU:40, one launch (start us, length us, event | category | flops | bytes accessed | tf_op | source)
XLA Modules:
  0.0 128.6 jit_solution(16932121141618202442)
XLA Ops:
  0.6 0.7 multiply_convert_fusion
  1.4 0.8 tile.21
  2.2 1.2 reshape.369
  3.4 1.0 neg.53
  4.4 3.6 %copy.28 = bf16[1,2,256,1535]{3,2,1,0:T(8,128)(2,1)S(1)} copy(bf16[1,2,256,1535]{2,1,3,0:T(2,128)(2,1)} %param.5) | data formatting | bytes 3143680 | tf_op args[0]
  8.0 1.2 slice_bitcast_fusion.3
  9.3 0.8 tile.9
  10.0 2.1 %reshape.368 = bf16[256,1279]{1,0:T(8,128)(2,1)} reshape(bf16[327424]{0:T(1024)(128)(2,1)S(1)} %bitcast.121) | data formatting | bytes 1309696 | tf_op jit(solution)/shard_map/reshape | solution.py:126
  12.1 0.0 copy-start
  12.1 0.0 copy-start.1
  12.1 3.0 %fusion.2 = f32[512,256]{1,0:T(8,128)S(1)} fusion(bf16[256,1279]{1,0:T(8,128)(2,1)} %get-tuple-element.11, bf16[256,1279]{1,0:T(8,128)(2,1)} %get-tuple-element.8, bf16[256,1279]{1,0:T(8,128)(2,1)} %reshape.368, bf16[256,1279]{1,0:T(8,128)(2,1)} %neg.53, bf16[256,1279]{1,0:T(8,128)(2,1)S(1)} %reshape.369), kind=kOutput, calls=%fused_computation.8 | convolution fusion | flops 683661312 | bytes 3798528 | tf_op jit(solution)/shard_map/dot_general | solution.py:39
  15.2 0.0 copy-done
  15.2 0.0 copy-done.1
  15.2 1.0 fusion.6
  16.9 0.1 maximum_bitcast_fusion
  17.0 0.0 copy-start.3
  17.0 0.1 fusion.12
  17.1 1.3 %copy.29 = bf16[2,512,256]{2,0,1:T(2,128)(2,1)} copy(bf16[2,512,256]{2,1,0:T(8,128)(2,1)S(1)} %fusion.12) | data formatting | bytes 1048576 | tf_op jit(solution)/shard_map/convert_element_type | solution.py:47
  18.4 17.1 %all-to-all-start = ((bf16[2,512,256]{2,0,1:T(2,128)(2,1)}), bf16[2,512,256]{2,0,1:T(2,128)(2,1)S(1)}, u32[]{:S(2)}, u32[]{:S(2)}) async-start(bf16[2,512,256]{2,0,1:T(2,128)(2,1)} %copy.29), calls=%async_computation | async-start | bytes 1048576 | tf_op jit(solution)/shard_map/all_to_all | solution.py:137
  35.5 0.1 fusion.70
  35.7 0.1 fusion.66
  35.8 0.1 fusion.68
  36.0 0.1 fusion.67
  36.1 0.3 fusion.65
  36.4 0.3 fusion.59
  36.8 0.0 copy-done.3
  36.8 32.5 %all-to-all-done = bf16[2,512,256]{2,0,1:T(2,128)(2,1)S(1)} async-done(((bf16[2,512,256]{2,0,1:T(2,128)(2,1)}), bf16[2,512,256]{2,0,1:T(2,128)(2,1)S(1)}, u32[]{:S(2)}, u32[]{:S(2)}) %all-to-all-start) | async-done | bytes 524320 | tf_op jit(solution)/shard_map/all_to_all | solution.py:137
  69.3 0.3 copy.65
  69.6 0.2 reshape.372
  69.7 0.6 convolution_bitcast_fusion.3
  70.4 0.2 multiply_subtract_fusion.3
  70.5 1.0 convolution_bitcast_fusion.2
  71.6 2.1 %fusion.23 = (f32[1,16,64,128]{3,2,1,0:T(8,128)S(1)}, f32[1,16,64,128]{3,2,1,0:T(8,128)S(1)}) fusion(f32[2,16,64,128]{3,2,1,0:T(8,128)S(1)} %convolution_bitcast_fusion.2, f32[64,128]{1,0:T(8,128)S(1)} %fusion.56, f32[16]{0:T(128)S(1)} %broadcast_multiply_fusion), kind=kLoop, calls=%fused_computation.37 | loop fusion | flops 1048576 | bytes 2129984 | tf_op jit(solution)/shard_map/sub | solution.py:29
  73.7 1.0 convolution_bitcast_fusion.1
  74.7 0.0 copy-start.2
  74.7 0.2 multiply_subtract_fusion.2
  74.9 1.1 fusion.11
  76.0 0.2 convert_element_type.148
  76.2 3.3 %collective-permute-start = (bf16[2,16,8192]{2,1,0:T(8,128)(2,1)S(1)}, bf16[2,16,8192]{2,1,0:T(8,128)(2,1)S(1)}, u32[]{:S(2)}, u32[]{:S(2)}) collective-permute-start(bf16[2,16,8192]{2,1,0:T(8,128)(2,1)S(1)} %convert_element_type.148), channel_id=1, source_target_pairs={{0,256},{32,288},{64,320},{96,352},{128,384},{160,416},{192,448},{... | collective-permute-start | bytes 1572872 | tf_op jit(solution)/shard_map/ppermute | solution.py:15
  79.5 4.9 %collective-permute-start.1 = (bf16[2,16,8192]{2,1,0:T(8,128)(2,1)S(1)}, bf16[2,16,8192]{2,1,0:T(8,128)(2,1)S(1)}, u32[]{:S(2)}, u32[]{:S(2)}) collective-permute-start(bf16[2,16,8192]{2,1,0:T(8,128)(2,1)S(1)} %convert_element_type.148), channel_id=1, source_target_pairs={{0,128},{32,160},{64,192},{96,224},{128,0},{160,32},{192,64},{224,... | collective-permute-start | bytes 1572872 | tf_op jit(solution)/shard_map/ppermute | solution.py:15
  84.4 2.5 %collective-permute-start.2 = (bf16[2,16,8192]{2,1,0:T(8,128)(2,1)S(1)}, bf16[2,16,8192]{2,1,0:T(8,128)(2,1)S(1)}, u32[]{:S(2)}, u32[]{:S(2)}) collective-permute-start(bf16[2,16,8192]{2,1,0:T(8,128)(2,1)S(1)} %convert_element_type.148), channel_id=1, source_target_pairs={{0,64},{32,96},{64,0},{96,32},{128,192},{160,224},{192,128},{224,1... | collective-permute-start | bytes 1572872 | tf_op jit(solution)/shard_map/ppermute | solution.py:15
  86.9 2.1 %collective-permute-start.3 = (bf16[2,16,8192]{2,1,0:T(8,128)(2,1)S(1)}, bf16[2,16,8192]{2,1,0:T(8,128)(2,1)S(1)}, u32[]{:S(2)}, u32[]{:S(2)}) collective-permute-start(bf16[2,16,8192]{2,1,0:T(8,128)(2,1)S(1)} %convert_element_type.148), channel_id=1, source_target_pairs={{0,32},{32,0},{64,96},{96,64},{128,160},{160,128},{192,224},{224,1... | collective-permute-start | bytes 1572872 | tf_op jit(solution)/shard_map/ppermute | solution.py:15
  89.1 0.0 copy-done.2
  89.1 0.6 fusion.78
  93.6 0.1 convert_element_type.149
  93.6 0.0 collective-permute-done
  93.7 4.1 %collective-permute-done.1 = bf16[2,16,8192]{2,1,0:T(8,128)(2,1)S(1)} collective-permute-done((bf16[2,16,8192]{2,1,0:T(8,128)(2,1)S(1)}, bf16[2,16,8192]{2,1,0:T(8,128)(2,1)S(1)}, u32[]{:S(2)}, u32[]{:S(2)}) %collective-permute-start.1) | collective-permute-done | bytes 524320 | tf_op jit(solution)/shard_map/ppermute | solution.py:15
  97.7 7.9 %collective-permute-done.2 = bf16[2,16,8192]{2,1,0:T(8,128)(2,1)S(1)} collective-permute-done((bf16[2,16,8192]{2,1,0:T(8,128)(2,1)S(1)}, bf16[2,16,8192]{2,1,0:T(8,128)(2,1)S(1)}, u32[]{:S(2)}, u32[]{:S(2)}) %collective-permute-start.2) | collective-permute-done | bytes 524320 | tf_op jit(solution)/shard_map/ppermute | solution.py:15
  105.6 0.0 collective-permute-done.3
  105.6 0.2 select_convert_fusion.1
  105.8 0.2 multiply_subtract_fusion.1
  106.0 2.8 %sub.45 = f32[4,4,512,16]{3,2,1,0:T(8,128)} reshape(f32[1,16,8192]{2,1,0:T(8,128)S(1)} %get-tuple-element.19) | data formatting | bytes 1048576 | tf_op jit(solution)/shard_map/sub | solution.py:111
  108.8 2.5 %reduce_sum.39 = f32[4,512]{1,0:T(4,128)S(1)} reduce(f32[4,4,512,16]{3,2,1,0:T(8,128)} %sub.45, f32[]{:T(128)} %constant.104.clone.1), dimensions={1,3}, to_apply=%region_3.4 | reduce | flops 129024 | bytes 532484 | tf_op jit(solution)/shard_map/reduce_sum | solution.py:104
  111.4 2.8 %sub.43 = f32[4,4,512,16]{3,2,1,0:T(8,128)} reshape(f32[1,16,8192]{2,1,0:T(8,128)S(1)} %get-tuple-element.2) | data formatting | bytes 1048576 | tf_op jit(solution)/shard_map/sub | solution.py:111
  114.2 2.5 %reduce_sum.38 = f32[4,512]{1,0:T(4,128)S(1)} reduce(f32[4,4,512,16]{3,2,1,0:T(8,128)} %sub.43, f32[]{:T(128)} %constant.104.clone.1), dimensions={1,3}, to_apply=%region_2.3 | reduce | flops 129024 | bytes 532484 | tf_op jit(solution)/shard_map/reduce_sum | solution.py:104
  116.7 2.8 %add.187 = f32[4,4,512,16]{3,2,1,0:T(8,128)} reshape(f32[1,16,8192]{2,1,0:T(8,128)S(1)} %get-tuple-element.18) | data formatting | bytes 1048576 | tf_op jit(solution)/shard_map/add | solution.py:110
  119.5 2.5 %reduce_sum.37 = f32[4,512]{1,0:T(4,128)S(1)} reduce(f32[4,4,512,16]{3,2,1,0:T(8,128)} %add.187, f32[]{:T(128)} %constant.104.clone.1), dimensions={1,3}, to_apply=%region_1.2 | reduce | flops 129024 | bytes 532484 | tf_op jit(solution)/shard_map/reduce_sum | solution.py:104
  122.1 2.8 %add.185 = f32[4,4,512,16]{3,2,1,0:T(8,128)} reshape(f32[1,16,8192]{2,1,0:T(8,128)S(1)} %get-tuple-element.3) | data formatting | bytes 1048576 | tf_op jit(solution)/shard_map/add | solution.py:110
  124.8 2.5 %reduce_sum.36 = f32[4,512]{1,0:T(4,128)S(1)} reduce(f32[4,4,512,16]{3,2,1,0:T(8,128)} %add.185, f32[]{:T(128)} %constant.104.clone.1), dimensions={1,3}, to_apply=%region_0.1 | reduce | flops 129024 | bytes 532484 | tf_op jit(solution)/shard_map/reduce_sum | solution.py:104
  127.4 0.6 maximum_bitcast_fusion.9
  128.0 0.6 maximum_bitcast_fusion.8
  (16 shorter events, 0.3 us)
Async XLA Ops:
  12.1 3.0 %copy-start = (bf16[256,1279]{1,0:T(8,128)(2,1)S(1)}, bf16[256,1279]{1,0:T(8,128)(2,1)}, u32[]{:S(2)}) copy-start(bf16[256,1279]{1,0:T(8,128)(2,1)} %neg.53) | copy-start | bytes 1964548
  12.1 3.1 %copy-start.1 = (bf16[256,1279]{1,0:T(8,128)(2,1)S(1)}, bf16[256,1279]{1,0:T(8,128)(2,1)}, u32[]{:S(2)}) copy-start(bf16[256,1279]{1,0:T(8,128)(2,1)} %reshape.368) | copy-start | bytes 1964548
  17.0 19.8 %copy-start.3 = (f32[16]{0:T(128)S(1)}, f32[16]{0:T(128)}, u32[]{:S(2)}) copy-start(f32[16]{0:T(128)} %param.8) | copy-start | bytes 196
  18.4 50.8 %all-to-all-start = ((bf16[2,512,256]{2,0,1:T(2,128)(2,1)}), bf16[2,512,256]{2,0,1:T(2,128)(2,1)S(1)}, u32[]{:S(2)}, u32[]{:S(2)}) async-start(bf16[2,512,256]{2,0,1:T(2,128)(2,1)} %copy.29), calls=%async_computation | async-start | bytes 1048576 | tf_op jit(solution)/shard_map/all_to_all | solution.py:137
  74.7 14.4 %copy-start.2 = (s32[1,2]{1,0:T(1,128)S(1)}, s32[1,2]{1,0:T(1,128)}, u32[]{:S(2)}) copy-start(s32[1,2]{1,0:T(1,128)} %param.9) | copy-start | bytes 28
  76.2 17.4 %collective-permute-start = (bf16[2,16,8192]{2,1,0:T(8,128)(2,1)S(1)}, bf16[2,16,8192]{2,1,0:T(8,128)(2,1)S(1)}, u32[]{:S(2)}, u32[]{:S(2)}) collective-permute-start(bf16[2,16,8192]{2,1,0:T(8,128)(2,1)S(1)} %convert_element_type.148), channel_id=1, source_target_pairs={{0,256},{32,288},{64,320},{96,352},{128,384},{160,416},{192,448},{... | collective-permute-start | bytes 1572872 | tf_op jit(solution)/shard_map/ppermute | solution.py:15
  79.5 18.3 %collective-permute-start.1 = (bf16[2,16,8192]{2,1,0:T(8,128)(2,1)S(1)}, bf16[2,16,8192]{2,1,0:T(8,128)(2,1)S(1)}, u32[]{:S(2)}, u32[]{:S(2)}) collective-permute-start(bf16[2,16,8192]{2,1,0:T(8,128)(2,1)S(1)} %convert_element_type.148), channel_id=1, source_target_pairs={{0,128},{32,160},{64,192},{96,224},{128,0},{160,32},{192,64},{224,... | collective-permute-start | bytes 1572872 | tf_op jit(solution)/shard_map/ppermute | solution.py:15
  84.4 21.2 %collective-permute-start.2 = (bf16[2,16,8192]{2,1,0:T(8,128)(2,1)S(1)}, bf16[2,16,8192]{2,1,0:T(8,128)(2,1)S(1)}, u32[]{:S(2)}, u32[]{:S(2)}) collective-permute-start(bf16[2,16,8192]{2,1,0:T(8,128)(2,1)S(1)} %convert_element_type.148), channel_id=1, source_target_pairs={{0,64},{32,96},{64,0},{96,32},{128,192},{160,224},{192,128},{224,1... | collective-permute-start | bytes 1572872 | tf_op jit(solution)/shard_map/ppermute | solution.py:15
  86.9 18.7 %collective-permute-start.3 = (bf16[2,16,8192]{2,1,0:T(8,128)(2,1)S(1)}, bf16[2,16,8192]{2,1,0:T(8,128)(2,1)S(1)}, u32[]{:S(2)}, u32[]{:S(2)}) collective-permute-start(bf16[2,16,8192]{2,1,0:T(8,128)(2,1)S(1)} %convert_element_type.148), channel_id=1, source_target_pairs={{0,32},{32,0},{64,96},{96,64},{128,160},{160,128},{192,224},{224,1... | collective-permute-start | bytes 1572872 | tf_op jit(solution)/shard_map/ppermute | solution.py:15
where the time goes:
time: 130 us; the launch traced here: 129 us
  waiting for transfers between devices  44.4 us (34%)
  starting transfers between devices  29.9 us (23%)
  local copies, waits for them, and re-layouts  23.6 us (18%)
  other arithmetic  17.4 us (13%)
  matrix products  7.7 us (6%)
  between operations  5.54 us (4%)
    all_to_all x1, waiting for transfers between devices, per_device(): lax.all_to_all(compressed, 'pulse', split_axis=1, concat_axis=2, tiled=True)  32.5 us
    all_to_all x1, starting transfers between devices, per_device(): lax.all_to_all(compressed, 'pulse', split_axis=1, concat_axis=2, tiled=True)  17.1 us
    ppermute x4, starting transfers between devices, partner_2(): lax.ppermute(shard, axis, [(i, i ^ 1 << bit) for i in range(lax.axis_size...  12.8 us
    ppermute x4, waiting for transfers between devices, partner_2(): lax.ppermute(shard, axis, [(i, i ^ 1 << bit) for i in range(lax.axis_size...  12 us
    reduce_sum x4, other arithmetic, multilook(): return jnp.mean(shaped, axis=(1, 3))  10.2 us
    sub x2, local copies, waits for them, and re-layouts, cross_looks(): prod_im = own_f[1] * other_f[0] - own_f[0] * other_f[1]  5.56 us
    add x2, local copies, waits for them, and re-layouts, cross_looks(): prod_re = own_f[0] * other_f[0] + own_f[1] * other_f[1]  5.56 us
    dot_general x2, matrix products, compress(): lax.dot_general(toeplitz, stacked, (((1,), (1,)), ((), ())), preferred_el...  3.99 us
  transfers between devices with their start and end apart: 5, of which 3 were waited for; matrix products, arithmetic and copies ran while one was open for 1% of the time, Pallas kernels for 0%

commit v1 on v0

--- a/solution.py
+++ b/solution.py
@@ -9,10 +9,6 @@
 TAPS = 1024
 LOOK_RNG = 4
 LOOK_AZ = 16
-
-
-def partner_2(shard, axis, bit):
-    return lax.ppermute(shard, axis, [(i, i ^ 1 << bit) for i in range(lax.axis_size(axis))])
 
 
 def part_tables(length, inverse):
@@ -97,19 +93,32 @@
     return (restored / length).reshape(2, columns, length)
 
 
-def multilook(values):
-    columns = values.shape[0]
-    pulse_len = values.shape[1]
-    shaped = values.reshape(columns // LOOK_RNG, LOOK_RNG, pulse_len // LOOK_AZ, LOOK_AZ)
-    return jnp.mean(shaped, axis=(1, 3))
+def parity(index):
+    return bin(index).count("1") % 2
 
 
-def cross_looks(own_block, partner):
+def multilook(stacked):
+    count, columns, pulse_len = stacked.shape
+    inner = 128
+    shaped = stacked.reshape(count, columns // LOOK_RNG, LOOK_RNG, pulse_len // inner, inner)
+    summed = jnp.sum(shaped, axis=2)
+    lanes = jnp.arange(inner, dtype=jnp.int32)
+    groups = jnp.arange(inner // LOOK_AZ, dtype=jnp.int32)
+    pool = (lanes[:, None] // LOOK_AZ == groups[None, :]).astype(jnp.float32)
+    looked = jnp.einsum("nrab,bg->nrag", summed, pool, precision=lax.Precision.HIGHEST)
+    scale = 1.0 / (LOOK_RNG * LOOK_AZ)
+    return looked.reshape(count, columns // LOOK_RNG, pulse_len // LOOK_AZ) * scale
+
+
+def cross_looks(own_block, partners):
     own_f = own_block.astype(jnp.float32)
-    other_f = partner.astype(jnp.float32)
-    prod_re = own_f[0] * other_f[0] + own_f[1] * other_f[1]
-    prod_im = own_f[1] * other_f[0] - own_f[0] * other_f[1]
-    return jnp.stack([multilook(prod_re), multilook(prod_im)])
+    prods = []
+    for partner in partners:
+        other_f = partner.astype(jnp.float32)
+        prods.append(own_f[0] * other_f[0] + own_f[1] * other_f[1])
+        prods.append(own_f[1] * other_f[0] - own_f[0] * other_f[1])
+    looked = multilook(jnp.stack(prods))
+    return looked.reshape(len(partners), 2, *looked.shape[1:])
 
 
 def per_device(raw_echo, chirp_phase, pulse_counts, azimuth_rate, partner_bits):
@@ -137,14 +146,40 @@
     turned = lax.all_to_all(compressed, "pulse", split_axis=1, concat_axis=2, tiled=True)
     focused = azimuth(turned, azimuth_rate).astype(jnp.bfloat16)
     chosen = partner_bits[0]
-    bit_count = lax.axis_size("acq").bit_length() - 1
-    arrived = [partner_2(focused, "acq", which) for which in range(bit_count)]
+    acq_size = lax.axis_size("acq")
+    me = lax.axis_index("acq")
+    me_parity = jnp.int32(0)
+    for which in range(acq_size.bit_length() - 1):
+        me_parity = me_parity ^ ((me >> which) & 1)
+    low_bits = (0, 1)
+    high_bits = (2, 3)
+    edge_pairs = []
+    for slot in range(2):
+        edge_pairs.append(
+            [
+                (i, i ^ (1 << (high_bits[slot] if parity(i) else low_bits[slot])))
+                for i in range(acq_size)
+            ]
+        )
+    arrived = [lax.ppermute(focused, "acq", pairs) for pairs in edge_pairs]
+    looked = cross_looks(focused, arrived)
+    returned = [
+        lax.ppermute(looked[slot], "acq", [(dst, src) for src, dst in edge_pairs[slot]])
+        for slot in range(2)
+    ]
+    candidates = []
+    for slot in range(2):
+        recv_bit = jnp.where(me_parity == 1, low_bits[slot], high_bits[slot])
+        send_bit = jnp.where(me_parity == 1, high_bits[slot], low_bits[slot])
+        candidates.append((recv_bit, looked[slot]))
+        back = returned[slot]
+        candidates.append((send_bit, jnp.stack([back[0], -back[1]])))
     results = []
     for slot in range(2):
-        partner = arrived[0]
-        for which in range(1, bit_count):
-            partner = jnp.where(chosen[slot] == which, arrived[which], partner)
-        results.append(cross_looks(focused, partner))
+        pick = candidates[0][1]
+        for bit, value in candidates[1:]:
+            pick = jnp.where(chosen[slot] == bit, value, pick)
+        results.append(pick)
     interfere_real = jnp.stack([item[0] for item in results])[None]
     interfere_imag = jnp.stack([item[1] for item in results])[None]
     return (interfere_real, interfere_imag)

time: 130 us -> 114 us (0.88)
  the two profiles are of different devices: /device:TPU:40 before, /device:TPU:36 now
where the time goes in v1:
time: 114 us
  waiting for transfers between devices  47.1 us (41%)
  starting transfers between devices  31.6 us (28%)
  local copies, waits for them, and re-layouts  13.5 us (12%)
  matrix products  8.41 us (7%)
  other arithmetic  7.39 us (6%)
  between operations  5.63 us (5%)
    all_to_all x1, waiting for transfers between devices, per_device(): lax.all_to_all(compressed, 'pulse', split_axis=1, concat_axis=2, tiled=True)  32.5 us
    all_to_all x1, starting transfers between devices, per_device(): lax.all_to_all(compressed, 'pulse', split_axis=1, concat_axis=2, tiled=True)  18 us
    ppermute x2, waiting for transfers between devices, per_device(): arrived = [lax.ppermute(focused, 'acq', pairs) for pairs in edge_pairs]  9.46 us
    ppermute x2, starting transfers between devices, per_device(): lax.ppermute(looked[slot], 'acq', [(dst, src) for src, dst in edge_pairs[...  9.13 us
    ppermute x2, waiting for transfers between devices, per_device(): lax.ppermute(looked[slot], 'acq', [(dst, src) for src, dst in edge_pairs[...  5.19 us
    ppermute x2, starting transfers between devices, per_device(): arrived = [lax.ppermute(focused, 'acq', pairs) for pairs in edge_pairs]  4.51 us
    unnamed x13, local copies, waits for them, and re-layouts  4.04 us
    dot_general x2, matrix products, compress(): lax.dot_general(toeplitz, stacked, (((1,), (1,)), ((), ())), preferred_el...  3.99 us
  transfers between devices with their start and end apart: 5, of which 4 were waited for; matrix products, arithmetic and copies ran while one was open for 2% of the time, Pallas kernels for 0%

profile of v1, /device:TPU:36, one launch (start us, length us, event | category | flops | bytes accessed | tf_op | source)
XLA Modules:
  0.0 113.7 jit_solution(9805634354367197942)
XLA Ops:
  0.6 0.7 multiply_convert_fusion
  1.4 0.8 tile.21
  2.2 1.2 %reshape.341 = bf16[256,1279]{1,0:T(8,128)(2,1)S(1)} reshape(bf16[327424]{0:T(1024)(128)(2,1)S(1)} %bitcast.138) | data formatting | bytes 1309696 | tf_op jit(solution)/shard_map/reshape | solution.py:138
  3.4 1.0 neg.61
  4.4 3.6 %copy.30 = bf16[1,2,256,1535]{3,2,1,0:T(8,128)(2,1)S(1)} copy(bf16[1,2,256,1535]{2,1,3,0:T(2,128)(2,1)} %param.5) | data formatting | bytes 3143680 | tf_op args[0]
  8.0 1.2 %slice_bitcast_fusion.3 = (bf16[256,1279]{1,0:T(8,128)(2,1)}, bf16[256,1279]{1,0:T(8,128)(2,1)S(1)}, bf16[256,1279]{1,0:T(8,128)(2,1)S(1)}, bf16[256,1279]{1,0:T(8,128)(2,1)}) fusion(bf16[2,256,1535]{2,1,0:T(8,128)(2,1)S(1)} %bitcast.137), kind=kLoop, calls=%fused_computation.38 | loop fusion | bytes 5238784 | tf_op jit(solution)/shard_map/squeeze | solution.py:34
  9.3 0.8 tile.9
  10.1 2.1 %reshape.340 = bf16[256,1279]{1,0:T(8,128)(2,1)} reshape(bf16[327424]{0:T(1024)(128)(2,1)S(1)} %bitcast.139) | data formatting | bytes 1309696 | tf_op jit(solution)/shard_map/reshape | solution.py:135
  12.1 0.0 copy-start
  12.1 0.0 copy-start.1
  12.1 3.0 %fusion.2 = f32[512,256]{1,0:T(8,128)S(1)} fusion(bf16[256,1279]{1,0:T(8,128)(2,1)} %get-tuple-element.9, bf16[256,1279]{1,0:T(8,128)(2,1)} %get-tuple-element.6, bf16[256,1279]{1,0:T(8,128)(2,1)} %reshape.340, bf16[256,1279]{1,0:T(8,128)(2,1)} %neg.61, bf16[256,1279]{1,0:T(8,128)(2,1)S(1)} %reshape.341), kind=kOutput, calls=%fused_computation.9 | convolution fusion | flops 683661312 | bytes 3798528 | tf_op jit(solution)/shard_map/dot_general | solution.py:35
  15.2 0.0 copy-done
  15.2 0.0 copy-done.1
  15.2 1.0 fusion.6
  16.9 0.1 maximum_bitcast_fusion
  17.0 0.1 fusion.12
  17.1 0.0 copy-start.3
  17.1 1.4 %copy.31 = bf16[2,512,256]{2,0,1:T(2,128)(2,1)} copy(bf16[2,512,256]{2,1,0:T(8,128)(2,1)S(1)} %fusion.12) | data formatting | bytes 1048576 | tf_op jit(solution)/shard_map/convert_element_type | solution.py:43
  18.5 18.0 %all-to-all-start = ((bf16[2,512,256]{2,0,1:T(2,128)(2,1)}), bf16[2,512,256]{2,0,1:T(2,128)(2,1)S(1)}, u32[]{:S(2)}, u32[]{:S(2)}) async-start(bf16[2,512,256]{2,0,1:T(2,128)(2,1)} %copy.31), calls=%async_computation | async-start | bytes 1048576 | tf_op jit(solution)/shard_map/all_to_all | solution.py:146
  36.5 0.1 fusion.70
  36.6 0.1 fusion.66
  36.8 0.1 fusion.68
  36.9 0.1 fusion.67
  37.1 0.3 fusion.65
  37.3 0.3 fusion.59
  37.7 0.0 copy-done.3
  37.7 32.5 %all-to-all-done = bf16[2,512,256]{2,0,1:T(2,128)(2,1)S(1)} async-done(((bf16[2,512,256]{2,0,1:T(2,128)(2,1)}), bf16[2,512,256]{2,0,1:T(2,128)(2,1)S(1)}, u32[]{:S(2)}, u32[]{:S(2)}) %all-to-all-start) | async-done | bytes 524320 | tf_op jit(solution)/shard_map/all_to_all | solution.py:146
  70.2 0.3 copy.74
  70.5 0.2 reshape.344
  70.7 0.6 convolution_bitcast_fusion.3
  71.3 0.2 multiply_subtract_fusion.1
  71.5 1.0 convolution_bitcast_fusion.2
  72.5 2.1 %fusion.23 = (f32[1,16,64,128]{3,2,1,0:T(8,128)S(1)}, f32[1,16,64,128]{3,2,1,0:T(8,128)S(1)}) fusion(f32[2,16,64,128]{3,2,1,0:T(8,128)S(1)} %convolution_bitcast_fusion.2, f32[64,128]{1,0:T(8,128)S(1)} %fusion.56, f32[16]{0:T(128)S(1)} %broadcast_multiply_fusion), kind=kLoop, calls=%fused_computation.39 | loop fusion | flops 1048576 | bytes 2129984 | tf_op jit(solution)/shard_map/sub | solution.py:25
  74.6 1.0 convolution_bitcast_fusion.1
  75.6 0.2 multiply_subtract_fusion
  75.8 1.1 fusion.11
  76.9 0.2 convert_element_type.148
  77.1 2.4 %collective-permute-start = (bf16[2,16,8192]{2,1,0:T(8,128)(2,1)S(1)}, bf16[2,16,8192]{2,1,0:T(8,128)(2,1)S(1)}, u32[]{:S(2)}, u32[]{:S(2)}) collective-permute-start(bf16[2,16,8192]{2,1,0:T(8,128)(2,1)S(1)} %convert_element_type.148), channel_id=1, source_target_pairs={{0,32},{32,160},{64,192},{96,64},{128,0},{160,128},{192,224},{224,... | collective-permute-start | bytes 1572872 | tf_op jit(solution)/shard_map/ppermute | solution.py:164
  79.6 2.1 %collective-permute-start.1 = (bf16[2,16,8192]{2,1,0:T(8,128)(2,1)S(1)}, bf16[2,16,8192]{2,1,0:T(8,128)(2,1)S(1)}, u32[]{:S(2)}, u32[]{:S(2)}) collective-permute-start(bf16[2,16,8192]{2,1,0:T(8,128)(2,1)S(1)} %convert_element_type.148), channel_id=1, source_target_pairs={{0,64},{32,288},{64,320},{96,32},{128,384},{160,224},{192,128},{22... | collective-permute-start | bytes 1572872 | tf_op jit(solution)/shard_map/ppermute | solution.py:164
  81.7 0.1 convert_element_type.149
  81.7 8.8 %collective-permute-done = bf16[2,16,8192]{2,1,0:T(8,128)(2,1)S(1)} collective-permute-done((bf16[2,16,8192]{2,1,0:T(8,128)(2,1)S(1)}, bf16[2,16,8192]{2,1,0:T(8,128)(2,1)S(1)}, u32[]{:S(2)}, u32[]{:S(2)}) %collective-permute-start) | collective-permute-done | bytes 524320 | tf_op jit(solution)/shard_map/ppermute | solution.py:164
  90.6 0.1 convert_element_type.150
  90.7 0.6 collective-permute-done.1
  91.3 0.1 convert_element_type.151
  91.4 0.2 add_bitcast_fusion.1
  91.6 0.1 copy.53
  91.7 0.1 copy.54
  91.8 0.1 copy.55
  91.9 0.1 copy.56
  92.0 0.0 copy-start.2
  92.0 0.2 maximum_reduce_fusion
  92.2 0.7 convolution_multiply_fusion
  93.0 0.1 copy.38
  93.1 0.2 slice.158
  93.3 7.2 %collective-permute-start.2 = (f32[2,4,512]{2,1,0:T(4,128)S(1)}, f32[2,4,512]{2,1,0:T(4,128)S(1)}, u32[]{:S(2)}, u32[]{:S(2)}) collective-permute-start(f32[2,4,512]{2,1,0:T(4,128)S(1)} %slice.158), channel_id=1, source_target_pairs={{64,0},{288,32},{320,64},{32,96},{384,128},{224,160},{128,192},{48... | collective-permute-start | bytes 49160 | tf_op jit(solution)/shard_map/ppermute | solution.py:167
  100.5 0.0 copy-done.2
  100.5 0.6 fusion.86
  105.0 0.1 copy.39
  105.1 0.2 slice.162
  105.3 1.9 %collective-permute-start.3 = (f32[2,4,512]{2,1,0:T(4,128)S(1)}, f32[2,4,512]{2,1,0:T(4,128)S(1)}, u32[]{:S(2)}, u32[]{:S(2)}) collective-permute-start(f32[2,4,512]{2,1,0:T(4,128)S(1)} %slice.162), channel_id=1, source_target_pairs={{32,0},{160,32},{192,64},{64,96},{0,128},{128,160},{224,192},{96,2... | collective-permute-start | bytes 49160 | tf_op jit(solution)/shard_map/ppermute | solution.py:167
  107.2 0.0 collective-permute-done.2
  107.2 5.2 %collective-permute-done.3 = f32[2,4,512]{2,1,0:T(4,128)S(1)} collective-permute-done((f32[2,4,512]{2,1,0:T(4,128)S(1)}, f32[2,4,512]{2,1,0:T(4,128)S(1)}, u32[]{:S(2)}, u32[]{:S(2)}) %collective-permute-start.3) | collective-permute-done | bytes 16416 | tf_op jit(solution)/shard_map/ppermute | solution.py:167
  112.4 0.6 maximum_bitcast_fusion.9
  113.1 0.6 maximum_bitcast_fusion.8
  (19 shorter events, 0.3 us)
Async XLA Ops:
  12.1 3.0 %copy-start = (bf16[256,1279]{1,0:T(8,128)(2,1)S(1)}, bf16[256,1279]{1,0:T(8,128)(2,1)}, u32[]{:S(2)}) copy-start(bf16[256,1279]{1,0:T(8,128)(2,1)} %neg.61) | copy-start | bytes 1964548
  12.1 3.1 %copy-start.1 = (bf16[256,1279]{1,0:T(8,128)(2,1)S(1)}, bf16[256,1279]{1,0:T(8,128)(2,1)}, u32[]{:S(2)}) copy-start(bf16[256,1279]{1,0:T(8,128)(2,1)} %reshape.340) | copy-start | bytes 1964548
  17.1 20.6 %copy-start.3 = (f32[16]{0:T(128)S(1)}, f32[16]{0:T(128)}, u32[]{:S(2)}) copy-start(f32[16]{0:T(128)} %param.8) | copy-start | bytes 196
  18.5 51.7 %all-to-all-start = ((bf16[2,512,256]{2,0,1:T(2,128)(2,1)}), bf16[2,512,256]{2,0,1:T(2,128)(2,1)S(1)}, u32[]{:S(2)}, u32[]{:S(2)}) async-start(bf16[2,512,256]{2,0,1:T(2,128)(2,1)} %copy.31), calls=%async_computation | async-start | bytes 1048576 | tf_op jit(solution)/shard_map/all_to_all | solution.py:146
  77.1 13.5 %collective-permute-start = (bf16[2,16,8192]{2,1,0:T(8,128)(2,1)S(1)}, bf16[2,16,8192]{2,1,0:T(8,128)(2,1)S(1)}, u32[]{:S(2)}, u32[]{:S(2)}) collective-permute-start(bf16[2,16,8192]{2,1,0:T(8,128)(2,1)S(1)} %convert_element_type.148), channel_id=1, source_target_pairs={{0,32},{32,160},{64,192},{96,64},{128,0},{160,128},{192,224},{224,... | collective-permute-start | bytes 1572872 | tf_op jit(solution)/shard_map/ppermute | solution.py:164
  79.6 11.7 %collective-permute-start.1 = (bf16[2,16,8192]{2,1,0:T(8,128)(2,1)S(1)}, bf16[2,16,8192]{2,1,0:T(8,128)(2,1)S(1)}, u32[]{:S(2)}, u32[]{:S(2)}) collective-permute-start(bf16[2,16,8192]{2,1,0:T(8,128)(2,1)S(1)} %convert_element_type.148), channel_id=1, source_target_pairs={{0,64},{32,288},{64,320},{96,32},{128,384},{160,224},{192,128},{22... | collective-permute-start | bytes 1572872 | tf_op jit(solution)/shard_map/ppermute | solution.py:164
  92.0 8.5 %copy-start.2 = (s32[1,2]{1,0:T(1,128)S(1)}, s32[1,2]{1,0:T(1,128)}, u32[]{:S(2)}) copy-start(s32[1,2]{1,0:T(1,128)} %param.9) | copy-start | bytes 28
  93.3 13.9 %collective-permute-start.2 = (f32[2,4,512]{2,1,0:T(4,128)S(1)}, f32[2,4,512]{2,1,0:T(4,128)S(1)}, u32[]{:S(2)}, u32[]{:S(2)}) collective-permute-start(f32[2,4,512]{2,1,0:T(4,128)S(1)} %slice.158), channel_id=1, source_target_pairs={{64,0},{288,32},{320,64},{32,96},{384,128},{224,160},{128,192},{48... | collective-permute-start | bytes 49160 | tf_op jit(solution)/shard_map/ppermute | solution.py:167
  105.3 7.1 %collective-permute-start.3 = (f32[2,4,512]{2,1,0:T(4,128)S(1)}, f32[2,4,512]{2,1,0:T(4,128)S(1)}, u32[]{:S(2)}, u32[]{:S(2)}) collective-permute-start(f32[2,4,512]{2,1,0:T(4,128)S(1)} %slice.162), channel_id=1, source_target_pairs={{32,0},{160,32},{192,64},{64,96},{0,128},{128,160},{224,192},{96,2... | collective-permute-start | bytes 49160 | tf_op jit(solution)/shard_map/ppermute | solution.py:167

commit v2 on v1

--- a/solution.py
+++ b/solution.py
@@ -3,6 +3,8 @@
 import jax
 import jax.numpy as jnp
 from jax import lax
+from jax.experimental import pallas as pl
+from jax.experimental.pallas import tpu as pltpu
 from jax.sharding import PartitionSpec as P
 
 RNG = 512
@@ -25,19 +27,35 @@
     return (left_re * right_re - left_im * right_im, left_re * right_im + left_im * right_re)
 
 
-def compress(echoes, toeplitz, first_pulse, live_pulses, block_cols, window):
+def band_kernel(re_ref, im_ref, first_ref, second_ref):
+    width = first_ref.shape[1]
+    span = re_ref.shape[1]
+    block = 128
+    for start in range(0, RNG, block):
+        re_band = pltpu.roll(jnp.broadcast_to(re_ref[...], (block, span)), start, 1, stride=1, stride_axis=0)
+        im_band = pltpu.roll(jnp.broadcast_to(im_ref[...], (block, span)), start, 1, stride=1, stride_axis=0)
+        first_ref[start : start + block, :] = re_band[:, :width].astype(first_ref.dtype)
+        first_ref[RNG + start : RNG + start + block, :] = (-im_band)[:, :width].astype(first_ref.dtype)
+        second_ref[start : start + block, :] = im_band[:, :width].astype(second_ref.dtype)
+        second_ref[RNG + start : RNG + start + block, :] = re_band[:, :width].astype(second_ref.dtype)
+
+
+def band_tables(table_re, table_im, width):
+    span = -(-(width + 1) // 128) * 128
+    pad = jnp.zeros((span - table_re.shape[0],), jnp.float32)
+    re_row = jnp.concatenate([table_re.astype(jnp.float32), pad])[None]
+    im_row = jnp.concatenate([table_im.astype(jnp.float32), pad])[None]
+    shape = jax.ShapeDtypeStruct((2 * RNG, width), jnp.bfloat16)
+    return pl.pallas_call(band_kernel, out_shape=[shape, shape])(re_row, im_row)
+
+
+def compress(echoes, first_band, second_band, first_pulse, live_pulses):
     pulse_rows = echoes.shape[1]
-    parts_re = []
-    parts_im = []
-    for start in range(0, RNG, block_cols):
-        segment = echoes[:, :, start : start + window]
-        stacked = jnp.concatenate([segment[0], segment[1]], axis=1)
-        result = lax.dot_general(
-            toeplitz, stacked, (((1,), (1,)), ((), ())), preferred_element_type=jnp.float32
-        )
-        parts_re.append(result[:block_cols])
-        parts_im.append(result[block_cols:])
-    joined = jnp.stack([jnp.concatenate(parts_re, axis=0), jnp.concatenate(parts_im, axis=0)])
+    dims = (((1,), (1,)), ((), ()))
+    result = lax.dot_general(
+        first_band, echoes[0], dims, preferred_element_type=jnp.float32
+    ) + lax.dot_general(second_band, echoes[1], dims, preferred_element_type=jnp.float32)
+    joined = result.reshape(2, RNG, pulse_rows)
     pulse_ids = first_pulse + jnp.arange(pulse_rows, dtype=jnp.int32)
     keep = (pulse_ids < live_pulses).astype(jnp.float32)
     return (joined * keep[None, None, :]).astype(jnp.bfloat16)
@@ -124,25 +142,13 @@
 def per_device(raw_echo, chirp_phase, pulse_counts, azimuth_rate, partner_bits):
     echoes = raw_echo[0]
     pulses_dev = echoes.shape[1]
-    block_cols = min(256, RNG)
-    window = block_cols + TAPS - 1
     amplitude = 2.0 / math.sqrt(TAPS)
     table_re = (amplitude * jnp.cos(chirp_phase)).astype(jnp.bfloat16)
     table_im = (amplitude * jnp.sin(chirp_phase)).astype(jnp.bfloat16)
-    padding = jnp.zeros((block_cols,), jnp.bfloat16)
-    band_re = jnp.tile(jnp.concatenate([table_re, padding]), block_cols)[
-        : block_cols * window
-    ].reshape(block_cols, window)
-    band_im = jnp.tile(jnp.concatenate([table_im, padding]), block_cols)[
-        : block_cols * window
-    ].reshape(block_cols, window)
-    toeplitz = jnp.concatenate(
-        [jnp.concatenate([band_re, band_im], axis=1), jnp.concatenate([-band_im, band_re], axis=1)],
-        axis=0,
-    )
+    first_band, second_band = band_tables(table_re, table_im, echoes.shape[2])
     live_pulses = pulse_counts[0]
     first_pulse = lax.axis_index("pulse") * pulses_dev
-    compressed = compress(echoes, toeplitz, first_pulse, live_pulses, block_cols, window)
+    compressed = compress(echoes, first_band, second_band, first_pulse, live_pulses)
     turned = lax.all_to_all(compressed, "pulse", split_axis=1, concat_axis=2, tiled=True)
     focused = azimuth(turned, azimuth_rate).astype(jnp.bfloat16)
     chosen = partner_bits[0]

time: 114 us -> 119 us (1.044)
  the two profiles are of different devices: /device:TPU:36 before, /device:TPU:32 now
where the time goes in v2:
time: 119 us; the launch traced here: 118 us
  waiting for transfers between devices  46.6 us (39%)
  starting transfers between devices  30.6 us (26%)
  local copies, waits for them, and re-layouts  16.2 us (14%)
  matrix products  8.49 us (7%)
  other arithmetic  6.37 us (5%)
  between operations  5.58 us (5%)
  Pallas kernels  4.57 us (4%)
    all_to_all x1, waiting for transfers between devices, per_device(): lax.all_to_all(compressed, 'pulse', split_axis=1, concat_axis=2, tiled=True)  32.5 us
    all_to_all x1, starting transfers between devices, per_device(): lax.all_to_all(compressed, 'pulse', split_axis=1, concat_axis=2, tiled=True)  18 us
    ppermute x2, waiting for transfers between devices, per_device(): arrived = [lax.ppermute(focused, 'acq', pairs) for pairs in edge_pairs]  10.5 us
    ppermute x2, starting transfers between devices, per_device(): lax.ppermute(looked[slot], 'acq', [(dst, src) for src, dst in edge_pairs[...  7.26 us
    unnamed x14, local copies, waits for them, and re-layouts  7.21 us
    ppermute x2, starting transfers between devices, per_device(): arrived = [lax.ppermute(focused, 'acq', pairs) for pairs in edge_pairs]  5.34 us
    pallas_call x1, Pallas kernels, band_tables(): return pl.pallas_call(band_kernel, out_shape=[shape, shape])(re_row, im_row)  4.57 us
    slice x1, local copies, waits for them, and re-layouts, compress(): echoes[1]  4.55 us
  transfers between devices with their start and end apart: 5, of which 4 were waited for; matrix products, arithmetic and copies ran while one was open for 2% of the time, Pallas kernels for 0%

profile of v2, /device:TPU:32, one launch (start us, length us, event | category | flops | bytes accessed | tf_op | source)
XLA Modules:
  0.0 118.4 jit_solution(11797920836125691311)
XLA Ops:
  1.3 0.7 multiply_convert_fusion.1
  2.0 0.6 reshape.342.im_ref
  2.6 0.6 reshape.341.re_ref
  3.2 4.6 %fusion.68 = (bf16[1,1,256,1535]{2,1,3,0:T(2,128)(2,1)S(1)}, bf16[1,1,256,1535]{2,1,3,0:T(2,128)(2,1)S(1)}) fusion(bf16[1,2,256,1535]{2,1,3,0:T(2,128)(2,1)} %param.5), kind=kLoop, calls=%fused_computation.131 | loop fusion | bytes 3143680 | tf_op jit(solution)/shard_map/slice | solution.py:57
  7.8 3.9 %copy.67 = bf16[1,1,256,1535]{3,2,1,0:T(8,128)(2,1)} copy(bf16[1,1,256,1535]{2,1,3,0:T(2,128)(2,1)S(1)} %get-tuple-element.10) | data formatting | bytes 1571840
  11.7 2.9 %copy.66 = bf16[1,1,256,1535]{3,2,1,0:T(8,128)(2,1)S(1)} copy(bf16[1,1,256,1535]{2,1,3,0:T(2,128)(2,1)S(1)} %get-tuple-element.11) | data formatting | bytes 1571840
  14.6 4.6 %shard_map.68 = (bf16[1024,1535]{1,0:T(8,128)(2,1)}, bf16[1024,1535]{1,0:T(8,128)(2,1)}) custom-call(f32[1,1536]{1,0:T(1,128)} %reshape.341.re_ref, f32[1,1536]{1,0:T(1,128)} %reshape.342.im_ref), custom_call_target="tpu_custom_call" | custom-call | tf_op jit(solution)/shard_map/pallas_call | solution.py:49
  19.2 0.0 copy-start
  19.2 0.0 copy-start.1
  19.2 3.1 %fusion.10 = f32[1024,256]{1,0:T(8,128)S(1)} fusion(bf16[1024,1535]{1,0:T(8,128)(2,1)} %get-tuple-element.4, bf16[1,1,256,1535]{3,2,1,0:T(8,128)(2,1)S(1)} %copy.66), kind=kOutput, calls=%fused_computation.21 | convolution fusion | flops 804782080 | bytes 4978176 | tf_op jit(solution)/shard_map/dot_general | solution.py:55
  22.2 0.0 copy-done
  22.2 0.0 copy-done.1
  22.2 1.0 convolution_add_fusion
  23.3 0.1 multiply_convert_fusion
  23.4 0.0 copy-start.3
  23.4 1.4 %copy.44 = bf16[2,512,256]{2,0,1:T(2,128)(2,1)} copy(bf16[2,512,256]{2,1,0:T(8,128)(2,1)S(1)} %multiply_convert_fusion) | data formatting | bytes 1048576 | tf_op jit(solution)/shard_map/convert_element_type | solution.py:61
  24.7 18.0 %all-to-all-start = ((bf16[2,512,256]{2,0,1:T(2,128)(2,1)}), bf16[2,512,256]{2,0,1:T(2,128)(2,1)S(1)}, u32[]{:S(2)}, u32[]{:S(2)}) async-start(bf16[2,512,256]{2,0,1:T(2,128)(2,1)} %copy.44), calls=%async_computation | async-start | bytes 1048576 | tf_op jit(solution)/shard_map/all_to_all | solution.py:152
  42.7 0.1 fusion.61
  42.9 0.1 fusion.57
  43.0 0.3 fusion.56
  43.3 0.1 fusion.59
  43.4 0.1 fusion.58
  43.6 0.3 fusion.50
  44.0 0.0 copy-done.3
  44.0 32.5 %all-to-all-done = bf16[2,512,256]{2,0,1:T(2,128)(2,1)S(1)} async-done(((bf16[2,512,256]{2,0,1:T(2,128)(2,1)}), bf16[2,512,256]{2,0,1:T(2,128)(2,1)S(1)}, u32[]{:S(2)}, u32[]{:S(2)}) %all-to-all-start) | async-done | bytes 524320 | tf_op jit(solution)/shard_map/all_to_all | solution.py:152
  76.5 0.3 copy.89
  76.8 0.2 reshape.344
  77.0 0.6 convolution_bitcast_fusion.3
  77.6 0.2 multiply_subtract_fusion.1
  77.7 1.0 convolution_bitcast_fusion.2
  78.8 2.1 %fusion.14 = (f32[1,16,64,128]{3,2,1,0:T(8,128)S(1)}, f32[1,16,64,128]{3,2,1,0:T(8,128)S(1)}) fusion(f32[2,16,64,128]{3,2,1,0:T(8,128)S(1)} %convolution_bitcast_fusion.2, f32[64,128]{1,0:T(8,128)S(1)} %fusion.47, f32[16]{0:T(128)S(1)} %broadcast_multiply_fusion), kind=kLoop, calls=%fused_computation.27 | loop fusion | flops 1048576 | bytes 2129984 | tf_op jit(solution)/shard_map/sub | solution.py:27
  80.9 1.0 convolution_bitcast_fusion.1
  81.9 0.2 multiply_subtract_fusion
  82.1 1.1 fusion.2
  83.2 0.2 convert_element_type.150
  83.4 3.4 %collective-permute-start.1 = (bf16[2,16,8192]{2,1,0:T(8,128)(2,1)S(1)}, bf16[2,16,8192]{2,1,0:T(8,128)(2,1)S(1)}, u32[]{:S(2)}, u32[]{:S(2)}) collective-permute-start(bf16[2,16,8192]{2,1,0:T(8,128)(2,1)S(1)} %convert_element_type.150), channel_id=1, source_target_pairs={{0,64},{32,288},{64,320},{96,32},{128,384},{160,224},{192,128},{22... | collective-permute-start | bytes 1572872 | tf_op jit(solution)/shard_map/ppermute | solution.py:170
  86.8 1.9 %collective-permute-start = (bf16[2,16,8192]{2,1,0:T(8,128)(2,1)S(1)}, bf16[2,16,8192]{2,1,0:T(8,128)(2,1)S(1)}, u32[]{:S(2)}, u32[]{:S(2)}) collective-permute-start(bf16[2,16,8192]{2,1,0:T(8,128)(2,1)S(1)} %convert_element_type.150), channel_id=1, source_target_pairs={{0,32},{32,160},{64,192},{96,64},{128,0},{160,128},{192,224},{224,... | collective-permute-start | bytes 1572872 | tf_op jit(solution)/shard_map/ppermute | solution.py:170
  88.8 0.1 convert_element_type.151
  88.8 9.0 %collective-permute-done.1 = bf16[2,16,8192]{2,1,0:T(8,128)(2,1)S(1)} collective-permute-done((bf16[2,16,8192]{2,1,0:T(8,128)(2,1)S(1)}, bf16[2,16,8192]{2,1,0:T(8,128)(2,1)S(1)}, u32[]{:S(2)}, u32[]{:S(2)}) %collective-permute-start.1) | collective-permute-done | bytes 524320 | tf_op jit(solution)/shard_map/ppermute | solution.py:170
  97.9 0.1 convert_element_type.153
  97.9 1.5 %collective-permute-done = bf16[2,16,8192]{2,1,0:T(8,128)(2,1)S(1)} collective-permute-done((bf16[2,16,8192]{2,1,0:T(8,128)(2,1)S(1)}, bf16[2,16,8192]{2,1,0:T(8,128)(2,1)S(1)}, u32[]{:S(2)}, u32[]{:S(2)}) %collective-permute-start) | collective-permute-done | bytes 524320 | tf_op jit(solution)/shard_map/ppermute | solution.py:170
  99.4 0.1 convert_element_type.152
  99.5 0.2 add_bitcast_fusion.1
  99.7 0.1 copy.68
  99.8 0.1 copy.69
  99.9 0.1 copy.71
  100.1 0.1 copy.70
  100.2 0.0 copy-start.2
  100.2 0.2 maximum_reduce_fusion
  100.4 0.7 convolution_multiply_fusion
  101.1 0.1 copy.52
  101.2 0.2 slice.126
  101.4 5.3 %collective-permute-start.3 = (f32[2,4,512]{2,1,0:T(4,128)S(1)}, f32[2,4,512]{2,1,0:T(4,128)S(1)}, u32[]{:S(2)}, u32[]{:S(2)}) collective-permute-start(f32[2,4,512]{2,1,0:T(4,128)S(1)} %slice.126), channel_id=1, source_target_pairs={{32,0},{160,32},{192,64},{64,96},{0,128},{128,160},{224,192},{96,2... | collective-permute-start | bytes 49160 | tf_op jit(solution)/shard_map/ppermute | solution.py:173
  106.7 0.0 copy-done.2
  106.7 0.6 fusion.74
  111.2 0.1 copy.51
  111.4 0.2 slice.122
  111.5 1.9 %collective-permute-start.2 = (f32[2,4,512]{2,1,0:T(4,128)S(1)}, f32[2,4,512]{2,1,0:T(4,128)S(1)}, u32[]{:S(2)}, u32[]{:S(2)}) collective-permute-start(f32[2,4,512]{2,1,0:T(4,128)S(1)} %slice.122), channel_id=1, source_target_pairs={{64,0},{288,32},{320,64},{32,96},{384,128},{224,160},{128,192},{48... | collective-permute-start | bytes 49160 | tf_op jit(solution)/shard_map/ppermute | solution.py:173
  113.4 0.0 collective-permute-done.3
  113.5 3.7 %collective-permute-done.2 = f32[2,4,512]{2,1,0:T(4,128)S(1)} collective-permute-done((f32[2,4,512]{2,1,0:T(4,128)S(1)}, f32[2,4,512]{2,1,0:T(4,128)S(1)}, u32[]{:S(2)}, u32[]{:S(2)}) %collective-permute-start.2) | collective-permute-done | bytes 16416 | tf_op jit(solution)/shard_map/ppermute | solution.py:173
  117.2 0.6 maximum_bitcast_fusion.7
  117.8 0.6 maximum_bitcast_fusion.6
  (14 shorter events, 0.2 us)
Async XLA Ops:
  19.2 3.1 %copy-start = (bf16[1024,1535]{1,0:T(8,128)(2,1)S(1)}, bf16[1024,1535]{1,0:T(8,128)(2,1)}, u32[]{:S(2)}) copy-start(bf16[1024,1535]{1,0:T(8,128)(2,1)} %get-tuple-element.5) | copy-start | bytes 9431044
  19.2 3.1 %copy-start.1 = (bf16[1,1,256,1535]{3,2,1,0:T(8,128)(2,1)S(1)}, bf16[1,1,256,1535]{3,2,1,0:T(8,128)(2,1)}, u32[]{:S(2)}) copy-start(bf16[1,1,256,1535]{3,2,1,0:T(8,128)(2,1)} %copy.67) | copy-start | bytes 2357764
  23.4 20.6 %copy-start.3 = (f32[16]{0:T(128)S(1)}, f32[16]{0:T(128)}, u32[]{:S(2)}) copy-start(f32[16]{0:T(128)} %param.8) | copy-start | bytes 196
  24.7 51.7 %all-to-all-start = ((bf16[2,512,256]{2,0,1:T(2,128)(2,1)}), bf16[2,512,256]{2,0,1:T(2,128)(2,1)S(1)}, u32[]{:S(2)}, u32[]{:S(2)}) async-start(bf16[2,512,256]{2,0,1:T(2,128)(2,1)} %copy.44), calls=%async_computation | async-start | bytes 1048576 | tf_op jit(solution)/shard_map/all_to_all | solution.py:152
  83.4 14.5 %collective-permute-start.1 = (bf16[2,16,8192]{2,1,0:T(8,128)(2,1)S(1)}, bf16[2,16,8192]{2,1,0:T(8,128)(2,1)S(1)}, u32[]{:S(2)}, u32[]{:S(2)}) collective-permute-start(bf16[2,16,8192]{2,1,0:T(8,128)(2,1)S(1)} %convert_element_type.150), channel_id=1, source_target_pairs={{0,64},{32,288},{64,320},{96,32},{128,384},{160,224},{192,128},{22... | collective-permute-start | bytes 1572872 | tf_op jit(solution)/shard_map/ppermute | solution.py:170
  86.8 12.6 %collective-permute-start = (bf16[2,16,8192]{2,1,0:T(8,128)(2,1)S(1)}, bf16[2,16,8192]{2,1,0:T(8,128)(2,1)S(1)}, u32[]{:S(2)}, u32[]{:S(2)}) collective-permute-start(bf16[2,16,8192]{2,1,0:T(8,128)(2,1)S(1)} %convert_element_type.150), channel_id=1, source_target_pairs={{0,32},{32,160},{64,192},{96,64},{128,0},{160,128},{192,224},{224,... | collective-permute-start | bytes 1572872 | tf_op jit(solution)/shard_map/ppermute | solution.py:170
  100.2 6.6 %copy-start.2 = (s32[1,2]{1,0:T(1,128)S(1)}, s32[1,2]{1,0:T(1,128)}, u32[]{:S(2)}) copy-start(s32[1,2]{1,0:T(1,128)} %param.9) | copy-start | bytes 28
  101.4 12.1 %collective-permute-start.3 = (f32[2,4,512]{2,1,0:T(4,128)S(1)}, f32[2,4,512]{2,1,0:T(4,128)S(1)}, u32[]{:S(2)}, u32[]{:S(2)}) collective-permute-start(f32[2,4,512]{2,1,0:T(4,128)S(1)} %slice.126), channel_id=1, source_target_pairs={{32,0},{160,32},{192,64},{64,96},{0,128},{128,160},{224,192},{96,2... | collective-permute-start | bytes 49160 | tf_op jit(solution)/shard_map/ppermute | solution.py:173
  111.5 5.6 %collective-permute-start.2 = (f32[2,4,512]{2,1,0:T(4,128)S(1)}, f32[2,4,512]{2,1,0:T(4,128)S(1)}, u32[]{:S(2)}, u32[]{:S(2)}) collective-permute-start(f32[2,4,512]{2,1,0:T(4,128)S(1)} %slice.122), channel_id=1, source_target_pairs={{64,0},{288,32},{320,64},{32,96},{384,128},{224,160},{128,192},{48... | collective-permute-start | bytes 49160 | tf_op jit(solution)/shard_map/ppermute | solution.py:173

commit v3 on v2

--- a/solution.py
+++ b/solution.py
@@ -27,34 +27,45 @@
     return (left_re * right_re - left_im * right_im, left_re * right_im + left_im * right_re)
 
 
-def band_kernel(re_ref, im_ref, first_ref, second_ref):
-    width = first_ref.shape[1]
+def band_kernel(re_ref, im_ref, band_ref):
+    block = band_ref.shape[2]
+    width = band_ref.shape[3]
     span = re_ref.shape[1]
-    block = 128
-    for start in range(0, RNG, block):
-        re_band = pltpu.roll(jnp.broadcast_to(re_ref[...], (block, span)), start, 1, stride=1, stride_axis=0)
-        im_band = pltpu.roll(jnp.broadcast_to(im_ref[...], (block, span)), start, 1, stride=1, stride_axis=0)
-        first_ref[start : start + block, :] = re_band[:, :width].astype(first_ref.dtype)
-        first_ref[RNG + start : RNG + start + block, :] = (-im_band)[:, :width].astype(first_ref.dtype)
-        second_ref[start : start + block, :] = im_band[:, :width].astype(second_ref.dtype)
-        second_ref[RNG + start : RNG + start + block, :] = re_band[:, :width].astype(second_ref.dtype)
+    re_band = pltpu.roll(jnp.broadcast_to(re_ref[0:1, :], (block, span)), 0, 1, stride=1, stride_axis=0)
+    im_band = pltpu.roll(jnp.broadcast_to(im_ref[0:1, :], (block, span)), 0, 1, stride=1, stride_axis=0)
+    band_ref[0, 0] = re_band[:, :width].astype(band_ref.dtype)
+    band_ref[0, 1] = (-im_band)[:, :width].astype(band_ref.dtype)
+    band_ref[1, 0] = im_band[:, :width].astype(band_ref.dtype)
+    band_ref[1, 1] = re_band[:, :width].astype(band_ref.dtype)
 
 
 def band_tables(table_re, table_im, width):
     span = -(-(width + 1) // 128) * 128
+    block = 128
+    steps = RNG // block
     pad = jnp.zeros((span - table_re.shape[0],), jnp.float32)
-    re_row = jnp.concatenate([table_re.astype(jnp.float32), pad])[None]
-    im_row = jnp.concatenate([table_im.astype(jnp.float32), pad])[None]
-    shape = jax.ShapeDtypeStruct((2 * RNG, width), jnp.bfloat16)
-    return pl.pallas_call(band_kernel, out_shape=[shape, shape])(re_row, im_row)
-
-
-def compress(echoes, first_band, second_band, first_pulse, live_pulses):
+    rows = []
+    for table in (table_re, table_im):
+        row = jnp.concatenate([table.astype(jnp.float32), pad])
+        shifted = jnp.stack([jnp.roll(row, block * step) for step in range(steps)])
+        rows.append(jnp.repeat(shifted, 8, axis=0))
+    row_spec = pl.BlockSpec((8, span), lambda i: (i, 0))
+    out_spec = pl.BlockSpec((2, 2, block, width), lambda i: (0, 0, i, 0))
+    shape = jax.ShapeDtypeStruct((2, 2, RNG, width), jnp.bfloat16)
+    band = pl.pallas_call(
+        band_kernel,
+        grid=(steps,),
+        in_specs=[row_spec, row_spec],
+        out_specs=out_spec,
+        out_shape=shape,
+    )(*rows)
+    return band.reshape(2, 2 * RNG, width)
+
+
+def compress(echoes, band, first_pulse, live_pulses):
     pulse_rows = echoes.shape[1]
-    dims = (((1,), (1,)), ((), ()))
-    result = lax.dot_general(
-        first_band, echoes[0], dims, preferred_element_type=jnp.float32
-    ) + lax.dot_general(second_band, echoes[1], dims, preferred_element_type=jnp.float32)
+    dims = (((0, 2), (0, 2)), ((), ()))
+    result = lax.dot_general(band, echoes, dims, preferred_element_type=jnp.float32)
     joined = result.reshape(2, RNG, pulse_rows)
     pulse_ids = first_pulse + jnp.arange(pulse_rows, dtype=jnp.int32)
     keep = (pulse_ids < live_pulses).astype(jnp.float32)
@@ -145,10 +156,10 @@
     amplitude = 2.0 / math.sqrt(TAPS)
     table_re = (amplitude * jnp.cos(chirp_phase)).astype(jnp.bfloat16)
     table_im = (amplitude * jnp.sin(chirp_phase)).astype(jnp.bfloat16)
-    first_band, second_band = band_tables(table_re, table_im, echoes.shape[2])
+    band = band_tables(table_re, table_im, echoes.shape[2])
     live_pulses = pulse_counts[0]
     first_pulse = lax.axis_index("pulse") * pulses_dev
-    compressed = compress(echoes, first_band, second_band, first_pulse, live_pulses)
+    compressed = compress(echoes, band, first_pulse, live_pulses)
     turned = lax.all_to_all(compressed, "pulse", split_axis=1, concat_axis=2, tiled=True)
     focused = azimuth(turned, azimuth_rate).astype(jnp.bfloat16)
     chosen = partner_bits[0]

time: 119 us -> 110 us (0.924)
  the two profiles are of different devices: /device:TPU:32 before, /device:TPU:36 now
where the time goes in v3:
time: 110 us
  waiting for transfers between devices  47.1 us (43%)
  starting transfers between devices  31.6 us (29%)
  matrix products  9.01 us (8%)
  other arithmetic  6.44 us (6%)
  between operations  5.65 us (5%)
  local copies, waits for them, and re-layouts  5.16 us (5%)
  Pallas kernels  4.76 us (4%)
    all_to_all x1, waiting for transfers between devices, per_device(): lax.all_to_all(compressed, 'pulse', split_axis=1, concat_axis=2, tiled=True)  32.5 us
    all_to_all x1, starting transfers between devices, per_device(): lax.all_to_all(compressed, 'pulse', split_axis=1, concat_axis=2, tiled=True)  18 us
    ppermute x2, waiting for transfers between devices, per_device(): arrived = [lax.ppermute(focused, 'acq', pairs) for pairs in edge_pairs]  9.45 us
    ppermute x2, starting transfers between devices, per_device(): lax.ppermute(looked[slot], 'acq', [(dst, src) for src, dst in edge_pairs[...  9.11 us
    ppermute x2, waiting for transfers between devices, per_device(): lax.ppermute(looked[slot], 'acq', [(dst, src) for src, dst in edge_pairs[...  5.19 us
    pallas_call x1, Pallas kernels, band_tables(): pl.pallas_call(band_kernel, grid=(steps,), in_specs=[row_spec, row_spec],...  4.76 us
    dot_general x1, matrix products, compress(): lax.dot_general(band, echoes, dims, preferred_element_type=jnp.float32)  4.57 us
    ppermute x2, starting transfers between devices, per_device(): arrived = [lax.ppermute(focused, 'acq', pairs) for pairs in edge_pairs]  4.5 us
  transfers between devices with their start and end apart: 5, of which 4 were waited for; matrix products, arithmetic and copies ran while one was open for 2% of the time, Pallas kernels for 0%

profile of v3, /device:TPU:36, one launch (start us, length us, event | category | flops | bytes accessed | tf_op | source)
XLA Modules:
  0.0 109.7 jit_solution(130554896817631373)
XLA Ops:
  0.6 0.0 copy-start
  0.6 0.8 multiply_convert_fusion
  1.6 0.7 broadcast_bitcast_fusion.im_ref
  2.5 0.7 broadcast_bitcast_fusion.1.re_ref
  3.8 4.8 %shard_map.68 = bf16[2,2,512,1535]{3,2,1,0:T(8,128)(2,1)} custom-call(f32[32,1536]{1,0:T(8,128)} %broadcast_bitcast_fusion.1.re_ref, f32[32,1536]{1,0:T(8,128)} %broadcast_bitcast_fusion.im_ref), custom_call_target="tpu_custom_call" | custom-call | tf_op jit(solution)/shard_map/pallas_call | solution.py:55
  8.6 0.0 copy-done
  8.6 4.6 %fusion.14 = bf16[2,512,256]{2,1,0:T(8,128)(2,1)S(1)} fusion(bf16[2,256,1535,1]{1,0,2,3:T(2,128)(2,1)S(1)} %bitcast.154, bf16[2,2,512,1535]{3,2,1,0:T(8,128)(2,1)} %shard_map.68, f32[256]{0:T(256)S(1)} %compare_convert_fusion), kind=kOutput, calls=%fused_computation.11 | convolution fusion | flops 1610088448 | bytes 8384512 | tf_op jit(solution)/shard_map/dot_general | solution.py:68
  13.2 0.0 copy-start.2
  13.2 1.3 %copy.31 = bf16[2,512,256]{2,0,1:T(2,128)(2,1)} copy(bf16[2,512,256]{2,1,0:T(8,128)(2,1)S(1)} %fusion.14) | data formatting | bytes 1048576 | tf_op jit(solution)/shard_map/convert_element_type | solution.py:72
  14.5 18.0 %all-to-all-start = ((bf16[2,512,256]{2,0,1:T(2,128)(2,1)}), bf16[2,512,256]{2,0,1:T(2,128)(2,1)S(1)}, u32[]{:S(2)}, u32[]{:S(2)}) async-start(bf16[2,512,256]{2,0,1:T(2,128)(2,1)} %copy.31), calls=%async_computation | async-start | bytes 1048576 | tf_op jit(solution)/shard_map/all_to_all | solution.py:163
  32.5 0.1 fusion.76
  32.7 0.1 fusion.72
  32.8 0.1 fusion.74
  33.0 0.1 fusion.73
  33.1 0.3 fusion.71
  33.4 0.3 fusion.65
  33.8 0.0 copy-done.2
  33.8 32.5 %all-to-all-done = bf16[2,512,256]{2,0,1:T(2,128)(2,1)S(1)} async-done(((bf16[2,512,256]{2,0,1:T(2,128)(2,1)}), bf16[2,512,256]{2,0,1:T(2,128)(2,1)S(1)}, u32[]{:S(2)}, u32[]{:S(2)}) %all-to-all-start) | async-done | bytes 524320 | tf_op jit(solution)/shard_map/all_to_all | solution.py:163
  66.3 0.3 copy.85
  66.6 0.2 reshape.350
  66.8 0.6 convolution_bitcast_fusion.3
  67.4 0.2 multiply_subtract_fusion.1
  67.6 1.0 convolution_bitcast_fusion.2
  68.6 2.1 %fusion.29 = (f32[1,16,64,128]{3,2,1,0:T(8,128)S(1)}, f32[1,16,64,128]{3,2,1,0:T(8,128)S(1)}) fusion(f32[2,16,64,128]{3,2,1,0:T(8,128)S(1)} %convolution_bitcast_fusion.2, f32[64,128]{1,0:T(8,128)S(1)} %fusion.62, f32[16]{0:T(128)S(1)} %broadcast_multiply_fusion), kind=kLoop, calls=%fused_computation.28 | loop fusion | flops 1048576 | bytes 2129984 | tf_op jit(solution)/shard_map/sub | solution.py:27
  70.7 1.0 convolution_bitcast_fusion.1
  71.7 0.2 multiply_subtract_fusion
  71.9 1.1 fusion.20
  73.0 0.2 convert_element_type.150
  73.2 2.4 %collective-permute-start = (bf16[2,16,8192]{2,1,0:T(8,128)(2,1)S(1)}, bf16[2,16,8192]{2,1,0:T(8,128)(2,1)S(1)}, u32[]{:S(2)}, u32[]{:S(2)}) collective-permute-start(bf16[2,16,8192]{2,1,0:T(8,128)(2,1)S(1)} %convert_element_type.150), channel_id=1, source_target_pairs={{0,32},{32,160},{64,192},{96,64},{128,0},{160,128},{192,224},{224,... | collective-permute-start | bytes 1572872 | tf_op jit(solution)/shard_map/ppermute | solution.py:181
  75.6 2.1 %collective-permute-start.1 = (bf16[2,16,8192]{2,1,0:T(8,128)(2,1)S(1)}, bf16[2,16,8192]{2,1,0:T(8,128)(2,1)S(1)}, u32[]{:S(2)}, u32[]{:S(2)}) collective-permute-start(bf16[2,16,8192]{2,1,0:T(8,128)(2,1)S(1)} %convert_element_type.150), channel_id=1, source_target_pairs={{0,64},{32,288},{64,320},{96,32},{128,384},{160,224},{192,128},{22... | collective-permute-start | bytes 1572872 | tf_op jit(solution)/shard_map/ppermute | solution.py:181
  77.8 0.1 convert_element_type.151
  77.8 8.8 %collective-permute-done = bf16[2,16,8192]{2,1,0:T(8,128)(2,1)S(1)} collective-permute-done((bf16[2,16,8192]{2,1,0:T(8,128)(2,1)S(1)}, bf16[2,16,8192]{2,1,0:T(8,128)(2,1)S(1)}, u32[]{:S(2)}, u32[]{:S(2)}) %collective-permute-start) | collective-permute-done | bytes 524320 | tf_op jit(solution)/shard_map/ppermute | solution.py:181
  86.6 0.1 convert_element_type.152
  86.7 0.7 collective-permute-done.1
  87.4 0.1 convert_element_type.153
  87.4 0.2 add_bitcast_fusion.1
  87.7 0.1 copy.56
  87.8 0.1 copy.57
  87.9 0.1 copy.58
  88.0 0.1 copy.59
  88.1 0.0 copy-start.1
  88.1 0.2 maximum_reduce_fusion
  88.3 0.7 convolution_multiply_fusion
  89.1 0.1 copy.38
  89.2 0.2 slice.148
  89.4 7.2 %collective-permute-start.2 = (f32[2,4,512]{2,1,0:T(4,128)S(1)}, f32[2,4,512]{2,1,0:T(4,128)S(1)}, u32[]{:S(2)}, u32[]{:S(2)}) collective-permute-start(f32[2,4,512]{2,1,0:T(4,128)S(1)} %slice.148), channel_id=1, source_target_pairs={{64,0},{288,32},{320,64},{32,96},{384,128},{224,160},{128,192},{48... | collective-permute-start | bytes 49160 | tf_op jit(solution)/shard_map/ppermute | solution.py:184
  96.6 0.0 copy-done.1
  96.6 0.6 fusion.88
  101.0 0.1 copy.39
  101.2 0.2 slice.152
  101.3 1.9 %collective-permute-start.3 = (f32[2,4,512]{2,1,0:T(4,128)S(1)}, f32[2,4,512]{2,1,0:T(4,128)S(1)}, u32[]{:S(2)}, u32[]{:S(2)}) collective-permute-start(f32[2,4,512]{2,1,0:T(4,128)S(1)} %slice.152), channel_id=1, source_target_pairs={{32,0},{160,32},{192,64},{64,96},{0,128},{128,160},{224,192},{96,2... | collective-permute-start | bytes 49160 | tf_op jit(solution)/shard_map/ppermute | solution.py:184
  103.3 0.0 collective-permute-done.2
  103.3 5.2 %collective-permute-done.3 = f32[2,4,512]{2,1,0:T(4,128)S(1)} collective-permute-done((f32[2,4,512]{2,1,0:T(4,128)S(1)}, f32[2,4,512]{2,1,0:T(4,128)S(1)}, u32[]{:S(2)}, u32[]{:S(2)}) %collective-permute-start.3) | collective-permute-done | bytes 16416 | tf_op jit(solution)/shard_map/ppermute | solution.py:184
  108.5 0.6 maximum_bitcast_fusion.7
  109.1 0.6 maximum_bitcast_fusion.6
  (30 shorter events, 0.3 us)
Async XLA Ops:
  0.6 8.0 %copy-start = (bf16[1,2,256,1535]{2,1,3,0:T(2,128)(2,1)S(1)}, bf16[1,2,256,1535]{2,1,3,0:T(2,128)(2,1)}, u32[]{:S(2)}) copy-start(bf16[1,2,256,1535]{2,1,3,0:T(2,128)(2,1)} %param.5) | copy-start | bytes 4715524
  13.2 20.6 %copy-start.2 = (f32[16]{0:T(128)S(1)}, f32[16]{0:T(128)}, u32[]{:S(2)}) copy-start(f32[16]{0:T(128)} %param.8) | copy-start | bytes 196
  14.5 51.7 %all-to-all-start = ((bf16[2,512,256]{2,0,1:T(2,128)(2,1)}), bf16[2,512,256]{2,0,1:T(2,128)(2,1)S(1)}, u32[]{:S(2)}, u32[]{:S(2)}) async-start(bf16[2,512,256]{2,0,1:T(2,128)(2,1)} %copy.31), calls=%async_computation | async-start | bytes 1048576 | tf_op jit(solution)/shard_map/all_to_all | solution.py:163
  73.2 13.4 %collective-permute-start = (bf16[2,16,8192]{2,1,0:T(8,128)(2,1)S(1)}, bf16[2,16,8192]{2,1,0:T(8,128)(2,1)S(1)}, u32[]{:S(2)}, u32[]{:S(2)}) collective-permute-start(bf16[2,16,8192]{2,1,0:T(8,128)(2,1)S(1)} %convert_element_type.150), channel_id=1, source_target_pairs={{0,32},{32,160},{64,192},{96,64},{128,0},{160,128},{192,224},{224,... | collective-permute-start | bytes 1572872 | tf_op jit(solution)/shard_map/ppermute | solution.py:181
  75.6 11.7 %collective-permute-start.1 = (bf16[2,16,8192]{2,1,0:T(8,128)(2,1)S(1)}, bf16[2,16,8192]{2,1,0:T(8,128)(2,1)S(1)}, u32[]{:S(2)}, u32[]{:S(2)}) collective-permute-start(bf16[2,16,8192]{2,1,0:T(8,128)(2,1)S(1)} %convert_element_type.150), channel_id=1, source_target_pairs={{0,64},{32,288},{64,320},{96,32},{128,384},{160,224},{192,128},{22... | collective-permute-start | bytes 1572872 | tf_op jit(solution)/shard_map/ppermute | solution.py:181
  88.1 8.4 %copy-start.1 = (s32[1,2]{1,0:T(1,128)S(1)}, s32[1,2]{1,0:T(1,128)}, u32[]{:S(2)}) copy-start(s32[1,2]{1,0:T(1,128)} %param.9) | copy-start | bytes 28
  89.4 13.9 %collective-permute-start.2 = (f32[2,4,512]{2,1,0:T(4,128)S(1)}, f32[2,4,512]{2,1,0:T(4,128)S(1)}, u32[]{:S(2)}, u32[]{:S(2)}) collective-permute-start(f32[2,4,512]{2,1,0:T(4,128)S(1)} %slice.148), channel_id=1, source_target_pairs={{64,0},{288,32},{320,64},{32,96},{384,128},{224,160},{128,192},{48... | collective-permute-start | bytes 49160 | tf_op jit(solution)/shard_map/ppermute | solution.py:184
  101.3 7.1 %collective-permute-start.3 = (f32[2,4,512]{2,1,0:T(4,128)S(1)}, f32[2,4,512]{2,1,0:T(4,128)S(1)}, u32[]{:S(2)}, u32[]{:S(2)}) collective-permute-start(f32[2,4,512]{2,1,0:T(4,128)S(1)} %slice.152), channel_id=1, source_target_pairs={{32,0},{160,32},{192,64},{64,96},{0,128},{128,160},{224,192},{96,2... | collective-permute-start | bytes 49160 | tf_op jit(solution)/shard_map/ppermute | solution.py:184

commit v4 on v3

--- a/solution.py
+++ b/solution.py
@@ -158,9 +158,15 @@
     table_im = (amplitude * jnp.sin(chirp_phase)).astype(jnp.bfloat16)
     band = band_tables(table_re, table_im, echoes.shape[2])
     live_pulses = pulse_counts[0]
-    first_pulse = lax.axis_index("pulse") * pulses_dev
+    first_pulse = lax.axis_index(("pulse_hi", "pulse_lo")) * pulses_dev
     compressed = compress(echoes, band, first_pulse, live_pulses)
-    turned = lax.all_to_all(compressed, "pulse", split_axis=1, concat_axis=2, tiled=True)
+    outer = lax.axis_size("pulse_hi")
+    inner = lax.axis_size("pulse_lo")
+    cells = RNG // (outer * inner)
+    parts = compressed.reshape(2, outer, inner, cells, pulses_dev)
+    parts = lax.all_to_all(parts, "pulse_lo", 2, 2, tiled=True)
+    parts = lax.all_to_all(parts, "pulse_hi", 1, 1, tiled=True)
+    turned = parts.transpose(0, 3, 1, 2, 4).reshape(2, cells, outer * inner * pulses_dev)
     focused = azimuth(turned, azimuth_rate).astype(jnp.bfloat16)
     chosen = partner_bits[0]
     acq_size = lax.axis_size("acq")
@@ -203,8 +209,13 @@
 
 
 def solution(mesh):
-    in_specs = (P("acq", None, "pulse", None), P(), P("acq"), P("pulse"), P("acq", None))
-    out_specs = (P("acq", None, "pulse", None), P("acq", None, "pulse", None))
+    pulse_axis = mesh.devices.shape[1]
+    outer = 2 if pulse_axis % 2 == 0 else 1
+    devices = mesh.devices.reshape(mesh.devices.shape[0], outer, pulse_axis // outer)
+    split_mesh = jax.sharding.Mesh(devices, ("acq", "pulse_hi", "pulse_lo"))
+    pulse = ("pulse_hi", "pulse_lo")
+    in_specs = (P("acq", None, pulse, None), P(), P("acq"), P(pulse), P("acq", None))
+    out_specs = (P("acq", None, pulse, None), P("acq", None, pulse, None))
     return jax.shard_map(
-        per_device, mesh=mesh, in_specs=in_specs, out_specs=out_specs, check_vma=False
-    )
+        per_device, mesh=split_mesh, in_specs=in_specs, out_specs=out_specs, check_vma=False
+    )

time: 110 us -> 115 us (1.045)
  the two profiles are of different devices: /device:TPU:36 before, /device:TPU:4 now
where the time goes in v4:
time: 115 us
  waiting for transfers between devices  49.9 us (43%)
  starting transfers between devices  33.6 us (29%)
  matrix products  9.01 us (8%)
  other arithmetic  6.44 us (6%)
  between operations  5.65 us (5%)
  local copies, waits for them, and re-layouts  5.37 us (5%)
  Pallas kernels  4.76 us (4%)
    all_to_all x1, waiting for transfers between devices, per_device(): parts = lax.all_to_all(parts, 'pulse_lo', 2, 2, tiled=True)  27.9 us
    all_to_all x1, starting transfers between devices, per_device(): parts = lax.all_to_all(parts, 'pulse_lo', 2, 2, tiled=True)  15.2 us
    ppermute x2, starting transfers between devices, per_device(): lax.ppermute(looked[slot], 'acq', [(dst, src) for src, dst in edge_pairs[...  9.44 us
    ppermute x2, waiting for transfers between devices, per_device(): arrived = [lax.ppermute(focused, 'acq', pairs) for pairs in edge_pairs]  8.81 us
    all_to_all x1, waiting for transfers between devices, per_device(): parts = lax.all_to_all(parts, 'pulse_hi', 1, 1, tiled=True)  8.06 us
    ppermute x2, waiting for transfers between devices, per_device(): lax.ppermute(looked[slot], 'acq', [(dst, src) for src, dst in edge_pairs[...  5.19 us
    pallas_call x1, Pallas kernels, band_tables(): pl.pallas_call(band_kernel, grid=(steps,), in_specs=[row_spec, row_spec],...  4.76 us
    dot_general x1, matrix products, compress(): lax.dot_general(band, echoes, dims, preferred_element_type=jnp.float32)  4.57 us
  transfers between devices with their start and end apart: 6, of which 4 were waited for; matrix products, arithmetic and copies ran while one was open for 2% of the time, Pallas kernels for 0%

profile of v4, /device:TPU:4, one launch (start us, length us, event | category | flops | bytes accessed | tf_op | source)
XLA Modules:
  0.0 114.7 jit_solution(14064904628463806873)
XLA Ops:
  0.6 0.0 copy-start
  0.6 0.8 multiply_convert_fusion
  1.6 0.7 broadcast_bitcast_fusion.im_ref
  2.4 0.7 broadcast_bitcast_fusion.1.re_ref
  3.8 4.8 %shard_map.68 = bf16[2,2,512,1535]{3,2,1,0:T(8,128)(2,1)} custom-call(f32[32,1536]{1,0:T(8,128)} %broadcast_bitcast_fusion.1.re_ref, f32[32,1536]{1,0:T(8,128)} %broadcast_bitcast_fusion.im_ref), custom_call_target="tpu_custom_call" | custom-call | tf_op jit(solution)/shard_map/pallas_call | solution.py:55
  8.6 0.0 copy-done
  8.6 4.6 %fusion.14 = bf16[2,512,256]{2,1,0:T(8,128)(2,1)S(1)} fusion(bf16[2,256,1535,1]{1,0,2,3:T(2,128)(2,1)S(1)} %bitcast.152, bf16[2,2,512,1535]{3,2,1,0:T(8,128)(2,1)} %shard_map.68, f32[256]{0:T(256)S(1)} %compare_convert_fusion), kind=kOutput, calls=%fused_computation.11 | convolution fusion | flops 1610088448 | bytes 8384512 | tf_op jit(solution)/shard_map/dot_general | solution.py:68
  13.2 0.0 copy-start.2
  13.2 0.9 copy.31
  14.0 15.2 %all-to-all-start = ((bf16[2,2,16,16,256]{4,3,1,0,2:T(8,128)(2,1)}), bf16[2,2,16,16,256]{4,3,1,0,2:T(8,128)(2,1)S(1)}, u32[]{:S(2)}, u32[]{:S(2)}) async-start(bf16[2,2,16,16,256]{4,3,1,0,2:T(8,128)(2,1)} %copy.31), calls=%async_computation | async-start | bytes 1048576 | tf_op jit(solution)/shard_map/all_to_all | solution.py:167
  29.2 0.1 fusion.76
  29.4 0.1 fusion.72
  29.5 0.1 fusion.74
  29.7 0.1 fusion.73
  29.8 0.3 fusion.71
  30.1 0.3 fusion.65
  30.5 0.0 copy-done.2
  30.5 27.9 %all-to-all-done = bf16[2,2,16,16,256]{4,3,1,0,2:T(8,128)(2,1)S(1)} async-done(((bf16[2,2,16,16,256]{4,3,1,0,2:T(8,128)(2,1)}), bf16[2,2,16,16,256]{4,3,1,0,2:T(8,128)(2,1)S(1)}, u32[]{:S(2)}, u32[]{:S(2)}) %all-to-all-start) | async-done | bytes 524320 | tf_op jit(solution)/shard_map/all_to_all | solution.py:167
  58.3 0.8 copy.32
  59.2 4.5 %all-to-all-start.1 = ((bf16[2,2,16,16,256]{4,3,2,0,1:T(8,128)(2,1)}), bf16[2,2,16,16,256]{4,3,2,0,1:T(8,128)(2,1)S(1)}, u32[]{:S(2)}, u32[]{:S(2)}) async-start(bf16[2,2,16,16,256]{4,3,2,0,1:T(8,128)(2,1)} %copy.32), calls=%async_computation.1 | async-start | bytes 1048576 | tf_op jit(solution)/shard_map/all_to_all | solution.py:168
  63.7 8.1 %all-to-all-done.1 = bf16[2,2,16,16,256]{4,3,2,0,1:T(8,128)(2,1)S(1)} async-done(((bf16[2,2,16,16,256]{4,3,2,0,1:T(8,128)(2,1)}), bf16[2,2,16,16,256]{4,3,2,0,1:T(8,128)(2,1)S(1)}, u32[]{:S(2)}, u32[]{:S(2)}) %all-to-all-start.1) | async-done | bytes 524320 | tf_op jit(solution)/shard_map/all_to_all | solution.py:168
  71.7 0.2 copy.33
  71.9 0.2 reshape.355
  72.1 0.6 convolution_bitcast_fusion.3
  72.7 0.2 multiply_subtract_fusion.1
  72.9 1.0 convolution_bitcast_fusion.2
  73.9 2.1 %fusion.29 = (f32[1,16,64,128]{3,2,1,0:T(8,128)S(1)}, f32[1,16,64,128]{3,2,1,0:T(8,128)S(1)}) fusion(f32[2,16,64,128]{3,2,1,0:T(8,128)S(1)} %convolution_bitcast_fusion.2, f32[64,128]{1,0:T(8,128)S(1)} %fusion.62, f32[16]{0:T(128)S(1)} %broadcast_multiply_fusion), kind=kLoop, calls=%fused_computation.28 | loop fusion | flops 1048576 | bytes 2129984 | tf_op jit(solution)/shard_map/sub | solution.py:27
  76.0 1.0 convolution_bitcast_fusion.1
  77.0 0.2 multiply_subtract_fusion
  77.2 1.1 fusion.20
  78.3 0.2 convert_element_type.150
  78.5 2.4 %collective-permute-start = (bf16[2,16,8192]{2,1,0:T(8,128)(2,1)S(1)}, bf16[2,16,8192]{2,1,0:T(8,128)(2,1)S(1)}, u32[]{:S(2)}, u32[]{:S(2)}) collective-permute-start(bf16[2,16,8192]{2,1,0:T(8,128)(2,1)S(1)} %convert_element_type.150), channel_id=1, source_target_pairs={{0,32},{32,160},{64,192},{96,64},{128,0},{160,128},{192,224},{224,... | collective-permute-start | bytes 1572872 | tf_op jit(solution)/shard_map/ppermute | solution.py:187
  81.0 2.1 %collective-permute-start.1 = (bf16[2,16,8192]{2,1,0:T(8,128)(2,1)S(1)}, bf16[2,16,8192]{2,1,0:T(8,128)(2,1)S(1)}, u32[]{:S(2)}, u32[]{:S(2)}) collective-permute-start(bf16[2,16,8192]{2,1,0:T(8,128)(2,1)S(1)} %convert_element_type.150), channel_id=1, source_target_pairs={{0,64},{32,288},{64,320},{96,32},{128,384},{160,224},{192,128},{22... | collective-permute-start | bytes 1572872 | tf_op jit(solution)/shard_map/ppermute | solution.py:187
  83.1 0.1 convert_element_type.151
  83.1 8.8 %collective-permute-done = bf16[2,16,8192]{2,1,0:T(8,128)(2,1)S(1)} collective-permute-done((bf16[2,16,8192]{2,1,0:T(8,128)(2,1)S(1)}, bf16[2,16,8192]{2,1,0:T(8,128)(2,1)S(1)}, u32[]{:S(2)}, u32[]{:S(2)}) %collective-permute-start) | collective-permute-done | bytes 524320 | tf_op jit(solution)/shard_map/ppermute | solution.py:187
  92.0 0.1 convert_element_type.152
  92.0 0.0 collective-permute-done.1
  92.0 0.1 convert_element_type.153
  92.1 0.2 add_bitcast_fusion.1
  92.4 0.1 copy.57
  92.5 0.1 copy.58
  92.6 0.1 copy.59
  92.7 0.1 copy.60
  92.8 0.0 copy-start.1
  92.8 0.2 maximum_reduce_fusion
  93.0 0.7 convolution_multiply_fusion
  93.7 0.1 copy.39
  93.9 0.2 slice.148
  94.0 7.5 %collective-permute-start.2 = (f32[2,4,512]{2,1,0:T(4,128)S(1)}, f32[2,4,512]{2,1,0:T(4,128)S(1)}, u32[]{:S(2)}, u32[]{:S(2)}) collective-permute-start(f32[2,4,512]{2,1,0:T(4,128)S(1)} %slice.148), channel_id=1, source_target_pairs={{64,0},{288,32},{320,64},{32,96},{384,128},{224,160},{128,192},{48... | collective-permute-start | bytes 49160 | tf_op jit(solution)/shard_map/ppermute | solution.py:190
  101.6 0.0 copy-done.1
  101.6 0.6 fusion.88
  106.0 0.1 copy.40
  106.2 0.2 slice.152
  106.3 1.9 %collective-permute-start.3 = (f32[2,4,512]{2,1,0:T(4,128)S(1)}, f32[2,4,512]{2,1,0:T(4,128)S(1)}, u32[]{:S(2)}, u32[]{:S(2)}) collective-permute-start(f32[2,4,512]{2,1,0:T(4,128)S(1)} %slice.152), channel_id=1, source_target_pairs={{32,0},{160,32},{192,64},{64,96},{0,128},{128,160},{224,192},{96,2... | collective-permute-start | bytes 49160 | tf_op jit(solution)/shard_map/ppermute | solution.py:190
  108.3 0.0 collective-permute-done.2
  108.3 5.2 %collective-permute-done.3 = f32[2,4,512]{2,1,0:T(4,128)S(1)} collective-permute-done((f32[2,4,512]{2,1,0:T(4,128)S(1)}, f32[2,4,512]{2,1,0:T(4,128)S(1)}, u32[]{:S(2)}, u32[]{:S(2)}) %collective-permute-start.3) | collective-permute-done | bytes 16416 | tf_op jit(solution)/shard_map/ppermute | solution.py:190
  113.5 0.6 maximum_bitcast_fusion.7
  114.1 0.6 maximum_bitcast_fusion.6
  (30 shorter events, 0.3 us)
Async XLA Ops:
  0.6 7.9 %copy-start = (bf16[1,2,256,1535]{2,1,3,0:T(2,128)(2,1)S(1)}, bf16[1,2,256,1535]{2,1,3,0:T(2,128)(2,1)}, u32[]{:S(2)}) copy-start(bf16[1,2,256,1535]{2,1,3,0:T(2,128)(2,1)} %param.5) | copy-start | bytes 4715524
  13.2 17.3 %copy-start.2 = (f32[16]{0:T(128)S(1)}, f32[16]{0:T(128)}, u32[]{:S(2)}) copy-start(f32[16]{0:T(128)} %param.8) | copy-start | bytes 196
  14.0 44.3 %all-to-all-start = ((bf16[2,2,16,16,256]{4,3,1,0,2:T(8,128)(2,1)}), bf16[2,2,16,16,256]{4,3,1,0,2:T(8,128)(2,1)S(1)}, u32[]{:S(2)}, u32[]{:S(2)}) async-start(bf16[2,2,16,16,256]{4,3,1,0,2:T(8,128)(2,1)} %copy.31), calls=%async_computation | async-start | bytes 1048576 | tf_op jit(solution)/shard_map/all_to_all | solution.py:167
  59.2 12.5 %all-to-all-start.1 = ((bf16[2,2,16,16,256]{4,3,2,0,1:T(8,128)(2,1)}), bf16[2,2,16,16,256]{4,3,2,0,1:T(8,128)(2,1)S(1)}, u32[]{:S(2)}, u32[]{:S(2)}) async-start(bf16[2,2,16,16,256]{4,3,2,0,1:T(8,128)(2,1)} %copy.32), calls=%async_computation.1 | async-start | bytes 1048576 | tf_op jit(solution)/shard_map/all_to_all | solution.py:168
  78.5 13.4 %collective-permute-start = (bf16[2,16,8192]{2,1,0:T(8,128)(2,1)S(1)}, bf16[2,16,8192]{2,1,0:T(8,128)(2,1)S(1)}, u32[]{:S(2)}, u32[]{:S(2)}) collective-permute-start(bf16[2,16,8192]{2,1,0:T(8,128)(2,1)S(1)} %convert_element_type.150), channel_id=1, source_target_pairs={{0,32},{32,160},{64,192},{96,64},{128,0},{160,128},{192,224},{224,... | collective-permute-start | bytes 1572872 | tf_op jit(solution)/shard_map/ppermute | solution.py:187
  81.0 11.1 %collective-permute-start.1 = (bf16[2,16,8192]{2,1,0:T(8,128)(2,1)S(1)}, bf16[2,16,8192]{2,1,0:T(8,128)(2,1)S(1)}, u32[]{:S(2)}, u32[]{:S(2)}) collective-permute-start(bf16[2,16,8192]{2,1,0:T(8,128)(2,1)S(1)} %convert_element_type.150), channel_id=1, source_target_pairs={{0,64},{32,288},{64,320},{96,32},{128,384},{160,224},{192,128},{22... | collective-permute-start | bytes 1572872 | tf_op jit(solution)/shard_map/ppermute | solution.py:187
  92.8 8.8 %copy-start.1 = (s32[1,2]{1,0:T(1,128)S(1)}, s32[1,2]{1,0:T(1,128)}, u32[]{:S(2)}) copy-start(s32[1,2]{1,0:T(1,128)} %param.9) | copy-start | bytes 28
  94.0 14.2 %collective-permute-start.2 = (f32[2,4,512]{2,1,0:T(4,128)S(1)}, f32[2,4,512]{2,1,0:T(4,128)S(1)}, u32[]{:S(2)}, u32[]{:S(2)}) collective-permute-start(f32[2,4,512]{2,1,0:T(4,128)S(1)} %slice.148), channel_id=1, source_target_pairs={{64,0},{288,32},{320,64},{32,96},{384,128},{224,160},{128,192},{48... | collective-permute-start | bytes 49160 | tf_op jit(solution)/shard_map/ppermute | solution.py:190
  106.3 7.1 %collective-permute-start.3 = (f32[2,4,512]{2,1,0:T(4,128)S(1)}, f32[2,4,512]{2,1,0:T(4,128)S(1)}, u32[]{:S(2)}, u32[]{:S(2)}) collective-permute-start(f32[2,4,512]{2,1,0:T(4,128)S(1)} %slice.152), channel_id=1, source_target_pairs={{32,0},{160,32},{192,64},{64,96},{0,128},{128,160},{224,192},{96,2... | collective-permute-start | bytes 49160 | tf_op jit(solution)/shard_map/ppermute | solution.py:190

commit v5 on v3

--- a/solution.py
+++ b/solution.py
@@ -11,6 +11,7 @@
 TAPS = 1024
 LOOK_RNG = 4
 LOOK_AZ = 16
+CHUNKS = 2
 
 
 def part_tables(length, inverse):
@@ -160,8 +161,10 @@
     live_pulses = pulse_counts[0]
     first_pulse = lax.axis_index("pulse") * pulses_dev
     compressed = compress(echoes, band, first_pulse, live_pulses)
-    turned = lax.all_to_all(compressed, "pulse", split_axis=1, concat_axis=2, tiled=True)
-    focused = azimuth(turned, azimuth_rate).astype(jnp.bfloat16)
+    devices = lax.axis_size("pulse")
+    cells = RNG // devices
+    chunk_cells = cells // CHUNKS
+    pieces = compressed.reshape(2, devices, CHUNKS, chunk_cells, pulses_dev).transpose(2, 0, 1, 3, 4)
     chosen = partner_bits[0]
     acq_size = lax.axis_size("acq")
     me = lax.axis_index("acq")
@@ -178,25 +181,40 @@
                 for i in range(acq_size)
             ]
         )
-    arrived = [lax.ppermute(focused, "acq", pairs) for pairs in edge_pairs]
-    looked = cross_looks(focused, arrived)
-    returned = [
-        lax.ppermute(looked[slot], "acq", [(dst, src) for src, dst in edge_pairs[slot]])
-        for slot in range(2)
-    ]
-    candidates = []
-    for slot in range(2):
-        recv_bit = jnp.where(me_parity == 1, low_bits[slot], high_bits[slot])
-        send_bit = jnp.where(me_parity == 1, high_bits[slot], low_bits[slot])
-        candidates.append((recv_bit, looked[slot]))
-        back = returned[slot]
-        candidates.append((send_bit, jnp.stack([back[0], -back[1]])))
-    results = []
-    for slot in range(2):
-        pick = candidates[0][1]
-        for bit, value in candidates[1:]:
-            pick = jnp.where(chosen[slot] == bit, value, pick)
-        results.append(pick)
+    def finish(focused, arrived, chunk):
+        looked = cross_looks(focused, arrived)
+        returned = [
+            lax.ppermute(looked[slot], "acq", [(dst, src) for src, dst in edge_pairs[slot]])
+            for slot in range(2)
+        ]
+        candidates = []
+        for slot in range(2):
+            recv_bit = jnp.where(me_parity == 1, low_bits[slot], high_bits[slot])
+            send_bit = jnp.where(me_parity == 1, high_bits[slot], low_bits[slot])
+            candidates.append((recv_bit, looked[slot]))
+            back = returned[slot]
+            candidates.append((send_bit, jnp.stack([back[0], -back[1]])))
+        for slot in range(2):
+            pick = candidates[0][1]
+            for bit, value in candidates[1:]:
+                pick = jnp.where(chosen[slot] == bit, value, pick)
+            looks[slot].append(pick)
+
+    looks = [[], []]
+    previous = None
+    for chunk in range(CHUNKS):
+        piece = pieces[chunk].reshape(2, devices * chunk_cells, pulses_dev)
+        if previous is not None:
+            previous, piece = lax.optimization_barrier((previous, piece))
+            arrived = [lax.ppermute(previous, "acq", pairs) for pairs in edge_pairs]
+            finish(previous, arrived, chunk - 1)
+        turned = lax.all_to_all(piece, "pulse", split_axis=1, concat_axis=2, tiled=True)
+        rate = azimuth_rate[chunk * chunk_cells : (chunk + 1) * chunk_cells]
+        previous = azimuth(turned, rate).astype(jnp.bfloat16)
+    arrived = [lax.ppermute(previous, "acq", pairs) for pairs in edge_pairs]
+    finish(previous, arrived, CHUNKS - 1)
+    results = [jnp.concatenate(parts, axis=1) for parts in looks]
+
     interfere_real = jnp.stack([item[0] for item in results])[None]
     interfere_imag = jnp.stack([item[1] for item in results])[None]
     return (interfere_real, interfere_imag)

time: 110 us -> 123 us (1.12)
  the two profiles are of different devices: /device:TPU:36 before, /device:TPU:4 now
where the time goes in v5:
time: 123 us; the launch traced here: 122 us
  waiting for transfers between devices  44.5 us (36%)
  starting transfers between devices  44.2 us (36%)
  matrix products  9.89 us (8%)
  other arithmetic  6.68 us (5%)
  local copies, waits for them, and re-layouts  5.94 us (5%)
  between operations  5.93 us (5%)
  Pallas kernels  4.72 us (4%)
    all_to_all x2, waiting for transfers between devices, per_device(): lax.all_to_all(piece, 'pulse', split_axis=1, concat_axis=2, tiled=True)  33.6 us
    all_to_all x2, starting transfers between devices, per_device(): lax.all_to_all(piece, 'pulse', split_axis=1, concat_axis=2, tiled=True)  22 us
    ppermute x4, starting transfers between devices, finish(): lax.ppermute(looked[slot], 'acq', [(dst, src) for src, dst in edge_pairs[...  12.1 us
    ppermute x4, starting transfers between devices, per_device(): arrived = [lax.ppermute(previous, 'acq', pairs) for pairs in edge_pairs]  10.2 us
    ppermute x4, waiting for transfers between devices, per_device(): arrived = [lax.ppermute(previous, 'acq', pairs) for pairs in edge_pairs]  5.81 us
    ppermute x4, waiting for transfers between devices, finish(): lax.ppermute(looked[slot], 'acq', [(dst, src) for src, dst in edge_pairs[...  5.11 us
    pallas_call x1, Pallas kernels, band_tables(): pl.pallas_call(band_kernel, grid=(steps,), in_specs=[row_spec, row_spec],...  4.72 us
    dot_general x1, matrix products, compress(): lax.dot_general(band, echoes, dims, preferred_element_type=jnp.float32)  4.57 us
  transfers between devices with their start and end apart: 10, of which 5 were waited for; matrix products, arithmetic and copies ran while one was open for 7% of the time, Pallas kernels for 0%

profile of v5, /device:TPU:4, one launch (start us, length us, event | category | flops | bytes accessed | tf_op | source)
XLA Modules:
  0.0 121.9 jit_solution(10209469734838923073)
XLA Ops:
  0.6 0.8 multiply_convert_fusion
  1.6 0.7 broadcast_bitcast_fusion.im_ref
  2.5 0.7 broadcast_bitcast_fusion.1.re_ref
  3.8 4.7 %shard_map.68 = bf16[2,2,512,1535]{3,2,1,0:T(8,128)(2,1)} custom-call(f32[32,1536]{1,0:T(8,128)} %broadcast_bitcast_fusion.1.re_ref, f32[32,1536]{1,0:T(8,128)} %broadcast_bitcast_fusion.im_ref), custom_call_target="tpu_custom_call" | custom-call | tf_op jit(solution)/shard_map/pallas_call | solution.py:56
  8.5 4.6 %fusion.13 = bf16[2,512,256]{2,1,0:T(8,128)(2,1)S(1)} fusion(bf16[2,256,1535,1]{1,0,2,3:T(2,128)(2,1)S(1)} %bitcast.241, bf16[2,2,512,1535]{3,2,1,0:T(8,128)(2,1)} %shard_map.68, f32[256]{0:T(256)S(1)} %compare_convert_fusion), kind=kOutput, calls=%fused_computation.5 | convolution fusion | flops 1610088448 | bytes 8384512 | tf_op jit(solution)/shard_map/dot_general | solution.py:69
  13.2 1.0 copy.43
  14.1 18.1 %all-to-all-start = ((bf16[2,256,256]{2,0,1:T(2,128)(2,1)}), bf16[2,256,256]{2,0,1:T(2,128)(2,1)S(1)}, u32[]{:S(2)}, u32[]{:S(2)}) async-start(bf16[2,256,256]{2,0,1:T(2,128)(2,1)} %bitcast.28), calls=%async_computation | async-start | bytes 524288 | tf_op jit(solution)/shard_map/all_to_all | solution.py:211
  32.3 0.1 fusion.91
  32.4 0.1 fusion.93
  32.6 0.1 fusion.90
  32.7 0.1 fusion.89
  32.9 1.0 copy.51
  33.8 0.3 fusion.85
  34.1 0.3 fusion.79
  34.5 0.1 slice_multiply_fusion
  34.6 21.5 %all-to-all-done = bf16[2,256,256]{2,0,1:T(2,128)(2,1)S(1)} async-done(((bf16[2,256,256]{2,0,1:T(2,128)(2,1)}), bf16[2,256,256]{2,0,1:T(2,128)(2,1)S(1)}, u32[]{:S(2)}, u32[]{:S(2)}) %all-to-all-start) | async-done | bytes 262176 | tf_op jit(solution)/shard_map/all_to_all | solution.py:211
  56.1 0.1 reshape.389
  56.2 0.4 convolution_bitcast_fusion.7
  56.6 0.1 multiply_subtract_fusion.3
  56.7 0.6 convolution_bitcast_fusion.6
  57.3 1.2 fusion.42
  58.5 0.6 convolution_bitcast_fusion.5
  59.1 0.1 multiply_subtract_fusion.2
  59.2 0.6 fusion.23
  59.8 0.1 convert_element_type.194
  59.9 2.4 %collective-permute-start = (bf16[2,8,8192]{2,1,0:T(8,128)(2,1)S(1)}, bf16[2,8,8192]{2,1,0:T(8,128)(2,1)S(1)}, u32[]{:S(2)}, u32[]{:S(2)}) collective-permute-start(bf16[2,8,8192]{2,1,0:T(8,128)(2,1)S(1)} %convert_element_type.194), channel_id=1, source_target_pairs={{0,32},{32,160},{64,192},{96,64},{128,0},{160,128},{192,224},{224,... | collective-permute-start | bytes 786440 | tf_op jit(solution)/shard_map/ppermute | solution.py:209
  62.4 2.1 %collective-permute-start.1 = (bf16[2,8,8192]{2,1,0:T(8,128)(2,1)S(1)}, bf16[2,8,8192]{2,1,0:T(8,128)(2,1)S(1)}, u32[]{:S(2)}, u32[]{:S(2)}) collective-permute-start(bf16[2,8,8192]{2,1,0:T(8,128)(2,1)S(1)} %convert_element_type.194), channel_id=1, source_target_pairs={{0,64},{32,288},{64,320},{96,32},{128,384},{160,224},{192,128},{22... | collective-permute-start | bytes 786440 | tf_op jit(solution)/shard_map/ppermute | solution.py:209
  64.5 3.9 %all-to-all-start.1 = ((bf16[2,256,256]{2,0,1:T(2,128)(2,1)}), bf16[2,256,256]{2,0,1:T(2,128)(2,1)S(1)}, u32[]{:S(2)}, u32[]{:S(2)}) async-start(bf16[2,256,256]{2,0,1:T(2,128)(2,1)} %bitcast.50), calls=%async_computation.1 | async-start | bytes 524288 | tf_op jit(solution)/shard_map/all_to_all | solution.py:211
  68.4 0.6 fusion.113
  73.0 0.1 add_bitcast_fusion.3
  73.4 0.1 maximum_reduce_fusion
  73.5 0.4 convolution_multiply_fusion.1
  73.9 0.1 copy.52
  74.0 0.1 slice.243
  74.1 3.8 %collective-permute-start.2 = (f32[2,2,512]{2,1,0:T(2,128)S(1)}, f32[2,2,512]{2,1,0:T(2,128)S(1)}, u32[]{:S(2)}, u32[]{:S(2)}) collective-permute-start(f32[2,2,512]{2,1,0:T(2,128)S(1)} %slice.243), channel_id=1, source_target_pairs={{64,0},{288,32},{320,64},{32,96},{384,128},{224,160},{128,192},{48... | collective-permute-start | bytes 24584 | tf_op jit(solution)/shard_map/ppermute | solution.py:187
  77.9 0.1 copy.53
  78.0 0.1 slice.247
  78.1 2.1 %collective-permute-start.3 = (f32[2,2,512]{2,1,0:T(2,128)S(1)}, f32[2,2,512]{2,1,0:T(2,128)S(1)}, u32[]{:S(2)}, u32[]{:S(2)}) collective-permute-start(f32[2,2,512]{2,1,0:T(2,128)S(1)} %slice.247), channel_id=1, source_target_pairs={{32,0},{160,32},{192,64},{64,96},{0,128},{128,160},{224,192},{96,2... | collective-permute-start | bytes 24584 | tf_op jit(solution)/shard_map/ppermute | solution.py:187
  80.2 12.1 %all-to-all-done.1 = bf16[2,256,256]{2,0,1:T(2,128)(2,1)S(1)} async-done(((bf16[2,256,256]{2,0,1:T(2,128)(2,1)}), bf16[2,256,256]{2,0,1:T(2,128)(2,1)S(1)}, u32[]{:S(2)}, u32[]{:S(2)}) %all-to-all-start.1) | async-done | bytes 262176 | tf_op jit(solution)/shard_map/all_to_all | solution.py:211
  92.4 0.1 reshape.401
  92.5 0.4 convolution_bitcast_fusion.3
  92.9 0.1 multiply_subtract_fusion.1
  93.0 0.6 convolution_bitcast_fusion.2
  93.6 1.2 fusion.40
  94.8 0.6 convolution_bitcast_fusion.1
  95.4 0.1 multiply_subtract_fusion
  95.5 0.6 fusion.22
  96.1 0.1 convert_element_type.200
  96.2 3.3 %collective-permute-start.4 = (bf16[2,8,8192]{2,1,0:T(8,128)(2,1)S(1)}, bf16[2,8,8192]{2,1,0:T(8,128)(2,1)S(1)}, u32[]{:S(2)}, u32[]{:S(2)}) collective-permute-start(bf16[2,8,8192]{2,1,0:T(8,128)(2,1)S(1)} %convert_element_type.200), channel_id=1, source_target_pairs={{0,32},{32,160},{64,192},{96,64},{128,0},{160,128},{192,224},{224,... | collective-permute-start | bytes 786440 | tf_op jit(solution)/shard_map/ppermute | solution.py:214
  99.6 2.3 %collective-permute-start.5 = (bf16[2,8,8192]{2,1,0:T(8,128)(2,1)S(1)}, bf16[2,8,8192]{2,1,0:T(8,128)(2,1)S(1)}, u32[]{:S(2)}, u32[]{:S(2)}) collective-permute-start(bf16[2,8,8192]{2,1,0:T(8,128)(2,1)S(1)} %convert_element_type.200), channel_id=1, source_target_pairs={{0,64},{32,288},{64,320},{96,32},{128,384},{160,224},{192,128},{22... | collective-permute-start | bytes 786440 | tf_op jit(solution)/shard_map/ppermute | solution.py:214
  102.0 3.9 %collective-permute-done.4 = bf16[2,8,8192]{2,1,0:T(8,128)(2,1)S(1)} collective-permute-done((bf16[2,8,8192]{2,1,0:T(8,128)(2,1)S(1)}, bf16[2,8,8192]{2,1,0:T(8,128)(2,1)S(1)}, u32[]{:S(2)}, u32[]{:S(2)}) %collective-permute-start.4) | collective-permute-done | bytes 262176 | tf_op jit(solution)/shard_map/ppermute | solution.py:214
  106.0 1.9 %collective-permute-done.5 = bf16[2,8,8192]{2,1,0:T(8,128)(2,1)S(1)} collective-permute-done((bf16[2,8,8192]{2,1,0:T(8,128)(2,1)S(1)}, bf16[2,8,8192]{2,1,0:T(8,128)(2,1)S(1)}, u32[]{:S(2)}, u32[]{:S(2)}) %collective-permute-start.5) | collective-permute-done | bytes 262176 | tf_op jit(solution)/shard_map/ppermute | solution.py:214
  107.9 0.1 add_bitcast_fusion.1
  108.3 0.1 maximum_reduce_fusion.1
  108.3 0.4 convolution_multiply_fusion
  108.7 0.1 copy.61
  108.9 0.1 slice.264
  109.0 4.3 %collective-permute-start.6 = (f32[2,2,512]{2,1,0:T(2,128)S(1)}, f32[2,2,512]{2,1,0:T(2,128)S(1)}, u32[]{:S(2)}, u32[]{:S(2)}) collective-permute-start(f32[2,2,512]{2,1,0:T(2,128)S(1)} %slice.264), channel_id=1, source_target_pairs={{64,0},{288,32},{320,64},{32,96},{384,128},{224,160},{128,192},{48... | collective-permute-start | bytes 24584 | tf_op jit(solution)/shard_map/ppermute | solution.py:187
  113.3 0.1 copy.62
  113.4 0.1 slice.268
  113.6 1.9 %collective-permute-start.7 = (f32[2,2,512]{2,1,0:T(2,128)S(1)}, f32[2,2,512]{2,1,0:T(2,128)S(1)}, u32[]{:S(2)}, u32[]{:S(2)}) collective-permute-start(f32[2,2,512]{2,1,0:T(2,128)S(1)} %slice.268), channel_id=1, source_target_pairs={{32,0},{160,32},{192,64},{64,96},{0,128},{128,160},{224,192},{96,2... | collective-permute-start | bytes 24584 | tf_op jit(solution)/shard_map/ppermute | solution.py:187
  115.5 5.1 %collective-permute-done.7 = f32[2,2,512]{2,1,0:T(2,128)S(1)} collective-permute-done((f32[2,2,512]{2,1,0:T(2,128)S(1)}, f32[2,2,512]{2,1,0:T(2,128)S(1)}, u32[]{:S(2)}, u32[]{:S(2)}) %collective-permute-start.7) | collective-permute-done | bytes 8224 | tf_op jit(solution)/shard_map/ppermute | solution.py:187
  120.6 0.6 fusion.88
  121.3 0.6 maximum_bitcast_fusion.8
  (63 shorter events, 1.2 us)
Async XLA Ops:
  0.6 7.9 %copy-start = (bf16[1,2,256,1535]{2,1,3,0:T(2,128)(2,1)S(1)}, bf16[1,2,256,1535]{2,1,3,0:T(2,128)(2,1)}, u32[]{:S(2)}) copy-start(bf16[1,2,256,1535]{2,1,3,0:T(2,128)(2,1)} %param.5) | copy-start | bytes 4715524
  13.2 21.3 %copy-start.1 = (f32[16]{0:T(128)S(1)}, f32[16]{0:T(128)}, u32[]{:S(2)}) copy-start(f32[16]{0:T(128)} %param.8) | copy-start | bytes 196
  14.1 41.9 %all-to-all-start = ((bf16[2,256,256]{2,0,1:T(2,128)(2,1)}), bf16[2,256,256]{2,0,1:T(2,128)(2,1)S(1)}, u32[]{:S(2)}, u32[]{:S(2)}) async-start(bf16[2,256,256]{2,0,1:T(2,128)(2,1)} %bitcast.28), calls=%async_computation | async-start | bytes 524288 | tf_op jit(solution)/shard_map/all_to_all | solution.py:211
  59.1 9.3 %copy-start.2 = (s32[1,2]{1,0:T(1,128)S(1)}, s32[1,2]{1,0:T(1,128)}, u32[]{:S(2)}) copy-start(s32[1,2]{1,0:T(1,128)} %param.9) | copy-start | bytes 28
  59.9 13.0 %collective-permute-start = (bf16[2,8,8192]{2,1,0:T(8,128)(2,1)S(1)}, bf16[2,8,8192]{2,1,0:T(8,128)(2,1)S(1)}, u32[]{:S(2)}, u32[]{:S(2)}) collective-permute-start(bf16[2,8,8192]{2,1,0:T(8,128)(2,1)S(1)} %convert_element_type.194), channel_id=1, source_target_pairs={{0,32},{32,160},{64,192},{96,64},{128,0},{160,128},{192,224},{224,... | collective-permute-start | bytes 786440 | tf_op jit(solution)/shard_map/ppermute | solution.py:209
  62.4 10.6 %collective-permute-start.1 = (bf16[2,8,8192]{2,1,0:T(8,128)(2,1)S(1)}, bf16[2,8,8192]{2,1,0:T(8,128)(2,1)S(1)}, u32[]{:S(2)}, u32[]{:S(2)}) collective-permute-start(bf16[2,8,8192]{2,1,0:T(8,128)(2,1)S(1)} %convert_element_type.194), channel_id=1, source_target_pairs={{0,64},{32,288},{64,320},{96,32},{128,384},{160,224},{192,128},{22... | collective-permute-start | bytes 786440 | tf_op jit(solution)/shard_map/ppermute | solution.py:209
  64.5 27.9 %all-to-all-start.1 = ((bf16[2,256,256]{2,0,1:T(2,128)(2,1)}), bf16[2,256,256]{2,0,1:T(2,128)(2,1)S(1)}, u32[]{:S(2)}, u32[]{:S(2)}) async-start(bf16[2,256,256]{2,0,1:T(2,128)(2,1)} %bitcast.50), calls=%async_computation.1 | async-start | bytes 524288 | tf_op jit(solution)/shard_map/all_to_all | solution.py:211
  74.1 27.8 %collective-permute-start.2 = (f32[2,2,512]{2,1,0:T(2,128)S(1)}, f32[2,2,512]{2,1,0:T(2,128)S(1)}, u32[]{:S(2)}, u32[]{:S(2)}) collective-permute-start(f32[2,2,512]{2,1,0:T(2,128)S(1)} %slice.243), channel_id=1, source_target_pairs={{64,0},{288,32},{320,64},{32,96},{384,128},{224,160},{128,192},{48... | collective-permute-start | bytes 24584 | tf_op jit(solution)/shard_map/ppermute | solution.py:187
  78.1 23.9 %collective-permute-start.3 = (f32[2,2,512]{2,1,0:T(2,128)S(1)}, f32[2,2,512]{2,1,0:T(2,128)S(1)}, u32[]{:S(2)}, u32[]{:S(2)}) collective-permute-start(f32[2,2,512]{2,1,0:T(2,128)S(1)} %slice.247), channel_id=1, source_target_pairs={{32,0},{160,32},{192,64},{64,96},{0,128},{128,160},{224,192},{96,2... | collective-permute-start | bytes 24584 | tf_op jit(solution)/shard_map/ppermute | solution.py:187
  96.2 9.7 %collective-permute-start.4 = (bf16[2,8,8192]{2,1,0:T(8,128)(2,1)S(1)}, bf16[2,8,8192]{2,1,0:T(8,128)(2,1)S(1)}, u32[]{:S(2)}, u32[]{:S(2)}) collective-permute-start(bf16[2,8,8192]{2,1,0:T(8,128)(2,1)S(1)} %convert_element_type.200), channel_id=1, source_target_pairs={{0,32},{32,160},{64,192},{96,64},{128,0},{160,128},{192,224},{224,... | collective-permute-start | bytes 786440 | tf_op jit(solution)/shard_map/ppermute | solution.py:214
  99.6 8.3 %collective-permute-start.5 = (bf16[2,8,8192]{2,1,0:T(8,128)(2,1)S(1)}, bf16[2,8,8192]{2,1,0:T(8,128)(2,1)S(1)}, u32[]{:S(2)}, u32[]{:S(2)}) collective-permute-start(bf16[2,8,8192]{2,1,0:T(8,128)(2,1)S(1)} %convert_element_type.200), channel_id=1, source_target_pairs={{0,64},{32,288},{64,320},{96,32},{128,384},{160,224},{192,128},{22... | collective-permute-start | bytes 786440 | tf_op jit(solution)/shard_map/ppermute | solution.py:214
  109.0 6.5 %collective-permute-start.6 = (f32[2,2,512]{2,1,0:T(2,128)S(1)}, f32[2,2,512]{2,1,0:T(2,128)S(1)}, u32[]{:S(2)}, u32[]{:S(2)}) collective-permute-start(f32[2,2,512]{2,1,0:T(2,128)S(1)} %slice.264), channel_id=1, source_target_pairs={{64,0},{288,32},{320,64},{32,96},{384,128},{224,160},{128,192},{48... | collective-permute-start | bytes 24584 | tf_op jit(solution)/shard_map/ppermute | solution.py:187
  113.6 7.0 %collective-permute-start.7 = (f32[2,2,512]{2,1,0:T(2,128)S(1)}, f32[2,2,512]{2,1,0:T(2,128)S(1)}, u32[]{:S(2)}, u32[]{:S(2)}) collective-permute-start(f32[2,2,512]{2,1,0:T(2,128)S(1)} %slice.268), channel_id=1, source_target_pairs={{32,0},{160,32},{192,64},{64,96},{0,128},{128,160},{224,192},{96,2... | collective-permute-start | bytes 24584 | tf_op jit(solution)/shard_map/ppermute | solution.py:187

commit v6 on v3

--- a/solution.py
+++ b/solution.py
@@ -160,8 +160,6 @@
     live_pulses = pulse_counts[0]
     first_pulse = lax.axis_index("pulse") * pulses_dev
     compressed = compress(echoes, band, first_pulse, live_pulses)
-    turned = lax.all_to_all(compressed, "pulse", split_axis=1, concat_axis=2, tiled=True)
-    focused = azimuth(turned, azimuth_rate).astype(jnp.bfloat16)
     chosen = partner_bits[0]
     acq_size = lax.axis_size("acq")
     me = lax.axis_index("acq")
@@ -178,6 +176,14 @@
                 for i in range(acq_size)
             ]
         )
+    cand_bits = []
+    for slot in range(2):
+        cand_bits.append(jnp.where(me_parity == 1, low_bits[slot], high_bits[slot]))
+        cand_bits.append(jnp.where(me_parity == 1, high_bits[slot], low_bits[slot]))
+    masks = jnp.stack([jnp.stack([chosen[slot] == bit for bit in cand_bits]) for slot in range(2)])
+    masks, compressed = lax.optimization_barrier((masks, compressed))
+    turned = lax.all_to_all(compressed, "pulse", split_axis=1, concat_axis=2, tiled=True)
+    focused = azimuth(turned, azimuth_rate).astype(jnp.bfloat16)
     arrived = [lax.ppermute(focused, "acq", pairs) for pairs in edge_pairs]
     looked = cross_looks(focused, arrived)
     returned = [
@@ -186,16 +192,14 @@
     ]
     candidates = []
     for slot in range(2):
-        recv_bit = jnp.where(me_parity == 1, low_bits[slot], high_bits[slot])
-        send_bit = jnp.where(me_parity == 1, high_bits[slot], low_bits[slot])
-        candidates.append((recv_bit, looked[slot]))
+        candidates.append(looked[slot])
         back = returned[slot]
-        candidates.append((send_bit, jnp.stack([back[0], -back[1]])))
+        candidates.append(jnp.stack([back[0], -back[1]]))
     results = []
     for slot in range(2):
-        pick = candidates[0][1]
-        for bit, value in candidates[1:]:
-            pick = jnp.where(chosen[slot] == bit, value, pick)
+        pick = candidates[0]
+        for index in range(1, len(candidates)):
+            pick = jnp.where(masks[slot, index], candidates[index], pick)
         results.append(pick)
     interfere_real = jnp.stack([item[0] for item in results])[None]
     interfere_imag = jnp.stack([item[1] for item in results])[None]

time: 110 us -> 117 us (1.064)
  other arithmetic: 6.44 us -> 10.3 us
  local copies, waits for them, and re-layouts: 5.16 us -> 6.61 us
  between operations: 5.65 us -> 6.95 us
    select_n x1, other arithmetic: 0.01 us -> 3.92 us  [per_device(): pick = jnp.where(masks[slot, index], candidates[index], pick)]
    slice x1 -> x2, local copies, waits for them, and re-layouts: 0.58 us -> 2.05 us  [the longest x1 1.37 us: per_device(): chosen[slot] == bit]
    convert_element_type x1 -> x0, local copies, waits for them, and re-layouts: 1.35 us -> none  [compress(): return (joined * keep[None, None, :]).astype(jnp.bfloat16)]
    optimization_barrier x0 -> x1, local copies, waits for them, and re-layouts: none -> 1.34 us  [per_device(): masks, compressed = lax.optimization_barrier((masks, compressed))]
where the time goes in v6:
time: 117 us; the launch traced here: 116 us
  waiting for transfers between devices  47.1 us (40%)
  starting transfers between devices  31.6 us (27%)
  other arithmetic  10.3 us (9%)
  matrix products  9.01 us (8%)
  between operations  6.95 us (6%)
  local copies, waits for them, and re-layouts  6.61 us (6%)
  Pallas kernels  4.74 us (4%)
    all_to_all x1, waiting for transfers between devices, per_device(): lax.all_to_all(compressed, 'pulse', split_axis=1, concat_axis=2, tiled=True)  32.5 us
    all_to_all x1, starting transfers between devices, per_device(): lax.all_to_all(compressed, 'pulse', split_axis=1, concat_axis=2, tiled=True)  18 us
    ppermute x2, waiting for transfers between devices, per_device(): arrived = [lax.ppermute(focused, 'acq', pairs) for pairs in edge_pairs]  9.47 us
    ppermute x2, starting transfers between devices, per_device(): lax.ppermute(looked[slot], 'acq', [(dst, src) for src, dst in edge_pairs[...  9.12 us
    ppermute x2, waiting for transfers between devices, per_device(): lax.ppermute(looked[slot], 'acq', [(dst, src) for src, dst in edge_pairs[...  5.19 us
    pallas_call x1, Pallas kernels, band_tables(): pl.pallas_call(band_kernel, grid=(steps,), in_specs=[row_spec, row_spec],...  4.74 us
    dot_general x1, matrix products, compress(): lax.dot_general(band, echoes, dims, preferred_element_type=jnp.float32)  4.57 us
    ppermute x2, starting transfers between devices, per_device(): arrived = [lax.ppermute(focused, 'acq', pairs) for pairs in edge_pairs]  4.49 us
  transfers between devices with their start and end apart: 5, of which 4 were waited for; matrix products, arithmetic and copies ran while one was open for 2% of the time, Pallas kernels for 0%

profile of v6, /device:TPU:36, one launch (start us, length us, event | category | flops | bytes accessed | tf_op | source)
XLA Modules:
  0.0 116.4 jit_solution(4061286829091522911)
XLA Ops:
  0.6 0.0 copy-start
  0.7 1.4 %fusion.89 = (s32[1,1]{1,0:T(1,128)}, s32[1,1]{1,0:T(1,128)}) fusion(s32[1,2]{1,0:T(1,128)} %param.9), kind=kLoop, calls=%fused_computation.145 | loop fusion | bytes 16 | tf_op jit(solution)/shard_map/slice | solution.py:183
  7.2 0.7 multiply_convert_fusion
  8.1 0.7 broadcast_bitcast_fusion.im_ref
  8.9 0.7 broadcast_bitcast_fusion.1.re_ref
  10.3 0.1 add_bitcast_fusion.2
  10.4 4.7 %shard_map.68 = bf16[2,2,512,1535]{3,2,1,0:T(8,128)(2,1)} custom-call(f32[32,1536]{1,0:T(8,128)} %broadcast_bitcast_fusion.1.re_ref, f32[32,1536]{1,0:T(8,128)} %broadcast_bitcast_fusion.im_ref), custom_call_target="tpu_custom_call" | custom-call | tf_op jit(solution)/shard_map/pallas_call | solution.py:55
  15.1 0.0 copy-done
  15.1 4.6 %fusion.14 = bf16[2,512,256]{2,1,0:T(8,128)(2,1)S(1)} fusion(bf16[2,256,1535,1]{1,0,2,3:T(2,128)(2,1)S(1)} %bitcast.172, bf16[2,2,512,1535]{3,2,1,0:T(8,128)(2,1)} %shard_map.68, f32[256]{0:T(256)S(1)} %compare_convert_fusion), kind=kOutput, calls=%fused_computation.11 | convolution fusion | flops 1610088448 | bytes 8384512 | tf_op jit(solution)/shard_map/dot_general | solution.py:68
  19.7 0.0 copy-start.1
  19.7 1.3 %copy.31 = bf16[2,512,256]{2,0,1:T(2,128)(2,1)} copy(bf16[2,512,256]{2,1,0:T(8,128)(2,1)S(1)} %fusion.14) | data formatting | bytes 1048576 | tf_op jit(solution)/shard_map/optimization_barrier | solution.py:184
  21.1 18.0 %all-to-all-start = ((bf16[2,512,256]{2,0,1:T(2,128)(2,1)}), bf16[2,512,256]{2,0,1:T(2,128)(2,1)S(1)}, u32[]{:S(2)}, u32[]{:S(2)}) async-start(bf16[2,512,256]{2,0,1:T(2,128)(2,1)} %copy.31), calls=%async_computation | async-start | bytes 1048576 | tf_op jit(solution)/shard_map/all_to_all | solution.py:185
  39.1 0.1 fusion.76
  39.2 0.1 fusion.72
  39.4 0.1 fusion.74
  39.5 0.1 fusion.73
  39.7 0.3 fusion.71
  39.9 0.3 fusion.65
  40.3 0.0 copy-done.1
  40.3 32.5 %all-to-all-done = bf16[2,512,256]{2,0,1:T(2,128)(2,1)S(1)} async-done(((bf16[2,512,256]{2,0,1:T(2,128)(2,1)}), bf16[2,512,256]{2,0,1:T(2,128)(2,1)S(1)}, u32[]{:S(2)}, u32[]{:S(2)}) %all-to-all-start) | async-done | bytes 524320 | tf_op jit(solution)/shard_map/all_to_all | solution.py:185
  72.8 0.3 copy.85
  73.1 0.2 reshape.350
  73.3 0.6 convolution_bitcast_fusion.3
  73.9 0.2 multiply_subtract_fusion.1
  74.1 1.0 convolution_bitcast_fusion.2
  75.1 2.1 %fusion.29 = (f32[1,16,64,128]{3,2,1,0:T(8,128)S(1)}, f32[1,16,64,128]{3,2,1,0:T(8,128)S(1)}) fusion(f32[2,16,64,128]{3,2,1,0:T(8,128)S(1)} %convolution_bitcast_fusion.2, f32[64,128]{1,0:T(8,128)S(1)} %fusion.62, f32[16]{0:T(128)S(1)} %broadcast_multiply_fusion), kind=kLoop, calls=%fused_computation.28 | loop fusion | flops 1048576 | bytes 2129984 | tf_op jit(solution)/shard_map/sub | solution.py:27
  77.2 1.0 convolution_bitcast_fusion.1
  78.2 0.2 multiply_subtract_fusion
  78.4 1.1 fusion.20
  79.5 0.2 convert_element_type.150
  79.7 2.4 %collective-permute-start = (bf16[2,16,8192]{2,1,0:T(8,128)(2,1)S(1)}, bf16[2,16,8192]{2,1,0:T(8,128)(2,1)S(1)}, u32[]{:S(2)}, u32[]{:S(2)}) collective-permute-start(bf16[2,16,8192]{2,1,0:T(8,128)(2,1)S(1)} %convert_element_type.150), channel_id=1, source_target_pairs={{0,32},{32,160},{64,192},{96,64},{128,0},{160,128},{192,224},{224,... | collective-permute-start | bytes 1572872 | tf_op jit(solution)/shard_map/ppermute | solution.py:187
  82.2 2.1 %collective-permute-start.1 = (bf16[2,16,8192]{2,1,0:T(8,128)(2,1)S(1)}, bf16[2,16,8192]{2,1,0:T(8,128)(2,1)S(1)}, u32[]{:S(2)}, u32[]{:S(2)}) collective-permute-start(bf16[2,16,8192]{2,1,0:T(8,128)(2,1)S(1)} %convert_element_type.150), channel_id=1, source_target_pairs={{0,64},{32,288},{64,320},{96,32},{128,384},{160,224},{192,128},{22... | collective-permute-start | bytes 1572872 | tf_op jit(solution)/shard_map/ppermute | solution.py:187
  84.3 0.1 convert_element_type.151
  84.3 8.8 %collective-permute-done = bf16[2,16,8192]{2,1,0:T(8,128)(2,1)S(1)} collective-permute-done((bf16[2,16,8192]{2,1,0:T(8,128)(2,1)S(1)}, bf16[2,16,8192]{2,1,0:T(8,128)(2,1)S(1)}, u32[]{:S(2)}, u32[]{:S(2)}) %collective-permute-start) | collective-permute-done | bytes 524320 | tf_op jit(solution)/shard_map/ppermute | solution.py:187
  93.2 0.1 convert_element_type.152
  93.2 0.6 collective-permute-done.1
  93.9 0.1 convert_element_type.153
  94.0 0.2 add_bitcast_fusion.1
  94.2 0.1 copy.56
  94.3 0.1 copy.57
  94.4 0.1 copy.58
  94.5 0.1 copy.59
  94.6 0.2 maximum_reduce_fusion
  94.8 0.7 convolution_multiply_fusion
  95.6 0.1 copy.38
  95.7 0.2 slice.170
  95.9 7.2 %collective-permute-start.2 = (f32[2,4,512]{2,1,0:T(4,128)S(1)}, f32[2,4,512]{2,1,0:T(4,128)S(1)}, u32[]{:S(2)}, u32[]{:S(2)}) collective-permute-start(f32[2,4,512]{2,1,0:T(4,128)S(1)} %slice.170), channel_id=1, source_target_pairs={{64,0},{288,32},{320,64},{32,96},{384,128},{224,160},{128,192},{48... | collective-permute-start | bytes 49160 | tf_op jit(solution)/shard_map/ppermute | solution.py:190
  103.1 0.7 fusion.88
  103.8 0.1 copy.39
  103.9 0.2 slice.176
  104.0 1.9 %collective-permute-start.3 = (f32[2,4,512]{2,1,0:T(4,128)S(1)}, f32[2,4,512]{2,1,0:T(4,128)S(1)}, u32[]{:S(2)}, u32[]{:S(2)}) collective-permute-start(f32[2,4,512]{2,1,0:T(4,128)S(1)} %slice.176), channel_id=1, source_target_pairs={{32,0},{160,32},{192,64},{64,96},{0,128},{128,160},{224,192},{96,2... | collective-permute-start | bytes 49160 | tf_op jit(solution)/shard_map/ppermute | solution.py:190
  106.0 0.0 collective-permute-done.2
  106.0 5.2 %collective-permute-done.3 = f32[2,4,512]{2,1,0:T(4,128)S(1)} collective-permute-done((f32[2,4,512]{2,1,0:T(4,128)S(1)}, f32[2,4,512]{2,1,0:T(4,128)S(1)}, u32[]{:S(2)}, u32[]{:S(2)}) %collective-permute-start.3) | collective-permute-done | bytes 16416 | tf_op jit(solution)/shard_map/ppermute | solution.py:190
  111.2 3.9 %select_select_fusion.1 = (f32[2,4,512]{2,1,0:T(4,128)S(1)}, f32[2,4,512]{2,1,0:T(4,128)S(1)}) fusion(f32[2,4,512]{2,1,0:T(4,128)S(1)} %slice.170, f32[2,4,512]{2,1,0:T(4,128)S(1)} %slice.176, f32[1,4,512]{2,1,0:T(4,128)S(1)} %get-tuple-element.41, f32[1,4,512]{2,1,0:T(4,128)S(1)} %get-tuple-element.40, f32[1,4,512]{2,1,0:T(4,128)S(1)} %get-tuple-element.39, ...), kind=kLoop, calls=%fused_computation.111 | loop fusion | flops 32768 | bytes 98310 | tf_op jit(solution)/shard_map/jit(_where)/select_n | solution.py:202
  115.1 0.6 maximum_bitcast_fusion.7
  115.8 0.6 maximum_bitcast_fusion.6
  (30 shorter events, 0.3 us)
Async XLA Ops:
  0.6 14.5 %copy-start = (bf16[1,2,256,1535]{2,1,3,0:T(2,128)(2,1)S(1)}, bf16[1,2,256,1535]{2,1,3,0:T(2,128)(2,1)}, u32[]{:S(2)}) copy-start(bf16[1,2,256,1535]{2,1,3,0:T(2,128)(2,1)} %param.5) | copy-start | bytes 4715524
  19.7 20.6 %copy-start.1 = (f32[16]{0:T(128)S(1)}, f32[16]{0:T(128)}, u32[]{:S(2)}) copy-start(f32[16]{0:T(128)} %param.8) | copy-start | bytes 196
  21.1 51.7 %all-to-all-start = ((bf16[2,512,256]{2,0,1:T(2,128)(2,1)}), bf16[2,512,256]{2,0,1:T(2,128)(2,1)S(1)}, u32[]{:S(2)}, u32[]{:S(2)}) async-start(bf16[2,512,256]{2,0,1:T(2,128)(2,1)} %copy.31), calls=%async_computation | async-start | bytes 1048576 | tf_op jit(solution)/shard_map/all_to_all | solution.py:185
  79.7 13.4 %collective-permute-start = (bf16[2,16,8192]{2,1,0:T(8,128)(2,1)S(1)}, bf16[2,16,8192]{2,1,0:T(8,128)(2,1)S(1)}, u32[]{:S(2)}, u32[]{:S(2)}) collective-permute-start(bf16[2,16,8192]{2,1,0:T(8,128)(2,1)S(1)} %convert_element_type.150), channel_id=1, source_target_pairs={{0,32},{32,160},{64,192},{96,64},{128,0},{160,128},{192,224},{224,... | collective-permute-start | bytes 1572872 | tf_op jit(solution)/shard_map/ppermute | solution.py:187
  82.2 11.7 %collective-permute-start.1 = (bf16[2,16,8192]{2,1,0:T(8,128)(2,1)S(1)}, bf16[2,16,8192]{2,1,0:T(8,128)(2,1)S(1)}, u32[]{:S(2)}, u32[]{:S(2)}) collective-permute-start(bf16[2,16,8192]{2,1,0:T(8,128)(2,1)S(1)} %convert_element_type.150), channel_id=1, source_target_pairs={{0,64},{32,288},{64,320},{96,32},{128,384},{160,224},{192,128},{22... | collective-permute-start | bytes 1572872 | tf_op jit(solution)/shard_map/ppermute | solution.py:187
  95.9 10.1 %collective-permute-start.2 = (f32[2,4,512]{2,1,0:T(4,128)S(1)}, f32[2,4,512]{2,1,0:T(4,128)S(1)}, u32[]{:S(2)}, u32[]{:S(2)}) collective-permute-start(f32[2,4,512]{2,1,0:T(4,128)S(1)} %slice.170), channel_id=1, source_target_pairs={{64,0},{288,32},{320,64},{32,96},{384,128},{224,160},{128,192},{48... | collective-permute-start | bytes 49160 | tf_op jit(solution)/shard_map/ppermute | solution.py:190
  104.0 7.1 %collective-permute-start.3 = (f32[2,4,512]{2,1,0:T(4,128)S(1)}, f32[2,4,512]{2,1,0:T(4,128)S(1)}, u32[]{:S(2)}, u32[]{:S(2)}) collective-permute-start(f32[2,4,512]{2,1,0:T(4,128)S(1)} %slice.176), channel_id=1, source_target_pairs={{32,0},{160,32},{192,64},{64,96},{0,128},{128,160},{224,192},{96,2... | collective-permute-start | bytes 49160 | tf_op jit(solution)/shard_map/ppermute | solution.py:190

commit v7 on v3

--- a/solution.py
+++ b/solution.py
@@ -153,6 +153,9 @@
 def per_device(raw_echo, chirp_phase, pulse_counts, azimuth_rate, partner_bits):
     echoes = raw_echo[0]
     pulses_dev = echoes.shape[1]
+    devices = lax.axis_size("pulse")
+    warm = jnp.broadcast_to(azimuth_rate[:1], (devices, 128))
+    warm = lax.all_to_all(warm, "pulse", 0, 0, tiled=True)
     amplitude = 2.0 / math.sqrt(TAPS)
     table_re = (amplitude * jnp.cos(chirp_phase)).astype(jnp.bfloat16)
     table_im = (amplitude * jnp.sin(chirp_phase)).astype(jnp.bfloat16)
@@ -160,8 +163,10 @@
     live_pulses = pulse_counts[0]
     first_pulse = lax.axis_index("pulse") * pulses_dev
     compressed = compress(echoes, band, first_pulse, live_pulses)
+    warm, compressed = lax.optimization_barrier((warm, compressed))
+    live_rate = azimuth_rate + 0.0 * warm[0, 0]
     turned = lax.all_to_all(compressed, "pulse", split_axis=1, concat_axis=2, tiled=True)
-    focused = azimuth(turned, azimuth_rate).astype(jnp.bfloat16)
+    focused = azimuth(turned, live_rate).astype(jnp.bfloat16)
     chosen = partner_bits[0]
     acq_size = lax.axis_size("acq")
     me = lax.axis_index("acq")

time: 110 us -> 125 us (1.14)
  the two profiles are of different devices: /device:TPU:36 before, /device:TPU:4 now
where the time goes in v7:
time: 125 us
  waiting for transfers between devices  47.1 us (38%)
  starting transfers between devices  44.3 us (35%)
  matrix products  8.99 us (7%)
  local copies, waits for them, and re-layouts  7.02 us (6%)
  other arithmetic  6.33 us (5%)
  between operations  6.32 us (5%)
  Pallas kernels  4.76 us (4%)
    all_to_all x1, waiting for transfers between devices, per_device(): lax.all_to_all(compressed, 'pulse', split_axis=1, concat_axis=2, tiled=True)  30.7 us
    all_to_all x1, starting transfers between devices, per_device(): warm = lax.all_to_all(warm, 'pulse', 0, 0, tiled=True)  18.1 us
    all_to_all x1, starting transfers between devices, per_device(): lax.all_to_all(compressed, 'pulse', split_axis=1, concat_axis=2, tiled=True)  12.3 us
    ppermute x2, starting transfers between devices, per_device(): lax.ppermute(looked[slot], 'acq', [(dst, src) for src, dst in edge_pairs[...  9.38 us
    ppermute x2, waiting for transfers between devices, per_device(): arrived = [lax.ppermute(focused, 'acq', pairs) for pairs in edge_pairs]  8.87 us
    ppermute x2, waiting for transfers between devices, per_device(): lax.ppermute(looked[slot], 'acq', [(dst, src) for src, dst in edge_pairs[...  5.19 us
    pallas_call x1, Pallas kernels, band_tables(): pl.pallas_call(band_kernel, grid=(steps,), in_specs=[row_spec, row_spec],...  4.76 us
    dot_general x1, matrix products, compress(): lax.dot_general(band, echoes, dims, preferred_element_type=jnp.float32)  4.57 us
  transfers between devices with their start and end apart: 6, of which 4 were waited for; matrix products, arithmetic and copies ran while one was open for 8% of the time, Pallas kernels for 4%

profile of v7, /device:TPU:4, one launch (start us, length us, event | category | flops | bytes accessed | tf_op | source)
XLA Modules:
  0.0 124.8 jit_solution(3951896958628824849)
XLA Ops:
  0.6 0.0 copy-start
  0.6 1.4 %broadcast_in_dim.10 = f32[32,1,128]{2,1,0:T(1,128)} broadcast(f32[]{:T(128)} %bitcast.172), dimensions={} | broadcast | bytes 16388 | tf_op jit(solution)/shard_map/broadcast_in_dim | solution.py:157
  2.0 18.1 %all-to-all-start = ((f32[32,1,128]{2,1,0:T(1,128)}), f32[32,1,128]{2,1,0:T(1,128)S(1)}, u32[]{:S(2)}, u32[]{:S(2)}) async-start(f32[32,1,128]{2,1,0:T(1,128)} %broadcast_in_dim.10), calls=%async_computation | async-start | bytes 32768 | tf_op jit(solution)/shard_map/all_to_all | solution.py:158
  20.1 0.7 multiply_convert_fusion
  21.0 0.7 broadcast_bitcast_fusion.im_ref
  21.8 0.7 broadcast_bitcast_fusion.1.re_ref
  23.2 4.8 %shard_map.68 = bf16[2,2,512,1535]{3,2,1,0:T(8,128)(2,1)} custom-call(f32[32,1536]{1,0:T(8,128)} %broadcast_bitcast_fusion.1.re_ref, f32[32,1536]{1,0:T(8,128)} %broadcast_bitcast_fusion.im_ref), custom_call_target="tpu_custom_call" | custom-call | tf_op jit(solution)/shard_map/pallas_call | solution.py:55
  28.0 0.0 copy-done
  28.0 4.6 %fusion.14 = bf16[2,512,256]{2,1,0:T(8,128)(2,1)S(1)} fusion(bf16[2,256,1535,1]{1,0,2,3:T(2,128)(2,1)S(1)} %bitcast.158, bf16[2,2,512,1535]{3,2,1,0:T(8,128)(2,1)} %shard_map.68, f32[256]{0:T(256)S(1)} %compare_convert_fusion), kind=kOutput, calls=%fused_computation.11 | convolution fusion | flops 1610088448 | bytes 8384512 | tf_op jit(solution)/shard_map/dot_general | solution.py:68
  32.5 0.0 copy-start.2
  32.6 2.3 %all-to-all-done = f32[32,1,128]{2,1,0:T(1,128)S(1)} async-done(((f32[32,1,128]{2,1,0:T(1,128)}), f32[32,1,128]{2,1,0:T(1,128)S(1)}, u32[]{:S(2)}, u32[]{:S(2)}) %all-to-all-start) | async-done | bytes 16416 | tf_op jit(solution)/shard_map/all_to_all | solution.py:158
  34.9 1.3 %copy.31 = bf16[2,512,256]{2,0,1:T(2,128)(2,1)} copy(bf16[2,512,256]{2,1,0:T(8,128)(2,1)S(1)} %fusion.14) | data formatting | bytes 1048576 | tf_op jit(solution)/shard_map/optimization_barrier | solution.py:166
  36.2 12.3 %all-to-all-start.1 = ((bf16[2,512,256]{2,0,1:T(2,128)(2,1)}), bf16[2,512,256]{2,0,1:T(2,128)(2,1)S(1)}, u32[]{:S(2)}, u32[]{:S(2)}) async-start(bf16[2,512,256]{2,0,1:T(2,128)(2,1)} %copy.31), calls=%async_computation.1 | async-start | bytes 1048576 | tf_op jit(solution)/shard_map/all_to_all | solution.py:168
  48.5 0.1 fusion.76
  48.7 0.1 fusion.72
  48.8 0.1 fusion.74
  49.0 0.1 fusion.73
  49.1 0.3 fusion.71
  49.4 0.3 fusion.65
  49.8 0.5 slice.148
  50.9 0.0 copy-done.2
  51.0 30.7 %all-to-all-done.1 = bf16[2,512,256]{2,0,1:T(2,128)(2,1)S(1)} async-done(((bf16[2,512,256]{2,0,1:T(2,128)(2,1)}), bf16[2,512,256]{2,0,1:T(2,128)(2,1)S(1)}, u32[]{:S(2)}, u32[]{:S(2)}) %all-to-all-start.1) | async-done | bytes 524320 | tf_op jit(solution)/shard_map/all_to_all | solution.py:168
  81.7 0.3 copy.85
  81.9 0.2 reshape.355
  82.1 0.6 convolution_bitcast_fusion.3
  82.8 0.2 multiply_subtract_fusion.1
  82.9 1.0 convolution_bitcast_fusion.2
  83.9 2.1 %fusion.29 = (f32[1,16,64,128]{3,2,1,0:T(8,128)S(1)}, f32[1,16,64,128]{3,2,1,0:T(8,128)S(1)}) fusion(f32[2,16,64,128]{3,2,1,0:T(8,128)S(1)} %convolution_bitcast_fusion.2, f32[64,128]{1,0:T(8,128)S(1)} %fusion.62, f32[16]{0:T(128)S(1)} %add_multiply_fusion), kind=kLoop, calls=%fused_computation.28 | loop fusion | flops 1048576 | bytes 2129984 | tf_op jit(solution)/shard_map/sub | solution.py:27
  86.1 1.0 convolution_bitcast_fusion.1
  87.1 0.2 multiply_subtract_fusion
  87.3 1.1 fusion.20
  88.4 0.2 convert_element_type.150
  88.6 2.4 %collective-permute-start = (bf16[2,16,8192]{2,1,0:T(8,128)(2,1)S(1)}, bf16[2,16,8192]{2,1,0:T(8,128)(2,1)S(1)}, u32[]{:S(2)}, u32[]{:S(2)}) collective-permute-start(bf16[2,16,8192]{2,1,0:T(8,128)(2,1)S(1)} %convert_element_type.150), channel_id=1, source_target_pairs={{0,32},{32,160},{64,192},{96,64},{128,0},{160,128},{192,224},{224,... | collective-permute-start | bytes 1572872 | tf_op jit(solution)/shard_map/ppermute | solution.py:186
  91.0 2.1 %collective-permute-start.1 = (bf16[2,16,8192]{2,1,0:T(8,128)(2,1)S(1)}, bf16[2,16,8192]{2,1,0:T(8,128)(2,1)S(1)}, u32[]{:S(2)}, u32[]{:S(2)}) collective-permute-start(bf16[2,16,8192]{2,1,0:T(8,128)(2,1)S(1)} %convert_element_type.150), channel_id=1, source_target_pairs={{0,64},{32,288},{64,320},{96,32},{128,384},{160,224},{192,128},{22... | collective-permute-start | bytes 1572872 | tf_op jit(solution)/shard_map/ppermute | solution.py:186
  93.1 0.1 convert_element_type.151
  93.2 8.9 %collective-permute-done = bf16[2,16,8192]{2,1,0:T(8,128)(2,1)S(1)} collective-permute-done((bf16[2,16,8192]{2,1,0:T(8,128)(2,1)S(1)}, bf16[2,16,8192]{2,1,0:T(8,128)(2,1)S(1)}, u32[]{:S(2)}, u32[]{:S(2)}) %collective-permute-start) | collective-permute-done | bytes 524320 | tf_op jit(solution)/shard_map/ppermute | solution.py:186
  102.1 0.1 convert_element_type.152
  102.1 0.0 collective-permute-done.1
  102.1 0.1 convert_element_type.153
  102.2 0.2 add_bitcast_fusion.1
  102.5 0.1 copy.56
  102.6 0.1 copy.57
  102.7 0.1 copy.58
  102.8 0.1 copy.59
  102.9 0.0 copy-start.1
  102.9 0.2 maximum_reduce_fusion
  103.1 0.7 convolution_multiply_fusion
  103.8 0.1 copy.38
  104.0 0.2 slice.159
  104.1 7.5 %collective-permute-start.2 = (f32[2,4,512]{2,1,0:T(4,128)S(1)}, f32[2,4,512]{2,1,0:T(4,128)S(1)}, u32[]{:S(2)}, u32[]{:S(2)}) collective-permute-start(f32[2,4,512]{2,1,0:T(4,128)S(1)} %slice.159), channel_id=1, source_target_pairs={{64,0},{288,32},{320,64},{32,96},{384,128},{224,160},{128,192},{48... | collective-permute-start | bytes 49160 | tf_op jit(solution)/shard_map/ppermute | solution.py:189
  111.6 0.0 copy-done.1
  111.6 0.6 fusion.88
  116.1 0.1 copy.39
  116.2 0.2 slice.163
  116.4 1.9 %collective-permute-start.3 = (f32[2,4,512]{2,1,0:T(4,128)S(1)}, f32[2,4,512]{2,1,0:T(4,128)S(1)}, u32[]{:S(2)}, u32[]{:S(2)}) collective-permute-start(f32[2,4,512]{2,1,0:T(4,128)S(1)} %slice.163), channel_id=1, source_target_pairs={{32,0},{160,32},{192,64},{64,96},{0,128},{128,160},{224,192},{96,2... | collective-permute-start | bytes 49160 | tf_op jit(solution)/shard_map/ppermute | solution.py:189
  118.3 0.0 collective-permute-done.2
  118.3 5.2 %collective-permute-done.3 = f32[2,4,512]{2,1,0:T(4,128)S(1)} collective-permute-done((f32[2,4,512]{2,1,0:T(4,128)S(1)}, f32[2,4,512]{2,1,0:T(4,128)S(1)}, u32[]{:S(2)}, u32[]{:S(2)}) %collective-permute-start.3) | collective-permute-done | bytes 16416 | tf_op jit(solution)/shard_map/ppermute | solution.py:189
  123.6 0.6 maximum_bitcast_fusion.7
  124.2 0.6 maximum_bitcast_fusion.6
  (30 shorter events, 0.3 us)
Async XLA Ops:
  0.6 27.3 %copy-start = (bf16[1,2,256,1535]{2,1,3,0:T(2,128)(2,1)S(1)}, bf16[1,2,256,1535]{2,1,3,0:T(2,128)(2,1)}, u32[]{:S(2)}) copy-start(bf16[1,2,256,1535]{2,1,3,0:T(2,128)(2,1)} %param.5) | copy-start | bytes 4715524
  2.0 32.9 %all-to-all-start = ((f32[32,1,128]{2,1,0:T(1,128)}), f32[32,1,128]{2,1,0:T(1,128)S(1)}, u32[]{:S(2)}, u32[]{:S(2)}) async-start(f32[32,1,128]{2,1,0:T(1,128)} %broadcast_in_dim.10), calls=%async_computation | async-start | bytes 32768 | tf_op jit(solution)/shard_map/all_to_all | solution.py:158
  32.5 18.4 %copy-start.2 = (f32[16]{0:T(128)S(1)}, f32[16]{0:T(128)}, u32[]{:S(2)}) copy-start(f32[16]{0:T(128)} %param.8) | copy-start | bytes 196
  36.2 45.4 %all-to-all-start.1 = ((bf16[2,512,256]{2,0,1:T(2,128)(2,1)}), bf16[2,512,256]{2,0,1:T(2,128)(2,1)S(1)}, u32[]{:S(2)}, u32[]{:S(2)}) async-start(bf16[2,512,256]{2,0,1:T(2,128)(2,1)} %copy.31), calls=%async_computation.1 | async-start | bytes 1048576 | tf_op jit(solution)/shard_map/all_to_all | solution.py:168
  88.6 13.5 %collective-permute-start = (bf16[2,16,8192]{2,1,0:T(8,128)(2,1)S(1)}, bf16[2,16,8192]{2,1,0:T(8,128)(2,1)S(1)}, u32[]{:S(2)}, u32[]{:S(2)}) collective-permute-start(bf16[2,16,8192]{2,1,0:T(8,128)(2,1)S(1)} %convert_element_type.150), channel_id=1, source_target_pairs={{0,32},{32,160},{64,192},{96,64},{128,0},{160,128},{192,224},{224,... | collective-permute-start | bytes 1572872 | tf_op jit(solution)/shard_map/ppermute | solution.py:186
  91.0 11.1 %collective-permute-start.1 = (bf16[2,16,8192]{2,1,0:T(8,128)(2,1)S(1)}, bf16[2,16,8192]{2,1,0:T(8,128)(2,1)S(1)}, u32[]{:S(2)}, u32[]{:S(2)}) collective-permute-start(bf16[2,16,8192]{2,1,0:T(8,128)(2,1)S(1)} %convert_element_type.150), channel_id=1, source_target_pairs={{0,64},{32,288},{64,320},{96,32},{128,384},{160,224},{192,128},{22... | collective-permute-start | bytes 1572872 | tf_op jit(solution)/shard_map/ppermute | solution.py:186
  102.9 8.7 %copy-start.1 = (s32[1,2]{1,0:T(1,128)S(1)}, s32[1,2]{1,0:T(1,128)}, u32[]{:S(2)}) copy-start(s32[1,2]{1,0:T(1,128)} %param.9) | copy-start | bytes 28
  104.1 14.2 %collective-permute-start.2 = (f32[2,4,512]{2,1,0:T(4,128)S(1)}, f32[2,4,512]{2,1,0:T(4,128)S(1)}, u32[]{:S(2)}, u32[]{:S(2)}) collective-permute-start(f32[2,4,512]{2,1,0:T(4,128)S(1)} %slice.159), channel_id=1, source_target_pairs={{64,0},{288,32},{320,64},{32,96},{384,128},{224,160},{128,192},{48... | collective-permute-start | bytes 49160 | tf_op jit(solution)/shard_map/ppermute | solution.py:189
  116.4 7.1 %collective-permute-start.3 = (f32[2,4,512]{2,1,0:T(4,128)S(1)}, f32[2,4,512]{2,1,0:T(4,128)S(1)}, u32[]{:S(2)}, u32[]{:S(2)}) collective-permute-start(f32[2,4,512]{2,1,0:T(4,128)S(1)} %slice.163), channel_id=1, source_target_pairs={{32,0},{160,32},{192,64},{64,96},{0,128},{128,160},{224,192},{96,2... | collective-permute-start | bytes 49160 | tf_op jit(solution)/shard_map/ppermute | solution.py:189

commit v8 on v6

--- a/solution.py
+++ b/solution.py
@@ -180,9 +180,9 @@
     for slot in range(2):
         cand_bits.append(jnp.where(me_parity == 1, low_bits[slot], high_bits[slot]))
         cand_bits.append(jnp.where(me_parity == 1, high_bits[slot], low_bits[slot]))
-    masks = jnp.stack([jnp.stack([chosen[slot] == bit for bit in cand_bits]) for slot in range(2)])
-    masks, compressed = lax.optimization_barrier((masks, compressed))
+    preds = tuple(chosen[slot] == bit for slot in range(2) for bit in cand_bits)
     turned = lax.all_to_all(compressed, "pulse", split_axis=1, concat_axis=2, tiled=True)
+    *preds, turned = lax.optimization_barrier((*preds, turned))
     focused = azimuth(turned, azimuth_rate).astype(jnp.bfloat16)
     arrived = [lax.ppermute(focused, "acq", pairs) for pairs in edge_pairs]
     looked = cross_looks(focused, arrived)
@@ -199,7 +199,7 @@
     for slot in range(2):
         pick = candidates[0]
         for index in range(1, len(candidates)):
-            pick = jnp.where(masks[slot, index], candidates[index], pick)
+            pick = jnp.where(preds[slot * len(candidates) + index], candidates[index], pick)
         results.append(pick)
     interfere_real = jnp.stack([item[0] for item in results])[None]
     interfere_imag = jnp.stack([item[1] for item in results])[None]

time: 117 us -> 106 us (0.906)
  waiting for transfers between devices: 47.1 us -> 42.6 us
  other arithmetic: 10.3 us -> 6.44 us
  between operations: 6.95 us -> 5.67 us
  local copies, waits for them, and re-layouts: 6.61 us -> 5.35 us
    all_to_all x1, waiting for transfers between devices: 32.5 us -> 28 us  [per_device(): lax.all_to_all(compressed, 'pulse', split_axis=1, concat_axis=2, tiled=True)]
    select_n x1, other arithmetic: 3.92 us -> 0.01 us  [per_device(): jnp.where(preds[slot * len(candidates) + index], candidates[index], pick)]
    convert_element_type x0 -> x1, local copies, waits for them, and re-layouts: none -> 1.35 us  [compress(): return (joined * keep[None, None, :]).astype(jnp.bfloat16)]
    optimization_barrier x1 -> x0, local copies, waits for them, and re-layouts: 1.34 us -> none  [per_device(): masks, compressed = lax.optimization_barrier((masks, compressed))]
where the time goes in v8:
time: 106 us; the launch traced here: 105 us
  waiting for transfers between devices  42.6 us (40%)
  starting transfers between devices  31.6 us (30%)
  matrix products  9.01 us (8%)
  other arithmetic  6.44 us (6%)
  between operations  5.67 us (5%)
  local copies, waits for them, and re-layouts  5.35 us (5%)
  Pallas kernels  4.76 us (4%)
    all_to_all x1, waiting for transfers between devices, per_device(): lax.all_to_all(compressed, 'pulse', split_axis=1, concat_axis=2, tiled=True)  28 us
    all_to_all x1, starting transfers between devices, per_device(): lax.all_to_all(compressed, 'pulse', split_axis=1, concat_axis=2, tiled=True)  18 us
    ppermute x2, waiting for transfers between devices, per_device(): arrived = [lax.ppermute(focused, 'acq', pairs) for pairs in edge_pairs]  9.46 us
    ppermute x2, starting transfers between devices, per_device(): lax.ppermute(looked[slot], 'acq', [(dst, src) for src, dst in edge_pairs[...  9.13 us
    ppermute x2, waiting for transfers between devices, per_device(): lax.ppermute(looked[slot], 'acq', [(dst, src) for src, dst in edge_pairs[...  5.19 us
    pallas_call x1, Pallas kernels, band_tables(): pl.pallas_call(band_kernel, grid=(steps,), in_specs=[row_spec, row_spec],...  4.76 us
    dot_general x1, matrix products, compress(): lax.dot_general(band, echoes, dims, preferred_element_type=jnp.float32)  4.57 us
    ppermute x2, starting transfers between devices, per_device(): arrived = [lax.ppermute(focused, 'acq', pairs) for pairs in edge_pairs]  4.49 us
  transfers between devices with their start and end apart: 5, of which 4 were waited for; matrix products, arithmetic and copies ran while one was open for 2% of the time, Pallas kernels for 0%

profile of v8, /device:TPU:36, one launch (start us, length us, event | category | flops | bytes accessed | tf_op | source)
XLA Modules:
  0.0 105.5 jit_solution(3450222592831422984)
XLA Ops:
  0.6 0.0 copy-start
  0.6 0.8 multiply_convert_fusion
  1.6 0.7 broadcast_bitcast_fusion.im_ref
  2.5 0.7 broadcast_bitcast_fusion.1.re_ref
  3.8 4.8 %shard_map.68 = bf16[2,2,512,1535]{3,2,1,0:T(8,128)(2,1)} custom-call(f32[32,1536]{1,0:T(8,128)} %broadcast_bitcast_fusion.1.re_ref, f32[32,1536]{1,0:T(8,128)} %broadcast_bitcast_fusion.im_ref), custom_call_target="tpu_custom_call" | custom-call | tf_op jit(solution)/shard_map/pallas_call | solution.py:55
  8.6 0.0 copy-done
  8.6 4.6 %fusion.14 = bf16[2,512,256]{2,1,0:T(8,128)(2,1)S(1)} fusion(bf16[2,256,1535,1]{1,0,2,3:T(2,128)(2,1)S(1)} %bitcast.164, bf16[2,2,512,1535]{3,2,1,0:T(8,128)(2,1)} %shard_map.68, f32[256]{0:T(256)S(1)} %compare_convert_fusion), kind=kOutput, calls=%fused_computation.11 | convolution fusion | flops 1610088448 | bytes 8384512 | tf_op jit(solution)/shard_map/dot_general | solution.py:68
  13.2 0.0 copy-start.1
  13.2 0.0 copy-start.2
  13.2 1.3 %copy.29 = bf16[2,512,256]{2,0,1:T(2,128)(2,1)} copy(bf16[2,512,256]{2,1,0:T(8,128)(2,1)S(1)} %fusion.14) | data formatting | bytes 1048576 | tf_op jit(solution)/shard_map/convert_element_type | solution.py:72
  14.6 18.0 %all-to-all-start = ((bf16[2,512,256]{2,0,1:T(2,128)(2,1)}), bf16[2,512,256]{2,0,1:T(2,128)(2,1)S(1)}, u32[]{:S(2)}, u32[]{:S(2)}) async-start(bf16[2,512,256]{2,0,1:T(2,128)(2,1)} %copy.29), calls=%async_computation | async-start | bytes 1048576 | tf_op jit(solution)/shard_map/all_to_all | solution.py:184
  32.6 0.0 copy-done.1
  32.6 0.6 fusion.90
  37.1 0.1 fusion.78
  37.2 0.1 fusion.74
  37.4 0.1 fusion.76
  37.5 0.1 fusion.75
  37.7 0.3 fusion.73
  37.9 0.3 fusion.67
  38.3 0.0 copy-done.2
  38.3 28.0 %all-to-all-done = bf16[2,512,256]{2,0,1:T(2,128)(2,1)S(1)} async-done(((bf16[2,512,256]{2,0,1:T(2,128)(2,1)}), bf16[2,512,256]{2,0,1:T(2,128)(2,1)S(1)}, u32[]{:S(2)}, u32[]{:S(2)}) %all-to-all-start) | async-done | bytes 524320 | tf_op jit(solution)/shard_map/all_to_all | solution.py:184
  66.3 0.3 copy.91
  66.6 0.2 all_to_all.16
  66.8 0.1 copy.57
  67.0 0.6 convolution_bitcast_fusion.3
  67.6 0.2 multiply_subtract_fusion.1
  67.8 1.0 convolution_bitcast_fusion.2
  68.8 2.1 %fusion.29 = (f32[1,16,64,128]{3,2,1,0:T(8,128)S(1)}, f32[1,16,64,128]{3,2,1,0:T(8,128)S(1)}) fusion(f32[2,16,64,128]{3,2,1,0:T(8,128)S(1)} %convolution_bitcast_fusion.2, f32[64,128]{1,0:T(8,128)S(1)} %fusion.64, f32[16]{0:T(128)S(1)} %broadcast_multiply_fusion), kind=kLoop, calls=%fused_computation.28 | loop fusion | flops 1048576 | bytes 2129984 | tf_op jit(solution)/shard_map/sub | solution.py:27
  70.9 1.0 convolution_bitcast_fusion.1
  71.9 0.2 multiply_subtract_fusion
  72.1 1.1 %fusion.20 = bf16[2,16,64,128]{3,2,1,0:T(8,128)(2,1)S(1)} fusion(f32[1,16,64,128]{3,2,1,0:T(8,128)S(1)} %get-tuple-element.21, f32[1,16,64,128]{3,2,1,0:T(8,128)S(1)} %get-tuple-element.20, f32[1,2,64,64]{2,3,1,0:T(8,128)S(1)} %get-tuple-element.43, f32[1,2,64,64]{2,3,1,0:T(8,128)S(1)} %get-tuple-element.36), kind=kOutput, calls=%fused_computation.13 | convolution fusion | flops 403456000 | bytes 1638400 | tf_op jit(solution)/shard_map/pckb,pqka->qcab/dot_general | solution.py:116
  73.2 0.2 convert_element_type.150
  73.4 2.4 %collective-permute-start = (bf16[2,16,8192]{2,1,0:T(8,128)(2,1)S(1)}, bf16[2,16,8192]{2,1,0:T(8,128)(2,1)S(1)}, u32[]{:S(2)}, u32[]{:S(2)}) collective-permute-start(bf16[2,16,8192]{2,1,0:T(8,128)(2,1)S(1)} %convert_element_type.150), channel_id=1, source_target_pairs={{0,32},{32,160},{64,192},{96,64},{128,0},{160,128},{192,224},{224,... | collective-permute-start | bytes 1572872 | tf_op jit(solution)/shard_map/ppermute | solution.py:187
  75.9 2.1 %collective-permute-start.1 = (bf16[2,16,8192]{2,1,0:T(8,128)(2,1)S(1)}, bf16[2,16,8192]{2,1,0:T(8,128)(2,1)S(1)}, u32[]{:S(2)}, u32[]{:S(2)}) collective-permute-start(bf16[2,16,8192]{2,1,0:T(8,128)(2,1)S(1)} %convert_element_type.150), channel_id=1, source_target_pairs={{0,64},{32,288},{64,320},{96,32},{128,384},{160,224},{192,128},{22... | collective-permute-start | bytes 1572872 | tf_op jit(solution)/shard_map/ppermute | solution.py:187
  78.0 0.1 convert_element_type.151
  78.0 8.9 %collective-permute-done = bf16[2,16,8192]{2,1,0:T(8,128)(2,1)S(1)} collective-permute-done((bf16[2,16,8192]{2,1,0:T(8,128)(2,1)S(1)}, bf16[2,16,8192]{2,1,0:T(8,128)(2,1)S(1)}, u32[]{:S(2)}, u32[]{:S(2)}) %collective-permute-start) | collective-permute-done | bytes 524320 | tf_op jit(solution)/shard_map/ppermute | solution.py:187
  86.9 0.1 convert_element_type.152
  87.0 0.6 collective-permute-done.1
  87.6 0.1 convert_element_type.153
  87.6 0.2 add_bitcast_fusion.1
  87.9 0.1 copy.58
  88.0 0.1 copy.59
  88.1 0.1 copy.60
  88.2 0.1 copy.61
  88.3 0.2 maximum_reduce_fusion
  88.5 0.7 convolution_multiply_fusion
  89.2 0.1 copy.39
  89.4 0.2 slice.151
  89.5 7.2 %collective-permute-start.2 = (f32[2,4,512]{2,1,0:T(4,128)S(1)}, f32[2,4,512]{2,1,0:T(4,128)S(1)}, u32[]{:S(2)}, u32[]{:S(2)}) collective-permute-start(f32[2,4,512]{2,1,0:T(4,128)S(1)} %slice.151), channel_id=1, source_target_pairs={{64,0},{288,32},{320,64},{32,96},{384,128},{224,160},{128,192},{48... | collective-permute-start | bytes 49160 | tf_op jit(solution)/shard_map/ppermute | solution.py:190
  96.8 0.1 copy.40
  96.9 0.2 slice.155
  97.1 1.9 %collective-permute-start.3 = (f32[2,4,512]{2,1,0:T(4,128)S(1)}, f32[2,4,512]{2,1,0:T(4,128)S(1)}, u32[]{:S(2)}, u32[]{:S(2)}) collective-permute-start(f32[2,4,512]{2,1,0:T(4,128)S(1)} %slice.155), channel_id=1, source_target_pairs={{32,0},{160,32},{192,64},{64,96},{0,128},{128,160},{224,192},{96,2... | collective-permute-start | bytes 49160 | tf_op jit(solution)/shard_map/ppermute | solution.py:190
  99.0 0.0 collective-permute-done.2
  99.0 5.2 %collective-permute-done.3 = f32[2,4,512]{2,1,0:T(4,128)S(1)} collective-permute-done((f32[2,4,512]{2,1,0:T(4,128)S(1)}, f32[2,4,512]{2,1,0:T(4,128)S(1)}, u32[]{:S(2)}, u32[]{:S(2)}) %collective-permute-start.3) | collective-permute-done | bytes 16416 | tf_op jit(solution)/shard_map/ppermute | solution.py:190
  104.2 0.6 maximum_bitcast_fusion.7
  104.8 0.6 maximum_bitcast_fusion.6
  (30 shorter events, 0.3 us)
Async XLA Ops:
  0.6 8.0 %copy-start = (bf16[1,2,256,1535]{2,1,3,0:T(2,128)(2,1)S(1)}, bf16[1,2,256,1535]{2,1,3,0:T(2,128)(2,1)}, u32[]{:S(2)}) copy-start(bf16[1,2,256,1535]{2,1,3,0:T(2,128)(2,1)} %param.5) | copy-start | bytes 4715524
  13.2 19.4 %copy-start.1 = (s32[1,2]{1,0:T(1,128)S(1)}, s32[1,2]{1,0:T(1,128)}, u32[]{:S(2)}) copy-start(s32[1,2]{1,0:T(1,128)} %param.9) | copy-start | bytes 28
  13.2 25.1 %copy-start.2 = (f32[16]{0:T(128)S(1)}, f32[16]{0:T(128)}, u32[]{:S(2)}) copy-start(f32[16]{0:T(128)} %param.8) | copy-start | bytes 196
  14.6 51.7 %all-to-all-start = ((bf16[2,512,256]{2,0,1:T(2,128)(2,1)}), bf16[2,512,256]{2,0,1:T(2,128)(2,1)S(1)}, u32[]{:S(2)}, u32[]{:S(2)}) async-start(bf16[2,512,256]{2,0,1:T(2,128)(2,1)} %copy.29), calls=%async_computation | async-start | bytes 1048576 | tf_op jit(solution)/shard_map/all_to_all | solution.py:184
  73.4 13.4 %collective-permute-start = (bf16[2,16,8192]{2,1,0:T(8,128)(2,1)S(1)}, bf16[2,16,8192]{2,1,0:T(8,128)(2,1)S(1)}, u32[]{:S(2)}, u32[]{:S(2)}) collective-permute-start(bf16[2,16,8192]{2,1,0:T(8,128)(2,1)S(1)} %convert_element_type.150), channel_id=1, source_target_pairs={{0,32},{32,160},{64,192},{96,64},{128,0},{160,128},{192,224},{224,... | collective-permute-start | bytes 1572872 | tf_op jit(solution)/shard_map/ppermute | solution.py:187
  75.9 11.7 %collective-permute-start.1 = (bf16[2,16,8192]{2,1,0:T(8,128)(2,1)S(1)}, bf16[2,16,8192]{2,1,0:T(8,128)(2,1)S(1)}, u32[]{:S(2)}, u32[]{:S(2)}) collective-permute-start(bf16[2,16,8192]{2,1,0:T(8,128)(2,1)S(1)} %convert_element_type.150), channel_id=1, source_target_pairs={{0,64},{32,288},{64,320},{96,32},{128,384},{160,224},{192,128},{22... | collective-permute-start | bytes 1572872 | tf_op jit(solution)/shard_map/ppermute | solution.py:187
  89.5 9.4 %collective-permute-start.2 = (f32[2,4,512]{2,1,0:T(4,128)S(1)}, f32[2,4,512]{2,1,0:T(4,128)S(1)}, u32[]{:S(2)}, u32[]{:S(2)}) collective-permute-start(f32[2,4,512]{2,1,0:T(4,128)S(1)} %slice.151), channel_id=1, source_target_pairs={{64,0},{288,32},{320,64},{32,96},{384,128},{224,160},{128,192},{48... | collective-permute-start | bytes 49160 | tf_op jit(solution)/shard_map/ppermute | solution.py:190
  97.1 7.1 %collective-permute-start.3 = (f32[2,4,512]{2,1,0:T(4,128)S(1)}, f32[2,4,512]{2,1,0:T(4,128)S(1)}, u32[]{:S(2)}, u32[]{:S(2)}) collective-permute-start(f32[2,4,512]{2,1,0:T(4,128)S(1)} %slice.155), channel_id=1, source_target_pairs={{32,0},{160,32},{192,64},{64,96},{0,128},{128,160},{224,192},{96,2... | collective-permute-start | bytes 49160 | tf_op jit(solution)/shard_map/ppermute | solution.py:190

commit v9 on v8

--- a/solution.py
+++ b/solution.py
@@ -11,6 +11,7 @@
 TAPS = 1024
 LOOK_RNG = 4
 LOOK_AZ = 16
+BAND_ROWS = 128
 
 
 def part_tables(length, inverse):
@@ -28,37 +29,36 @@
 
 
 def band_kernel(re_ref, im_ref, band_ref):
-    block = band_ref.shape[2]
+    rows = BAND_ROWS
+    strip = re_ref.shape[1]
     width = band_ref.shape[3]
-    span = re_ref.shape[1]
-    re_band = pltpu.roll(jnp.broadcast_to(re_ref[0:1, :], (block, span)), 0, 1, stride=1, stride_axis=0)
-    im_band = pltpu.roll(jnp.broadcast_to(im_ref[0:1, :], (block, span)), 0, 1, stride=1, stride_axis=0)
-    band_ref[0, 0] = re_band[:, :width].astype(band_ref.dtype)
-    band_ref[0, 1] = (-im_band)[:, :width].astype(band_ref.dtype)
-    band_ref[1, 0] = im_band[:, :width].astype(band_ref.dtype)
-    band_ref[1, 1] = re_band[:, :width].astype(band_ref.dtype)
+    dtype = band_ref.dtype
+    re_strip = pltpu.roll(jnp.broadcast_to(re_ref[...], (rows, strip)), 0, 1, stride=1, stride_axis=0)
+    im_strip = pltpu.roll(jnp.broadcast_to(im_ref[...], (rows, strip)), 0, 1, stride=1, stride_axis=0)
+    pieces = (
+        (0, 0, re_strip.astype(dtype)),
+        (0, 1, (-im_strip).astype(dtype)),
+        (1, 0, im_strip.astype(dtype)),
+        (1, 1, re_strip.astype(dtype)),
+    )
+    for start in range(0, band_ref.shape[2], rows):
+        stop = min(start + strip, width)
+        for part, half, values in pieces:
+            band_ref[part, half, start : start + rows, start:stop] = values[:, : stop - start]
+            if start > 0:
+                band_ref[part, half, start : start + rows, :start] = jnp.zeros((rows, start), dtype)
+            if stop < width:
+                band_ref[part, half, start : start + rows, stop:] = jnp.zeros((rows, width - stop), dtype)
 
 
 def band_tables(table_re, table_im, width):
-    span = -(-(width + 1) // 128) * 128
-    block = 128
-    steps = RNG // block
-    pad = jnp.zeros((span - table_re.shape[0],), jnp.float32)
-    rows = []
-    for table in (table_re, table_im):
-        row = jnp.concatenate([table.astype(jnp.float32), pad])
-        shifted = jnp.stack([jnp.roll(row, block * step) for step in range(steps)])
-        rows.append(jnp.repeat(shifted, 8, axis=0))
-    row_spec = pl.BlockSpec((8, span), lambda i: (i, 0))
-    out_spec = pl.BlockSpec((2, 2, block, width), lambda i: (0, 0, i, 0))
+    rows = BAND_ROWS
+    strip = -(-(TAPS + rows - 1) // 128) * 128
+    pad = jnp.zeros((strip - table_re.shape[0],), jnp.float32)
+    re_row = jnp.concatenate([table_re.astype(jnp.float32), pad])[None]
+    im_row = jnp.concatenate([table_im.astype(jnp.float32), pad])[None]
     shape = jax.ShapeDtypeStruct((2, 2, RNG, width), jnp.bfloat16)
-    band = pl.pallas_call(
-        band_kernel,
-        grid=(steps,),
-        in_specs=[row_spec, row_spec],
-        out_specs=out_spec,
-        out_shape=shape,
-    )(*rows)
+    band = pl.pallas_call(band_kernel, out_shape=shape)(re_row, im_row)
     return band.reshape(2, 2 * RNG, width)
 
 

time: 106 us -> 105 us (level)
    reshape x2 -> x0, local copies, waits for them, and re-layouts: 1.42 us -> none  [band_tables(): rows.append(jnp.repeat(shifted, 8, axis=0))]
    broadcast_in_dim x0 -> x2, local copies, waits for them, and re-layouts: none -> 1.19 us  [the longest x1 0.6 us: band_tables(): re_row = jnp.concatenate([table_re.astype(jnp.float32), pad])[None]]
where the time goes in v9:
time: 105 us; the launch traced here: 104 us
  waiting for transfers between devices  42.6 us (41%)
  starting transfers between devices  31.6 us (30%)
  matrix products  9.01 us (9%)
  other arithmetic  6.38 us (6%)
  between operations  5.56 us (5%)
  local copies, waits for them, and re-layouts  5.03 us (5%)
  Pallas kernels  3.94 us (4%)
    all_to_all x1, waiting for transfers between devices, per_device(): lax.all_to_all(compressed, 'pulse', split_axis=1, concat_axis=2, tiled=True)  28 us
    all_to_all x1, starting transfers between devices, per_device(): lax.all_to_all(compressed, 'pulse', split_axis=1, concat_axis=2, tiled=True)  18 us
    ppermute x2, waiting for transfers between devices, per_device(): arrived = [lax.ppermute(focused, 'acq', pairs) for pairs in edge_pairs]  9.47 us
    ppermute x2, starting transfers between devices, per_device(): lax.ppermute(looked[slot], 'acq', [(dst, src) for src, dst in edge_pairs[...  9.1 us
    ppermute x2, waiting for transfers between devices, per_device(): lax.ppermute(looked[slot], 'acq', [(dst, src) for src, dst in edge_pairs[...  5.19 us
    dot_general x1, matrix products, compress(): lax.dot_general(band, echoes, dims, preferred_element_type=jnp.float32)  4.57 us
    ppermute x2, starting transfers between devices, per_device(): arrived = [lax.ppermute(focused, 'acq', pairs) for pairs in edge_pairs]  4.49 us
    pallas_call x1, Pallas kernels, band_tables(): band = pl.pallas_call(band_kernel, out_shape=shape)(re_row, im_row)  3.94 us
  transfers between devices with their start and end apart: 5, of which 4 were waited for; matrix products, arithmetic and copies ran while one was open for 2% of the time, Pallas kernels for 0%

profile of v9, /device:TPU:36, one launch (start us, length us, event | category | flops | bytes accessed | tf_op | source)
XLA Modules:
  0.0 104.1 jit_solution(6909144308509043585)
XLA Ops:
  0.6 0.0 copy-start
  0.6 0.8 multiply_convert_fusion
  1.5 0.6 reshape.338.re_ref
  2.1 0.6 reshape.339.im_ref
  3.4 3.9 %shard_map.68 = bf16[2,2,512,1535]{3,2,1,0:T(8,128)(2,1)} custom-call(f32[1,1152]{1,0:T(1,128)} %reshape.338.re_ref, f32[1,1152]{1,0:T(1,128)} %reshape.339.im_ref), custom_call_target="tpu_custom_call" | custom-call | tf_op jit(solution)/shard_map/pallas_call | solution.py:61
  7.3 0.0 copy-done
  7.3 4.6 %fusion.14 = bf16[2,512,256]{2,1,0:T(8,128)(2,1)S(1)} fusion(bf16[2,256,1535,1]{1,0,2,3:T(2,128)(2,1)S(1)} %bitcast.154, bf16[2,2,512,1535]{3,2,1,0:T(8,128)(2,1)} %shard_map.68, f32[256]{0:T(256)S(1)} %compare_convert_fusion), kind=kOutput, calls=%fused_computation.11 | convolution fusion | flops 1610088448 | bytes 8384512 | tf_op jit(solution)/shard_map/dot_general | solution.py:68
  11.9 0.0 copy-start.1
  11.9 0.0 copy-start.2
  11.9 1.3 %copy.29 = bf16[2,512,256]{2,0,1:T(2,128)(2,1)} copy(bf16[2,512,256]{2,1,0:T(8,128)(2,1)S(1)} %fusion.14) | data formatting | bytes 1048576 | tf_op jit(solution)/shard_map/convert_element_type | solution.py:72
  13.2 18.0 %all-to-all-start = ((bf16[2,512,256]{2,0,1:T(2,128)(2,1)}), bf16[2,512,256]{2,0,1:T(2,128)(2,1)S(1)}, u32[]{:S(2)}, u32[]{:S(2)}) async-start(bf16[2,512,256]{2,0,1:T(2,128)(2,1)} %copy.29), calls=%async_computation | async-start | bytes 1048576 | tf_op jit(solution)/shard_map/all_to_all | solution.py:184
  31.3 0.0 copy-done.1
  31.3 0.6 fusion.90
  35.8 0.1 fusion.78
  35.9 0.1 fusion.74
  36.0 0.1 fusion.76
  36.2 0.1 fusion.75
  36.3 0.3 fusion.73
  36.6 0.3 fusion.67
  37.0 0.0 copy-done.2
  37.0 28.0 %all-to-all-done = bf16[2,512,256]{2,0,1:T(2,128)(2,1)S(1)} async-done(((bf16[2,512,256]{2,0,1:T(2,128)(2,1)}), bf16[2,512,256]{2,0,1:T(2,128)(2,1)S(1)}, u32[]{:S(2)}, u32[]{:S(2)}) %all-to-all-start) | async-done | bytes 524320 | tf_op jit(solution)/shard_map/all_to_all | solution.py:184
  65.0 0.3 copy.91
  65.3 0.2 all_to_all.16
  65.5 0.1 copy.57
  65.7 0.6 convolution_bitcast_fusion.3
  66.3 0.2 multiply_subtract_fusion.1
  66.5 1.0 convolution_bitcast_fusion.2
  67.5 2.1 %fusion.29 = (f32[1,16,64,128]{3,2,1,0:T(8,128)S(1)}, f32[1,16,64,128]{3,2,1,0:T(8,128)S(1)}) fusion(f32[2,16,64,128]{3,2,1,0:T(8,128)S(1)} %convolution_bitcast_fusion.2, f32[64,128]{1,0:T(8,128)S(1)} %fusion.64, f32[16]{0:T(128)S(1)} %broadcast_multiply_fusion), kind=kLoop, calls=%fused_computation.28 | loop fusion | flops 1048576 | bytes 2129984 | tf_op jit(solution)/shard_map/sub | solution.py:28
  69.6 1.0 convolution_bitcast_fusion.1
  70.6 0.2 multiply_subtract_fusion
  70.8 1.1 %fusion.20 = bf16[2,16,64,128]{3,2,1,0:T(8,128)(2,1)S(1)} fusion(f32[1,16,64,128]{3,2,1,0:T(8,128)S(1)} %get-tuple-element.21, f32[1,16,64,128]{3,2,1,0:T(8,128)S(1)} %get-tuple-element.20, f32[1,2,64,64]{2,3,1,0:T(8,128)S(1)} %get-tuple-element.43, f32[1,2,64,64]{2,3,1,0:T(8,128)S(1)} %get-tuple-element.36), kind=kOutput, calls=%fused_computation.13 | convolution fusion | flops 403456000 | bytes 1638400 | tf_op jit(solution)/shard_map/pckb,pqka->qcab/dot_general | solution.py:116
  71.9 0.2 convert_element_type.150
  72.1 2.4 %collective-permute-start = (bf16[2,16,8192]{2,1,0:T(8,128)(2,1)S(1)}, bf16[2,16,8192]{2,1,0:T(8,128)(2,1)S(1)}, u32[]{:S(2)}, u32[]{:S(2)}) collective-permute-start(bf16[2,16,8192]{2,1,0:T(8,128)(2,1)S(1)} %convert_element_type.150), channel_id=1, source_target_pairs={{0,32},{32,160},{64,192},{96,64},{128,0},{160,128},{192,224},{224,... | collective-permute-start | bytes 1572872 | tf_op jit(solution)/shard_map/ppermute | solution.py:187
  74.5 2.1 %collective-permute-start.1 = (bf16[2,16,8192]{2,1,0:T(8,128)(2,1)S(1)}, bf16[2,16,8192]{2,1,0:T(8,128)(2,1)S(1)}, u32[]{:S(2)}, u32[]{:S(2)}) collective-permute-start(bf16[2,16,8192]{2,1,0:T(8,128)(2,1)S(1)} %convert_element_type.150), channel_id=1, source_target_pairs={{0,64},{32,288},{64,320},{96,32},{128,384},{160,224},{192,128},{22... | collective-permute-start | bytes 1572872 | tf_op jit(solution)/shard_map/ppermute | solution.py:187
  76.7 0.1 convert_element_type.151
  76.7 8.8 %collective-permute-done = bf16[2,16,8192]{2,1,0:T(8,128)(2,1)S(1)} collective-permute-done((bf16[2,16,8192]{2,1,0:T(8,128)(2,1)S(1)}, bf16[2,16,8192]{2,1,0:T(8,128)(2,1)S(1)}, u32[]{:S(2)}, u32[]{:S(2)}) %collective-permute-start) | collective-permute-done | bytes 524320 | tf_op jit(solution)/shard_map/ppermute | solution.py:187
  85.5 0.1 convert_element_type.152
  85.6 0.7 collective-permute-done.1
  86.3 0.1 convert_element_type.153
  86.3 0.2 add_bitcast_fusion.1
  86.6 0.1 copy.58
  86.7 0.1 copy.59
  86.8 0.1 copy.60
  86.9 0.1 copy.61
  87.0 0.2 maximum_reduce_fusion
  87.2 0.7 convolution_multiply_fusion
  88.0 0.1 copy.39
  88.1 0.2 slice.115
  88.2 7.2 %collective-permute-start.2 = (f32[2,4,512]{2,1,0:T(4,128)S(1)}, f32[2,4,512]{2,1,0:T(4,128)S(1)}, u32[]{:S(2)}, u32[]{:S(2)}) collective-permute-start(f32[2,4,512]{2,1,0:T(4,128)S(1)} %slice.115), channel_id=1, source_target_pairs={{64,0},{288,32},{320,64},{32,96},{384,128},{224,160},{128,192},{48... | collective-permute-start | bytes 49160 | tf_op jit(solution)/shard_map/ppermute | solution.py:190
  95.4 0.1 copy.40
  95.6 0.2 slice.119
  95.7 1.9 %collective-permute-start.3 = (f32[2,4,512]{2,1,0:T(4,128)S(1)}, f32[2,4,512]{2,1,0:T(4,128)S(1)}, u32[]{:S(2)}, u32[]{:S(2)}) collective-permute-start(f32[2,4,512]{2,1,0:T(4,128)S(1)} %slice.119), channel_id=1, source_target_pairs={{32,0},{160,32},{192,64},{64,96},{0,128},{128,160},{224,192},{96,2... | collective-permute-start | bytes 49160 | tf_op jit(solution)/shard_map/ppermute | solution.py:190
  97.7 0.0 collective-permute-done.2
  97.7 5.2 %collective-permute-done.3 = f32[2,4,512]{2,1,0:T(4,128)S(1)} collective-permute-done((f32[2,4,512]{2,1,0:T(4,128)S(1)}, f32[2,4,512]{2,1,0:T(4,128)S(1)}, u32[]{:S(2)}, u32[]{:S(2)}) %collective-permute-start.3) | collective-permute-done | bytes 16416 | tf_op jit(solution)/shard_map/ppermute | solution.py:190
  102.9 0.6 maximum_bitcast_fusion.7
  103.5 0.6 maximum_bitcast_fusion.6
  (14 shorter events, 0.1 us)
Async XLA Ops:
  0.6 6.7 %copy-start = (bf16[1,2,256,1535]{2,1,3,0:T(2,128)(2,1)S(1)}, bf16[1,2,256,1535]{2,1,3,0:T(2,128)(2,1)}, u32[]{:S(2)}) copy-start(bf16[1,2,256,1535]{2,1,3,0:T(2,128)(2,1)} %param.5) | copy-start | bytes 4715524
  11.9 19.4 %copy-start.1 = (s32[1,2]{1,0:T(1,128)S(1)}, s32[1,2]{1,0:T(1,128)}, u32[]{:S(2)}) copy-start(s32[1,2]{1,0:T(1,128)} %param.9) | copy-start | bytes 28
  11.9 25.1 %copy-start.2 = (f32[16]{0:T(128)S(1)}, f32[16]{0:T(128)}, u32[]{:S(2)}) copy-start(f32[16]{0:T(128)} %param.8) | copy-start | bytes 196
  13.2 51.7 %all-to-all-start = ((bf16[2,512,256]{2,0,1:T(2,128)(2,1)}), bf16[2,512,256]{2,0,1:T(2,128)(2,1)S(1)}, u32[]{:S(2)}, u32[]{:S(2)}) async-start(bf16[2,512,256]{2,0,1:T(2,128)(2,1)} %copy.29), calls=%async_computation | async-start | bytes 1048576 | tf_op jit(solution)/shard_map/all_to_all | solution.py:184
  72.1 13.4 %collective-permute-start = (bf16[2,16,8192]{2,1,0:T(8,128)(2,1)S(1)}, bf16[2,16,8192]{2,1,0:T(8,128)(2,1)S(1)}, u32[]{:S(2)}, u32[]{:S(2)}) collective-permute-start(bf16[2,16,8192]{2,1,0:T(8,128)(2,1)S(1)} %convert_element_type.150), channel_id=1, source_target_pairs={{0,32},{32,160},{64,192},{96,64},{128,0},{160,128},{192,224},{224,... | collective-permute-start | bytes 1572872 | tf_op jit(solution)/shard_map/ppermute | solution.py:187
  74.5 11.7 %collective-permute-start.1 = (bf16[2,16,8192]{2,1,0:T(8,128)(2,1)S(1)}, bf16[2,16,8192]{2,1,0:T(8,128)(2,1)S(1)}, u32[]{:S(2)}, u32[]{:S(2)}) collective-permute-start(bf16[2,16,8192]{2,1,0:T(8,128)(2,1)S(1)} %convert_element_type.150), channel_id=1, source_target_pairs={{0,64},{32,288},{64,320},{96,32},{128,384},{160,224},{192,128},{22... | collective-permute-start | bytes 1572872 | tf_op jit(solution)/shard_map/ppermute | solution.py:187
  88.2 9.4 %collective-permute-start.2 = (f32[2,4,512]{2,1,0:T(4,128)S(1)}, f32[2,4,512]{2,1,0:T(4,128)S(1)}, u32[]{:S(2)}, u32[]{:S(2)}) collective-permute-start(f32[2,4,512]{2,1,0:T(4,128)S(1)} %slice.115), channel_id=1, source_target_pairs={{64,0},{288,32},{320,64},{32,96},{384,128},{224,160},{128,192},{48... | collective-permute-start | bytes 49160 | tf_op jit(solution)/shard_map/ppermute | solution.py:190
  95.7 7.1 %collective-permute-start.3 = (f32[2,4,512]{2,1,0:T(4,128)S(1)}, f32[2,4,512]{2,1,0:T(4,128)S(1)}, u32[]{:S(2)}, u32[]{:S(2)}) collective-permute-start(f32[2,4,512]{2,1,0:T(4,128)S(1)} %slice.119), channel_id=1, source_target_pairs={{32,0},{160,32},{192,64},{64,96},{0,128},{128,160},{224,192},{96,2... | collective-permute-start | bytes 49160 | tf_op jit(solution)/shard_map/ppermute | solution.py:190

commit v10 on v9

--- a/solution.py
+++ b/solution.py
@@ -77,7 +77,7 @@
     length = turned.shape[2]
     outer_len = 64
     inner_len = length // outer_len
-    highest = lax.Precision.HIGHEST
+    highest = lax.Precision.HIGH
     signal = turned.astype(jnp.float32).reshape(2, columns, outer_len, inner_len)
     section_one = jnp.einsum(
         "pcab,pqak->qckb", signal, part_tables(outer_len, False), precision=highest

time: 105 us -> 103 us (0.981)
  matrix products: 9.01 us -> 7.59 us
where the time goes in v10:
time: 103 us
  waiting for transfers between devices  42.6 us (41%)
  starting transfers between devices  31.6 us (31%)
  matrix products  7.59 us (7%)
  other arithmetic  6.38 us (6%)
  between operations  5.56 us (5%)
  local copies, waits for them, and re-layouts  5.03 us (5%)
  Pallas kernels  3.94 us (4%)
    all_to_all x1, waiting for transfers between devices, per_device(): lax.all_to_all(compressed, 'pulse', split_axis=1, concat_axis=2, tiled=True)  28 us
    all_to_all x1, starting transfers between devices, per_device(): lax.all_to_all(compressed, 'pulse', split_axis=1, concat_axis=2, tiled=True)  18 us
    ppermute x2, waiting for transfers between devices, per_device(): arrived = [lax.ppermute(focused, 'acq', pairs) for pairs in edge_pairs]  9.46 us
    ppermute x2, starting transfers between devices, per_device(): lax.ppermute(looked[slot], 'acq', [(dst, src) for src, dst in edge_pairs[...  9.12 us
    ppermute x2, waiting for transfers between devices, per_device(): lax.ppermute(looked[slot], 'acq', [(dst, src) for src, dst in edge_pairs[...  5.19 us
    dot_general x1, matrix products, compress(): lax.dot_general(band, echoes, dims, preferred_element_type=jnp.float32)  4.57 us
    ppermute x2, starting transfers between devices, per_device(): arrived = [lax.ppermute(focused, 'acq', pairs) for pairs in edge_pairs]  4.51 us
    pallas_call x1, Pallas kernels, band_tables(): band = pl.pallas_call(band_kernel, out_shape=shape)(re_row, im_row)  3.94 us
  transfers between devices with their start and end apart: 5, of which 4 were waited for; matrix products, arithmetic and copies ran while one was open for 2% of the time, Pallas kernels for 0%

profile of v10, /device:TPU:36, one launch (start us, length us, event | category | flops | bytes accessed | tf_op | source)
XLA Modules:
  0.0 102.7 jit_solution(1190257590411659197)
XLA Ops:
  0.6 0.0 copy-start
  0.6 0.8 multiply_convert_fusion
  1.5 0.6 reshape.338.re_ref
  2.1 0.6 reshape.339.im_ref
  3.4 3.9 %shard_map.68 = bf16[2,2,512,1535]{3,2,1,0:T(8,128)(2,1)} custom-call(f32[1,1152]{1,0:T(1,128)} %reshape.338.re_ref, f32[1,1152]{1,0:T(1,128)} %reshape.339.im_ref), custom_call_target="tpu_custom_call" | custom-call | tf_op jit(solution)/shard_map/pallas_call | solution.py:61
  7.3 0.0 copy-done
  7.3 4.6 %fusion.14 = bf16[2,512,256]{2,1,0:T(8,128)(2,1)S(1)} fusion(bf16[2,256,1535,1]{1,0,2,3:T(2,128)(2,1)S(1)} %bitcast.154, bf16[2,2,512,1535]{3,2,1,0:T(8,128)(2,1)} %shard_map.68, f32[256]{0:T(256)S(1)} %compare_convert_fusion), kind=kOutput, calls=%fused_computation.11 | convolution fusion | flops 1610088448 | bytes 8384512 | tf_op jit(solution)/shard_map/dot_general | solution.py:68
  11.9 0.0 copy-start.1
  11.9 0.0 copy-start.2
  11.9 1.3 %copy.29 = bf16[2,512,256]{2,0,1:T(2,128)(2,1)} copy(bf16[2,512,256]{2,1,0:T(8,128)(2,1)S(1)} %fusion.14) | data formatting | bytes 1048576 | tf_op jit(solution)/shard_map/convert_element_type | solution.py:72
  13.2 18.0 %all-to-all-start = ((bf16[2,512,256]{2,0,1:T(2,128)(2,1)}), bf16[2,512,256]{2,0,1:T(2,128)(2,1)S(1)}, u32[]{:S(2)}, u32[]{:S(2)}) async-start(bf16[2,512,256]{2,0,1:T(2,128)(2,1)} %copy.29), calls=%async_computation | async-start | bytes 1048576 | tf_op jit(solution)/shard_map/all_to_all | solution.py:184
  31.3 0.0 copy-done.1
  31.3 0.6 fusion.90
  35.8 0.1 fusion.78
  35.9 0.1 fusion.74
  36.0 0.1 fusion.76
  36.2 0.1 fusion.75
  36.3 0.3 fusion.73
  36.6 0.3 fusion.67
  37.0 0.0 copy-done.2
  37.0 28.0 %all-to-all-done = bf16[2,512,256]{2,0,1:T(2,128)(2,1)S(1)} async-done(((bf16[2,512,256]{2,0,1:T(2,128)(2,1)}), bf16[2,512,256]{2,0,1:T(2,128)(2,1)S(1)}, u32[]{:S(2)}, u32[]{:S(2)}) %all-to-all-start) | async-done | bytes 524320 | tf_op jit(solution)/shard_map/all_to_all | solution.py:184
  65.0 0.3 copy.91
  65.3 0.2 all_to_all.16
  65.5 0.1 copy.57
  65.7 0.5 convolution_bitcast_fusion.3
  66.1 0.2 multiply_subtract_fusion.1
  66.3 0.6 convolution_bitcast_fusion.2
  66.9 2.1 %fusion.29 = (f32[1,16,64,128]{3,2,1,0:T(8,128)S(1)}, f32[1,16,64,128]{3,2,1,0:T(8,128)S(1)}) fusion(f32[2,16,64,128]{3,2,1,0:T(8,128)S(1)} %convolution_bitcast_fusion.2, f32[64,128]{1,0:T(8,128)S(1)} %fusion.64, f32[16]{0:T(128)S(1)} %broadcast_multiply_fusion), kind=kLoop, calls=%fused_computation.28 | loop fusion | flops 1048576 | bytes 2129984 | tf_op jit(solution)/shard_map/sub | solution.py:28
  69.1 0.6 convolution_bitcast_fusion.1
  69.7 0.2 multiply_subtract_fusion
  69.8 0.6 fusion.20
  70.5 0.2 convert_element_type.150
  70.7 2.4 %collective-permute-start = (bf16[2,16,8192]{2,1,0:T(8,128)(2,1)S(1)}, bf16[2,16,8192]{2,1,0:T(8,128)(2,1)S(1)}, u32[]{:S(2)}, u32[]{:S(2)}) collective-permute-start(bf16[2,16,8192]{2,1,0:T(8,128)(2,1)S(1)} %convert_element_type.150), channel_id=1, source_target_pairs={{0,32},{32,160},{64,192},{96,64},{128,0},{160,128},{192,224},{224,... | collective-permute-start | bytes 1572872 | tf_op jit(solution)/shard_map/ppermute | solution.py:187
  73.1 2.1 %collective-permute-start.1 = (bf16[2,16,8192]{2,1,0:T(8,128)(2,1)S(1)}, bf16[2,16,8192]{2,1,0:T(8,128)(2,1)S(1)}, u32[]{:S(2)}, u32[]{:S(2)}) collective-permute-start(bf16[2,16,8192]{2,1,0:T(8,128)(2,1)S(1)} %convert_element_type.150), channel_id=1, source_target_pairs={{0,64},{32,288},{64,320},{96,32},{128,384},{160,224},{192,128},{22... | collective-permute-start | bytes 1572872 | tf_op jit(solution)/shard_map/ppermute | solution.py:187
  75.2 0.1 convert_element_type.151
  75.3 8.8 %collective-permute-done = bf16[2,16,8192]{2,1,0:T(8,128)(2,1)S(1)} collective-permute-done((bf16[2,16,8192]{2,1,0:T(8,128)(2,1)S(1)}, bf16[2,16,8192]{2,1,0:T(8,128)(2,1)S(1)}, u32[]{:S(2)}, u32[]{:S(2)}) %collective-permute-start) | collective-permute-done | bytes 524320 | tf_op jit(solution)/shard_map/ppermute | solution.py:187
  84.1 0.1 convert_element_type.152
  84.2 0.6 collective-permute-done.1
  84.9 0.1 convert_element_type.153
  84.9 0.2 add_bitcast_fusion.1
  85.2 0.1 copy.58
  85.3 0.1 copy.59
  85.4 0.1 copy.60
  85.5 0.1 copy.61
  85.6 0.2 maximum_reduce_fusion
  85.8 0.7 convolution_multiply_fusion
  86.5 0.1 copy.39
  86.7 0.2 slice.115
  86.8 7.2 %collective-permute-start.2 = (f32[2,4,512]{2,1,0:T(4,128)S(1)}, f32[2,4,512]{2,1,0:T(4,128)S(1)}, u32[]{:S(2)}, u32[]{:S(2)}) collective-permute-start(f32[2,4,512]{2,1,0:T(4,128)S(1)} %slice.115), channel_id=1, source_target_pairs={{64,0},{288,32},{320,64},{32,96},{384,128},{224,160},{128,192},{48... | collective-permute-start | bytes 49160 | tf_op jit(solution)/shard_map/ppermute | solution.py:190
  94.0 0.1 copy.40
  94.2 0.2 slice.119
  94.3 1.9 %collective-permute-start.3 = (f32[2,4,512]{2,1,0:T(4,128)S(1)}, f32[2,4,512]{2,1,0:T(4,128)S(1)}, u32[]{:S(2)}, u32[]{:S(2)}) collective-permute-start(f32[2,4,512]{2,1,0:T(4,128)S(1)} %slice.119), channel_id=1, source_target_pairs={{32,0},{160,32},{192,64},{64,96},{0,128},{128,160},{224,192},{96,2... | collective-permute-start | bytes 49160 | tf_op jit(solution)/shard_map/ppermute | solution.py:190
  96.3 0.0 collective-permute-done.2
  96.3 5.2 %collective-permute-done.3 = f32[2,4,512]{2,1,0:T(4,128)S(1)} collective-permute-done((f32[2,4,512]{2,1,0:T(4,128)S(1)}, f32[2,4,512]{2,1,0:T(4,128)S(1)}, u32[]{:S(2)}, u32[]{:S(2)}) %collective-permute-start.3) | collective-permute-done | bytes 16416 | tf_op jit(solution)/shard_map/ppermute | solution.py:190
  101.5 0.6 maximum_bitcast_fusion.7
  102.1 0.6 maximum_bitcast_fusion.6
  (14 shorter events, 0.1 us)
Async XLA Ops:
  0.6 6.7 %copy-start = (bf16[1,2,256,1535]{2,1,3,0:T(2,128)(2,1)S(1)}, bf16[1,2,256,1535]{2,1,3,0:T(2,128)(2,1)}, u32[]{:S(2)}) copy-start(bf16[1,2,256,1535]{2,1,3,0:T(2,128)(2,1)} %param.5) | copy-start | bytes 4715524
  11.9 19.4 %copy-start.1 = (s32[1,2]{1,0:T(1,128)S(1)}, s32[1,2]{1,0:T(1,128)}, u32[]{:S(2)}) copy-start(s32[1,2]{1,0:T(1,128)} %param.9) | copy-start | bytes 28
  11.9 25.1 %copy-start.2 = (f32[16]{0:T(128)S(1)}, f32[16]{0:T(128)}, u32[]{:S(2)}) copy-start(f32[16]{0:T(128)} %param.8) | copy-start | bytes 196
  13.2 51.7 %all-to-all-start = ((bf16[2,512,256]{2,0,1:T(2,128)(2,1)}), bf16[2,512,256]{2,0,1:T(2,128)(2,1)S(1)}, u32[]{:S(2)}, u32[]{:S(2)}) async-start(bf16[2,512,256]{2,0,1:T(2,128)(2,1)} %copy.29), calls=%async_computation | async-start | bytes 1048576 | tf_op jit(solution)/shard_map/all_to_all | solution.py:184
  70.7 13.4 %collective-permute-start = (bf16[2,16,8192]{2,1,0:T(8,128)(2,1)S(1)}, bf16[2,16,8192]{2,1,0:T(8,128)(2,1)S(1)}, u32[]{:S(2)}, u32[]{:S(2)}) collective-permute-start(bf16[2,16,8192]{2,1,0:T(8,128)(2,1)S(1)} %convert_element_type.150), channel_id=1, source_target_pairs={{0,32},{32,160},{64,192},{96,64},{128,0},{160,128},{192,224},{224,... | collective-permute-start | bytes 1572872 | tf_op jit(solution)/shard_map/ppermute | solution.py:187
  73.1 11.7 %collective-permute-start.1 = (bf16[2,16,8192]{2,1,0:T(8,128)(2,1)S(1)}, bf16[2,16,8192]{2,1,0:T(8,128)(2,1)S(1)}, u32[]{:S(2)}, u32[]{:S(2)}) collective-permute-start(bf16[2,16,8192]{2,1,0:T(8,128)(2,1)S(1)} %convert_element_type.150), channel_id=1, source_target_pairs={{0,64},{32,288},{64,320},{96,32},{128,384},{160,224},{192,128},{22... | collective-permute-start | bytes 1572872 | tf_op jit(solution)/shard_map/ppermute | solution.py:187
  86.8 9.4 %collective-permute-start.2 = (f32[2,4,512]{2,1,0:T(4,128)S(1)}, f32[2,4,512]{2,1,0:T(4,128)S(1)}, u32[]{:S(2)}, u32[]{:S(2)}) collective-permute-start(f32[2,4,512]{2,1,0:T(4,128)S(1)} %slice.115), channel_id=1, source_target_pairs={{64,0},{288,32},{320,64},{32,96},{384,128},{224,160},{128,192},{48... | collective-permute-start | bytes 49160 | tf_op jit(solution)/shard_map/ppermute | solution.py:190
  94.3 7.1 %collective-permute-start.3 = (f32[2,4,512]{2,1,0:T(4,128)S(1)}, f32[2,4,512]{2,1,0:T(4,128)S(1)}, u32[]{:S(2)}, u32[]{:S(2)}) collective-permute-start(f32[2,4,512]{2,1,0:T(4,128)S(1)} %slice.119), channel_id=1, source_target_pairs={{32,0},{160,32},{192,64},{64,96},{0,128},{128,160},{224,192},{96,2... | collective-permute-start | bytes 49160 | tf_op jit(solution)/shard_map/ppermute | solution.py:190

commit v11 on v10

--- a/solution.py
+++ b/solution.py
@@ -28,37 +28,45 @@
     return (left_re * right_re - left_im * right_im, left_re * right_im + left_im * right_re)
 
 
-def band_kernel(re_ref, im_ref, band_ref):
+def band_kernel(re_ref, im_ref, band_ref, strip_ref):
     rows = BAND_ROWS
-    strip = re_ref.shape[1]
+    span = re_ref.shape[1]
     width = band_ref.shape[3]
     dtype = band_ref.dtype
-    re_strip = pltpu.roll(jnp.broadcast_to(re_ref[...], (rows, strip)), 0, 1, stride=1, stride_axis=0)
-    im_strip = pltpu.roll(jnp.broadcast_to(im_ref[...], (rows, strip)), 0, 1, stride=1, stride_axis=0)
-    pieces = (
-        (0, 0, re_strip.astype(dtype)),
-        (0, 1, (-im_strip).astype(dtype)),
-        (1, 0, im_strip.astype(dtype)),
-        (1, 1, re_strip.astype(dtype)),
-    )
-    for start in range(0, band_ref.shape[2], rows):
-        stop = min(start + strip, width)
-        for part, half, values in pieces:
-            band_ref[part, half, start : start + rows, start:stop] = values[:, : stop - start]
-            if start > 0:
-                band_ref[part, half, start : start + rows, :start] = jnp.zeros((rows, start), dtype)
-            if stop < width:
-                band_ref[part, half, start : start + rows, stop:] = jnp.zeros((rows, width - stop), dtype)
+    step = pl.program_id(0)
+
+    @pl.when(step == 0)
+    def _():
+        strip_ref[0] = pltpu.roll(jnp.broadcast_to(re_ref[...], (rows, span)), 0, 1, stride=1, stride_axis=0)
+        strip_ref[1] = pltpu.roll(jnp.broadcast_to(im_ref[...], (rows, span)), 0, 1, stride=1, stride_axis=0)
+
+    shift = pl.multiple_of(step * rows, rows)
+    re_band = pltpu.roll(strip_ref[0], shift, 1)[:, :width]
+    im_band = pltpu.roll(strip_ref[1], shift, 1)[:, :width]
+    band_ref[0, 0] = re_band.astype(dtype)
+    band_ref[0, 1] = (-im_band).astype(dtype)
+    band_ref[1, 0] = im_band.astype(dtype)
+    band_ref[1, 1] = re_band.astype(dtype)
 
 
 def band_tables(table_re, table_im, width):
     rows = BAND_ROWS
-    strip = -(-(TAPS + rows - 1) // 128) * 128
-    pad = jnp.zeros((strip - table_re.shape[0],), jnp.float32)
+    span = -(-(width + 1) // 128) * 128
+    pad = jnp.zeros((span - table_re.shape[0],), jnp.float32)
     re_row = jnp.concatenate([table_re.astype(jnp.float32), pad])[None]
     im_row = jnp.concatenate([table_im.astype(jnp.float32), pad])[None]
+    row_spec = pl.BlockSpec((1, span), lambda i: (0, 0))
+    out_spec = pl.BlockSpec((2, 2, rows, width), lambda i: (0, 0, i, 0))
     shape = jax.ShapeDtypeStruct((2, 2, RNG, width), jnp.bfloat16)
-    band = pl.pallas_call(band_kernel, out_shape=shape)(re_row, im_row)
+    band = pl.pallas_call(
+        band_kernel,
+        grid=(RNG // rows,),
+        in_specs=[row_spec, row_spec],
+        out_specs=out_spec,
+        out_shape=shape,
+        scratch_shapes=[pltpu.VMEM((2, rows, span), jnp.float32)],
+        compiler_params=pltpu.CompilerParams(dimension_semantics=("arbitrary",)),
+    )(re_row, im_row)
     return band.reshape(2, 2 * RNG, width)
 
 

time: 103 us -> 105 us (1.019)
  Pallas kernels: 3.94 us -> 5.38 us
    pallas_call x1, Pallas kernels: 3.94 us -> 5.38 us  [band_tables(): pl.pallas_call(band_kernel, grid=(RNG // rows,), in_specs=[row_spec, row_...]
where the time goes in v11:
time: 105 us; the launch traced here: 104 us
  waiting for transfers between devices  42.6 us (41%)
  starting transfers between devices  31.6 us (30%)
  matrix products  7.59 us (7%)
  other arithmetic  6.38 us (6%)
  between operations  5.57 us (5%)
  Pallas kernels  5.38 us (5%)
  local copies, waits for them, and re-layouts  5.04 us (5%)
    all_to_all x1, waiting for transfers between devices, per_device(): lax.all_to_all(compressed, 'pulse', split_axis=1, concat_axis=2, tiled=True)  28 us
    all_to_all x1, starting transfers between devices, per_device(): lax.all_to_all(compressed, 'pulse', split_axis=1, concat_axis=2, tiled=True)  18 us
    ppermute x2, waiting for transfers between devices, per_device(): arrived = [lax.ppermute(focused, 'acq', pairs) for pairs in edge_pairs]  9.47 us
    ppermute x2, starting transfers between devices, per_device(): lax.ppermute(looked[slot], 'acq', [(dst, src) for src, dst in edge_pairs[...  9.11 us
    pallas_call x1, Pallas kernels, band_tables(): pl.pallas_call(band_kernel, grid=(RNG // rows,), in_specs=[row_spec, row_...  5.38 us
    ppermute x2, waiting for transfers between devices, per_device(): lax.ppermute(looked[slot], 'acq', [(dst, src) for src, dst in edge_pairs[...  5.19 us
    dot_general x1, matrix products, compress(): lax.dot_general(band, echoes, dims, preferred_element_type=jnp.float32)  4.57 us
    ppermute x2, starting transfers between devices, per_device(): arrived = [lax.ppermute(focused, 'acq', pairs) for pairs in edge_pairs]  4.51 us
  transfers between devices with their start and end apart: 5, of which 4 were waited for; matrix products, arithmetic and copies ran while one was open for 2% of the time, Pallas kernels for 0%

profile of v11, /device:TPU:36, one launch (start us, length us, event | category | flops | bytes accessed | tf_op | source)
XLA Modules:
  0.0 104.2 jit_solution(11514988979267459715)
XLA Ops:
  0.6 0.0 copy-start
  0.6 0.8 multiply_convert_fusion
  1.5 0.6 reshape.338.re_ref
  2.1 0.6 reshape.339.im_ref
  3.4 5.4 %shard_map.68 = bf16[2,2,512,1535]{3,2,1,0:T(8,128)(2,1)} custom-call(f32[1,1536]{1,0:T(1,128)} %reshape.338.re_ref, f32[1,1536]{1,0:T(1,128)} %reshape.339.im_ref), custom_call_target="tpu_custom_call" | custom-call | tf_op jit(solution)/shard_map/pallas_call | solution.py:61
  8.7 0.0 copy-done
  8.7 4.6 %fusion.14 = bf16[2,512,256]{2,1,0:T(8,128)(2,1)S(1)} fusion(bf16[2,256,1535,1]{1,0,2,3:T(2,128)(2,1)S(1)} %bitcast.154, bf16[2,2,512,1535]{3,2,1,0:T(8,128)(2,1)} %shard_map.68, f32[256]{0:T(256)S(1)} %compare_convert_fusion), kind=kOutput, calls=%fused_computation.11 | convolution fusion | flops 1610088448 | bytes 8384512 | tf_op jit(solution)/shard_map/dot_general | solution.py:76
  13.3 0.0 copy-start.1
  13.3 0.0 copy-start.2
  13.3 1.3 %copy.29 = bf16[2,512,256]{2,0,1:T(2,128)(2,1)} copy(bf16[2,512,256]{2,1,0:T(8,128)(2,1)S(1)} %fusion.14) | data formatting | bytes 1048576 | tf_op jit(solution)/shard_map/convert_element_type | solution.py:80
  14.7 18.0 %all-to-all-start = ((bf16[2,512,256]{2,0,1:T(2,128)(2,1)}), bf16[2,512,256]{2,0,1:T(2,128)(2,1)S(1)}, u32[]{:S(2)}, u32[]{:S(2)}) async-start(bf16[2,512,256]{2,0,1:T(2,128)(2,1)} %copy.29), calls=%async_computation | async-start | bytes 1048576 | tf_op jit(solution)/shard_map/all_to_all | solution.py:192
  32.7 0.0 copy-done.1
  32.7 0.6 fusion.90
  37.2 0.1 fusion.78
  37.3 0.1 fusion.74
  37.5 0.1 fusion.76
  37.6 0.1 fusion.75
  37.8 0.3 fusion.73
  38.1 0.3 fusion.67
  38.4 0.0 copy-done.2
  38.5 28.0 %all-to-all-done = bf16[2,512,256]{2,0,1:T(2,128)(2,1)S(1)} async-done(((bf16[2,512,256]{2,0,1:T(2,128)(2,1)}), bf16[2,512,256]{2,0,1:T(2,128)(2,1)S(1)}, u32[]{:S(2)}, u32[]{:S(2)}) %all-to-all-start) | async-done | bytes 524320 | tf_op jit(solution)/shard_map/all_to_all | solution.py:192
  66.4 0.3 copy.91
  66.7 0.2 all_to_all.16
  67.0 0.1 copy.57
  67.1 0.5 convolution_bitcast_fusion.3
  67.6 0.2 multiply_subtract_fusion.1
  67.8 0.6 convolution_bitcast_fusion.2
  68.4 2.1 %fusion.29 = (f32[1,16,64,128]{3,2,1,0:T(8,128)S(1)}, f32[1,16,64,128]{3,2,1,0:T(8,128)S(1)}) fusion(f32[2,16,64,128]{3,2,1,0:T(8,128)S(1)} %convolution_bitcast_fusion.2, f32[64,128]{1,0:T(8,128)S(1)} %fusion.64, f32[16]{0:T(128)S(1)} %broadcast_multiply_fusion), kind=kLoop, calls=%fused_computation.28 | loop fusion | flops 1048576 | bytes 2129984 | tf_op jit(solution)/shard_map/sub | solution.py:28
  70.5 0.6 convolution_bitcast_fusion.1
  71.1 0.2 multiply_subtract_fusion
  71.3 0.6 fusion.20
  71.9 0.2 convert_element_type.150
  72.1 2.4 %collective-permute-start = (bf16[2,16,8192]{2,1,0:T(8,128)(2,1)S(1)}, bf16[2,16,8192]{2,1,0:T(8,128)(2,1)S(1)}, u32[]{:S(2)}, u32[]{:S(2)}) collective-permute-start(bf16[2,16,8192]{2,1,0:T(8,128)(2,1)S(1)} %convert_element_type.150), channel_id=1, source_target_pairs={{0,32},{32,160},{64,192},{96,64},{128,0},{160,128},{192,224},{224,... | collective-permute-start | bytes 1572872 | tf_op jit(solution)/shard_map/ppermute | solution.py:195
  74.6 2.1 %collective-permute-start.1 = (bf16[2,16,8192]{2,1,0:T(8,128)(2,1)S(1)}, bf16[2,16,8192]{2,1,0:T(8,128)(2,1)S(1)}, u32[]{:S(2)}, u32[]{:S(2)}) collective-permute-start(bf16[2,16,8192]{2,1,0:T(8,128)(2,1)S(1)} %convert_element_type.150), channel_id=1, source_target_pairs={{0,64},{32,288},{64,320},{96,32},{128,384},{160,224},{192,128},{22... | collective-permute-start | bytes 1572872 | tf_op jit(solution)/shard_map/ppermute | solution.py:195
  76.7 0.1 convert_element_type.151
  76.8 8.8 %collective-permute-done = bf16[2,16,8192]{2,1,0:T(8,128)(2,1)S(1)} collective-permute-done((bf16[2,16,8192]{2,1,0:T(8,128)(2,1)S(1)}, bf16[2,16,8192]{2,1,0:T(8,128)(2,1)S(1)}, u32[]{:S(2)}, u32[]{:S(2)}) %collective-permute-start) | collective-permute-done | bytes 524320 | tf_op jit(solution)/shard_map/ppermute | solution.py:195
  85.6 0.1 convert_element_type.152
  85.7 0.6 collective-permute-done.1
  86.3 0.1 convert_element_type.153
  86.4 0.2 add_bitcast_fusion.1
  86.6 0.1 copy.58
  86.7 0.1 copy.59
  86.8 0.1 copy.60
  86.9 0.1 copy.61
  87.1 0.2 maximum_reduce_fusion
  87.2 0.7 convolution_multiply_fusion
  88.0 0.1 copy.39
  88.1 0.2 slice.115
  88.3 7.2 %collective-permute-start.2 = (f32[2,4,512]{2,1,0:T(4,128)S(1)}, f32[2,4,512]{2,1,0:T(4,128)S(1)}, u32[]{:S(2)}, u32[]{:S(2)}) collective-permute-start(f32[2,4,512]{2,1,0:T(4,128)S(1)} %slice.115), channel_id=1, source_target_pairs={{64,0},{288,32},{320,64},{32,96},{384,128},{224,160},{128,192},{48... | collective-permute-start | bytes 49160 | tf_op jit(solution)/shard_map/ppermute | solution.py:198
  95.5 0.1 copy.40
  95.6 0.2 slice.119
  95.8 1.9 %collective-permute-start.3 = (f32[2,4,512]{2,1,0:T(4,128)S(1)}, f32[2,4,512]{2,1,0:T(4,128)S(1)}, u32[]{:S(2)}, u32[]{:S(2)}) collective-permute-start(f32[2,4,512]{2,1,0:T(4,128)S(1)} %slice.119), channel_id=1, source_target_pairs={{32,0},{160,32},{192,64},{64,96},{0,128},{128,160},{224,192},{96,2... | collective-permute-start | bytes 49160 | tf_op jit(solution)/shard_map/ppermute | solution.py:198
  97.7 0.0 collective-permute-done.2
  97.7 5.2 %collective-permute-done.3 = f32[2,4,512]{2,1,0:T(4,128)S(1)} collective-permute-done((f32[2,4,512]{2,1,0:T(4,128)S(1)}, f32[2,4,512]{2,1,0:T(4,128)S(1)}, u32[]{:S(2)}, u32[]{:S(2)}) %collective-permute-start.3) | collective-permute-done | bytes 16416 | tf_op jit(solution)/shard_map/ppermute | solution.py:198
  102.9 0.6 maximum_bitcast_fusion.7
  103.6 0.6 maximum_bitcast_fusion.6
  (14 shorter events, 0.1 us)
Async XLA Ops:
  0.6 8.1 %copy-start = (bf16[1,2,256,1535]{2,1,3,0:T(2,128)(2,1)S(1)}, bf16[1,2,256,1535]{2,1,3,0:T(2,128)(2,1)}, u32[]{:S(2)}) copy-start(bf16[1,2,256,1535]{2,1,3,0:T(2,128)(2,1)} %param.5) | copy-start | bytes 4715524
  13.3 19.4 %copy-start.1 = (s32[1,2]{1,0:T(1,128)S(1)}, s32[1,2]{1,0:T(1,128)}, u32[]{:S(2)}) copy-start(s32[1,2]{1,0:T(1,128)} %param.9) | copy-start | bytes 28
  13.3 25.1 %copy-start.2 = (f32[16]{0:T(128)S(1)}, f32[16]{0:T(128)}, u32[]{:S(2)}) copy-start(f32[16]{0:T(128)} %param.8) | copy-start | bytes 196
  14.7 51.7 %all-to-all-start = ((bf16[2,512,256]{2,0,1:T(2,128)(2,1)}), bf16[2,512,256]{2,0,1:T(2,128)(2,1)S(1)}, u32[]{:S(2)}, u32[]{:S(2)}) async-start(bf16[2,512,256]{2,0,1:T(2,128)(2,1)} %copy.29), calls=%async_computation | async-start | bytes 1048576 | tf_op jit(solution)/shard_map/all_to_all | solution.py:192
  72.1 13.4 %collective-permute-start = (bf16[2,16,8192]{2,1,0:T(8,128)(2,1)S(1)}, bf16[2,16,8192]{2,1,0:T(8,128)(2,1)S(1)}, u32[]{:S(2)}, u32[]{:S(2)}) collective-permute-start(bf16[2,16,8192]{2,1,0:T(8,128)(2,1)S(1)} %convert_element_type.150), channel_id=1, source_target_pairs={{0,32},{32,160},{64,192},{96,64},{128,0},{160,128},{192,224},{224,... | collective-permute-start | bytes 1572872 | tf_op jit(solution)/shard_map/ppermute | solution.py:195
  74.6 11.7 %collective-permute-start.1 = (bf16[2,16,8192]{2,1,0:T(8,128)(2,1)S(1)}, bf16[2,16,8192]{2,1,0:T(8,128)(2,1)S(1)}, u32[]{:S(2)}, u32[]{:S(2)}) collective-permute-start(bf16[2,16,8192]{2,1,0:T(8,128)(2,1)S(1)} %convert_element_type.150), channel_id=1, source_target_pairs={{0,64},{32,288},{64,320},{96,32},{128,384},{160,224},{192,128},{22... | collective-permute-start | bytes 1572872 | tf_op jit(solution)/shard_map/ppermute | solution.py:195
  88.3 9.4 %collective-permute-start.2 = (f32[2,4,512]{2,1,0:T(4,128)S(1)}, f32[2,4,512]{2,1,0:T(4,128)S(1)}, u32[]{:S(2)}, u32[]{:S(2)}) collective-permute-start(f32[2,4,512]{2,1,0:T(4,128)S(1)} %slice.115), channel_id=1, source_target_pairs={{64,0},{288,32},{320,64},{32,96},{384,128},{224,160},{128,192},{48... | collective-permute-start | bytes 49160 | tf_op jit(solution)/shard_map/ppermute | solution.py:198
  95.8 7.1 %collective-permute-start.3 = (f32[2,4,512]{2,1,0:T(4,128)S(1)}, f32[2,4,512]{2,1,0:T(4,128)S(1)}, u32[]{:S(2)}, u32[]{:S(2)}) collective-permute-start(f32[2,4,512]{2,1,0:T(4,128)S(1)} %slice.119), channel_id=1, source_target_pairs={{32,0},{160,32},{192,64},{64,96},{0,128},{128,160},{224,192},{96,2... | collective-permute-start | bytes 49160 | tf_op jit(solution)/shard_map/ppermute | solution.py:198

commit v12 on v10

--- a/solution.py
+++ b/solution.py
@@ -163,44 +163,23 @@
     chosen = partner_bits[0]
     acq_size = lax.axis_size("acq")
     me = lax.axis_index("acq")
-    me_parity = jnp.int32(0)
-    for which in range(acq_size.bit_length() - 1):
-        me_parity = me_parity ^ ((me >> which) & 1)
-    low_bits = (0, 1)
-    high_bits = (2, 3)
-    edge_pairs = []
-    for slot in range(2):
-        edge_pairs.append(
-            [
-                (i, i ^ (1 << (high_bits[slot] if parity(i) else low_bits[slot])))
-                for i in range(acq_size)
-            ]
-        )
-    cand_bits = []
-    for slot in range(2):
-        cand_bits.append(jnp.where(me_parity == 1, low_bits[slot], high_bits[slot]))
-        cand_bits.append(jnp.where(me_parity == 1, high_bits[slot], low_bits[slot]))
-    preds = tuple(chosen[slot] == bit for slot in range(2) for bit in cand_bits)
+    bit_count = acq_size.bit_length() - 1
+    preds = tuple(chosen[slot] == which for slot in range(2) for which in range(bit_count))
     turned = lax.all_to_all(compressed, "pulse", split_axis=1, concat_axis=2, tiled=True)
     *preds, turned = lax.optimization_barrier((*preds, turned))
     focused = azimuth(turned, azimuth_rate).astype(jnp.bfloat16)
-    arrived = [lax.ppermute(focused, "acq", pairs) for pairs in edge_pairs]
-    looked = cross_looks(focused, arrived)
-    returned = [
-        lax.ppermute(looked[slot], "acq", [(dst, src) for src, dst in edge_pairs[slot]])
-        for slot in range(2)
+    arrived = [
+        lax.ppermute(focused, "acq", [(i, i ^ (1 << which)) for i in range(acq_size)])
+        for which in range(bit_count)
     ]
-    candidates = []
+    partners = []
     for slot in range(2):
-        candidates.append(looked[slot])
-        back = returned[slot]
-        candidates.append(jnp.stack([back[0], -back[1]]))
-    results = []
-    for slot in range(2):
-        pick = candidates[0]
-        for index in range(1, len(candidates)):
-            pick = jnp.where(preds[slot * len(candidates) + index], candidates[index], pick)
-        results.append(pick)
+        pick = arrived[0]
+        for which in range(1, bit_count):
+            pick = jnp.where(preds[slot * bit_count + which], arrived[which], pick)
+        partners.append(pick)
+    looked = cross_looks(focused, partners)
+    results = [looked[slot] for slot in range(2)]
     interfere_real = jnp.stack([item[0] for item in results])[None]
     interfere_imag = jnp.stack([item[1] for item in results])[None]
     return (interfere_real, interfere_imag)

time: 103 us -> 104 us (level)
  the two profiles are of different devices: /device:TPU:36 before, /device:TPU:2 now
where the time goes in v12:
time: 104 us
  waiting for transfers between devices  44.8 us (43%)
  starting transfers between devices  30 us (29%)
  matrix products  7.59 us (7%)
  other arithmetic  6.41 us (6%)
  between operations  5.52 us (5%)
  local copies, waits for them, and re-layouts  5.29 us (5%)
  Pallas kernels  3.94 us (4%)
    all_to_all x1, waiting for transfers between devices, per_device(): lax.all_to_all(compressed, 'pulse', split_axis=1, concat_axis=2, tiled=True)  27 us
    all_to_all x1, starting transfers between devices, per_device(): lax.all_to_all(compressed, 'pulse', split_axis=1, concat_axis=2, tiled=True)  18.1 us
    ppermute x4, waiting for transfers between devices, per_device(): lax.ppermute(focused, 'acq', [(i, i ^ 1 << which) for i in range(acq_size)])  17.8 us
    ppermute x4, starting transfers between devices, per_device(): lax.ppermute(focused, 'acq', [(i, i ^ 1 << which) for i in range(acq_size)])  11.9 us
    dot_general x1, matrix products, compress(): lax.dot_general(band, echoes, dims, preferred_element_type=jnp.float32)  4.57 us
    pallas_call x1, Pallas kernels, band_tables(): band = pl.pallas_call(band_kernel, out_shape=shape)(re_row, im_row)  3.94 us
    sub x3, other arithmetic, complex_product(): left_re * right_re - left_im * right_im  2.46 us
  transfers between devices with their start and end apart: 5, of which 4 were waited for; matrix products, arithmetic and copies ran while one was open for 2% of the time, Pallas kernels for 0%

profile of v12, /device:TPU:2, one launch (start us, length us, event | category | flops | bytes accessed | tf_op | source)
XLA Modules:
  0.0 103.5 jit_solution(14368700822637545007)
XLA Ops:
  0.6 0.0 copy-start
  0.6 0.8 multiply_convert_fusion
  1.5 0.6 reshape.354.re_ref
  2.1 0.6 reshape.355.im_ref
  3.4 3.9 %shard_map.68 = bf16[2,2,512,1535]{3,2,1,0:T(8,128)(2,1)} custom-call(f32[1,1152]{1,0:T(1,128)} %reshape.354.re_ref, f32[1,1152]{1,0:T(1,128)} %reshape.355.im_ref), custom_call_target="tpu_custom_call" | custom-call | tf_op jit(solution)/shard_map/pallas_call | solution.py:61
  7.3 0.0 copy-done
  7.3 4.6 %fusion.14 = bf16[2,512,256]{2,1,0:T(8,128)(2,1)S(1)} fusion(bf16[2,256,1535,1]{1,0,2,3:T(2,128)(2,1)S(1)} %bitcast.162, bf16[2,2,512,1535]{3,2,1,0:T(8,128)(2,1)} %shard_map.68, f32[256]{0:T(256)S(1)} %compare_convert_fusion), kind=kOutput, calls=%fused_computation.11 | convolution fusion | flops 1610088448 | bytes 8384512 | tf_op jit(solution)/shard_map/dot_general | solution.py:68
  11.9 0.0 copy-start.1
  11.9 0.0 copy-start.2
  11.9 1.3 %copy.33 = bf16[2,512,256]{2,0,1:T(2,128)(2,1)} copy(bf16[2,512,256]{2,1,0:T(8,128)(2,1)S(1)} %fusion.14) | data formatting | bytes 1048576 | tf_op jit(solution)/shard_map/convert_element_type | solution.py:72
  13.2 18.1 %all-to-all-start = ((bf16[2,512,256]{2,0,1:T(2,128)(2,1)}), bf16[2,512,256]{2,0,1:T(2,128)(2,1)S(1)}, u32[]{:S(2)}, u32[]{:S(2)}) async-start(bf16[2,512,256]{2,0,1:T(2,128)(2,1)} %copy.33), calls=%async_computation | async-start | bytes 1048576 | tf_op jit(solution)/shard_map/all_to_all | solution.py:168
  31.4 0.0 copy-done.1
  31.4 0.6 fusion.86
  35.8 0.1 fusion.78
  36.0 0.1 fusion.74
  36.1 0.1 fusion.76
  36.3 0.1 fusion.75
  36.4 0.3 fusion.73
  36.7 0.3 fusion.67
  37.1 0.0 copy-done.2
  37.1 27.0 %all-to-all-done = bf16[2,512,256]{2,0,1:T(2,128)(2,1)S(1)} async-done(((bf16[2,512,256]{2,0,1:T(2,128)(2,1)}), bf16[2,512,256]{2,0,1:T(2,128)(2,1)S(1)}, u32[]{:S(2)}, u32[]{:S(2)}) %all-to-all-start) | async-done | bytes 524320 | tf_op jit(solution)/shard_map/all_to_all | solution.py:168
  64.1 0.3 copy.95
  64.4 0.2 all_to_all.16
  64.6 0.1 copy.61
  64.7 0.5 convolution_bitcast_fusion.3
  65.2 0.2 multiply_subtract_fusion.1
  65.4 0.6 convolution_bitcast_fusion.2
  66.0 2.1 %fusion.29 = (f32[1,16,64,128]{3,2,1,0:T(8,128)S(1)}, f32[1,16,64,128]{3,2,1,0:T(8,128)S(1)}) fusion(f32[2,16,64,128]{3,2,1,0:T(8,128)S(1)} %convolution_bitcast_fusion.2, f32[64,128]{1,0:T(8,128)S(1)} %fusion.64, f32[16]{0:T(128)S(1)} %broadcast_multiply_fusion), kind=kLoop, calls=%fused_computation.28 | loop fusion | flops 1048576 | bytes 2129984 | tf_op jit(solution)/shard_map/sub | solution.py:28
  68.1 0.6 convolution_bitcast_fusion.1
  68.7 0.2 multiply_subtract_fusion
  68.9 0.6 fusion.20
  69.6 0.2 convert_element_type.150
  69.8 2.6 %collective-permute-start = (bf16[2,16,8192]{2,1,0:T(8,128)(2,1)S(1)}, bf16[2,16,8192]{2,1,0:T(8,128)(2,1)S(1)}, u32[]{:S(2)}, u32[]{:S(2)}) collective-permute-start(bf16[2,16,8192]{2,1,0:T(8,128)(2,1)S(1)} %convert_element_type.150), channel_id=1, source_target_pairs={{0,256},{32,288},{64,320},{96,352},{128,384},{160,416},{192,448},{... | collective-permute-start | bytes 1572872 | tf_op jit(solution)/shard_map/ppermute | solution.py:172
  72.4 4.0 %collective-permute-start.1 = (bf16[2,16,8192]{2,1,0:T(8,128)(2,1)S(1)}, bf16[2,16,8192]{2,1,0:T(8,128)(2,1)S(1)}, u32[]{:S(2)}, u32[]{:S(2)}) collective-permute-start(bf16[2,16,8192]{2,1,0:T(8,128)(2,1)S(1)} %convert_element_type.150), channel_id=1, source_target_pairs={{0,128},{32,160},{64,192},{96,224},{128,0},{160,32},{192,64},{224,... | collective-permute-start | bytes 1572872 | tf_op jit(solution)/shard_map/ppermute | solution.py:172
  76.4 3.3 %collective-permute-start.2 = (bf16[2,16,8192]{2,1,0:T(8,128)(2,1)S(1)}, bf16[2,16,8192]{2,1,0:T(8,128)(2,1)S(1)}, u32[]{:S(2)}, u32[]{:S(2)}) collective-permute-start(bf16[2,16,8192]{2,1,0:T(8,128)(2,1)S(1)} %convert_element_type.150), channel_id=1, source_target_pairs={{0,64},{32,96},{64,0},{96,32},{128,192},{160,224},{192,128},{224,1... | collective-permute-start | bytes 1572872 | tf_op jit(solution)/shard_map/ppermute | solution.py:172
  79.8 1.9 %collective-permute-start.3 = (bf16[2,16,8192]{2,1,0:T(8,128)(2,1)S(1)}, bf16[2,16,8192]{2,1,0:T(8,128)(2,1)S(1)}, u32[]{:S(2)}, u32[]{:S(2)}) collective-permute-start(bf16[2,16,8192]{2,1,0:T(8,128)(2,1)S(1)} %convert_element_type.150), channel_id=1, source_target_pairs={{0,32},{32,0},{64,96},{96,64},{128,160},{160,128},{192,224},{224,1... | collective-permute-start | bytes 1572872 | tf_op jit(solution)/shard_map/ppermute | solution.py:172
  81.7 0.1 convert_element_type.151
  81.8 2.7 %collective-permute-done = bf16[2,16,8192]{2,1,0:T(8,128)(2,1)S(1)} collective-permute-done((bf16[2,16,8192]{2,1,0:T(8,128)(2,1)S(1)}, bf16[2,16,8192]{2,1,0:T(8,128)(2,1)S(1)}, u32[]{:S(2)}, u32[]{:S(2)}) %collective-permute-start) | collective-permute-done | bytes 524320 | tf_op jit(solution)/shard_map/ppermute | solution.py:172
  84.5 6.1 %collective-permute-done.1 = bf16[2,16,8192]{2,1,0:T(8,128)(2,1)S(1)} collective-permute-done((bf16[2,16,8192]{2,1,0:T(8,128)(2,1)S(1)}, bf16[2,16,8192]{2,1,0:T(8,128)(2,1)S(1)}, u32[]{:S(2)}, u32[]{:S(2)}) %collective-permute-start.1) | collective-permute-done | bytes 524320 | tf_op jit(solution)/shard_map/ppermute | solution.py:172
  90.6 9.0 %collective-permute-done.2 = bf16[2,16,8192]{2,1,0:T(8,128)(2,1)S(1)} collective-permute-done((bf16[2,16,8192]{2,1,0:T(8,128)(2,1)S(1)}, bf16[2,16,8192]{2,1,0:T(8,128)(2,1)S(1)}, u32[]{:S(2)}, u32[]{:S(2)}) %collective-permute-start.2) | collective-permute-done | bytes 524320 | tf_op jit(solution)/shard_map/ppermute | solution.py:172
  99.6 0.0 collective-permute-done.3
  99.6 0.2 select_convert_fusion.1
  99.8 0.2 add_bitcast_fusion.1
  100.0 0.1 copy.62
  100.2 0.1 copy.63
  100.3 0.1 copy.64
  100.4 0.1 copy.65
  100.5 0.2 maximum_reduce_fusion
  100.7 0.7 convolution_multiply_fusion
  101.4 0.1 copy.43
  101.5 0.1 slice.113
  101.6 0.1 copy.44
  101.7 0.1 slice.115
  101.9 0.1 copy.41
  102.0 0.1 slice.109
  102.1 0.1 copy.42
  102.2 0.1 slice.111
  102.3 0.6 maximum_bitcast_fusion.7
  102.9 0.6 maximum_bitcast_fusion.6
  (9 shorter events, 0.1 us)
Async XLA Ops:
  0.6 6.7 %copy-start = (bf16[1,2,256,1535]{2,1,3,0:T(2,128)(2,1)S(1)}, bf16[1,2,256,1535]{2,1,3,0:T(2,128)(2,1)}, u32[]{:S(2)}) copy-start(bf16[1,2,256,1535]{2,1,3,0:T(2,128)(2,1)} %param.5) | copy-start | bytes 4715524
  11.9 19.5 %copy-start.1 = (s32[1,2]{1,0:T(1,128)S(1)}, s32[1,2]{1,0:T(1,128)}, u32[]{:S(2)}) copy-start(s32[1,2]{1,0:T(1,128)} %param.9) | copy-start | bytes 28
  11.9 25.2 %copy-start.2 = (f32[16]{0:T(128)S(1)}, f32[16]{0:T(128)}, u32[]{:S(2)}) copy-start(f32[16]{0:T(128)} %param.8) | copy-start | bytes 196
  13.2 50.8 %all-to-all-start = ((bf16[2,512,256]{2,0,1:T(2,128)(2,1)}), bf16[2,512,256]{2,0,1:T(2,128)(2,1)S(1)}, u32[]{:S(2)}, u32[]{:S(2)}) async-start(bf16[2,512,256]{2,0,1:T(2,128)(2,1)} %copy.33), calls=%async_computation | async-start | bytes 1048576 | tf_op jit(solution)/shard_map/all_to_all | solution.py:168
  69.8 14.7 %collective-permute-start = (bf16[2,16,8192]{2,1,0:T(8,128)(2,1)S(1)}, bf16[2,16,8192]{2,1,0:T(8,128)(2,1)S(1)}, u32[]{:S(2)}, u32[]{:S(2)}) collective-permute-start(bf16[2,16,8192]{2,1,0:T(8,128)(2,1)S(1)} %convert_element_type.150), channel_id=1, source_target_pairs={{0,256},{32,288},{64,320},{96,352},{128,384},{160,416},{192,448},{... | collective-permute-start | bytes 1572872 | tf_op jit(solution)/shard_map/ppermute | solution.py:172
  72.4 18.3 %collective-permute-start.1 = (bf16[2,16,8192]{2,1,0:T(8,128)(2,1)S(1)}, bf16[2,16,8192]{2,1,0:T(8,128)(2,1)S(1)}, u32[]{:S(2)}, u32[]{:S(2)}) collective-permute-start(bf16[2,16,8192]{2,1,0:T(8,128)(2,1)S(1)} %convert_element_type.150), channel_id=1, source_target_pairs={{0,128},{32,160},{64,192},{96,224},{128,0},{160,32},{192,64},{224,... | collective-permute-start | bytes 1572872 | tf_op jit(solution)/shard_map/ppermute | solution.py:172
  76.4 23.2 %collective-permute-start.2 = (bf16[2,16,8192]{2,1,0:T(8,128)(2,1)S(1)}, bf16[2,16,8192]{2,1,0:T(8,128)(2,1)S(1)}, u32[]{:S(2)}, u32[]{:S(2)}) collective-permute-start(bf16[2,16,8192]{2,1,0:T(8,128)(2,1)S(1)} %convert_element_type.150), channel_id=1, source_target_pairs={{0,64},{32,96},{64,0},{96,32},{128,192},{160,224},{192,128},{224,1... | collective-permute-start | bytes 1572872 | tf_op jit(solution)/shard_map/ppermute | solution.py:172
  79.8 19.8 %collective-permute-start.3 = (bf16[2,16,8192]{2,1,0:T(8,128)(2,1)S(1)}, bf16[2,16,8192]{2,1,0:T(8,128)(2,1)S(1)}, u32[]{:S(2)}, u32[]{:S(2)}) collective-permute-start(bf16[2,16,8192]{2,1,0:T(8,128)(2,1)S(1)} %convert_element_type.150), channel_id=1, source_target_pairs={{0,32},{32,0},{64,96},{96,64},{128,160},{160,128},{192,224},{224,1... | collective-permute-start | bytes 1572872 | tf_op jit(solution)/shard_map/ppermute | solution.py:172

commit v13 on v10

--- a/solution.py
+++ b/solution.py
@@ -72,7 +72,21 @@
     return (joined * keep[None, None, :]).astype(jnp.bfloat16)
 
 
-def azimuth(turned, azimuth_rate):
+def filter_tables(azimuth_rate, length):
+    outer_len = 64
+    inner_len = length // outer_len
+    outer_ids = jnp.arange(outer_len, dtype=jnp.int32)
+    inner_ids = jnp.arange(inner_len, dtype=jnp.int32)
+    freq_index = outer_ids[:, None] + outer_len * inner_ids[None, :]
+    signed = jnp.where(freq_index < length // 2, freq_index, freq_index - length).astype(
+        jnp.float32
+    )
+    quad = signed * signed / length
+    phase = (jnp.pi * azimuth_rate)[:, None, None] * quad[None, :, :]
+    return jnp.cos(phase), jnp.sin(phase)
+
+
+def azimuth(turned, filt_cos, filt_sin):
     columns = turned.shape[1]
     length = turned.shape[2]
     outer_len = 64
@@ -99,13 +113,7 @@
         part_tables(inner_len, False),
         precision=highest,
     )
-    freq_index = outer_ids[:, None] + outer_len * inner_ids[None, :]
-    signed = jnp.where(freq_index < length // 2, freq_index, freq_index - length).astype(
-        jnp.float32
-    )
-    quad = signed * signed / length
-    phase = (jnp.pi * azimuth_rate)[:, None, None] * quad[None, :, :]
-    filt_re, filt_im = complex_product(spectrum[0], spectrum[1], jnp.cos(phase), -jnp.sin(phase))
+    filt_re, filt_im = complex_product(spectrum[0], spectrum[1], filt_cos, -filt_sin)
     back_one = jnp.einsum(
         "pckm,pqmb->qckb",
         jnp.stack([filt_re, filt_im]),
@@ -182,8 +190,9 @@
         cand_bits.append(jnp.where(me_parity == 1, high_bits[slot], low_bits[slot]))
     preds = tuple(chosen[slot] == bit for slot in range(2) for bit in cand_bits)
     turned = lax.all_to_all(compressed, "pulse", split_axis=1, concat_axis=2, tiled=True)
-    *preds, turned = lax.optimization_barrier((*preds, turned))
-    focused = azimuth(turned, azimuth_rate).astype(jnp.bfloat16)
+    filt_cos, filt_sin = filter_tables(azimuth_rate, pulses_dev * lax.axis_size("pulse"))
+    *preds, filt_cos, filt_sin, turned = lax.optimization_barrier((*preds, filt_cos, filt_sin, turned))
+    focused = azimuth(turned, filt_cos, filt_sin).astype(jnp.bfloat16)
     arrived = [lax.ppermute(focused, "acq", pairs) for pairs in edge_pairs]
     looked = cross_looks(focused, arrived)
     returned = [

time: 103 us -> 103 us (level)
  waiting for transfers between devices: 42.6 us -> 37.3 us
  other arithmetic: 6.38 us -> 9.79 us
    all_to_all x1, waiting for transfers between devices: 28 us -> 22.7 us  [per_device(): lax.all_to_all(compressed, 'pulse', split_axis=1, concat_axis=2, tiled=True)]
    sin x0 -> x1, other arithmetic: none -> 2.73 us  [filter_tables(): return (jnp.cos(phase), jnp.sin(phase))]
    sub x3 -> x2, other arithmetic: 2.46 us -> 0.28 us  [complex_product(): left_re * right_re - left_im * right_im]
    another operation x2, other arithmetic: 0.06 us -> 1.4 us  [part_tables(): return jnp.stack([jnp.stack([cosine, -sine]), jnp.stack([sine, cosine])])]
  transfers between devices with their start and end apart: 5 -> 5, of which waited for: 4 -> 4; matrix products, arithmetic and copies ran while one was open for 2% -> 7% of each run, Pallas kernels for 0% -> 0%
where the time goes in v13:
time: 103 us; the launch traced here: 102 us
  waiting for transfers between devices  37.3 us (36%)
  starting transfers between devices  31.6 us (31%)
  other arithmetic  9.79 us (10%)
  matrix products  8.49 us (8%)
  between operations  5.6 us (5%)
  local copies, waits for them, and re-layouts  5.44 us (5%)
  Pallas kernels  3.9 us (4%)
    all_to_all x1, waiting for transfers between devices, per_device(): lax.all_to_all(compressed, 'pulse', split_axis=1, concat_axis=2, tiled=True)  22.7 us
    all_to_all x1, starting transfers between devices, per_device(): lax.all_to_all(compressed, 'pulse', split_axis=1, concat_axis=2, tiled=True)  18 us
    ppermute x2, waiting for transfers between devices, per_device(): arrived = [lax.ppermute(focused, 'acq', pairs) for pairs in edge_pairs]  9.46 us
    ppermute x2, starting transfers between devices, per_device(): lax.ppermute(looked[slot], 'acq', [(dst, src) for src, dst in edge_pairs[...  9.11 us
    ppermute x2, waiting for transfers between devices, per_device(): lax.ppermute(looked[slot], 'acq', [(dst, src) for src, dst in edge_pairs[...  5.19 us
    dot_general x1, matrix products, compress(): lax.dot_general(band, echoes, dims, preferred_element_type=jnp.float32)  4.57 us
    ppermute x2, starting transfers between devices, per_device(): arrived = [lax.ppermute(focused, 'acq', pairs) for pairs in edge_pairs]  4.51 us
    pallas_call x1, Pallas kernels, band_tables(): band = pl.pallas_call(band_kernel, out_shape=shape)(re_row, im_row)  3.9 us
  transfers between devices with their start and end apart: 5, of which 4 were waited for; matrix products, arithmetic and copies ran while one was open for 7% of the time, Pallas kernels for 0%

profile of v13, /device:TPU:36, one launch (start us, length us, event | category | flops | bytes accessed | tf_op | source)
XLA Modules:
  0.0 102.2 jit_solution(2135005159815445668)
XLA Ops:
  0.6 0.0 copy-start
  0.6 0.8 multiply_convert_fusion
  1.5 0.6 reshape.326.re_ref
  2.1 0.6 reshape.327.im_ref
  3.4 3.9 %shard_map.68 = bf16[2,2,512,1535]{3,2,1,0:T(8,128)(2,1)} custom-call(f32[1,1152]{1,0:T(1,128)} %reshape.326.re_ref, f32[1,1152]{1,0:T(1,128)} %reshape.327.im_ref), custom_call_target="tpu_custom_call" | custom-call | tf_op jit(solution)/shard_map/pallas_call | solution.py:61
  7.3 0.0 copy-done
  7.3 4.6 %fusion.14 = bf16[2,512,256]{2,1,0:T(8,128)(2,1)S(1)} fusion(bf16[2,256,1535,1]{1,0,2,3:T(2,128)(2,1)S(1)} %bitcast.170, bf16[2,2,512,1535]{3,2,1,0:T(8,128)(2,1)} %shard_map.68, f32[256]{0:T(256)S(1)} %compare_convert_fusion), kind=kOutput, calls=%fused_computation.11 | convolution fusion | flops 1610088448 | bytes 8384512 | tf_op jit(solution)/shard_map/dot_general | solution.py:68
  11.8 0.0 copy-start.8
  11.8 0.0 copy-start.9
  11.9 1.3 %copy.29 = bf16[2,512,256]{2,0,1:T(2,128)(2,1)} copy(bf16[2,512,256]{2,1,0:T(8,128)(2,1)S(1)} %fusion.14) | data formatting | bytes 1048576 | tf_op jit(solution)/shard_map/convert_element_type | solution.py:72
  13.2 18.0 %all-to-all-start = ((bf16[2,512,256]{2,0,1:T(2,128)(2,1)}), bf16[2,512,256]{2,0,1:T(2,128)(2,1)S(1)}, u32[]{:S(2)}, u32[]{:S(2)}) async-start(bf16[2,512,256]{2,0,1:T(2,128)(2,1)} %copy.29), calls=%async_computation | async-start | bytes 1048576 | tf_op jit(solution)/shard_map/all_to_all | solution.py:192
  31.2 0.0 copy-done.8
  31.2 0.6 fusion.83
  35.7 0.1 fusion.71
  35.9 0.8 fusion.67
  36.6 0.1 fusion.69
  36.8 0.8 fusion.68
  37.6 0.3 fusion.66
  37.8 0.3 fusion.60
  38.1 0.7 fusion.41
  38.8 0.7 fusion.34
  39.5 0.0 copy-done.9
  39.5 2.7 %multiply_sine_fusion = (f32[16,64,128]{2,1,0:T(8,128)S(1)}, f32[16,64,128]{2,1,0:T(8,128)}) fusion(f32[64,128]{1,0:T(8,128)S(1)} %fusion.57, f32[16]{0:T(128)S(1)} %broadcast_multiply_fusion), kind=kLoop, calls=%fused_computation.24 | loop fusion | flops 131072 | bytes 1081408 | tf_op jit(solution)/shard_map/sin | solution.py:86
  42.3 22.7 %all-to-all-done = bf16[2,512,256]{2,0,1:T(2,128)(2,1)S(1)} async-done(((bf16[2,512,256]{2,0,1:T(2,128)(2,1)}), bf16[2,512,256]{2,0,1:T(2,128)(2,1)S(1)}, u32[]{:S(2)}, u32[]{:S(2)}) %all-to-all-start) | async-done | bytes 524320 | tf_op jit(solution)/shard_map/all_to_all | solution.py:192
  64.9 0.3 copy.91
  65.2 0.2 all_to_all.16
  65.5 0.0 copy-start.3
  65.5 0.1 copy.57
  65.6 1.4 %convolution_bitcast_fusion.3 = f32[2,16,64,128]{3,2,1,0:T(8,128)S(1)} fusion(f32[1,2,64,64]{2,3,0,1:T(8,128)} %get-tuple-element.41, f32[1,2,64,64]{2,3,0,1:T(8,128)} %get-tuple-element.48, bf16[2,16,64,128]{3,2,1,0:T(8,128)(2,1)S(1)} %bitcast.176), kind=kOutput, calls=%fused_computation.9 | convolution fusion | flops 201342976 | bytes 1638400 | tf_op jit(solution)/shard_map/pcab,pqak->qckb/dot_general | solution.py:96
  67.1 0.1 multiply_subtract_fusion.1
  67.2 0.6 convolution_bitcast_fusion.2
  67.8 0.3 copy-done.1
  68.1 0.3 subtract_bitcast_fusion.2
  68.4 0.6 convolution_bitcast_fusion.1
  69.0 0.0 copy-done.4
  69.0 0.1 multiply_subtract_fusion
  69.2 0.1 copy-done.6
  69.2 0.0 copy-done.7
  69.3 0.6 fusion.20
  69.9 0.2 convert_element_type.150
  70.1 2.4 %collective-permute-start = (bf16[2,16,8192]{2,1,0:T(8,128)(2,1)S(1)}, bf16[2,16,8192]{2,1,0:T(8,128)(2,1)S(1)}, u32[]{:S(2)}, u32[]{:S(2)}) collective-permute-start(bf16[2,16,8192]{2,1,0:T(8,128)(2,1)S(1)} %convert_element_type.150), channel_id=1, source_target_pairs={{0,32},{32,160},{64,192},{96,64},{128,0},{160,128},{192,224},{224,... | collective-permute-start | bytes 1572872 | tf_op jit(solution)/shard_map/ppermute | solution.py:196
  72.6 2.1 %collective-permute-start.1 = (bf16[2,16,8192]{2,1,0:T(8,128)(2,1)S(1)}, bf16[2,16,8192]{2,1,0:T(8,128)(2,1)S(1)}, u32[]{:S(2)}, u32[]{:S(2)}) collective-permute-start(bf16[2,16,8192]{2,1,0:T(8,128)(2,1)S(1)} %convert_element_type.150), channel_id=1, source_target_pairs={{0,64},{32,288},{64,320},{96,32},{128,384},{160,224},{192,128},{22... | collective-permute-start | bytes 1572872 | tf_op jit(solution)/shard_map/ppermute | solution.py:196
  74.7 0.1 convert_element_type.151
  74.7 8.8 %collective-permute-done = bf16[2,16,8192]{2,1,0:T(8,128)(2,1)S(1)} collective-permute-done((bf16[2,16,8192]{2,1,0:T(8,128)(2,1)S(1)}, bf16[2,16,8192]{2,1,0:T(8,128)(2,1)S(1)}, u32[]{:S(2)}, u32[]{:S(2)}) %collective-permute-start) | collective-permute-done | bytes 524320 | tf_op jit(solution)/shard_map/ppermute | solution.py:196
  83.6 0.1 convert_element_type.152
  83.7 0.6 collective-permute-done.1
  84.3 0.1 convert_element_type.153
  84.4 0.2 add_bitcast_fusion.1
  84.6 0.1 copy.58
  84.7 0.1 copy.59
  84.8 0.1 copy.60
  84.9 0.1 copy.61
  85.0 0.2 maximum_reduce_fusion
  85.2 0.7 convolution_multiply_fusion
  86.0 0.1 copy.39
  86.1 0.2 slice.115
  86.3 7.2 %collective-permute-start.2 = (f32[2,4,512]{2,1,0:T(4,128)S(1)}, f32[2,4,512]{2,1,0:T(4,128)S(1)}, u32[]{:S(2)}, u32[]{:S(2)}) collective-permute-start(f32[2,4,512]{2,1,0:T(4,128)S(1)} %slice.115), channel_id=1, source_target_pairs={{64,0},{288,32},{320,64},{32,96},{384,128},{224,160},{128,192},{48... | collective-permute-start | bytes 49160 | tf_op jit(solution)/shard_map/ppermute | solution.py:199
  93.5 0.1 copy.40
  93.6 0.2 slice.119
  93.7 1.9 %collective-permute-start.3 = (f32[2,4,512]{2,1,0:T(4,128)S(1)}, f32[2,4,512]{2,1,0:T(4,128)S(1)}, u32[]{:S(2)}, u32[]{:S(2)}) collective-permute-start(f32[2,4,512]{2,1,0:T(4,128)S(1)} %slice.119), channel_id=1, source_target_pairs={{32,0},{160,32},{192,64},{64,96},{0,128},{128,160},{224,192},{96,2... | collective-permute-start | bytes 49160 | tf_op jit(solution)/shard_map/ppermute | solution.py:199
  95.7 0.0 collective-permute-done.2
  95.7 5.2 %collective-permute-done.3 = f32[2,4,512]{2,1,0:T(4,128)S(1)} collective-permute-done((f32[2,4,512]{2,1,0:T(4,128)S(1)}, f32[2,4,512]{2,1,0:T(4,128)S(1)}, u32[]{:S(2)}, u32[]{:S(2)}) %collective-permute-start.3) | collective-permute-done | bytes 16416 | tf_op jit(solution)/shard_map/ppermute | solution.py:199
  100.9 0.6 maximum_bitcast_fusion.7
  101.5 0.6 maximum_bitcast_fusion.6
  (21 shorter events, 0.1 us)
Async XLA Ops:
  0.6 6.6 %copy-start = (bf16[1,2,256,1535]{2,1,3,0:T(2,128)(2,1)S(1)}, bf16[1,2,256,1535]{2,1,3,0:T(2,128)(2,1)}, u32[]{:S(2)}) copy-start(bf16[1,2,256,1535]{2,1,3,0:T(2,128)(2,1)} %param.5) | copy-start | bytes 4715524
  11.8 19.4 %copy-start.8 = (s32[1,2]{1,0:T(1,128)S(1)}, s32[1,2]{1,0:T(1,128)}, u32[]{:S(2)}) copy-start(s32[1,2]{1,0:T(1,128)} %param.9) | copy-start | bytes 28
  11.8 27.7 %copy-start.9 = (f32[16]{0:T(128)S(1)}, f32[16]{0:T(128)}, u32[]{:S(2)}) copy-start(f32[16]{0:T(128)} %param.8) | copy-start | bytes 196
  13.2 51.7 %all-to-all-start = ((bf16[2,512,256]{2,0,1:T(2,128)(2,1)}), bf16[2,512,256]{2,0,1:T(2,128)(2,1)S(1)}, u32[]{:S(2)}, u32[]{:S(2)}) async-start(bf16[2,512,256]{2,0,1:T(2,128)(2,1)} %copy.29), calls=%async_computation | async-start | bytes 1048576 | tf_op jit(solution)/shard_map/all_to_all | solution.py:192
  65.5 1.6 %copy-start.3 = (f32[64,128]{1,0:T(8,128)S(1)}, f32[64,128]{1,0:T(8,128)}, u32[]{:S(2)}) copy-start(f32[64,128]{1,0:T(8,128)} %get-tuple-element.66) | copy-start | bytes 98308
  65.5 1.6 %copy-start.5 = (f32[64,128]{1,0:T(8,128)S(1)}, f32[64,128]{1,0:T(8,128)}, u32[]{:S(2)}) copy-start(f32[64,128]{1,0:T(8,128)} %get-tuple-element.67) | copy-start | bytes 98308
  65.6 1.6 %copy-start.2 = (f32[1,2,128,128]{3,2,0,1:T(8,128)S(1)}, f32[1,2,128,128]{3,2,0,1:T(8,128)}, u32[]{:S(2)}) copy-start(f32[1,2,128,128]{3,2,0,1:T(8,128)} %get-tuple-element.44) | copy-start | bytes 393220
  67.1 1.0 %copy-start.1 = (f32[16,64,128]{2,1,0:T(8,128)S(1)}, f32[16,64,128]{2,1,0:T(8,128)}, u32[]{:S(2)}) copy-start(f32[16,64,128]{2,1,0:T(8,128)} %get-tuple-element.13) | copy-start | bytes 1572868
  68.1 0.9 copy-start.4
  68.4 0.8 copy-start.6
  68.4 0.9 copy-start.7
  70.1 13.4 %collective-permute-start = (bf16[2,16,8192]{2,1,0:T(8,128)(2,1)S(1)}, bf16[2,16,8192]{2,1,0:T(8,128)(2,1)S(1)}, u32[]{:S(2)}, u32[]{:S(2)}) collective-permute-start(bf16[2,16,8192]{2,1,0:T(8,128)(2,1)S(1)} %convert_element_type.150), channel_id=1, source_target_pairs={{0,32},{32,160},{64,192},{96,64},{128,0},{160,128},{192,224},{224,... | collective-permute-start | bytes 1572872 | tf_op jit(solution)/shard_map/ppermute | solution.py:196
  72.6 11.7 %collective-permute-start.1 = (bf16[2,16,8192]{2,1,0:T(8,128)(2,1)S(1)}, bf16[2,16,8192]{2,1,0:T(8,128)(2,1)S(1)}, u32[]{:S(2)}, u32[]{:S(2)}) collective-permute-start(bf16[2,16,8192]{2,1,0:T(8,128)(2,1)S(1)} %convert_element_type.150), channel_id=1, source_target_pairs={{0,64},{32,288},{64,320},{96,32},{128,384},{160,224},{192,128},{22... | collective-permute-start | bytes 1572872 | tf_op jit(solution)/shard_map/ppermute | solution.py:196
  86.3 9.4 %collective-permute-start.2 = (f32[2,4,512]{2,1,0:T(4,128)S(1)}, f32[2,4,512]{2,1,0:T(4,128)S(1)}, u32[]{:S(2)}, u32[]{:S(2)}) collective-permute-start(f32[2,4,512]{2,1,0:T(4,128)S(1)} %slice.115), channel_id=1, source_target_pairs={{64,0},{288,32},{320,64},{32,96},{384,128},{224,160},{128,192},{48... | collective-permute-start | bytes 49160 | tf_op jit(solution)/shard_map/ppermute | solution.py:199
  93.7 7.1 %collective-permute-start.3 = (f32[2,4,512]{2,1,0:T(4,128)S(1)}, f32[2,4,512]{2,1,0:T(4,128)S(1)}, u32[]{:S(2)}, u32[]{:S(2)}) collective-permute-start(f32[2,4,512]{2,1,0:T(4,128)S(1)} %slice.119), channel_id=1, source_target_pairs={{32,0},{160,32},{192,64},{64,96},{0,128},{128,160},{224,192},{96,2... | collective-permute-start | bytes 49160 | tf_op jit(solution)/shard_map/ppermute | solution.py:199

commit v14 on v13

--- a/solution.py
+++ b/solution.py
@@ -193,12 +193,21 @@
     filt_cos, filt_sin = filter_tables(azimuth_rate, pulses_dev * lax.axis_size("pulse"))
     *preds, filt_cos, filt_sin, turned = lax.optimization_barrier((*preds, filt_cos, filt_sin, turned))
     focused = azimuth(turned, filt_cos, filt_sin).astype(jnp.bfloat16)
-    arrived = [lax.ppermute(focused, "acq", pairs) for pairs in edge_pairs]
-    looked = cross_looks(focused, arrived)
-    returned = [
-        lax.ppermute(looked[slot], "acq", [(dst, src) for src, dst in edge_pairs[slot]])
-        for slot in range(2)
-    ]
+    fast, slow = 1, 0
+    arrived = [None, None]
+    looked = [None, None]
+    returned = [None, None]
+    arrived[fast] = lax.ppermute(focused, "acq", edge_pairs[fast])
+    looked[fast] = cross_looks(focused, [arrived[fast]])[0]
+    returned[fast] = lax.ppermute(
+        looked[fast], "acq", [(dst, src) for src, dst in edge_pairs[fast]]
+    )
+    gate, held = lax.optimization_barrier((looked[fast], focused))
+    arrived[slow] = lax.ppermute(held, "acq", edge_pairs[slow])
+    looked[slow] = cross_looks(focused, [arrived[slow]])[0]
+    returned[slow] = lax.ppermute(
+        looked[slow], "acq", [(dst, src) for src, dst in edge_pairs[slow]]
+    )
     candidates = []
     for slot in range(2):
         candidates.append(looked[slot])

time: 103 us -> 105 us (1.019)
  the two profiles are of different devices: /device:TPU:36 before, /device:TPU:40 now
where the time goes in v14:
time: 105 us; the launch traced here: 104 us
  waiting for transfers between devices  40.9 us (39%)
  starting transfers between devices  29.1 us (28%)
  other arithmetic  9.68 us (9%)
  matrix products  8.59 us (8%)
  local copies, waits for them, and re-layouts  6.38 us (6%)
  between operations  5.59 us (5%)
  Pallas kernels  3.91 us (4%)
    all_to_all x1, waiting for transfers between devices, per_device(): lax.all_to_all(compressed, 'pulse', split_axis=1, concat_axis=2, tiled=True)  22.7 us
    all_to_all x1, starting transfers between devices, per_device(): lax.all_to_all(compressed, 'pulse', split_axis=1, concat_axis=2, tiled=True)  17.1 us
    ppermute x1, waiting for transfers between devices, per_device(): arrived[fast] = lax.ppermute(focused, 'acq', edge_pairs[fast])  7.72 us
    ppermute x1, waiting for transfers between devices, per_device(): lax.ppermute(looked[slow], 'acq', [(dst, src) for src, dst in edge_pairs[...  5.65 us
    ppermute x1, starting transfers between devices, per_device(): arrived[slow] = lax.ppermute(held, 'acq', edge_pairs[slow])  4.93 us
    ppermute x1, waiting for transfers between devices, per_device(): arrived[slow] = lax.ppermute(held, 'acq', edge_pairs[slow])  4.75 us
    dot_general x1, matrix products, compress(): lax.dot_general(band, echoes, dims, preferred_element_type=jnp.float32)  4.57 us
    pallas_call x1, Pallas kernels, band_tables(): band = pl.pallas_call(band_kernel, out_shape=shape)(re_row, im_row)  3.91 us
  transfers between devices with their start and end apart: 5, of which 4 were waited for; matrix products, arithmetic and copies ran while one was open for 8% of the time, Pallas kernels for 0%

profile of v14, /device:TPU:40, one launch (start us, length us, event | category | flops | bytes accessed | tf_op | source)
XLA Modules:
  0.0 104.1 jit_solution(15679785158395380687)
XLA Ops:
  0.6 0.0 copy-start
  0.6 0.8 multiply_convert_fusion
  1.5 0.6 reshape.323.re_ref
  2.1 0.6 reshape.324.im_ref
  3.4 3.9 %shard_map.68 = bf16[2,2,512,1535]{3,2,1,0:T(8,128)(2,1)} custom-call(f32[1,1152]{1,0:T(1,128)} %reshape.323.re_ref, f32[1,1152]{1,0:T(1,128)} %reshape.324.im_ref), custom_call_target="tpu_custom_call" | custom-call | tf_op jit(solution)/shard_map/pallas_call | solution.py:61
  7.3 4.6 %fusion.14 = bf16[2,512,256]{2,1,0:T(8,128)(2,1)S(1)} fusion(bf16[2,256,1535,1]{1,0,2,3:T(2,128)(2,1)S(1)} %bitcast.172, bf16[2,2,512,1535]{3,2,1,0:T(8,128)(2,1)} %shard_map.68, f32[256]{0:T(256)S(1)} %compare_convert_fusion), kind=kOutput, calls=%fused_computation.10 | convolution fusion | flops 1610088448 | bytes 8384512 | tf_op jit(solution)/shard_map/dot_general | solution.py:68
  11.9 0.0 copy-start.8
  11.9 0.0 copy-start.9
  11.9 1.3 %copy.29 = bf16[2,512,256]{2,0,1:T(2,128)(2,1)} copy(bf16[2,512,256]{2,1,0:T(8,128)(2,1)S(1)} %fusion.14) | data formatting | bytes 1048576 | tf_op jit(solution)/shard_map/convert_element_type | solution.py:72
  13.2 17.1 %all-to-all-start = ((bf16[2,512,256]{2,0,1:T(2,128)(2,1)}), bf16[2,512,256]{2,0,1:T(2,128)(2,1)S(1)}, u32[]{:S(2)}, u32[]{:S(2)}) async-start(bf16[2,512,256]{2,0,1:T(2,128)(2,1)} %copy.29), calls=%async_computation | async-start | bytes 1048576 | tf_op jit(solution)/shard_map/all_to_all | solution.py:192
  30.3 0.6 fusion.84
  34.8 0.1 fusion.71
  35.0 0.8 fusion.67
  35.7 0.1 fusion.69
  35.9 0.8 fusion.68
  36.6 0.3 fusion.66
  36.9 0.3 fusion.60
  37.2 0.7 fusion.41
  37.9 0.7 fusion.34
  38.6 0.0 copy-done.9
  38.6 2.7 %multiply_sine_fusion = (f32[16,64,128]{2,1,0:T(8,128)S(1)}, f32[16,64,128]{2,1,0:T(8,128)}) fusion(f32[64,128]{1,0:T(8,128)S(1)} %fusion.57, f32[16]{0:T(128)S(1)} %broadcast_multiply_fusion), kind=kLoop, calls=%fused_computation.26 | loop fusion | flops 131072 | bytes 1081408 | tf_op jit(solution)/shard_map/sin | solution.py:86
  41.3 22.7 %all-to-all-done = bf16[2,512,256]{2,0,1:T(2,128)(2,1)S(1)} async-done(((bf16[2,512,256]{2,0,1:T(2,128)(2,1)}), bf16[2,512,256]{2,0,1:T(2,128)(2,1)S(1)}, u32[]{:S(2)}, u32[]{:S(2)}) %all-to-all-start) | async-done | bytes 524320 | tf_op jit(solution)/shard_map/all_to_all | solution.py:192
  64.1 0.3 copy.91
  64.4 0.2 all_to_all.16
  64.6 0.1 copy.57
  64.8 1.4 %convolution_bitcast_fusion.3 = f32[2,16,64,128]{3,2,1,0:T(8,128)S(1)} fusion(f32[1,2,64,64]{2,3,0,1:T(8,128)} %get-tuple-element.39, f32[1,2,64,64]{2,3,0,1:T(8,128)} %get-tuple-element.46, bf16[2,16,64,128]{3,2,1,0:T(8,128)(2,1)S(1)} %bitcast.176), kind=kOutput, calls=%fused_computation.8 | convolution fusion | flops 201342976 | bytes 1638400 | tf_op jit(solution)/shard_map/pcab,pqak->qckb/dot_general | solution.py:96
  66.2 0.1 multiply_subtract_fusion.1
  66.3 0.6 convolution_bitcast_fusion.2
  66.9 0.4 copy-done.1
  67.4 0.3 subtract_bitcast_fusion.2
  67.7 0.6 convolution_bitcast_fusion.1
  68.2 0.2 copy-done.4
  68.4 0.1 multiply_subtract_fusion
  68.5 0.7 copy-done.6
  69.2 0.0 copy-done.7
  69.3 0.6 fusion.20
  69.9 0.2 convert_element_type.152
  70.1 3.3 %collective-permute-start = (bf16[2,16,8192]{2,1,0:T(8,128)(2,1)S(1)}, bf16[2,16,8192]{2,1,0:T(8,128)(2,1)S(1)}, u32[]{:S(2)}, u32[]{:S(2)}) collective-permute-start(bf16[2,16,8192]{2,1,0:T(8,128)(2,1)S(1)} %convert_element_type.152), channel_id=1, source_target_pairs={{0,64},{32,288},{64,320},{96,32},{128,384},{160,224},{192,128},{22... | collective-permute-start | bytes 1572872 | tf_op jit(solution)/shard_map/ppermute | solution.py:200
  73.4 0.1 convert_element_type.153
  73.5 7.7 %collective-permute-done = bf16[2,16,8192]{2,1,0:T(8,128)(2,1)S(1)} collective-permute-done((bf16[2,16,8192]{2,1,0:T(8,128)(2,1)S(1)}, bf16[2,16,8192]{2,1,0:T(8,128)(2,1)S(1)}, u32[]{:S(2)}, u32[]{:S(2)}) %collective-permute-start) | collective-permute-done | bytes 524320 | tf_op jit(solution)/shard_map/ppermute | solution.py:200
  81.2 0.1 convert_element_type.154
  81.3 0.1 add_bitcast_fusion.1
  81.4 0.1 copy.58
  81.5 0.1 copy.59
  81.6 0.1 maximum_reduce_fusion
  81.7 0.4 convolution_multiply_fusion.1
  82.1 0.1 copy.39
  82.3 0.2 mul.430
  82.4 4.9 %collective-permute-start.2 = (bf16[2,16,8192]{2,1,0:T(8,128)(2,1)S(1)}, bf16[2,16,8192]{2,1,0:T(8,128)(2,1)S(1)}, u32[]{:S(2)}, u32[]{:S(2)}) collective-permute-start(bf16[2,16,8192]{2,1,0:T(8,128)(2,1)S(1)} %convert_element_type.152), channel_id=1, source_target_pairs={{0,32},{32,160},{64,192},{96,64},{128,0},{160,128},{192,224},{224,... | collective-permute-start | bytes 1572872 | tf_op jit(solution)/shard_map/ppermute | solution.py:206
  87.4 1.9 %collective-permute-start.1 = (f32[2,4,512]{2,1,0:T(4,128)S(1)}, f32[2,4,512]{2,1,0:T(4,128)S(1)}, u32[]{:S(2)}, u32[]{:S(2)}) collective-permute-start(f32[2,4,512]{2,1,0:T(4,128)S(1)} %mul.430), channel_id=1, source_target_pairs={{64,0},{288,32},{320,64},{32,96},{384,128},{224,160},{128,192},{48... | collective-permute-start | bytes 49160 | tf_op jit(solution)/shard_map/ppermute | solution.py:202
  89.3 4.7 %collective-permute-done.2 = bf16[2,16,8192]{2,1,0:T(8,128)(2,1)S(1)} collective-permute-done((bf16[2,16,8192]{2,1,0:T(8,128)(2,1)S(1)}, bf16[2,16,8192]{2,1,0:T(8,128)(2,1)S(1)}, u32[]{:S(2)}, u32[]{:S(2)}) %collective-permute-start.2) | collective-permute-done | bytes 524320 | tf_op jit(solution)/shard_map/ppermute | solution.py:206
  94.0 0.1 convert_element_type.155
  94.1 0.1 add_bitcast_fusion
  94.2 0.1 copy.60
  94.4 0.1 copy.61
  94.5 0.1 maximum_reduce_fusion.1
  94.5 0.4 convolution_multiply_fusion
  94.9 0.1 copy.40
  95.1 0.2 mul.436
  95.3 1.9 %collective-permute-start.3 = (f32[2,4,512]{2,1,0:T(4,128)S(1)}, f32[2,4,512]{2,1,0:T(4,128)S(1)}, u32[]{:S(2)}, u32[]{:S(2)}) collective-permute-start(f32[2,4,512]{2,1,0:T(4,128)S(1)} %mul.436), channel_id=1, source_target_pairs={{32,0},{160,32},{192,64},{64,96},{0,128},{128,160},{224,192},{96,2... | collective-permute-start | bytes 49160 | tf_op jit(solution)/shard_map/ppermute | solution.py:208
  97.2 0.0 collective-permute-done.1
  97.2 5.7 %collective-permute-done.3 = f32[2,4,512]{2,1,0:T(4,128)S(1)} collective-permute-done((f32[2,4,512]{2,1,0:T(4,128)S(1)}, f32[2,4,512]{2,1,0:T(4,128)S(1)}, u32[]{:S(2)}, u32[]{:S(2)}) %collective-permute-start.3) | collective-permute-done | bytes 16416 | tf_op jit(solution)/shard_map/ppermute | solution.py:208
  102.9 0.6 maximum_bitcast_fusion.7
  103.5 0.6 maximum_bitcast_fusion.6
  (23 shorter events, 0.1 us)
Async XLA Ops:
  0.6 6.6 %copy-start = (bf16[1,2,256,1535]{2,1,3,0:T(2,128)(2,1)S(1)}, bf16[1,2,256,1535]{2,1,3,0:T(2,128)(2,1)}, u32[]{:S(2)}) copy-start(bf16[1,2,256,1535]{2,1,3,0:T(2,128)(2,1)} %param.5) | copy-start | bytes 4715524
  11.9 18.5 %copy-start.8 = (s32[1,2]{1,0:T(1,128)S(1)}, s32[1,2]{1,0:T(1,128)}, u32[]{:S(2)}) copy-start(s32[1,2]{1,0:T(1,128)} %param.9) | copy-start | bytes 28
  11.9 26.7 %copy-start.9 = (f32[16]{0:T(128)S(1)}, f32[16]{0:T(128)}, u32[]{:S(2)}) copy-start(f32[16]{0:T(128)} %param.8) | copy-start | bytes 196
  13.2 50.8 %all-to-all-start = ((bf16[2,512,256]{2,0,1:T(2,128)(2,1)}), bf16[2,512,256]{2,0,1:T(2,128)(2,1)S(1)}, u32[]{:S(2)}, u32[]{:S(2)}) async-start(bf16[2,512,256]{2,0,1:T(2,128)(2,1)} %copy.29), calls=%async_computation | async-start | bytes 1048576 | tf_op jit(solution)/shard_map/all_to_all | solution.py:192
  64.6 1.6 %copy-start.3 = (f32[64,128]{1,0:T(8,128)S(1)}, f32[64,128]{1,0:T(8,128)}, u32[]{:S(2)}) copy-start(f32[64,128]{1,0:T(8,128)} %get-tuple-element.64) | copy-start | bytes 98308
  64.6 1.6 %copy-start.5 = (f32[64,128]{1,0:T(8,128)S(1)}, f32[64,128]{1,0:T(8,128)}, u32[]{:S(2)}) copy-start(f32[64,128]{1,0:T(8,128)} %get-tuple-element.65) | copy-start | bytes 98308
  64.8 1.6 %copy-start.2 = (f32[1,2,128,128]{3,2,0,1:T(8,128)S(1)}, f32[1,2,128,128]{3,2,0,1:T(8,128)}, u32[]{:S(2)}) copy-start(f32[1,2,128,128]{3,2,0,1:T(8,128)} %get-tuple-element.42) | copy-start | bytes 393220
  66.3 1.0 %copy-start.1 = (f32[16,64,128]{2,1,0:T(8,128)S(1)}, f32[16,64,128]{2,1,0:T(8,128)}, u32[]{:S(2)}) copy-start(f32[16,64,128]{2,1,0:T(8,128)} %get-tuple-element.14) | copy-start | bytes 1572868
  67.6 0.8 copy-start.4
  68.4 0.8 copy-start.6
  68.4 0.9 copy-start.7
  70.1 11.1 %collective-permute-start = (bf16[2,16,8192]{2,1,0:T(8,128)(2,1)S(1)}, bf16[2,16,8192]{2,1,0:T(8,128)(2,1)S(1)}, u32[]{:S(2)}, u32[]{:S(2)}) collective-permute-start(bf16[2,16,8192]{2,1,0:T(8,128)(2,1)S(1)} %convert_element_type.152), channel_id=1, source_target_pairs={{0,64},{32,288},{64,320},{96,32},{128,384},{160,224},{192,128},{22... | collective-permute-start | bytes 1572872 | tf_op jit(solution)/shard_map/ppermute | solution.py:200
  82.4 11.6 %collective-permute-start.2 = (bf16[2,16,8192]{2,1,0:T(8,128)(2,1)S(1)}, bf16[2,16,8192]{2,1,0:T(8,128)(2,1)S(1)}, u32[]{:S(2)}, u32[]{:S(2)}) collective-permute-start(bf16[2,16,8192]{2,1,0:T(8,128)(2,1)S(1)} %convert_element_type.152), channel_id=1, source_target_pairs={{0,32},{32,160},{64,192},{96,64},{128,0},{160,128},{192,224},{224,... | collective-permute-start | bytes 1572872 | tf_op jit(solution)/shard_map/ppermute | solution.py:206
  87.4 9.8 %collective-permute-start.1 = (f32[2,4,512]{2,1,0:T(4,128)S(1)}, f32[2,4,512]{2,1,0:T(4,128)S(1)}, u32[]{:S(2)}, u32[]{:S(2)}) collective-permute-start(f32[2,4,512]{2,1,0:T(4,128)S(1)} %mul.430), channel_id=1, source_target_pairs={{64,0},{288,32},{320,64},{32,96},{384,128},{224,160},{128,192},{48... | collective-permute-start | bytes 49160 | tf_op jit(solution)/shard_map/ppermute | solution.py:202
  95.3 7.6 %collective-permute-start.3 = (f32[2,4,512]{2,1,0:T(4,128)S(1)}, f32[2,4,512]{2,1,0:T(4,128)S(1)}, u32[]{:S(2)}, u32[]{:S(2)}) collective-permute-start(f32[2,4,512]{2,1,0:T(4,128)S(1)} %mul.436), channel_id=1, source_target_pairs={{32,0},{160,32},{192,64},{64,96},{0,128},{128,160},{224,192},{96,2... | collective-permute-start | bytes 49160 | tf_op jit(solution)/shard_map/ppermute | solution.py:208

commit v15 on v13

--- a/solution.py
+++ b/solution.py
@@ -30,11 +30,14 @@
 
 def band_kernel(re_ref, im_ref, band_ref):
     rows = BAND_ROWS
-    strip = re_ref.shape[1]
+    strip = -(-(TAPS + BAND_ROWS - 1) // 128) * 128
     width = band_ref.shape[3]
     dtype = band_ref.dtype
-    re_strip = pltpu.roll(jnp.broadcast_to(re_ref[...], (rows, strip)), 0, 1, stride=1, stride_axis=0)
-    im_strip = pltpu.roll(jnp.broadcast_to(im_ref[...], (rows, strip)), 0, 1, stride=1, stride_axis=0)
+    pad = jnp.zeros((1, strip - re_ref.shape[1]), jnp.float32)
+    re_row = jnp.concatenate([re_ref[...].astype(jnp.float32), pad], axis=1)
+    im_row = jnp.concatenate([im_ref[...].astype(jnp.float32), pad], axis=1)
+    re_strip = pltpu.roll(jnp.broadcast_to(re_row, (rows, strip)), 0, 1, stride=1, stride_axis=0)
+    im_strip = pltpu.roll(jnp.broadcast_to(im_row, (rows, strip)), 0, 1, stride=1, stride_axis=0)
     pieces = (
         (0, 0, re_strip.astype(dtype)),
         (0, 1, (-im_strip).astype(dtype)),
@@ -52,11 +55,8 @@
 
 
 def band_tables(table_re, table_im, width):
-    rows = BAND_ROWS
-    strip = -(-(TAPS + rows - 1) // 128) * 128
-    pad = jnp.zeros((strip - table_re.shape[0],), jnp.float32)
-    re_row = jnp.concatenate([table_re.astype(jnp.float32), pad])[None]
-    im_row = jnp.concatenate([table_im.astype(jnp.float32), pad])[None]
+    re_row = table_re.astype(jnp.float32)[None]
+    im_row = table_im.astype(jnp.float32)[None]
     shape = jax.ShapeDtypeStruct((2, 2, RNG, width), jnp.bfloat16)
     band = pl.pallas_call(band_kernel, out_shape=shape)(re_row, im_row)
     return band.reshape(2, 2 * RNG, width)

time: 103 us -> 102 us (level)
  local copies, waits for them, and re-layouts: 5.44 us -> 4.25 us
    broadcast_in_dim x1, other arithmetic: 0.01 us -> 1.45 us  [band_tables(): im_row = table_im.astype(jnp.float32)[None]]
    broadcast_in_dim x2 -> x0, local copies, waits for them, and re-layouts: 1.19 us -> none  [the longest x1 0.6 us: band_tables(): re_row = jnp.concatenate([table_re.astype(jnp.float32), pad])[None]]
where the time goes in v15:
time: 102 us; the launch traced here: 101 us
  waiting for transfers between devices  37.4 us (37%)
  starting transfers between devices  31.6 us (31%)
  other arithmetic  10.3 us (10%)
  matrix products  8.48 us (8%)
  between operations  5.59 us (5%)
  local copies, waits for them, and re-layouts  4.25 us (4%)
  Pallas kernels  3.85 us (4%)
    all_to_all x1, waiting for transfers between devices, per_device(): lax.all_to_all(compressed, 'pulse', split_axis=1, concat_axis=2, tiled=True)  22.7 us
    all_to_all x1, starting transfers between devices, per_device(): lax.all_to_all(compressed, 'pulse', split_axis=1, concat_axis=2, tiled=True)  18 us
    ppermute x2, waiting for transfers between devices, per_device(): arrived = [lax.ppermute(focused, 'acq', pairs) for pairs in edge_pairs]  9.46 us
    ppermute x2, starting transfers between devices, per_device(): lax.ppermute(looked[slot], 'acq', [(dst, src) for src, dst in edge_pairs[...  9.11 us
    ppermute x2, waiting for transfers between devices, per_device(): lax.ppermute(looked[slot], 'acq', [(dst, src) for src, dst in edge_pairs[...  5.19 us
    dot_general x1, matrix products, compress(): lax.dot_general(band, echoes, dims, preferred_element_type=jnp.float32)  4.57 us
    ppermute x2, starting transfers between devices, per_device(): arrived = [lax.ppermute(focused, 'acq', pairs) for pairs in edge_pairs]  4.51 us
    pallas_call x1, Pallas kernels, band_tables(): band = pl.pallas_call(band_kernel, out_shape=shape)(re_row, im_row)  3.85 us
  transfers between devices with their start and end apart: 5, of which 4 were waited for; matrix products, arithmetic and copies ran while one was open for 7% of the time, Pallas kernels for 0%

profile of v15, /device:TPU:36, one launch (start us, length us, event | category | flops | bytes accessed | tf_op | source)
XLA Modules:
  0.0 101.5 jit_solution(6167839806516931525)
XLA Ops:
  0.6 0.0 copy-start
  0.6 1.4 %fusion.76 = (f32[1024]{0:T(1024)}, f32[1024]{0:T(1024)}) fusion(f32[1024]{0:T(1024)} %param.6), kind=kLoop, calls=%fused_computation.120 | loop fusion | flops 6144 | bytes 12288 | tf_op jit(solution)/shard_map/broadcast_in_dim | solution.py:59
  2.7 3.8 %shard_map.68 = bf16[2,2,512,1535]{3,2,1,0:T(8,128)(2,1)} custom-call(f32[1,1024]{1,0:T(1,128)} %bitcast.182, f32[1,1024]{1,0:T(1,128)} %bitcast.181), custom_call_target="tpu_custom_call" | custom-call | tf_op jit(solution)/shard_map/pallas_call | solution.py:61
  6.6 4.6 %fusion.14 = bf16[2,512,256]{2,1,0:T(8,128)(2,1)S(1)} fusion(bf16[2,256,1535,1]{1,0,2,3:T(2,128)(2,1)S(1)} %bitcast.172, bf16[2,2,512,1535]{3,2,1,0:T(8,128)(2,1)} %shard_map.68, f32[256]{0:T(256)S(1)} %compare_convert_fusion), kind=kOutput, calls=%fused_computation.11 | convolution fusion | flops 1610088448 | bytes 8384512 | tf_op jit(solution)/shard_map/dot_general | solution.py:68
  11.2 0.0 copy-start.8
  11.2 0.0 copy-start.9
  11.2 1.4 %copy.29 = bf16[2,512,256]{2,0,1:T(2,128)(2,1)} copy(bf16[2,512,256]{2,1,0:T(8,128)(2,1)S(1)} %fusion.14) | data formatting | bytes 1048576 | tf_op jit(solution)/shard_map/convert_element_type | solution.py:72
  12.6 18.0 %all-to-all-start = ((bf16[2,512,256]{2,0,1:T(2,128)(2,1)}), bf16[2,512,256]{2,0,1:T(2,128)(2,1)S(1)}, u32[]{:S(2)}, u32[]{:S(2)}) async-start(bf16[2,512,256]{2,0,1:T(2,128)(2,1)} %copy.29), calls=%async_computation | async-start | bytes 1048576 | tf_op jit(solution)/shard_map/all_to_all | solution.py:192
  30.6 0.6 fusion.85
  35.1 0.1 fusion.71
  35.2 0.7 fusion.67
  36.0 0.1 fusion.69
  36.1 0.8 fusion.68
  36.9 0.3 fusion.66
  37.1 0.3 fusion.60
  37.4 0.7 fusion.41
  38.1 0.7 fusion.34
  38.8 2.7 %multiply_sine_fusion = (f32[16,64,128]{2,1,0:T(8,128)S(1)}, f32[16,64,128]{2,1,0:T(8,128)}) fusion(f32[64,128]{1,0:T(8,128)S(1)} %fusion.57, f32[16]{0:T(128)S(1)} %broadcast_multiply_fusion), kind=kLoop, calls=%fused_computation.24 | loop fusion | flops 131072 | bytes 1081408 | tf_op jit(solution)/shard_map/sin | solution.py:86
  41.6 22.7 %all-to-all-done = bf16[2,512,256]{2,0,1:T(2,128)(2,1)S(1)} async-done(((bf16[2,512,256]{2,0,1:T(2,128)(2,1)}), bf16[2,512,256]{2,0,1:T(2,128)(2,1)S(1)}, u32[]{:S(2)}, u32[]{:S(2)}) %all-to-all-start) | async-done | bytes 524320 | tf_op jit(solution)/shard_map/all_to_all | solution.py:192
  64.3 0.3 copy.91
  64.6 0.2 all_to_all.16
  64.8 0.0 copy-start.3
  64.8 0.0 copy-start.5
  64.9 0.1 copy.57
  65.0 0.0 copy-start.2
  65.0 1.4 %convolution_bitcast_fusion.3 = f32[2,16,64,128]{3,2,1,0:T(8,128)S(1)} fusion(f32[1,2,64,64]{2,3,0,1:T(8,128)} %get-tuple-element.41, f32[1,2,64,64]{2,3,0,1:T(8,128)} %get-tuple-element.48, bf16[2,16,64,128]{3,2,1,0:T(8,128)(2,1)S(1)} %bitcast.178), kind=kOutput, calls=%fused_computation.9 | convolution fusion | flops 201342976 | bytes 1638400 | tf_op jit(solution)/shard_map/pcab,pqak->qckb/dot_general | solution.py:96
  66.4 0.0 copy-done.3
  66.4 0.0 copy-done.5
  66.4 0.0 copy-start.1
  66.4 0.1 multiply_subtract_fusion.1
  66.6 0.0 copy-done.2
  66.6 0.6 convolution_bitcast_fusion.2
  67.2 0.3 copy-done.1
  67.5 0.3 subtract_bitcast_fusion.2
  67.7 0.6 convolution_bitcast_fusion.1
  68.4 0.1 multiply_subtract_fusion
  68.5 0.1 copy-done.6
  68.6 0.0 copy-done.7
  68.6 0.6 fusion.20
  69.2 0.2 convert_element_type.150
  69.5 2.4 %collective-permute-start = (bf16[2,16,8192]{2,1,0:T(8,128)(2,1)S(1)}, bf16[2,16,8192]{2,1,0:T(8,128)(2,1)S(1)}, u32[]{:S(2)}, u32[]{:S(2)}) collective-permute-start(bf16[2,16,8192]{2,1,0:T(8,128)(2,1)S(1)} %convert_element_type.150), channel_id=1, source_target_pairs={{0,32},{32,160},{64,192},{96,64},{128,0},{160,128},{192,224},{224,... | collective-permute-start | bytes 1572872 | tf_op jit(solution)/shard_map/ppermute | solution.py:196
  71.9 2.1 %collective-permute-start.1 = (bf16[2,16,8192]{2,1,0:T(8,128)(2,1)S(1)}, bf16[2,16,8192]{2,1,0:T(8,128)(2,1)S(1)}, u32[]{:S(2)}, u32[]{:S(2)}) collective-permute-start(bf16[2,16,8192]{2,1,0:T(8,128)(2,1)S(1)} %convert_element_type.150), channel_id=1, source_target_pairs={{0,64},{32,288},{64,320},{96,32},{128,384},{160,224},{192,128},{22... | collective-permute-start | bytes 1572872 | tf_op jit(solution)/shard_map/ppermute | solution.py:196
  74.0 0.1 convert_element_type.151
  74.1 8.8 %collective-permute-done = bf16[2,16,8192]{2,1,0:T(8,128)(2,1)S(1)} collective-permute-done((bf16[2,16,8192]{2,1,0:T(8,128)(2,1)S(1)}, bf16[2,16,8192]{2,1,0:T(8,128)(2,1)S(1)}, u32[]{:S(2)}, u32[]{:S(2)}) %collective-permute-start) | collective-permute-done | bytes 524320 | tf_op jit(solution)/shard_map/ppermute | solution.py:196
  82.9 0.1 convert_element_type.152
  83.0 0.6 collective-permute-done.1
  83.6 0.1 convert_element_type.153
  83.7 0.2 add_bitcast_fusion.1
  83.9 0.1 copy.58
  84.0 0.1 copy.59
  84.2 0.1 copy.60
  84.3 0.1 copy.61
  84.4 0.2 maximum_reduce_fusion
  84.6 0.7 convolution_multiply_fusion
  85.3 0.1 copy.39
  85.4 0.2 slice.115
  85.6 7.2 %collective-permute-start.2 = (f32[2,4,512]{2,1,0:T(4,128)S(1)}, f32[2,4,512]{2,1,0:T(4,128)S(1)}, u32[]{:S(2)}, u32[]{:S(2)}) collective-permute-start(f32[2,4,512]{2,1,0:T(4,128)S(1)} %slice.115), channel_id=1, source_target_pairs={{64,0},{288,32},{320,64},{32,96},{384,128},{224,160},{128,192},{48... | collective-permute-start | bytes 49160 | tf_op jit(solution)/shard_map/ppermute | solution.py:199
  92.8 0.1 copy.40
  92.9 0.2 slice.119
  93.1 1.9 %collective-permute-start.3 = (f32[2,4,512]{2,1,0:T(4,128)S(1)}, f32[2,4,512]{2,1,0:T(4,128)S(1)}, u32[]{:S(2)}, u32[]{:S(2)}) collective-permute-start(f32[2,4,512]{2,1,0:T(4,128)S(1)} %slice.119), channel_id=1, source_target_pairs={{32,0},{160,32},{192,64},{64,96},{0,128},{128,160},{224,192},{96,2... | collective-permute-start | bytes 49160 | tf_op jit(solution)/shard_map/ppermute | solution.py:199
  95.0 0.0 collective-permute-done.2
  95.0 5.2 %collective-permute-done.3 = f32[2,4,512]{2,1,0:T(4,128)S(1)} collective-permute-done((f32[2,4,512]{2,1,0:T(4,128)S(1)}, f32[2,4,512]{2,1,0:T(4,128)S(1)}, u32[]{:S(2)}, u32[]{:S(2)}) %collective-permute-start.3) | collective-permute-done | bytes 16416 | tf_op jit(solution)/shard_map/ppermute | solution.py:199
  100.3 0.6 maximum_bitcast_fusion.7
  100.9 0.6 maximum_bitcast_fusion.6
  (18 shorter events, 0.1 us)
Async XLA Ops:
  0.6 6.0 %copy-start = (bf16[1,2,256,1535]{2,1,3,0:T(2,128)(2,1)S(1)}, bf16[1,2,256,1535]{2,1,3,0:T(2,128)(2,1)}, u32[]{:S(2)}) copy-start(bf16[1,2,256,1535]{2,1,3,0:T(2,128)(2,1)} %param.5) | copy-start | bytes 4715524
  11.2 19.4 %copy-start.8 = (s32[1,2]{1,0:T(1,128)S(1)}, s32[1,2]{1,0:T(1,128)}, u32[]{:S(2)}) copy-start(s32[1,2]{1,0:T(1,128)} %param.9) | copy-start | bytes 28
  11.2 27.6 %copy-start.9 = (f32[16]{0:T(128)S(1)}, f32[16]{0:T(128)}, u32[]{:S(2)}) copy-start(f32[16]{0:T(128)} %param.8) | copy-start | bytes 196
  12.6 51.7 %all-to-all-start = ((bf16[2,512,256]{2,0,1:T(2,128)(2,1)}), bf16[2,512,256]{2,0,1:T(2,128)(2,1)S(1)}, u32[]{:S(2)}, u32[]{:S(2)}) async-start(bf16[2,512,256]{2,0,1:T(2,128)(2,1)} %copy.29), calls=%async_computation | async-start | bytes 1048576 | tf_op jit(solution)/shard_map/all_to_all | solution.py:192
  64.8 1.6 %copy-start.3 = (f32[64,128]{1,0:T(8,128)S(1)}, f32[64,128]{1,0:T(8,128)}, u32[]{:S(2)}) copy-start(f32[64,128]{1,0:T(8,128)} %get-tuple-element.64) | copy-start | bytes 98308
  64.8 1.6 %copy-start.5 = (f32[64,128]{1,0:T(8,128)S(1)}, f32[64,128]{1,0:T(8,128)}, u32[]{:S(2)}) copy-start(f32[64,128]{1,0:T(8,128)} %get-tuple-element.65) | copy-start | bytes 98308
  65.0 1.6 %copy-start.2 = (f32[1,2,128,128]{3,2,0,1:T(8,128)S(1)}, f32[1,2,128,128]{3,2,0,1:T(8,128)}, u32[]{:S(2)}) copy-start(f32[1,2,128,128]{3,2,0,1:T(8,128)} %get-tuple-element.44) | copy-start | bytes 393220
  66.4 1.0 %copy-start.1 = (f32[16,64,128]{2,1,0:T(8,128)S(1)}, f32[16,64,128]{2,1,0:T(8,128)}, u32[]{:S(2)}) copy-start(f32[16,64,128]{2,1,0:T(8,128)} %get-tuple-element.13) | copy-start | bytes 1572868
  67.5 0.9 copy-start.4
  67.7 0.8 copy-start.6
  67.7 0.9 copy-start.7
  69.5 13.4 %collective-permute-start = (bf16[2,16,8192]{2,1,0:T(8,128)(2,1)S(1)}, bf16[2,16,8192]{2,1,0:T(8,128)(2,1)S(1)}, u32[]{:S(2)}, u32[]{:S(2)}) collective-permute-start(bf16[2,16,8192]{2,1,0:T(8,128)(2,1)S(1)} %convert_element_type.150), channel_id=1, source_target_pairs={{0,32},{32,160},{64,192},{96,64},{128,0},{160,128},{192,224},{224,... | collective-permute-start | bytes 1572872 | tf_op jit(solution)/shard_map/ppermute | solution.py:196
  71.9 11.7 %collective-permute-start.1 = (bf16[2,16,8192]{2,1,0:T(8,128)(2,1)S(1)}, bf16[2,16,8192]{2,1,0:T(8,128)(2,1)S(1)}, u32[]{:S(2)}, u32[]{:S(2)}) collective-permute-start(bf16[2,16,8192]{2,1,0:T(8,128)(2,1)S(1)} %convert_element_type.150), channel_id=1, source_target_pairs={{0,64},{32,288},{64,320},{96,32},{128,384},{160,224},{192,128},{22... | collective-permute-start | bytes 1572872 | tf_op jit(solution)/shard_map/ppermute | solution.py:196
  85.6 9.4 %collective-permute-start.2 = (f32[2,4,512]{2,1,0:T(4,128)S(1)}, f32[2,4,512]{2,1,0:T(4,128)S(1)}, u32[]{:S(2)}, u32[]{:S(2)}) collective-permute-start(f32[2,4,512]{2,1,0:T(4,128)S(1)} %slice.115), channel_id=1, source_target_pairs={{64,0},{288,32},{320,64},{32,96},{384,128},{224,160},{128,192},{48... | collective-permute-start | bytes 49160 | tf_op jit(solution)/shard_map/ppermute | solution.py:199
  93.1 7.1 %collective-permute-start.3 = (f32[2,4,512]{2,1,0:T(4,128)S(1)}, f32[2,4,512]{2,1,0:T(4,128)S(1)}, u32[]{:S(2)}, u32[]{:S(2)}) collective-permute-start(f32[2,4,512]{2,1,0:T(4,128)S(1)} %slice.119), channel_id=1, source_target_pairs={{32,0},{160,32},{192,64},{64,96},{0,128},{128,160},{224,192},{96,2... | collective-permute-start | bytes 49160 | tf_op jit(solution)/shard_map/ppermute | solution.py:199

commit v16 on v15

--- a/solution.py
+++ b/solution.py
@@ -28,14 +28,18 @@
     return (left_re * right_re - left_im * right_im, left_re * right_im + left_im * right_re)
 
 
-def band_kernel(re_ref, im_ref, band_ref):
+def band_kernel(phase_ref, band_ref):
     rows = BAND_ROWS
     strip = -(-(TAPS + BAND_ROWS - 1) // 128) * 128
     width = band_ref.shape[3]
     dtype = band_ref.dtype
-    pad = jnp.zeros((1, strip - re_ref.shape[1]), jnp.float32)
-    re_row = jnp.concatenate([re_ref[...].astype(jnp.float32), pad], axis=1)
-    im_row = jnp.concatenate([im_ref[...].astype(jnp.float32), pad], axis=1)
+    amplitude = 2.0 / math.sqrt(TAPS)
+    phase = phase_ref[...]
+    table_re = (amplitude * jnp.cos(phase)).astype(dtype).astype(jnp.float32)
+    table_im = (amplitude * jnp.sin(phase)).astype(dtype).astype(jnp.float32)
+    pad = jnp.zeros((1, strip - phase_ref.shape[1]), jnp.float32)
+    re_row = jnp.concatenate([table_re, pad], axis=1)
+    im_row = jnp.concatenate([table_im, pad], axis=1)
     re_strip = pltpu.roll(jnp.broadcast_to(re_row, (rows, strip)), 0, 1, stride=1, stride_axis=0)
     im_strip = pltpu.roll(jnp.broadcast_to(im_row, (rows, strip)), 0, 1, stride=1, stride_axis=0)
     pieces = (
@@ -54,11 +58,9 @@
                 band_ref[part, half, start : start + rows, stop:] = jnp.zeros((rows, width - stop), dtype)
 
 
-def band_tables(table_re, table_im, width):
-    re_row = table_re.astype(jnp.float32)[None]
-    im_row = table_im.astype(jnp.float32)[None]
+def band_tables(chirp_phase, width):
     shape = jax.ShapeDtypeStruct((2, 2, RNG, width), jnp.bfloat16)
-    band = pl.pallas_call(band_kernel, out_shape=shape)(re_row, im_row)
+    band = pl.pallas_call(band_kernel, out_shape=shape)(chirp_phase[None])
     return band.reshape(2, 2 * RNG, width)
 
 
@@ -161,10 +163,7 @@
 def per_device(raw_echo, chirp_phase, pulse_counts, azimuth_rate, partner_bits):
     echoes = raw_echo[0]
     pulses_dev = echoes.shape[1]
-    amplitude = 2.0 / math.sqrt(TAPS)
-    table_re = (amplitude * jnp.cos(chirp_phase)).astype(jnp.bfloat16)
-    table_im = (amplitude * jnp.sin(chirp_phase)).astype(jnp.bfloat16)
-    band = band_tables(table_re, table_im, echoes.shape[2])
+    band = band_tables(chirp_phase, echoes.shape[2])
     live_pulses = pulse_counts[0]
     first_pulse = lax.axis_index("pulse") * pulses_dev
     compressed = compress(echoes, band, first_pulse, live_pulses)

time: 102 us -> 101 us (level)
  other arithmetic: 10.3 us -> 8.93 us
    broadcast_in_dim x1 -> x0, other arithmetic: 1.45 us -> none  [band_tables(): im_row = table_im.astype(jnp.float32)[None]]
  transfers between devices with their start and end apart: 5 -> 5, of which waited for: 4 -> 4; matrix products, arithmetic and copies ran while one was open for 7% -> 8% of each run, Pallas kernels for 0% -> 0%
where the time goes in v16:
time: 101 us; the launch traced here: 100 us
  waiting for transfers between devices  37.3 us (37%)
  starting transfers between devices  31.6 us (31%)
  other arithmetic  8.93 us (9%)
  matrix products  8.48 us (8%)
  between operations  5.71 us (6%)
  local copies, waits for them, and re-layouts  4.26 us (4%)
  Pallas kernels  3.9 us (4%)
    all_to_all x1, waiting for transfers between devices, per_device(): lax.all_to_all(compressed, 'pulse', split_axis=1, concat_axis=2, tiled=True)  22.7 us
    all_to_all x1, starting transfers between devices, per_device(): lax.all_to_all(compressed, 'pulse', split_axis=1, concat_axis=2, tiled=True)  18 us
    ppermute x2, waiting for transfers between devices, per_device(): arrived = [lax.ppermute(focused, 'acq', pairs) for pairs in edge_pairs]  9.46 us
    ppermute x2, starting transfers between devices, per_device(): lax.ppermute(looked[slot], 'acq', [(dst, src) for src, dst in edge_pairs[...  9.11 us
    ppermute x2, waiting for transfers between devices, per_device(): lax.ppermute(looked[slot], 'acq', [(dst, src) for src, dst in edge_pairs[...  5.19 us
    dot_general x1, matrix products, compress(): lax.dot_general(band, echoes, dims, preferred_element_type=jnp.float32)  4.57 us
    ppermute x2, starting transfers between devices, per_device(): arrived = [lax.ppermute(focused, 'acq', pairs) for pairs in edge_pairs]  4.51 us
    pallas_call x1, Pallas kernels, band_tables(): band = pl.pallas_call(band_kernel, out_shape=shape)(chirp_phase[None])  3.9 us
  transfers between devices with their start and end apart: 5, of which 4 were waited for; matrix products, arithmetic and copies ran while one was open for 8% of the time, Pallas kernels for 0%

profile of v16, /device:TPU:36, one launch (start us, length us, event | category | flops | bytes accessed | tf_op | source)
XLA Modules:
  0.0 100.2 jit_solution(2021005460379978463)
XLA Ops:
  0.6 0.0 copy-start
  1.4 3.9 %shard_map.68 = bf16[2,2,512,1535]{3,2,1,0:T(8,128)(2,1)} custom-call(f32[1,1024]{1,0:T(1,128)} %bitcast.180), custom_call_target="tpu_custom_call" | custom-call | tf_op jit(solution)/shard_map/pallas_call | solution.py:63
  5.3 0.0 copy-done
  5.3 4.6 %fusion.14 = bf16[2,512,256]{2,1,0:T(8,128)(2,1)S(1)} fusion(bf16[2,256,1535,1]{1,0,2,3:T(2,128)(2,1)S(1)} %bitcast.171, bf16[2,2,512,1535]{3,2,1,0:T(8,128)(2,1)} %shard_map.68, f32[256]{0:T(256)S(1)} %compare_convert_fusion), kind=kOutput, calls=%fused_computation.11 | convolution fusion | flops 1610088448 | bytes 8384512 | tf_op jit(solution)/shard_map/dot_general | solution.py:70
  9.9 0.0 copy-start.8
  9.9 0.0 copy-start.9
  9.9 1.4 %copy.29 = bf16[2,512,256]{2,0,1:T(2,128)(2,1)} copy(bf16[2,512,256]{2,1,0:T(8,128)(2,1)S(1)} %fusion.14) | data formatting | bytes 1048576 | tf_op jit(solution)/shard_map/convert_element_type | solution.py:74
  11.3 18.0 %all-to-all-start = ((bf16[2,512,256]{2,0,1:T(2,128)(2,1)}), bf16[2,512,256]{2,0,1:T(2,128)(2,1)S(1)}, u32[]{:S(2)}, u32[]{:S(2)}) async-start(bf16[2,512,256]{2,0,1:T(2,128)(2,1)} %copy.29), calls=%async_computation | async-start | bytes 1048576 | tf_op jit(solution)/shard_map/all_to_all | solution.py:191
  29.3 0.0 copy-done.8
  29.3 0.6 fusion.83
  33.8 0.1 fusion.71
  33.9 0.8 fusion.67
  34.7 0.1 fusion.69
  34.8 0.8 fusion.68
  35.6 0.3 fusion.66
  35.9 0.3 fusion.60
  36.2 0.7 fusion.41
  36.9 0.7 fusion.34
  37.6 0.0 copy-done.9
  37.6 2.7 %multiply_sine_fusion = (f32[16,64,128]{2,1,0:T(8,128)S(1)}, f32[16,64,128]{2,1,0:T(8,128)}) fusion(f32[64,128]{1,0:T(8,128)S(1)} %fusion.57, f32[16]{0:T(128)S(1)} %broadcast_multiply_fusion), kind=kLoop, calls=%fused_computation.24 | loop fusion | flops 131072 | bytes 1081408 | tf_op jit(solution)/shard_map/sin | solution.py:88
  40.3 22.7 %all-to-all-done = bf16[2,512,256]{2,0,1:T(2,128)(2,1)S(1)} async-done(((bf16[2,512,256]{2,0,1:T(2,128)(2,1)}), bf16[2,512,256]{2,0,1:T(2,128)(2,1)S(1)}, u32[]{:S(2)}, u32[]{:S(2)}) %all-to-all-start) | async-done | bytes 524320 | tf_op jit(solution)/shard_map/all_to_all | solution.py:191
  63.0 0.3 copy.91
  63.3 0.2 all_to_all.16
  63.6 0.0 copy-start.3
  63.6 0.1 copy.57
  63.7 0.0 copy-start.2
  63.7 1.4 %convolution_bitcast_fusion.3 = f32[2,16,64,128]{3,2,1,0:T(8,128)S(1)} fusion(f32[1,2,64,64]{2,3,0,1:T(8,128)} %get-tuple-element.41, f32[1,2,64,64]{2,3,0,1:T(8,128)} %get-tuple-element.48, bf16[2,16,64,128]{3,2,1,0:T(8,128)(2,1)S(1)} %bitcast.177), kind=kOutput, calls=%fused_computation.9 | convolution fusion | flops 201342976 | bytes 1638400 | tf_op jit(solution)/shard_map/pcab,pqak->qckb/dot_general | solution.py:98
  65.1 0.0 copy-done.3
  65.1 0.0 copy-done.5
  65.1 0.0 copy-start.1
  65.2 0.1 multiply_subtract_fusion.1
  65.3 0.6 convolution_bitcast_fusion.2
  65.9 0.3 copy-done.1
  66.2 0.3 subtract_bitcast_fusion.2
  66.5 0.6 convolution_bitcast_fusion.1
  67.1 0.1 multiply_subtract_fusion
  67.2 0.1 copy-done.6
  67.3 0.0 copy-done.7
  67.3 0.6 fusion.20
  68.0 0.2 convert_element_type.140
  68.2 2.4 %collective-permute-start = (bf16[2,16,8192]{2,1,0:T(8,128)(2,1)S(1)}, bf16[2,16,8192]{2,1,0:T(8,128)(2,1)S(1)}, u32[]{:S(2)}, u32[]{:S(2)}) collective-permute-start(bf16[2,16,8192]{2,1,0:T(8,128)(2,1)S(1)} %convert_element_type.140), channel_id=1, source_target_pairs={{0,32},{32,160},{64,192},{96,64},{128,0},{160,128},{192,224},{224,... | collective-permute-start | bytes 1572872 | tf_op jit(solution)/shard_map/ppermute | solution.py:195
  70.6 2.1 %collective-permute-start.1 = (bf16[2,16,8192]{2,1,0:T(8,128)(2,1)S(1)}, bf16[2,16,8192]{2,1,0:T(8,128)(2,1)S(1)}, u32[]{:S(2)}, u32[]{:S(2)}) collective-permute-start(bf16[2,16,8192]{2,1,0:T(8,128)(2,1)S(1)} %convert_element_type.140), channel_id=1, source_target_pairs={{0,64},{32,288},{64,320},{96,32},{128,384},{160,224},{192,128},{22... | collective-permute-start | bytes 1572872 | tf_op jit(solution)/shard_map/ppermute | solution.py:195
  72.7 0.1 convert_element_type.141
  72.8 8.8 %collective-permute-done = bf16[2,16,8192]{2,1,0:T(8,128)(2,1)S(1)} collective-permute-done((bf16[2,16,8192]{2,1,0:T(8,128)(2,1)S(1)}, bf16[2,16,8192]{2,1,0:T(8,128)(2,1)S(1)}, u32[]{:S(2)}, u32[]{:S(2)}) %collective-permute-start) | collective-permute-done | bytes 524320 | tf_op jit(solution)/shard_map/ppermute | solution.py:195
  81.7 0.1 convert_element_type.142
  81.7 0.6 collective-permute-done.1
  82.4 0.1 convert_element_type.143
  82.4 0.2 add_bitcast_fusion.1
  82.7 0.1 copy.58
  82.8 0.1 copy.59
  82.9 0.1 copy.60
  83.0 0.1 copy.61
  83.1 0.2 maximum_reduce_fusion
  83.3 0.7 convolution_multiply_fusion
  84.0 0.1 copy.39
  84.2 0.2 slice.115
  84.3 7.2 %collective-permute-start.2 = (f32[2,4,512]{2,1,0:T(4,128)S(1)}, f32[2,4,512]{2,1,0:T(4,128)S(1)}, u32[]{:S(2)}, u32[]{:S(2)}) collective-permute-start(f32[2,4,512]{2,1,0:T(4,128)S(1)} %slice.115), channel_id=1, source_target_pairs={{64,0},{288,32},{320,64},{32,96},{384,128},{224,160},{128,192},{48... | collective-permute-start | bytes 49160 | tf_op jit(solution)/shard_map/ppermute | solution.py:198
  91.5 0.1 copy.40
  91.7 0.2 slice.119
  91.8 1.9 %collective-permute-start.3 = (f32[2,4,512]{2,1,0:T(4,128)S(1)}, f32[2,4,512]{2,1,0:T(4,128)S(1)}, u32[]{:S(2)}, u32[]{:S(2)}) collective-permute-start(f32[2,4,512]{2,1,0:T(4,128)S(1)} %slice.119), channel_id=1, source_target_pairs={{32,0},{160,32},{192,64},{64,96},{0,128},{128,160},{224,192},{96,2... | collective-permute-start | bytes 49160 | tf_op jit(solution)/shard_map/ppermute | solution.py:198
  93.8 0.0 collective-permute-done.2
  93.8 5.2 %collective-permute-done.3 = f32[2,4,512]{2,1,0:T(4,128)S(1)} collective-permute-done((f32[2,4,512]{2,1,0:T(4,128)S(1)}, f32[2,4,512]{2,1,0:T(4,128)S(1)}, u32[]{:S(2)}, u32[]{:S(2)}) %collective-permute-start.3) | collective-permute-done | bytes 16416 | tf_op jit(solution)/shard_map/ppermute | solution.py:198
  99.0 0.6 maximum_bitcast_fusion.7
  99.6 0.6 maximum_bitcast_fusion.6
  (17 shorter events, 0.1 us)
Async XLA Ops:
  0.6 4.7 %copy-start = (bf16[1,2,256,1535]{2,1,3,0:T(2,128)(2,1)S(1)}, bf16[1,2,256,1535]{2,1,3,0:T(2,128)(2,1)}, u32[]{:S(2)}) copy-start(bf16[1,2,256,1535]{2,1,3,0:T(2,128)(2,1)} %param.5) | copy-start | bytes 4715524
  9.9 19.4 %copy-start.8 = (s32[1,2]{1,0:T(1,128)S(1)}, s32[1,2]{1,0:T(1,128)}, u32[]{:S(2)}) copy-start(s32[1,2]{1,0:T(1,128)} %param.9) | copy-start | bytes 28
  9.9 27.7 %copy-start.9 = (f32[16]{0:T(128)S(1)}, f32[16]{0:T(128)}, u32[]{:S(2)}) copy-start(f32[16]{0:T(128)} %param.8) | copy-start | bytes 196
  11.3 51.7 %all-to-all-start = ((bf16[2,512,256]{2,0,1:T(2,128)(2,1)}), bf16[2,512,256]{2,0,1:T(2,128)(2,1)S(1)}, u32[]{:S(2)}, u32[]{:S(2)}) async-start(bf16[2,512,256]{2,0,1:T(2,128)(2,1)} %copy.29), calls=%async_computation | async-start | bytes 1048576 | tf_op jit(solution)/shard_map/all_to_all | solution.py:191
  63.6 1.6 %copy-start.3 = (f32[64,128]{1,0:T(8,128)S(1)}, f32[64,128]{1,0:T(8,128)}, u32[]{:S(2)}) copy-start(f32[64,128]{1,0:T(8,128)} %get-tuple-element.62) | copy-start | bytes 98308
  63.6 1.6 %copy-start.5 = (f32[64,128]{1,0:T(8,128)S(1)}, f32[64,128]{1,0:T(8,128)}, u32[]{:S(2)}) copy-start(f32[64,128]{1,0:T(8,128)} %get-tuple-element.63) | copy-start | bytes 98308
  63.7 1.6 %copy-start.2 = (f32[1,2,128,128]{3,2,0,1:T(8,128)S(1)}, f32[1,2,128,128]{3,2,0,1:T(8,128)}, u32[]{:S(2)}) copy-start(f32[1,2,128,128]{3,2,0,1:T(8,128)} %get-tuple-element.44) | copy-start | bytes 393220
  65.1 1.0 %copy-start.1 = (f32[16,64,128]{2,1,0:T(8,128)S(1)}, f32[16,64,128]{2,1,0:T(8,128)}, u32[]{:S(2)}) copy-start(f32[16,64,128]{2,1,0:T(8,128)} %get-tuple-element.13) | copy-start | bytes 1572868
  66.2 0.9 copy-start.4
  66.5 0.8 copy-start.6
  66.5 0.9 copy-start.7
  68.2 13.4 %collective-permute-start = (bf16[2,16,8192]{2,1,0:T(8,128)(2,1)S(1)}, bf16[2,16,8192]{2,1,0:T(8,128)(2,1)S(1)}, u32[]{:S(2)}, u32[]{:S(2)}) collective-permute-start(bf16[2,16,8192]{2,1,0:T(8,128)(2,1)S(1)} %convert_element_type.140), channel_id=1, source_target_pairs={{0,32},{32,160},{64,192},{96,64},{128,0},{160,128},{192,224},{224,... | collective-permute-start | bytes 1572872 | tf_op jit(solution)/shard_map/ppermute | solution.py:195
  70.6 11.7 %collective-permute-start.1 = (bf16[2,16,8192]{2,1,0:T(8,128)(2,1)S(1)}, bf16[2,16,8192]{2,1,0:T(8,128)(2,1)S(1)}, u32[]{:S(2)}, u32[]{:S(2)}) collective-permute-start(bf16[2,16,8192]{2,1,0:T(8,128)(2,1)S(1)} %convert_element_type.140), channel_id=1, source_target_pairs={{0,64},{32,288},{64,320},{96,32},{128,384},{160,224},{192,128},{22... | collective-permute-start | bytes 1572872 | tf_op jit(solution)/shard_map/ppermute | solution.py:195
  84.3 9.4 %collective-permute-start.2 = (f32[2,4,512]{2,1,0:T(4,128)S(1)}, f32[2,4,512]{2,1,0:T(4,128)S(1)}, u32[]{:S(2)}, u32[]{:S(2)}) collective-permute-start(f32[2,4,512]{2,1,0:T(4,128)S(1)} %slice.115), channel_id=1, source_target_pairs={{64,0},{288,32},{320,64},{32,96},{384,128},{224,160},{128,192},{48... | collective-permute-start | bytes 49160 | tf_op jit(solution)/shard_map/ppermute | solution.py:198
  91.8 7.1 %collective-permute-start.3 = (f32[2,4,512]{2,1,0:T(4,128)S(1)}, f32[2,4,512]{2,1,0:T(4,128)S(1)}, u32[]{:S(2)}, u32[]{:S(2)}) collective-permute-start(f32[2,4,512]{2,1,0:T(4,128)S(1)} %slice.119), channel_id=1, source_target_pairs={{32,0},{160,32},{192,64},{64,96},{0,128},{128,160},{224,192},{96,2... | collective-permute-start | bytes 49160 | tf_op jit(solution)/shard_map/ppermute | solution.py:198

commit v17 on v16

--- a/solution.py
+++ b/solution.py
@@ -170,45 +170,24 @@
     chosen = partner_bits[0]
     acq_size = lax.axis_size("acq")
     me = lax.axis_index("acq")
-    me_parity = jnp.int32(0)
-    for which in range(acq_size.bit_length() - 1):
-        me_parity = me_parity ^ ((me >> which) & 1)
-    low_bits = (0, 1)
-    high_bits = (2, 3)
-    edge_pairs = []
-    for slot in range(2):
-        edge_pairs.append(
-            [
-                (i, i ^ (1 << (high_bits[slot] if parity(i) else low_bits[slot])))
-                for i in range(acq_size)
-            ]
-        )
-    cand_bits = []
-    for slot in range(2):
-        cand_bits.append(jnp.where(me_parity == 1, low_bits[slot], high_bits[slot]))
-        cand_bits.append(jnp.where(me_parity == 1, high_bits[slot], low_bits[slot]))
-    preds = tuple(chosen[slot] == bit for slot in range(2) for bit in cand_bits)
+    bit_count = acq_size.bit_length() - 1
+    preds = tuple(chosen[slot] == which for slot in range(2) for which in range(bit_count))
     turned = lax.all_to_all(compressed, "pulse", split_axis=1, concat_axis=2, tiled=True)
     filt_cos, filt_sin = filter_tables(azimuth_rate, pulses_dev * lax.axis_size("pulse"))
     *preds, filt_cos, filt_sin, turned = lax.optimization_barrier((*preds, filt_cos, filt_sin, turned))
     focused = azimuth(turned, filt_cos, filt_sin).astype(jnp.bfloat16)
-    arrived = [lax.ppermute(focused, "acq", pairs) for pairs in edge_pairs]
-    looked = cross_looks(focused, arrived)
-    returned = [
-        lax.ppermute(looked[slot], "acq", [(dst, src) for src, dst in edge_pairs[slot]])
-        for slot in range(2)
+    arrived = [
+        lax.ppermute(focused, "acq", [(i, i ^ (1 << which)) for i in range(acq_size)])
+        for which in range(bit_count)
     ]
-    candidates = []
+    partners = []
     for slot in range(2):
-        candidates.append(looked[slot])
-        back = returned[slot]
-        candidates.append(jnp.stack([back[0], -back[1]]))
-    results = []
-    for slot in range(2):
-        pick = candidates[0]
-        for index in range(1, len(candidates)):
-            pick = jnp.where(preds[slot * len(candidates) + index], candidates[index], pick)
-        results.append(pick)
+        pick = arrived[0]
+        for which in range(1, bit_count):
+            pick = jnp.where(preds[slot * bit_count + which], arrived[which], pick)
+        partners.append(pick)
+    looked = cross_looks(focused, partners)
+    results = [looked[slot] for slot in range(2)]
     interfere_real = jnp.stack([item[0] for item in results])[None]
     interfere_imag = jnp.stack([item[1] for item in results])[None]
     return (interfere_real, interfere_imag)

time: 101 us -> 102 us (level)
  the two profiles are of different devices: /device:TPU:36 before, /device:TPU:2 now
where the time goes in v17:
time: 102 us; the launch traced here: 101 us
  waiting for transfers between devices  39.5 us (39%)
  starting transfers between devices  30 us (29%)
  other arithmetic  8.97 us (9%)
  matrix products  8.48 us (8%)
  between operations  5.57 us (5%)
  local copies, waits for them, and re-layouts  4.47 us (4%)
  Pallas kernels  4.04 us (4%)
    all_to_all x1, waiting for transfers between devices, per_device(): lax.all_to_all(compressed, 'pulse', split_axis=1, concat_axis=2, tiled=True)  21.7 us
    all_to_all x1, starting transfers between devices, per_device(): lax.all_to_all(compressed, 'pulse', split_axis=1, concat_axis=2, tiled=True)  18.1 us
    ppermute x4, waiting for transfers between devices, per_device(): lax.ppermute(focused, 'acq', [(i, i ^ 1 << which) for i in range(acq_size)])  17.8 us
    ppermute x4, starting transfers between devices, per_device(): lax.ppermute(focused, 'acq', [(i, i ^ 1 << which) for i in range(acq_size)])  11.9 us
    dot_general x1, matrix products, compress(): lax.dot_general(band, echoes, dims, preferred_element_type=jnp.float32)  4.57 us
    pallas_call x1, Pallas kernels, band_tables(): band = pl.pallas_call(band_kernel, out_shape=shape)(chirp_phase[None])  4.04 us
    sin x1, other arithmetic, filter_tables(): return (jnp.cos(phase), jnp.sin(phase))  2.72 us
  transfers between devices with their start and end apart: 5, of which 4 were waited for; matrix products, arithmetic and copies ran while one was open for 7% of the time, Pallas kernels for 0%

profile of v17, /device:TPU:2, one launch (start us, length us, event | category | flops | bytes accessed | tf_op | source)
XLA Modules:
  0.0 101.0 jit_solution(5706797715625340509)
XLA Ops:
  0.6 0.0 copy-start
  0.6 4.0 %shard_map.68 = bf16[2,2,512,1535]{3,2,1,0:T(8,128)(2,1)} custom-call(f32[1,1024]{1,0:T(1,128)} %bitcast.188), custom_call_target="tpu_custom_call" | custom-call | tf_op jit(solution)/shard_map/pallas_call | solution.py:63
  5.4 0.0 copy-done
  5.4 4.6 %fusion.14 = bf16[2,512,256]{2,1,0:T(8,128)(2,1)S(1)} fusion(bf16[2,256,1535,1]{1,0,2,3:T(2,128)(2,1)S(1)} %bitcast.179, bf16[2,2,512,1535]{3,2,1,0:T(8,128)(2,1)} %shard_map.68, f32[256]{0:T(256)S(1)} %compare_convert_fusion), kind=kOutput, calls=%fused_computation.11 | convolution fusion | flops 1610088448 | bytes 8384512 | tf_op jit(solution)/shard_map/dot_general | solution.py:70
  9.9 0.0 copy-start.8
  10.0 0.0 copy-start.9
  10.0 1.3 %copy.33 = bf16[2,512,256]{2,0,1:T(2,128)(2,1)} copy(bf16[2,512,256]{2,1,0:T(8,128)(2,1)S(1)} %fusion.14) | data formatting | bytes 1048576 | tf_op jit(solution)/shard_map/convert_element_type | solution.py:74
  11.3 18.1 %all-to-all-start = ((bf16[2,512,256]{2,0,1:T(2,128)(2,1)}), bf16[2,512,256]{2,0,1:T(2,128)(2,1)S(1)}, u32[]{:S(2)}, u32[]{:S(2)}) async-start(bf16[2,512,256]{2,0,1:T(2,128)(2,1)} %copy.33), calls=%async_computation | async-start | bytes 1048576 | tf_op jit(solution)/shard_map/all_to_all | solution.py:175
  29.4 0.0 copy-done.8
  29.4 0.6 fusion.79
  33.9 0.1 fusion.71
  34.1 0.8 fusion.67
  34.8 0.1 fusion.69
  35.0 0.8 fusion.68
  35.8 0.3 fusion.66
  36.0 0.3 fusion.60
  36.3 0.7 fusion.41
  37.0 0.7 fusion.34
  37.7 0.0 copy-done.9
  37.7 2.7 %multiply_sine_fusion = (f32[16,64,128]{2,1,0:T(8,128)S(1)}, f32[16,64,128]{2,1,0:T(8,128)}) fusion(f32[64,128]{1,0:T(8,128)S(1)} %fusion.57, f32[16]{0:T(128)S(1)} %broadcast_multiply_fusion), kind=kLoop, calls=%fused_computation.24 | loop fusion | flops 131072 | bytes 1081408 | tf_op jit(solution)/shard_map/sin | solution.py:88
  40.4 21.7 %all-to-all-done = bf16[2,512,256]{2,0,1:T(2,128)(2,1)S(1)} async-done(((bf16[2,512,256]{2,0,1:T(2,128)(2,1)}), bf16[2,512,256]{2,0,1:T(2,128)(2,1)S(1)}, u32[]{:S(2)}, u32[]{:S(2)}) %all-to-all-start) | async-done | bytes 524320 | tf_op jit(solution)/shard_map/all_to_all | solution.py:175
  62.1 0.3 copy.95
  62.4 0.2 all_to_all.16
  62.7 0.0 copy-start.3
  62.7 0.0 copy-start.5
  62.7 0.1 copy.61
  62.8 1.4 %convolution_bitcast_fusion.3 = f32[2,16,64,128]{3,2,1,0:T(8,128)S(1)} fusion(f32[1,2,64,64]{2,3,0,1:T(8,128)} %get-tuple-element.43, f32[1,2,64,64]{2,3,0,1:T(8,128)} %get-tuple-element.50, bf16[2,16,64,128]{3,2,1,0:T(8,128)(2,1)S(1)} %bitcast.185), kind=kOutput, calls=%fused_computation.9 | convolution fusion | flops 201342976 | bytes 1638400 | tf_op jit(solution)/shard_map/pcab,pqak->qckb/dot_general | solution.py:98
  64.3 0.1 multiply_subtract_fusion.1
  64.4 0.6 convolution_bitcast_fusion.2
  65.0 0.3 copy-done.1
  65.3 0.3 subtract_bitcast_fusion.2
  65.6 0.6 convolution_bitcast_fusion.1
  66.2 0.2 multiply_subtract_fusion
  66.4 0.0 copy-done.6
  66.4 0.0 copy-done.7
  66.4 0.6 fusion.20
  67.1 0.2 convert_element_type.140
  67.3 2.6 %collective-permute-start = (bf16[2,16,8192]{2,1,0:T(8,128)(2,1)S(1)}, bf16[2,16,8192]{2,1,0:T(8,128)(2,1)S(1)}, u32[]{:S(2)}, u32[]{:S(2)}) collective-permute-start(bf16[2,16,8192]{2,1,0:T(8,128)(2,1)S(1)} %convert_element_type.140), channel_id=1, source_target_pairs={{0,256},{32,288},{64,320},{96,352},{128,384},{160,416},{192,448},{... | collective-permute-start | bytes 1572872 | tf_op jit(solution)/shard_map/ppermute | solution.py:180
  69.9 4.0 %collective-permute-start.1 = (bf16[2,16,8192]{2,1,0:T(8,128)(2,1)S(1)}, bf16[2,16,8192]{2,1,0:T(8,128)(2,1)S(1)}, u32[]{:S(2)}, u32[]{:S(2)}) collective-permute-start(bf16[2,16,8192]{2,1,0:T(8,128)(2,1)S(1)} %convert_element_type.140), channel_id=1, source_target_pairs={{0,128},{32,160},{64,192},{96,224},{128,0},{160,32},{192,64},{224,... | collective-permute-start | bytes 1572872 | tf_op jit(solution)/shard_map/ppermute | solution.py:180
  74.0 3.3 %collective-permute-start.2 = (bf16[2,16,8192]{2,1,0:T(8,128)(2,1)S(1)}, bf16[2,16,8192]{2,1,0:T(8,128)(2,1)S(1)}, u32[]{:S(2)}, u32[]{:S(2)}) collective-permute-start(bf16[2,16,8192]{2,1,0:T(8,128)(2,1)S(1)} %convert_element_type.140), channel_id=1, source_target_pairs={{0,64},{32,96},{64,0},{96,32},{128,192},{160,224},{192,128},{224,1... | collective-permute-start | bytes 1572872 | tf_op jit(solution)/shard_map/ppermute | solution.py:180
  77.3 1.9 %collective-permute-start.3 = (bf16[2,16,8192]{2,1,0:T(8,128)(2,1)S(1)}, bf16[2,16,8192]{2,1,0:T(8,128)(2,1)S(1)}, u32[]{:S(2)}, u32[]{:S(2)}) collective-permute-start(bf16[2,16,8192]{2,1,0:T(8,128)(2,1)S(1)} %convert_element_type.140), channel_id=1, source_target_pairs={{0,32},{32,0},{64,96},{96,64},{128,160},{160,128},{192,224},{224,1... | collective-permute-start | bytes 1572872 | tf_op jit(solution)/shard_map/ppermute | solution.py:180
  79.2 0.1 convert_element_type.141
  79.3 2.7 %collective-permute-done = bf16[2,16,8192]{2,1,0:T(8,128)(2,1)S(1)} collective-permute-done((bf16[2,16,8192]{2,1,0:T(8,128)(2,1)S(1)}, bf16[2,16,8192]{2,1,0:T(8,128)(2,1)S(1)}, u32[]{:S(2)}, u32[]{:S(2)}) %collective-permute-start) | collective-permute-done | bytes 524320 | tf_op jit(solution)/shard_map/ppermute | solution.py:180
  82.1 6.1 %collective-permute-done.1 = bf16[2,16,8192]{2,1,0:T(8,128)(2,1)S(1)} collective-permute-done((bf16[2,16,8192]{2,1,0:T(8,128)(2,1)S(1)}, bf16[2,16,8192]{2,1,0:T(8,128)(2,1)S(1)}, u32[]{:S(2)}, u32[]{:S(2)}) %collective-permute-start.1) | collective-permute-done | bytes 524320 | tf_op jit(solution)/shard_map/ppermute | solution.py:180
  88.2 9.0 %collective-permute-done.2 = bf16[2,16,8192]{2,1,0:T(8,128)(2,1)S(1)} collective-permute-done((bf16[2,16,8192]{2,1,0:T(8,128)(2,1)S(1)}, bf16[2,16,8192]{2,1,0:T(8,128)(2,1)S(1)}, u32[]{:S(2)}, u32[]{:S(2)}) %collective-permute-start.2) | collective-permute-done | bytes 524320 | tf_op jit(solution)/shard_map/ppermute | solution.py:180
  97.1 0.0 collective-permute-done.3
  97.1 0.2 select_convert_fusion.1
  97.3 0.2 add_bitcast_fusion.1
  97.6 0.1 copy.62
  97.7 0.1 copy.63
  97.8 0.1 copy.64
  97.9 0.1 copy.65
  98.0 0.2 maximum_reduce_fusion
  98.2 0.7 convolution_multiply_fusion
  98.9 0.1 copy.43
  99.0 0.1 slice.113
  99.2 0.1 copy.44
  99.3 0.1 slice.115
  99.4 0.1 copy.41
  99.5 0.1 slice.109
  99.6 0.1 copy.42
  99.7 0.1 slice.111
  99.8 0.6 maximum_bitcast_fusion.7
  100.4 0.6 maximum_bitcast_fusion.6
  (15 shorter events, 0.1 us)
Async XLA Ops:
  0.6 4.7 %copy-start = (bf16[1,2,256,1535]{2,1,3,0:T(2,128)(2,1)S(1)}, bf16[1,2,256,1535]{2,1,3,0:T(2,128)(2,1)}, u32[]{:S(2)}) copy-start(bf16[1,2,256,1535]{2,1,3,0:T(2,128)(2,1)} %param.5) | copy-start | bytes 4715524
  9.9 19.5 %copy-start.8 = (s32[1,2]{1,0:T(1,128)S(1)}, s32[1,2]{1,0:T(1,128)}, u32[]{:S(2)}) copy-start(s32[1,2]{1,0:T(1,128)} %param.9) | copy-start | bytes 28
  10.0 27.7 %copy-start.9 = (f32[16]{0:T(128)S(1)}, f32[16]{0:T(128)}, u32[]{:S(2)}) copy-start(f32[16]{0:T(128)} %param.8) | copy-start | bytes 196
  11.3 50.8 %all-to-all-start = ((bf16[2,512,256]{2,0,1:T(2,128)(2,1)}), bf16[2,512,256]{2,0,1:T(2,128)(2,1)S(1)}, u32[]{:S(2)}, u32[]{:S(2)}) async-start(bf16[2,512,256]{2,0,1:T(2,128)(2,1)} %copy.33), calls=%async_computation | async-start | bytes 1048576 | tf_op jit(solution)/shard_map/all_to_all | solution.py:175
  62.7 1.5 %copy-start.3 = (f32[64,128]{1,0:T(8,128)S(1)}, f32[64,128]{1,0:T(8,128)}, u32[]{:S(2)}) copy-start(f32[64,128]{1,0:T(8,128)} %get-tuple-element.56) | copy-start | bytes 98308
  62.7 1.5 %copy-start.5 = (f32[64,128]{1,0:T(8,128)S(1)}, f32[64,128]{1,0:T(8,128)}, u32[]{:S(2)}) copy-start(f32[64,128]{1,0:T(8,128)} %get-tuple-element.57) | copy-start | bytes 98308
  62.8 1.6 %copy-start.2 = (f32[1,2,128,128]{3,2,0,1:T(8,128)S(1)}, f32[1,2,128,128]{3,2,0,1:T(8,128)}, u32[]{:S(2)}) copy-start(f32[1,2,128,128]{3,2,0,1:T(8,128)} %get-tuple-element.46) | copy-start | bytes 393220
  64.3 1.0 %copy-start.1 = (f32[16,64,128]{2,1,0:T(8,128)S(1)}, f32[16,64,128]{2,1,0:T(8,128)}, u32[]{:S(2)}) copy-start(f32[16,64,128]{2,1,0:T(8,128)} %get-tuple-element.12) | copy-start | bytes 1572868
  65.3 0.9 copy-start.4
  65.6 0.8 copy-start.6
  65.6 0.9 copy-start.7
  67.3 14.7 %collective-permute-start = (bf16[2,16,8192]{2,1,0:T(8,128)(2,1)S(1)}, bf16[2,16,8192]{2,1,0:T(8,128)(2,1)S(1)}, u32[]{:S(2)}, u32[]{:S(2)}) collective-permute-start(bf16[2,16,8192]{2,1,0:T(8,128)(2,1)S(1)} %convert_element_type.140), channel_id=1, source_target_pairs={{0,256},{32,288},{64,320},{96,352},{128,384},{160,416},{192,448},{... | collective-permute-start | bytes 1572872 | tf_op jit(solution)/shard_map/ppermute | solution.py:180
  69.9 18.3 %collective-permute-start.1 = (bf16[2,16,8192]{2,1,0:T(8,128)(2,1)S(1)}, bf16[2,16,8192]{2,1,0:T(8,128)(2,1)S(1)}, u32[]{:S(2)}, u32[]{:S(2)}) collective-permute-start(bf16[2,16,8192]{2,1,0:T(8,128)(2,1)S(1)} %convert_element_type.140), channel_id=1, source_target_pairs={{0,128},{32,160},{64,192},{96,224},{128,0},{160,32},{192,64},{224,... | collective-permute-start | bytes 1572872 | tf_op jit(solution)/shard_map/ppermute | solution.py:180
  74.0 23.2 %collective-permute-start.2 = (bf16[2,16,8192]{2,1,0:T(8,128)(2,1)S(1)}, bf16[2,16,8192]{2,1,0:T(8,128)(2,1)S(1)}, u32[]{:S(2)}, u32[]{:S(2)}) collective-permute-start(bf16[2,16,8192]{2,1,0:T(8,128)(2,1)S(1)} %convert_element_type.140), channel_id=1, source_target_pairs={{0,64},{32,96},{64,0},{96,32},{128,192},{160,224},{192,128},{224,1... | collective-permute-start | bytes 1572872 | tf_op jit(solution)/shard_map/ppermute | solution.py:180
  77.3 19.8 %collective-permute-start.3 = (bf16[2,16,8192]{2,1,0:T(8,128)(2,1)S(1)}, bf16[2,16,8192]{2,1,0:T(8,128)(2,1)S(1)}, u32[]{:S(2)}, u32[]{:S(2)}) collective-permute-start(bf16[2,16,8192]{2,1,0:T(8,128)(2,1)S(1)} %convert_element_type.140), channel_id=1, source_target_pairs={{0,32},{32,0},{64,96},{96,64},{128,160},{160,128},{192,224},{224,1... | collective-permute-start | bytes 1572872 | tf_op jit(solution)/shard_map/ppermute | solution.py:180

commit v18 on v16

--- a/solution.py
+++ b/solution.py
@@ -98,6 +98,7 @@
     section_one = jnp.einsum(
         "pcab,pqak->qckb", signal, part_tables(outer_len, False), precision=highest
     )
+    section_one, filt_cos, filt_sin = lax.optimization_barrier((section_one, filt_cos, filt_sin))
     outer_ids = jnp.arange(outer_len, dtype=jnp.int32)
     inner_ids = jnp.arange(inner_len, dtype=jnp.int32)
     twist = (
@@ -190,7 +191,7 @@
     preds = tuple(chosen[slot] == bit for slot in range(2) for bit in cand_bits)
     turned = lax.all_to_all(compressed, "pulse", split_axis=1, concat_axis=2, tiled=True)
     filt_cos, filt_sin = filter_tables(azimuth_rate, pulses_dev * lax.axis_size("pulse"))
-    *preds, filt_cos, filt_sin, turned = lax.optimization_barrier((*preds, filt_cos, filt_sin, turned))
+    *preds, turned = lax.optimization_barrier((*preds, turned))
     focused = azimuth(turned, filt_cos, filt_sin).astype(jnp.bfloat16)
     arrived = [lax.ppermute(focused, "acq", pairs) for pairs in edge_pairs]
     looked = cross_looks(focused, arrived)

time: 101 us -> 101 us (level)
  no operation moved by 1% of the time
where the time goes in v18:
time: 101 us; the launch traced here: 100 us
  waiting for transfers between devices  37.3 us (37%)
  starting transfers between devices  31.6 us (31%)
  other arithmetic  8.93 us (9%)
  matrix products  8.47 us (8%)
  between operations  5.71 us (6%)
  local copies, waits for them, and re-layouts  4.27 us (4%)
  Pallas kernels  3.9 us (4%)
    all_to_all x1, waiting for transfers between devices, per_device(): lax.all_to_all(compressed, 'pulse', split_axis=1, concat_axis=2, tiled=True)  22.7 us
    all_to_all x1, starting transfers between devices, per_device(): lax.all_to_all(compressed, 'pulse', split_axis=1, concat_axis=2, tiled=True)  18 us
    ppermute x2, waiting for transfers between devices, per_device(): arrived = [lax.ppermute(focused, 'acq', pairs) for pairs in edge_pairs]  9.46 us
    ppermute x2, starting transfers between devices, per_device(): lax.ppermute(looked[slot], 'acq', [(dst, src) for src, dst in edge_pairs[...  9.11 us
    ppermute x2, waiting for transfers between devices, per_device(): lax.ppermute(looked[slot], 'acq', [(dst, src) for src, dst in edge_pairs[...  5.19 us
    dot_general x1, matrix products, compress(): lax.dot_general(band, echoes, dims, preferred_element_type=jnp.float32)  4.57 us
    ppermute x2, starting transfers between devices, per_device(): arrived = [lax.ppermute(focused, 'acq', pairs) for pairs in edge_pairs]  4.5 us
    pallas_call x1, Pallas kernels, band_tables(): band = pl.pallas_call(band_kernel, out_shape=shape)(chirp_phase[None])  3.9 us
  transfers between devices with their start and end apart: 5, of which 4 were waited for; matrix products, arithmetic and copies ran while one was open for 8% of the time, Pallas kernels for 0%

profile of v18, /device:TPU:36, one launch (start us, length us, event | category | flops | bytes accessed | tf_op | source)
XLA Modules:
  0.0 100.2 jit_solution(8518855114431306842)
XLA Ops:
  0.6 0.0 copy-start
  1.4 3.9 %shard_map.68 = bf16[2,2,512,1535]{3,2,1,0:T(8,128)(2,1)} custom-call(f32[1,1024]{1,0:T(1,128)} %bitcast.180), custom_call_target="tpu_custom_call" | custom-call | tf_op jit(solution)/shard_map/pallas_call | solution.py:63
  5.3 0.0 copy-done
  5.3 4.6 %fusion.14 = bf16[2,512,256]{2,1,0:T(8,128)(2,1)S(1)} fusion(bf16[2,256,1535,1]{1,0,2,3:T(2,128)(2,1)S(1)} %bitcast.171, bf16[2,2,512,1535]{3,2,1,0:T(8,128)(2,1)} %shard_map.68, f32[256]{0:T(256)S(1)} %compare_convert_fusion), kind=kOutput, calls=%fused_computation.11 | convolution fusion | flops 1610088448 | bytes 8384512 | tf_op jit(solution)/shard_map/dot_general | solution.py:70
  9.9 0.0 copy-start.8
  9.9 0.0 copy-start.9
  9.9 1.4 %copy.29 = bf16[2,512,256]{2,0,1:T(2,128)(2,1)} copy(bf16[2,512,256]{2,1,0:T(8,128)(2,1)S(1)} %fusion.14) | data formatting | bytes 1048576 | tf_op jit(solution)/shard_map/convert_element_type | solution.py:74
  11.3 18.0 %all-to-all-start = ((bf16[2,512,256]{2,0,1:T(2,128)(2,1)}), bf16[2,512,256]{2,0,1:T(2,128)(2,1)S(1)}, u32[]{:S(2)}, u32[]{:S(2)}) async-start(bf16[2,512,256]{2,0,1:T(2,128)(2,1)} %copy.29), calls=%async_computation | async-start | bytes 1048576 | tf_op jit(solution)/shard_map/all_to_all | solution.py:192
  29.3 0.0 copy-done.8
  29.3 0.6 fusion.83
  33.8 0.1 fusion.71
  33.9 0.8 fusion.67
  34.7 0.1 fusion.69
  34.8 0.8 fusion.68
  35.6 0.3 fusion.66
  35.9 0.3 fusion.60
  36.2 0.7 fusion.41
  36.9 0.7 fusion.34
  37.6 0.0 copy-done.9
  37.6 2.7 %multiply_sine_fusion = (f32[16,64,128]{2,1,0:T(8,128)S(1)}, f32[16,64,128]{2,1,0:T(8,128)}) fusion(f32[64,128]{1,0:T(8,128)S(1)} %fusion.57, f32[16]{0:T(128)S(1)} %broadcast_multiply_fusion), kind=kLoop, calls=%fused_computation.24 | loop fusion | flops 131072 | bytes 1081408 | tf_op jit(solution)/shard_map/sin | solution.py:88
  40.3 22.7 %all-to-all-done = bf16[2,512,256]{2,0,1:T(2,128)(2,1)S(1)} async-done(((bf16[2,512,256]{2,0,1:T(2,128)(2,1)}), bf16[2,512,256]{2,0,1:T(2,128)(2,1)S(1)}, u32[]{:S(2)}, u32[]{:S(2)}) %all-to-all-start) | async-done | bytes 524320 | tf_op jit(solution)/shard_map/all_to_all | solution.py:192
  63.0 0.3 copy.91
  63.3 0.2 all_to_all.16
  63.6 0.0 copy-start.3
  63.6 0.0 copy-start.5
  63.6 0.1 copy.57
  63.7 0.0 copy-start.2
  63.7 1.4 %convolution_bitcast_fusion.3 = f32[2,16,64,128]{3,2,1,0:T(8,128)S(1)} fusion(f32[1,2,64,64]{2,3,0,1:T(8,128)} %get-tuple-element.43, f32[1,2,64,64]{2,3,0,1:T(8,128)} %get-tuple-element.50, bf16[2,16,64,128]{3,2,1,0:T(8,128)(2,1)S(1)} %bitcast.177), kind=kOutput, calls=%fused_computation.9 | convolution fusion | flops 201342976 | bytes 1638400 | tf_op jit(solution)/shard_map/pcab,pqak->qckb/dot_general | solution.py:98
  65.1 0.0 copy-done.3
  65.1 0.0 copy-done.5
  65.2 0.1 multiply_subtract_fusion.1
  65.3 0.6 convolution_bitcast_fusion.2
  65.9 0.3 copy-done.1
  66.2 0.3 subtract_bitcast_fusion.2
  66.5 0.6 convolution_bitcast_fusion.1
  67.1 0.1 multiply_subtract_fusion
  67.2 0.1 copy-done.6
  67.3 0.0 copy-done.7
  67.3 0.6 fusion.20
  68.0 0.2 convert_element_type.140
  68.2 2.4 %collective-permute-start = (bf16[2,16,8192]{2,1,0:T(8,128)(2,1)S(1)}, bf16[2,16,8192]{2,1,0:T(8,128)(2,1)S(1)}, u32[]{:S(2)}, u32[]{:S(2)}) collective-permute-start(bf16[2,16,8192]{2,1,0:T(8,128)(2,1)S(1)} %convert_element_type.140), channel_id=1, source_target_pairs={{0,32},{32,160},{64,192},{96,64},{128,0},{160,128},{192,224},{224,... | collective-permute-start | bytes 1572872 | tf_op jit(solution)/shard_map/ppermute | solution.py:196
  70.6 2.1 %collective-permute-start.1 = (bf16[2,16,8192]{2,1,0:T(8,128)(2,1)S(1)}, bf16[2,16,8192]{2,1,0:T(8,128)(2,1)S(1)}, u32[]{:S(2)}, u32[]{:S(2)}) collective-permute-start(bf16[2,16,8192]{2,1,0:T(8,128)(2,1)S(1)} %convert_element_type.140), channel_id=1, source_target_pairs={{0,64},{32,288},{64,320},{96,32},{128,384},{160,224},{192,128},{22... | collective-permute-start | bytes 1572872 | tf_op jit(solution)/shard_map/ppermute | solution.py:196
  72.7 0.1 convert_element_type.141
  72.8 8.8 %collective-permute-done = bf16[2,16,8192]{2,1,0:T(8,128)(2,1)S(1)} collective-permute-done((bf16[2,16,8192]{2,1,0:T(8,128)(2,1)S(1)}, bf16[2,16,8192]{2,1,0:T(8,128)(2,1)S(1)}, u32[]{:S(2)}, u32[]{:S(2)}) %collective-permute-start) | collective-permute-done | bytes 524320 | tf_op jit(solution)/shard_map/ppermute | solution.py:196
  81.7 0.1 convert_element_type.142
  81.7 0.6 collective-permute-done.1
  82.4 0.1 convert_element_type.143
  82.4 0.2 add_bitcast_fusion.1
  82.7 0.1 copy.58
  82.8 0.1 copy.59
  82.9 0.1 copy.60
  83.0 0.1 copy.61
  83.1 0.2 maximum_reduce_fusion
  83.3 0.7 convolution_multiply_fusion
  84.0 0.1 copy.39
  84.2 0.2 slice.115
  84.3 7.2 %collective-permute-start.2 = (f32[2,4,512]{2,1,0:T(4,128)S(1)}, f32[2,4,512]{2,1,0:T(4,128)S(1)}, u32[]{:S(2)}, u32[]{:S(2)}) collective-permute-start(f32[2,4,512]{2,1,0:T(4,128)S(1)} %slice.115), channel_id=1, source_target_pairs={{64,0},{288,32},{320,64},{32,96},{384,128},{224,160},{128,192},{48... | collective-permute-start | bytes 49160 | tf_op jit(solution)/shard_map/ppermute | solution.py:199
  91.5 0.1 copy.40
  91.7 0.2 slice.119
  91.8 1.9 %collective-permute-start.3 = (f32[2,4,512]{2,1,0:T(4,128)S(1)}, f32[2,4,512]{2,1,0:T(4,128)S(1)}, u32[]{:S(2)}, u32[]{:S(2)}) collective-permute-start(f32[2,4,512]{2,1,0:T(4,128)S(1)} %slice.119), channel_id=1, source_target_pairs={{32,0},{160,32},{192,64},{64,96},{0,128},{128,160},{224,192},{96,2... | collective-permute-start | bytes 49160 | tf_op jit(solution)/shard_map/ppermute | solution.py:199
  93.8 0.0 collective-permute-done.2
  93.8 5.2 %collective-permute-done.3 = f32[2,4,512]{2,1,0:T(4,128)S(1)} collective-permute-done((f32[2,4,512]{2,1,0:T(4,128)S(1)}, f32[2,4,512]{2,1,0:T(4,128)S(1)}, u32[]{:S(2)}, u32[]{:S(2)}) %collective-permute-start.3) | collective-permute-done | bytes 16416 | tf_op jit(solution)/shard_map/ppermute | solution.py:199
  99.0 0.6 maximum_bitcast_fusion.7
  99.6 0.6 maximum_bitcast_fusion.6
  (17 shorter events, 0.1 us)
Async XLA Ops:
  0.6 4.7 %copy-start = (bf16[1,2,256,1535]{2,1,3,0:T(2,128)(2,1)S(1)}, bf16[1,2,256,1535]{2,1,3,0:T(2,128)(2,1)}, u32[]{:S(2)}) copy-start(bf16[1,2,256,1535]{2,1,3,0:T(2,128)(2,1)} %param.5) | copy-start | bytes 4715524
  9.9 19.4 %copy-start.8 = (s32[1,2]{1,0:T(1,128)S(1)}, s32[1,2]{1,0:T(1,128)}, u32[]{:S(2)}) copy-start(s32[1,2]{1,0:T(1,128)} %param.9) | copy-start | bytes 28
  9.9 27.7 %copy-start.9 = (f32[16]{0:T(128)S(1)}, f32[16]{0:T(128)}, u32[]{:S(2)}) copy-start(f32[16]{0:T(128)} %param.8) | copy-start | bytes 196
  11.3 51.7 %all-to-all-start = ((bf16[2,512,256]{2,0,1:T(2,128)(2,1)}), bf16[2,512,256]{2,0,1:T(2,128)(2,1)S(1)}, u32[]{:S(2)}, u32[]{:S(2)}) async-start(bf16[2,512,256]{2,0,1:T(2,128)(2,1)} %copy.29), calls=%async_computation | async-start | bytes 1048576 | tf_op jit(solution)/shard_map/all_to_all | solution.py:192
  63.6 1.6 %copy-start.3 = (f32[64,128]{1,0:T(8,128)S(1)}, f32[64,128]{1,0:T(8,128)}, u32[]{:S(2)}) copy-start(f32[64,128]{1,0:T(8,128)} %get-tuple-element.64) | copy-start | bytes 98308
  63.6 1.6 %copy-start.5 = (f32[64,128]{1,0:T(8,128)S(1)}, f32[64,128]{1,0:T(8,128)}, u32[]{:S(2)}) copy-start(f32[64,128]{1,0:T(8,128)} %get-tuple-element.65) | copy-start | bytes 98308
  63.7 1.6 %copy-start.2 = (f32[1,2,128,128]{3,2,0,1:T(8,128)S(1)}, f32[1,2,128,128]{3,2,0,1:T(8,128)}, u32[]{:S(2)}) copy-start(f32[1,2,128,128]{3,2,0,1:T(8,128)} %get-tuple-element.46) | copy-start | bytes 393220
  65.1 1.0 %copy-start.1 = (f32[16,64,128]{2,1,0:T(8,128)S(1)}, f32[16,64,128]{2,1,0:T(8,128)}, u32[]{:S(2)}) copy-start(f32[16,64,128]{2,1,0:T(8,128)} %get-tuple-element.15) | copy-start | bytes 1572868
  66.2 0.9 copy-start.4
  66.5 0.8 copy-start.6
  66.5 0.9 copy-start.7
  68.2 13.4 %collective-permute-start = (bf16[2,16,8192]{2,1,0:T(8,128)(2,1)S(1)}, bf16[2,16,8192]{2,1,0:T(8,128)(2,1)S(1)}, u32[]{:S(2)}, u32[]{:S(2)}) collective-permute-start(bf16[2,16,8192]{2,1,0:T(8,128)(2,1)S(1)} %convert_element_type.140), channel_id=1, source_target_pairs={{0,32},{32,160},{64,192},{96,64},{128,0},{160,128},{192,224},{224,... | collective-permute-start | bytes 1572872 | tf_op jit(solution)/shard_map/ppermute | solution.py:196
  70.6 11.7 %collective-permute-start.1 = (bf16[2,16,8192]{2,1,0:T(8,128)(2,1)S(1)}, bf16[2,16,8192]{2,1,0:T(8,128)(2,1)S(1)}, u32[]{:S(2)}, u32[]{:S(2)}) collective-permute-start(bf16[2,16,8192]{2,1,0:T(8,128)(2,1)S(1)} %convert_element_type.140), channel_id=1, source_target_pairs={{0,64},{32,288},{64,320},{96,32},{128,384},{160,224},{192,128},{22... | collective-permute-start | bytes 1572872 | tf_op jit(solution)/shard_map/ppermute | solution.py:196
  84.3 9.4 %collective-permute-start.2 = (f32[2,4,512]{2,1,0:T(4,128)S(1)}, f32[2,4,512]{2,1,0:T(4,128)S(1)}, u32[]{:S(2)}, u32[]{:S(2)}) collective-permute-start(f32[2,4,512]{2,1,0:T(4,128)S(1)} %slice.115), channel_id=1, source_target_pairs={{64,0},{288,32},{320,64},{32,96},{384,128},{224,160},{128,192},{48... | collective-permute-start | bytes 49160 | tf_op jit(solution)/shard_map/ppermute | solution.py:199
  91.8 7.1 %collective-permute-start.3 = (f32[2,4,512]{2,1,0:T(4,128)S(1)}, f32[2,4,512]{2,1,0:T(4,128)S(1)}, u32[]{:S(2)}, u32[]{:S(2)}) collective-permute-start(f32[2,4,512]{2,1,0:T(4,128)S(1)} %slice.119), channel_id=1, source_target_pairs={{32,0},{160,32},{192,64},{64,96},{0,128},{128,160},{224,192},{96,2... | collective-permute-start | bytes 49160 | tf_op jit(solution)/shard_map/ppermute | solution.py:199

commit v19 on v16

--- a/solution.py
+++ b/solution.py
@@ -173,8 +173,8 @@
     me_parity = jnp.int32(0)
     for which in range(acq_size.bit_length() - 1):
         me_parity = me_parity ^ ((me >> which) & 1)
-    low_bits = (0, 1)
-    high_bits = (2, 3)
+    low_bits = (0, 2)
+    high_bits = (1, 3)
     edge_pairs = []
     for slot in range(2):
         edge_pairs.append(

time: 101 us -> 98.2 us (0.972)
  the two profiles are of different devices: /device:TPU:36 before, /device:TPU:34 now
where the time goes in v19:
time: 98.2 us; the launch traced here: 97.7 us
  waiting for transfers between devices  36.7 us (37%)
  starting transfers between devices  29.7 us (30%)
  other arithmetic  8.93 us (9%)
  matrix products  8.49 us (9%)
  between operations  5.71 us (6%)
  local copies, waits for them, and re-layouts  4.26 us (4%)
  Pallas kernels  3.9 us (4%)
    all_to_all x1, waiting for transfers between devices, per_device(): lax.all_to_all(compressed, 'pulse', split_axis=1, concat_axis=2, tiled=True)  22.7 us
    all_to_all x1, starting transfers between devices, per_device(): lax.all_to_all(compressed, 'pulse', split_axis=1, concat_axis=2, tiled=True)  18 us
    ppermute x2, waiting for transfers between devices, per_device(): arrived = [lax.ppermute(focused, 'acq', pairs) for pairs in edge_pairs]  10.3 us
    ppermute x2, starting transfers between devices, per_device(): lax.ppermute(looked[slot], 'acq', [(dst, src) for src, dst in edge_pairs[...  7.22 us
    dot_general x1, matrix products, compress(): lax.dot_general(band, echoes, dims, preferred_element_type=jnp.float32)  4.57 us
    ppermute x2, starting transfers between devices, per_device(): arrived = [lax.ppermute(focused, 'acq', pairs) for pairs in edge_pairs]  4.51 us
    pallas_call x1, Pallas kernels, band_tables(): band = pl.pallas_call(band_kernel, out_shape=shape)(chirp_phase[None])  3.9 us
    ppermute x2, waiting for transfers between devices, per_device(): lax.ppermute(looked[slot], 'acq', [(dst, src) for src, dst in edge_pairs[...  3.68 us
  transfers between devices with their start and end apart: 5, of which 4 were waited for; matrix products, arithmetic and copies ran while one was open for 8% of the time, Pallas kernels for 0%

profile of v19, /device:TPU:34, one launch (start us, length us, event | category | flops | bytes accessed | tf_op | source)
XLA Modules:
  0.0 97.7 jit_solution(10073107863445615543)
XLA Ops:
  0.6 0.0 copy-start
  1.4 3.9 %shard_map.68 = bf16[2,2,512,1535]{3,2,1,0:T(8,128)(2,1)} custom-call(f32[1,1024]{1,0:T(1,128)} %bitcast.180), custom_call_target="tpu_custom_call" | custom-call | tf_op jit(solution)/shard_map/pallas_call | solution.py:63
  5.3 0.0 copy-done
  5.3 4.6 %fusion.14 = bf16[2,512,256]{2,1,0:T(8,128)(2,1)S(1)} fusion(bf16[2,256,1535,1]{1,0,2,3:T(2,128)(2,1)S(1)} %bitcast.171, bf16[2,2,512,1535]{3,2,1,0:T(8,128)(2,1)} %shard_map.68, f32[256]{0:T(256)S(1)} %compare_convert_fusion), kind=kOutput, calls=%fused_computation.11 | convolution fusion | flops 1610088448 | bytes 8384512 | tf_op jit(solution)/shard_map/dot_general | solution.py:70
  9.9 0.0 copy-start.8
  9.9 0.0 copy-start.9
  9.9 1.4 %copy.29 = bf16[2,512,256]{2,0,1:T(2,128)(2,1)} copy(bf16[2,512,256]{2,1,0:T(8,128)(2,1)S(1)} %fusion.14) | data formatting | bytes 1048576 | tf_op jit(solution)/shard_map/convert_element_type | solution.py:74
  11.3 18.0 %all-to-all-start = ((bf16[2,512,256]{2,0,1:T(2,128)(2,1)}), bf16[2,512,256]{2,0,1:T(2,128)(2,1)S(1)}, u32[]{:S(2)}, u32[]{:S(2)}) async-start(bf16[2,512,256]{2,0,1:T(2,128)(2,1)} %copy.29), calls=%async_computation | async-start | bytes 1048576 | tf_op jit(solution)/shard_map/all_to_all | solution.py:191
  29.3 0.0 copy-done.8
  29.3 0.6 fusion.83
  33.8 0.1 fusion.71
  33.9 0.8 fusion.67
  34.7 0.1 fusion.69
  34.8 0.8 fusion.68
  35.6 0.3 fusion.66
  35.9 0.3 fusion.60
  36.2 0.7 fusion.41
  36.9 0.7 fusion.34
  37.6 0.0 copy-done.9
  37.6 2.7 %multiply_sine_fusion = (f32[16,64,128]{2,1,0:T(8,128)S(1)}, f32[16,64,128]{2,1,0:T(8,128)}) fusion(f32[64,128]{1,0:T(8,128)S(1)} %fusion.57, f32[16]{0:T(128)S(1)} %broadcast_multiply_fusion), kind=kLoop, calls=%fused_computation.24 | loop fusion | flops 131072 | bytes 1081408 | tf_op jit(solution)/shard_map/sin | solution.py:88
  40.3 22.7 %all-to-all-done = bf16[2,512,256]{2,0,1:T(2,128)(2,1)S(1)} async-done(((bf16[2,512,256]{2,0,1:T(2,128)(2,1)}), bf16[2,512,256]{2,0,1:T(2,128)(2,1)S(1)}, u32[]{:S(2)}, u32[]{:S(2)}) %all-to-all-start) | async-done | bytes 524320 | tf_op jit(solution)/shard_map/all_to_all | solution.py:191
  63.0 0.3 copy.91
  63.3 0.2 all_to_all.16
  63.6 0.0 copy-start.3
  63.6 0.0 copy-start.5
  63.6 0.1 copy.57
  63.7 0.0 copy-start.2
  63.7 1.4 %convolution_bitcast_fusion.3 = f32[2,16,64,128]{3,2,1,0:T(8,128)S(1)} fusion(f32[1,2,64,64]{2,3,0,1:T(8,128)} %get-tuple-element.41, f32[1,2,64,64]{2,3,0,1:T(8,128)} %get-tuple-element.48, bf16[2,16,64,128]{3,2,1,0:T(8,128)(2,1)S(1)} %bitcast.177), kind=kOutput, calls=%fused_computation.9 | convolution fusion | flops 201342976 | bytes 1638400 | tf_op jit(solution)/shard_map/pcab,pqak->qckb/dot_general | solution.py:98
  65.1 0.0 copy-done.3
  65.1 0.0 copy-done.5
  65.2 0.1 multiply_subtract_fusion.1
  65.3 0.6 convolution_bitcast_fusion.2
  65.9 0.3 copy-done.1
  66.2 0.3 subtract_bitcast_fusion.2
  66.5 0.6 convolution_bitcast_fusion.1
  67.1 0.1 multiply_subtract_fusion
  67.2 0.1 copy-done.6
  67.3 0.0 copy-done.7
  67.3 0.6 fusion.20
  68.0 0.2 convert_element_type.140
  68.2 2.4 %collective-permute-start = (bf16[2,16,8192]{2,1,0:T(8,128)(2,1)S(1)}, bf16[2,16,8192]{2,1,0:T(8,128)(2,1)S(1)}, u32[]{:S(2)}, u32[]{:S(2)}) collective-permute-start(bf16[2,16,8192]{2,1,0:T(8,128)(2,1)S(1)} %convert_element_type.140), channel_id=1, source_target_pairs={{0,32},{32,96},{64,0},{96,64},{128,192},{160,128},{192,224},{224,1... | collective-permute-start | bytes 1572872 | tf_op jit(solution)/shard_map/ppermute | solution.py:195
  70.7 2.1 %collective-permute-start.1 = (bf16[2,16,8192]{2,1,0:T(8,128)(2,1)S(1)}, bf16[2,16,8192]{2,1,0:T(8,128)(2,1)S(1)}, u32[]{:S(2)}, u32[]{:S(2)}) collective-permute-start(bf16[2,16,8192]{2,1,0:T(8,128)(2,1)S(1)} %convert_element_type.140), channel_id=1, source_target_pairs={{0,128},{32,288},{64,320},{96,224},{128,384},{160,32},{192,64},{22... | collective-permute-start | bytes 1572872 | tf_op jit(solution)/shard_map/ppermute | solution.py:195
  72.7 0.1 convert_element_type.141
  72.8 8.9 %collective-permute-done = bf16[2,16,8192]{2,1,0:T(8,128)(2,1)S(1)} collective-permute-done((bf16[2,16,8192]{2,1,0:T(8,128)(2,1)S(1)}, bf16[2,16,8192]{2,1,0:T(8,128)(2,1)S(1)}, u32[]{:S(2)}, u32[]{:S(2)}) %collective-permute-start) | collective-permute-done | bytes 524320 | tf_op jit(solution)/shard_map/ppermute | solution.py:195
  81.7 0.1 convert_element_type.142
  81.8 1.5 %collective-permute-done.1 = bf16[2,16,8192]{2,1,0:T(8,128)(2,1)S(1)} collective-permute-done((bf16[2,16,8192]{2,1,0:T(8,128)(2,1)S(1)}, bf16[2,16,8192]{2,1,0:T(8,128)(2,1)S(1)}, u32[]{:S(2)}, u32[]{:S(2)}) %collective-permute-start.1) | collective-permute-done | bytes 524320 | tf_op jit(solution)/shard_map/ppermute | solution.py:195
  83.2 0.1 convert_element_type.143
  83.3 0.2 add_bitcast_fusion.1
  83.6 0.1 copy.58
  83.7 0.1 copy.59
  83.8 0.1 copy.60
  83.9 0.1 copy.61
  84.0 0.2 maximum_reduce_fusion
  84.2 0.7 convolution_multiply_fusion
  84.9 0.1 copy.39
  85.1 0.2 slice.115
  85.2 5.3 %collective-permute-start.2 = (f32[2,4,512]{2,1,0:T(4,128)S(1)}, f32[2,4,512]{2,1,0:T(4,128)S(1)}, u32[]{:S(2)}, u32[]{:S(2)}) collective-permute-start(f32[2,4,512]{2,1,0:T(4,128)S(1)} %slice.115), channel_id=1, source_target_pairs={{128,0},{288,32},{320,64},{224,96},{384,128},{32,160},{64,192},{48... | collective-permute-start | bytes 49160 | tf_op jit(solution)/shard_map/ppermute | solution.py:198
  90.5 0.1 copy.40
  90.7 0.2 slice.119
  90.8 1.9 %collective-permute-start.3 = (f32[2,4,512]{2,1,0:T(4,128)S(1)}, f32[2,4,512]{2,1,0:T(4,128)S(1)}, u32[]{:S(2)}, u32[]{:S(2)}) collective-permute-start(f32[2,4,512]{2,1,0:T(4,128)S(1)} %slice.119), channel_id=1, source_target_pairs={{32,0},{96,32},{0,64},{64,96},{192,128},{128,160},{224,192},{160,2... | collective-permute-start | bytes 49160 | tf_op jit(solution)/shard_map/ppermute | solution.py:198
  92.7 0.0 collective-permute-done.2
  92.8 3.7 %collective-permute-done.3 = f32[2,4,512]{2,1,0:T(4,128)S(1)} collective-permute-done((f32[2,4,512]{2,1,0:T(4,128)S(1)}, f32[2,4,512]{2,1,0:T(4,128)S(1)}, u32[]{:S(2)}, u32[]{:S(2)}) %collective-permute-start.3) | collective-permute-done | bytes 16416 | tf_op jit(solution)/shard_map/ppermute | solution.py:198
  96.5 0.6 maximum_bitcast_fusion.7
  97.1 0.6 maximum_bitcast_fusion.6
  (17 shorter events, 0.1 us)
Async XLA Ops:
  0.6 4.7 %copy-start = (bf16[1,2,256,1535]{2,1,3,0:T(2,128)(2,1)S(1)}, bf16[1,2,256,1535]{2,1,3,0:T(2,128)(2,1)}, u32[]{:S(2)}) copy-start(bf16[1,2,256,1535]{2,1,3,0:T(2,128)(2,1)} %param.5) | copy-start | bytes 4715524
  9.9 19.4 %copy-start.8 = (s32[1,2]{1,0:T(1,128)S(1)}, s32[1,2]{1,0:T(1,128)}, u32[]{:S(2)}) copy-start(s32[1,2]{1,0:T(1,128)} %param.9) | copy-start | bytes 28
  9.9 27.7 %copy-start.9 = (f32[16]{0:T(128)S(1)}, f32[16]{0:T(128)}, u32[]{:S(2)}) copy-start(f32[16]{0:T(128)} %param.8) | copy-start | bytes 196
  11.3 51.7 %all-to-all-start = ((bf16[2,512,256]{2,0,1:T(2,128)(2,1)}), bf16[2,512,256]{2,0,1:T(2,128)(2,1)S(1)}, u32[]{:S(2)}, u32[]{:S(2)}) async-start(bf16[2,512,256]{2,0,1:T(2,128)(2,1)} %copy.29), calls=%async_computation | async-start | bytes 1048576 | tf_op jit(solution)/shard_map/all_to_all | solution.py:191
  63.6 1.6 %copy-start.3 = (f32[64,128]{1,0:T(8,128)S(1)}, f32[64,128]{1,0:T(8,128)}, u32[]{:S(2)}) copy-start(f32[64,128]{1,0:T(8,128)} %get-tuple-element.62) | copy-start | bytes 98308
  63.6 1.6 %copy-start.5 = (f32[64,128]{1,0:T(8,128)S(1)}, f32[64,128]{1,0:T(8,128)}, u32[]{:S(2)}) copy-start(f32[64,128]{1,0:T(8,128)} %get-tuple-element.63) | copy-start | bytes 98308
  63.7 1.6 %copy-start.2 = (f32[1,2,128,128]{3,2,0,1:T(8,128)S(1)}, f32[1,2,128,128]{3,2,0,1:T(8,128)}, u32[]{:S(2)}) copy-start(f32[1,2,128,128]{3,2,0,1:T(8,128)} %get-tuple-element.44) | copy-start | bytes 393220
  65.1 1.0 %copy-start.1 = (f32[16,64,128]{2,1,0:T(8,128)S(1)}, f32[16,64,128]{2,1,0:T(8,128)}, u32[]{:S(2)}) copy-start(f32[16,64,128]{2,1,0:T(8,128)} %get-tuple-element.13) | copy-start | bytes 1572868
  66.2 0.9 copy-start.4
  66.5 0.8 copy-start.6
  66.5 0.9 copy-start.7
  68.2 13.5 %collective-permute-start = (bf16[2,16,8192]{2,1,0:T(8,128)(2,1)S(1)}, bf16[2,16,8192]{2,1,0:T(8,128)(2,1)S(1)}, u32[]{:S(2)}, u32[]{:S(2)}) collective-permute-start(bf16[2,16,8192]{2,1,0:T(8,128)(2,1)S(1)} %convert_element_type.140), channel_id=1, source_target_pairs={{0,32},{32,96},{64,0},{96,64},{128,192},{160,128},{192,224},{224,1... | collective-permute-start | bytes 1572872 | tf_op jit(solution)/shard_map/ppermute | solution.py:195
  70.7 12.6 %collective-permute-start.1 = (bf16[2,16,8192]{2,1,0:T(8,128)(2,1)S(1)}, bf16[2,16,8192]{2,1,0:T(8,128)(2,1)S(1)}, u32[]{:S(2)}, u32[]{:S(2)}) collective-permute-start(bf16[2,16,8192]{2,1,0:T(8,128)(2,1)S(1)} %convert_element_type.140), channel_id=1, source_target_pairs={{0,128},{32,288},{64,320},{96,224},{128,384},{160,32},{192,64},{22... | collective-permute-start | bytes 1572872 | tf_op jit(solution)/shard_map/ppermute | solution.py:195
  85.2 7.5 %collective-permute-start.2 = (f32[2,4,512]{2,1,0:T(4,128)S(1)}, f32[2,4,512]{2,1,0:T(4,128)S(1)}, u32[]{:S(2)}, u32[]{:S(2)}) collective-permute-start(f32[2,4,512]{2,1,0:T(4,128)S(1)} %slice.115), channel_id=1, source_target_pairs={{128,0},{288,32},{320,64},{224,96},{384,128},{32,160},{64,192},{48... | collective-permute-start | bytes 49160 | tf_op jit(solution)/shard_map/ppermute | solution.py:198
  90.8 5.6 %collective-permute-start.3 = (f32[2,4,512]{2,1,0:T(4,128)S(1)}, f32[2,4,512]{2,1,0:T(4,128)S(1)}, u32[]{:S(2)}, u32[]{:S(2)}) collective-permute-start(f32[2,4,512]{2,1,0:T(4,128)S(1)} %slice.119), channel_id=1, source_target_pairs={{32,0},{96,32},{0,64},{64,96},{192,128},{128,160},{224,192},{160,2... | collective-permute-start | bytes 49160 | tf_op jit(solution)/shard_map/ppermute | solution.py:198

commit v20 on v19

--- a/solution.py
+++ b/solution.py
@@ -173,8 +173,8 @@
     me_parity = jnp.int32(0)
     for which in range(acq_size.bit_length() - 1):
         me_parity = me_parity ^ ((me >> which) & 1)
-    low_bits = (0, 2)
-    high_bits = (1, 3)
+    low_bits = (0, 3)
+    high_bits = (1, 2)
     edge_pairs = []
     for slot in range(2):
         edge_pairs.append(

time: 98.2 us -> 99.2 us (1.010)
  the two profiles are of different devices: /device:TPU:34 before, /device:TPU:40 now
where the time goes in v20:
time: 99.2 us; the launch traced here: 98.6 us
  waiting for transfers between devices  35 us (35%)
  starting transfers between devices  32.3 us (33%)
  other arithmetic  8.93 us (9%)
  matrix products  8.48 us (9%)
  between operations  5.71 us (6%)
  local copies, waits for them, and re-layouts  4.26 us (4%)
  Pallas kernels  3.9 us (4%)
    all_to_all x1, waiting for transfers between devices, per_device(): lax.all_to_all(compressed, 'pulse', split_axis=1, concat_axis=2, tiled=True)  22.7 us
    all_to_all x1, starting transfers between devices, per_device(): lax.all_to_all(compressed, 'pulse', split_axis=1, concat_axis=2, tiled=True)  17.1 us
    ppermute x2, waiting for transfers between devices, per_device(): arrived = [lax.ppermute(focused, 'acq', pairs) for pairs in edge_pairs]  8.67 us
    ppermute x2, starting transfers between devices, per_device(): lax.ppermute(looked[slot], 'acq', [(dst, src) for src, dst in edge_pairs[...  8.36 us
    ppermute x2, starting transfers between devices, per_device(): arrived = [lax.ppermute(focused, 'acq', pairs) for pairs in edge_pairs]  6.86 us
    dot_general x1, matrix products, compress(): lax.dot_general(band, echoes, dims, preferred_element_type=jnp.float32)  4.57 us
    pallas_call x1, Pallas kernels, band_tables(): band = pl.pallas_call(band_kernel, out_shape=shape)(chirp_phase[None])  3.9 us
    ppermute x2, waiting for transfers between devices, per_device(): lax.ppermute(looked[slot], 'acq', [(dst, src) for src, dst in edge_pairs[...  3.68 us
  transfers between devices with their start and end apart: 5, of which 4 were waited for; matrix products, arithmetic and copies ran while one was open for 8% of the time, Pallas kernels for 0%

profile of v20, /device:TPU:40, one launch (start us, length us, event | category | flops | bytes accessed | tf_op | source)
XLA Modules:
  0.0 98.6 jit_solution(3585445648370405837)
XLA Ops:
  0.6 0.0 copy-start
  1.4 3.9 %shard_map.68 = bf16[2,2,512,1535]{3,2,1,0:T(8,128)(2,1)} custom-call(f32[1,1024]{1,0:T(1,128)} %bitcast.180), custom_call_target="tpu_custom_call" | custom-call | tf_op jit(solution)/shard_map/pallas_call | solution.py:63
  5.3 0.0 copy-done
  5.3 4.6 %fusion.14 = bf16[2,512,256]{2,1,0:T(8,128)(2,1)S(1)} fusion(bf16[2,256,1535,1]{1,0,2,3:T(2,128)(2,1)S(1)} %bitcast.171, bf16[2,2,512,1535]{3,2,1,0:T(8,128)(2,1)} %shard_map.68, f32[256]{0:T(256)S(1)} %compare_convert_fusion), kind=kOutput, calls=%fused_computation.11 | convolution fusion | flops 1610088448 | bytes 8384512 | tf_op jit(solution)/shard_map/dot_general | solution.py:70
  9.9 0.0 copy-start.8
  9.9 0.0 copy-start.9
  9.9 1.4 %copy.29 = bf16[2,512,256]{2,0,1:T(2,128)(2,1)} copy(bf16[2,512,256]{2,1,0:T(8,128)(2,1)S(1)} %fusion.14) | data formatting | bytes 1048576 | tf_op jit(solution)/shard_map/convert_element_type | solution.py:74
  11.3 17.1 %all-to-all-start = ((bf16[2,512,256]{2,0,1:T(2,128)(2,1)}), bf16[2,512,256]{2,0,1:T(2,128)(2,1)S(1)}, u32[]{:S(2)}, u32[]{:S(2)}) async-start(bf16[2,512,256]{2,0,1:T(2,128)(2,1)} %copy.29), calls=%async_computation | async-start | bytes 1048576 | tf_op jit(solution)/shard_map/all_to_all | solution.py:191
  28.4 0.0 copy-done.8
  28.4 0.6 fusion.83
  32.9 0.1 fusion.71
  33.0 0.8 fusion.67
  33.8 0.1 fusion.69
  33.9 0.8 fusion.68
  34.7 0.3 fusion.66
  35.0 0.3 fusion.60
  35.3 0.7 fusion.41
  36.0 0.7 fusion.34
  36.7 0.0 copy-done.9
  36.7 2.7 %multiply_sine_fusion = (f32[16,64,128]{2,1,0:T(8,128)S(1)}, f32[16,64,128]{2,1,0:T(8,128)}) fusion(f32[64,128]{1,0:T(8,128)S(1)} %fusion.57, f32[16]{0:T(128)S(1)} %broadcast_multiply_fusion), kind=kLoop, calls=%fused_computation.24 | loop fusion | flops 131072 | bytes 1081408 | tf_op jit(solution)/shard_map/sin | solution.py:88
  39.4 22.7 %all-to-all-done = bf16[2,512,256]{2,0,1:T(2,128)(2,1)S(1)} async-done(((bf16[2,512,256]{2,0,1:T(2,128)(2,1)}), bf16[2,512,256]{2,0,1:T(2,128)(2,1)S(1)}, u32[]{:S(2)}, u32[]{:S(2)}) %all-to-all-start) | async-done | bytes 524320 | tf_op jit(solution)/shard_map/all_to_all | solution.py:191
  62.1 0.3 copy.91
  62.4 0.2 all_to_all.16
  62.7 0.0 copy-start.3
  62.7 0.0 copy-start.5
  62.7 0.1 copy.57
  62.8 1.4 %convolution_bitcast_fusion.3 = f32[2,16,64,128]{3,2,1,0:T(8,128)S(1)} fusion(f32[1,2,64,64]{2,3,0,1:T(8,128)} %get-tuple-element.41, f32[1,2,64,64]{2,3,0,1:T(8,128)} %get-tuple-element.48, bf16[2,16,64,128]{3,2,1,0:T(8,128)(2,1)S(1)} %bitcast.177), kind=kOutput, calls=%fused_computation.9 | convolution fusion | flops 201342976 | bytes 1638400 | tf_op jit(solution)/shard_map/pcab,pqak->qckb/dot_general | solution.py:98
  64.3 0.1 multiply_subtract_fusion.1
  64.4 0.6 convolution_bitcast_fusion.2
  65.0 0.3 copy-done.1
  65.3 0.3 subtract_bitcast_fusion.2
  65.6 0.0 copy-start.6
  65.6 0.0 copy-start.7
  65.6 0.6 convolution_bitcast_fusion.1
  66.2 0.0 copy-done.4
  66.2 0.1 multiply_subtract_fusion
  66.3 0.1 copy-done.6
  66.4 0.0 copy-done.7
  66.4 0.6 fusion.20
  67.1 0.2 convert_element_type.140
  67.3 3.4 %collective-permute-start = (bf16[2,16,8192]{2,1,0:T(8,128)(2,1)S(1)}, bf16[2,16,8192]{2,1,0:T(8,128)(2,1)S(1)}, u32[]{:S(2)}, u32[]{:S(2)}) collective-permute-start(bf16[2,16,8192]{2,1,0:T(8,128)(2,1)S(1)} %convert_element_type.140), channel_id=1, source_target_pairs={{0,32},{32,96},{64,0},{96,64},{128,192},{160,128},{192,224},{224,1... | collective-permute-start | bytes 1572872 | tf_op jit(solution)/shard_map/ppermute | solution.py:195
  70.7 3.5 %collective-permute-start.1 = (bf16[2,16,8192]{2,1,0:T(8,128)(2,1)S(1)}, bf16[2,16,8192]{2,1,0:T(8,128)(2,1)S(1)}, u32[]{:S(2)}, u32[]{:S(2)}) collective-permute-start(bf16[2,16,8192]{2,1,0:T(8,128)(2,1)S(1)} %convert_element_type.140), channel_id=1, source_target_pairs={{0,256},{32,160},{64,192},{96,352},{128,0},{160,416},{192,448},{22... | collective-permute-start | bytes 1572872 | tf_op jit(solution)/shard_map/ppermute | solution.py:195
  74.2 0.1 convert_element_type.141
  74.3 3.1 %collective-permute-done = bf16[2,16,8192]{2,1,0:T(8,128)(2,1)S(1)} collective-permute-done((bf16[2,16,8192]{2,1,0:T(8,128)(2,1)S(1)}, bf16[2,16,8192]{2,1,0:T(8,128)(2,1)S(1)}, u32[]{:S(2)}, u32[]{:S(2)}) %collective-permute-start) | collective-permute-done | bytes 524320 | tf_op jit(solution)/shard_map/ppermute | solution.py:195
  77.4 0.1 convert_element_type.142
  77.5 5.5 %collective-permute-done.1 = bf16[2,16,8192]{2,1,0:T(8,128)(2,1)S(1)} collective-permute-done((bf16[2,16,8192]{2,1,0:T(8,128)(2,1)S(1)}, bf16[2,16,8192]{2,1,0:T(8,128)(2,1)S(1)}, u32[]{:S(2)}, u32[]{:S(2)}) %collective-permute-start.1) | collective-permute-done | bytes 524320 | tf_op jit(solution)/shard_map/ppermute | solution.py:195
  83.0 0.1 convert_element_type.143
  83.1 0.2 add_bitcast_fusion.1
  83.3 0.1 copy.58
  83.4 0.1 copy.59
  83.6 0.1 copy.60
  83.7 0.1 copy.61
  83.8 0.2 maximum_reduce_fusion
  84.0 0.7 convolution_multiply_fusion
  84.7 0.1 copy.39
  84.8 0.2 slice.115
  85.0 6.4 %collective-permute-start.2 = (f32[2,4,512]{2,1,0:T(4,128)S(1)}, f32[2,4,512]{2,1,0:T(4,128)S(1)}, u32[]{:S(2)}, u32[]{:S(2)}) collective-permute-start(f32[2,4,512]{2,1,0:T(4,128)S(1)} %slice.115), channel_id=1, source_target_pairs={{256,0},{160,32},{192,64},{352,96},{0,128},{416,160},{448,192},{96... | collective-permute-start | bytes 49160 | tf_op jit(solution)/shard_map/ppermute | solution.py:198
  91.4 0.1 copy.40
  91.6 0.2 slice.119
  91.7 1.9 %collective-permute-start.3 = (f32[2,4,512]{2,1,0:T(4,128)S(1)}, f32[2,4,512]{2,1,0:T(4,128)S(1)}, u32[]{:S(2)}, u32[]{:S(2)}) collective-permute-start(f32[2,4,512]{2,1,0:T(4,128)S(1)} %slice.119), channel_id=1, source_target_pairs={{32,0},{96,32},{0,64},{64,96},{192,128},{128,160},{224,192},{160,2... | collective-permute-start | bytes 49160 | tf_op jit(solution)/shard_map/ppermute | solution.py:198
  93.7 0.0 collective-permute-done.2
  93.7 3.7 %collective-permute-done.3 = f32[2,4,512]{2,1,0:T(4,128)S(1)} collective-permute-done((f32[2,4,512]{2,1,0:T(4,128)S(1)}, f32[2,4,512]{2,1,0:T(4,128)S(1)}, u32[]{:S(2)}, u32[]{:S(2)}) %collective-permute-start.3) | collective-permute-done | bytes 16416 | tf_op jit(solution)/shard_map/ppermute | solution.py:198
  97.4 0.6 maximum_bitcast_fusion.7
  98.0 0.6 maximum_bitcast_fusion.6
  (17 shorter events, 0.1 us)
Async XLA Ops:
  0.6 4.7 %copy-start = (bf16[1,2,256,1535]{2,1,3,0:T(2,128)(2,1)S(1)}, bf16[1,2,256,1535]{2,1,3,0:T(2,128)(2,1)}, u32[]{:S(2)}) copy-start(bf16[1,2,256,1535]{2,1,3,0:T(2,128)(2,1)} %param.5) | copy-start | bytes 4715524
  9.9 18.5 %copy-start.8 = (s32[1,2]{1,0:T(1,128)S(1)}, s32[1,2]{1,0:T(1,128)}, u32[]{:S(2)}) copy-start(s32[1,2]{1,0:T(1,128)} %param.9) | copy-start | bytes 28
  9.9 26.8 %copy-start.9 = (f32[16]{0:T(128)S(1)}, f32[16]{0:T(128)}, u32[]{:S(2)}) copy-start(f32[16]{0:T(128)} %param.8) | copy-start | bytes 196
  11.3 50.8 %all-to-all-start = ((bf16[2,512,256]{2,0,1:T(2,128)(2,1)}), bf16[2,512,256]{2,0,1:T(2,128)(2,1)S(1)}, u32[]{:S(2)}, u32[]{:S(2)}) async-start(bf16[2,512,256]{2,0,1:T(2,128)(2,1)} %copy.29), calls=%async_computation | async-start | bytes 1048576 | tf_op jit(solution)/shard_map/all_to_all | solution.py:191
  62.7 1.6 %copy-start.3 = (f32[64,128]{1,0:T(8,128)S(1)}, f32[64,128]{1,0:T(8,128)}, u32[]{:S(2)}) copy-start(f32[64,128]{1,0:T(8,128)} %get-tuple-element.62) | copy-start | bytes 98308
  62.7 1.6 %copy-start.5 = (f32[64,128]{1,0:T(8,128)S(1)}, f32[64,128]{1,0:T(8,128)}, u32[]{:S(2)}) copy-start(f32[64,128]{1,0:T(8,128)} %get-tuple-element.63) | copy-start | bytes 98308
  62.8 1.6 %copy-start.2 = (f32[1,2,128,128]{3,2,0,1:T(8,128)S(1)}, f32[1,2,128,128]{3,2,0,1:T(8,128)}, u32[]{:S(2)}) copy-start(f32[1,2,128,128]{3,2,0,1:T(8,128)} %get-tuple-element.44) | copy-start | bytes 393220
  64.2 1.0 %copy-start.1 = (f32[16,64,128]{2,1,0:T(8,128)S(1)}, f32[16,64,128]{2,1,0:T(8,128)}, u32[]{:S(2)}) copy-start(f32[16,64,128]{2,1,0:T(8,128)} %get-tuple-element.13) | copy-start | bytes 1572868
  65.3 0.9 copy-start.4
  65.6 0.8 copy-start.6
  65.6 0.9 copy-start.7
  67.3 10.1 %collective-permute-start = (bf16[2,16,8192]{2,1,0:T(8,128)(2,1)S(1)}, bf16[2,16,8192]{2,1,0:T(8,128)(2,1)S(1)}, u32[]{:S(2)}, u32[]{:S(2)}) collective-permute-start(bf16[2,16,8192]{2,1,0:T(8,128)(2,1)S(1)} %convert_element_type.140), channel_id=1, source_target_pairs={{0,32},{32,96},{64,0},{96,64},{128,192},{160,128},{192,224},{224,1... | collective-permute-start | bytes 1572872 | tf_op jit(solution)/shard_map/ppermute | solution.py:195
  70.7 12.3 %collective-permute-start.1 = (bf16[2,16,8192]{2,1,0:T(8,128)(2,1)S(1)}, bf16[2,16,8192]{2,1,0:T(8,128)(2,1)S(1)}, u32[]{:S(2)}, u32[]{:S(2)}) collective-permute-start(bf16[2,16,8192]{2,1,0:T(8,128)(2,1)S(1)} %convert_element_type.140), channel_id=1, source_target_pairs={{0,256},{32,160},{64,192},{96,352},{128,0},{160,416},{192,448},{22... | collective-permute-start | bytes 1572872 | tf_op jit(solution)/shard_map/ppermute | solution.py:195
  85.0 8.7 %collective-permute-start.2 = (f32[2,4,512]{2,1,0:T(4,128)S(1)}, f32[2,4,512]{2,1,0:T(4,128)S(1)}, u32[]{:S(2)}, u32[]{:S(2)}) collective-permute-start(f32[2,4,512]{2,1,0:T(4,128)S(1)} %slice.115), channel_id=1, source_target_pairs={{256,0},{160,32},{192,64},{352,96},{0,128},{416,160},{448,192},{96... | collective-permute-start | bytes 49160 | tf_op jit(solution)/shard_map/ppermute | solution.py:198
  91.7 5.6 %collective-permute-start.3 = (f32[2,4,512]{2,1,0:T(4,128)S(1)}, f32[2,4,512]{2,1,0:T(4,128)S(1)}, u32[]{:S(2)}, u32[]{:S(2)}) collective-permute-start(f32[2,4,512]{2,1,0:T(4,128)S(1)} %slice.119), channel_id=1, source_target_pairs={{32,0},{96,32},{0,64},{64,96},{192,128},{128,160},{224,192},{160,2... | collective-permute-start | bytes 49160 | tf_op jit(solution)/shard_map/ppermute | solution.py:198

commit v21 on v19

--- a/solution.py
+++ b/solution.py
@@ -203,14 +203,14 @@
         candidates.append(looked[slot])
         back = returned[slot]
         candidates.append(jnp.stack([back[0], -back[1]]))
-    results = []
-    for slot in range(2):
-        pick = candidates[0]
-        for index in range(1, len(candidates)):
-            pick = jnp.where(preds[slot * len(candidates) + index], candidates[index], pick)
-        results.append(pick)
-    interfere_real = jnp.stack([item[0] for item in results])[None]
-    interfere_imag = jnp.stack([item[1] for item in results])[None]
+    count = len(candidates)
+    picked = [jnp.broadcast_to(candidates[0][part][None], (2, *candidates[0].shape[1:])) for part in range(2)]
+    for index in range(1, count):
+        choose = jnp.stack([preds[slot * count + index] for slot in range(2)])[:, None, None]
+        for part in range(2):
+            picked[part] = jnp.where(choose, candidates[index][part][None], picked[part])
+    interfere_real = picked[0][None]
+    interfere_imag = picked[1][None]
     return (interfere_real, interfere_imag)
 
 

time: 98.2 us -> 97.7 us (level)
  waiting for transfers between devices: 36.7 us -> 35.7 us
    broadcast_in_dim x2, other arithmetic: 1.22 us -> 0.01 us  [per_device(): jnp.where(choose, candidates[index][part][None], picked[part])]
  transfers between devices with their start and end apart: 5 -> 5, of which waited for: 4 -> 4; matrix products, arithmetic and copies ran while one was open for 8% -> 9% of each run, Pallas kernels for 0% -> 0%
where the time goes in v21:
time: 97.7 us; the launch traced here: 97.2 us
  waiting for transfers between devices  35.7 us (37%)
  starting transfers between devices  29.7 us (30%)
  other arithmetic  8.55 us (9%)
  matrix products  8.49 us (9%)
  between operations  5.73 us (6%)
  local copies, waits for them, and re-layouts  5.11 us (5%)
  Pallas kernels  3.9 us (4%)
    all_to_all x1, waiting for transfers between devices, per_device(): lax.all_to_all(compressed, 'pulse', split_axis=1, concat_axis=2, tiled=True)  22.7 us
    all_to_all x1, starting transfers between devices, per_device(): lax.all_to_all(compressed, 'pulse', split_axis=1, concat_axis=2, tiled=True)  18 us
    ppermute x2, waiting for transfers between devices, per_device(): arrived = [lax.ppermute(focused, 'acq', pairs) for pairs in edge_pairs]  10.2 us
    ppermute x2, starting transfers between devices, per_device(): lax.ppermute(looked[slot], 'acq', [(dst, src) for src, dst in edge_pairs[...  7.22 us
    dot_general x1, matrix products, compress(): lax.dot_general(band, echoes, dims, preferred_element_type=jnp.float32)  4.57 us
    ppermute x2, starting transfers between devices, per_device(): arrived = [lax.ppermute(focused, 'acq', pairs) for pairs in edge_pairs]  4.51 us
    pallas_call x1, Pallas kernels, band_tables(): band = pl.pallas_call(band_kernel, out_shape=shape)(chirp_phase[None])  3.9 us
    ppermute x2, waiting for transfers between devices, per_device(): lax.ppermute(looked[slot], 'acq', [(dst, src) for src, dst in edge_pairs[...  2.8 us
  transfers between devices with their start and end apart: 5, of which 4 were waited for; matrix products, arithmetic and copies ran while one was open for 9% of the time, Pallas kernels for 0%

profile of v21, /device:TPU:34, one launch (start us, length us, event | category | flops | bytes accessed | tf_op | source)
XLA Modules:
  0.0 97.2 jit_solution(16507864310577956661)
XLA Ops:
  0.6 0.0 copy-start
  1.4 3.9 %shard_map.68 = bf16[2,2,512,1535]{3,2,1,0:T(8,128)(2,1)} custom-call(f32[1,1024]{1,0:T(1,128)} %bitcast.198), custom_call_target="tpu_custom_call" | custom-call | tf_op jit(solution)/shard_map/pallas_call | solution.py:63
  5.3 4.6 %fusion.14 = bf16[2,512,256]{2,1,0:T(8,128)(2,1)S(1)} fusion(bf16[2,256,1535,1]{1,0,2,3:T(2,128)(2,1)S(1)} %bitcast.189, bf16[2,2,512,1535]{3,2,1,0:T(8,128)(2,1)} %shard_map.68, f32[256]{0:T(256)S(1)} %compare_convert_fusion), kind=kOutput, calls=%fused_computation.11 | convolution fusion | flops 1610088448 | bytes 8384512 | tf_op jit(solution)/shard_map/dot_general | solution.py:70
  9.9 0.0 copy-start.8
  9.9 0.0 copy-start.9
  9.9 1.4 %copy.33 = bf16[2,512,256]{2,0,1:T(2,128)(2,1)} copy(bf16[2,512,256]{2,1,0:T(8,128)(2,1)S(1)} %fusion.14) | data formatting | bytes 1048576 | tf_op jit(solution)/shard_map/convert_element_type | solution.py:74
  11.3 18.0 %all-to-all-start = ((bf16[2,512,256]{2,0,1:T(2,128)(2,1)}), bf16[2,512,256]{2,0,1:T(2,128)(2,1)S(1)}, u32[]{:S(2)}, u32[]{:S(2)}) async-start(bf16[2,512,256]{2,0,1:T(2,128)(2,1)} %copy.33), calls=%async_computation | async-start | bytes 1048576 | tf_op jit(solution)/shard_map/all_to_all | solution.py:191
  29.3 0.6 fusion.82
  33.8 0.1 fusion.71
  33.9 0.8 fusion.67
  34.7 0.1 fusion.69
  34.8 0.8 fusion.68
  35.6 0.3 fusion.66
  35.9 0.3 fusion.60
  36.2 0.7 fusion.41
  36.9 0.7 fusion.34
  37.6 2.7 %multiply_sine_fusion = (f32[16,64,128]{2,1,0:T(8,128)S(1)}, f32[16,64,128]{2,1,0:T(8,128)}) fusion(f32[64,128]{1,0:T(8,128)S(1)} %fusion.57, f32[16]{0:T(128)S(1)} %broadcast_multiply_fusion), kind=kLoop, calls=%fused_computation.24 | loop fusion | flops 131072 | bytes 1081408 | tf_op jit(solution)/shard_map/sin | solution.py:88
  40.3 22.7 %all-to-all-done = bf16[2,512,256]{2,0,1:T(2,128)(2,1)S(1)} async-done(((bf16[2,512,256]{2,0,1:T(2,128)(2,1)}), bf16[2,512,256]{2,0,1:T(2,128)(2,1)S(1)}, u32[]{:S(2)}, u32[]{:S(2)}) %all-to-all-start) | async-done | bytes 524320 | tf_op jit(solution)/shard_map/all_to_all | solution.py:191
  63.0 0.3 copy.99
  63.3 0.2 all_to_all.16
  63.6 0.1 copy.65
  63.7 1.4 %convolution_bitcast_fusion.3 = f32[2,16,64,128]{3,2,1,0:T(8,128)S(1)} fusion(f32[1,2,64,64]{2,3,0,1:T(8,128)} %get-tuple-element.43, f32[1,2,64,64]{2,3,0,1:T(8,128)} %get-tuple-element.50, bf16[2,16,64,128]{3,2,1,0:T(8,128)(2,1)S(1)} %bitcast.195), kind=kOutput, calls=%fused_computation.9 | convolution fusion | flops 201342976 | bytes 1638400 | tf_op jit(solution)/shard_map/pcab,pqak->qckb/dot_general | solution.py:98
  65.2 0.1 multiply_subtract_fusion.1
  65.3 0.6 convolution_bitcast_fusion.2
  65.9 0.3 copy-done.1
  66.2 0.3 subtract_bitcast_fusion.2
  66.5 0.6 convolution_bitcast_fusion.1
  67.1 0.1 multiply_subtract_fusion
  67.2 0.1 copy-done.6
  67.3 0.0 copy-done.7
  67.3 0.6 fusion.20
  68.0 0.2 convert_element_type.140
  68.2 2.4 %collective-permute-start = (bf16[2,16,8192]{2,1,0:T(8,128)(2,1)S(1)}, bf16[2,16,8192]{2,1,0:T(8,128)(2,1)S(1)}, u32[]{:S(2)}, u32[]{:S(2)}) collective-permute-start(bf16[2,16,8192]{2,1,0:T(8,128)(2,1)S(1)} %convert_element_type.140), channel_id=1, source_target_pairs={{0,32},{32,96},{64,0},{96,64},{128,192},{160,128},{192,224},{224,1... | collective-permute-start | bytes 1572872 | tf_op jit(solution)/shard_map/ppermute | solution.py:195
  70.7 2.1 %collective-permute-start.1 = (bf16[2,16,8192]{2,1,0:T(8,128)(2,1)S(1)}, bf16[2,16,8192]{2,1,0:T(8,128)(2,1)S(1)}, u32[]{:S(2)}, u32[]{:S(2)}) collective-permute-start(bf16[2,16,8192]{2,1,0:T(8,128)(2,1)S(1)} %convert_element_type.140), channel_id=1, source_target_pairs={{0,128},{32,288},{64,320},{96,224},{128,384},{160,32},{192,64},{22... | collective-permute-start | bytes 1572872 | tf_op jit(solution)/shard_map/ppermute | solution.py:195
  72.7 0.1 convert_element_type.141
  72.8 0.1 pad_add_fusion.2
  72.9 0.1 pad_add_fusion
  73.0 8.7 %collective-permute-done = bf16[2,16,8192]{2,1,0:T(8,128)(2,1)S(1)} collective-permute-done((bf16[2,16,8192]{2,1,0:T(8,128)(2,1)S(1)}, bf16[2,16,8192]{2,1,0:T(8,128)(2,1)S(1)}, u32[]{:S(2)}, u32[]{:S(2)}) %collective-permute-start) | collective-permute-done | bytes 524320 | tf_op jit(solution)/shard_map/ppermute | solution.py:195
  81.7 0.1 convert_element_type.142
  81.8 1.5 %collective-permute-done.1 = bf16[2,16,8192]{2,1,0:T(8,128)(2,1)S(1)} collective-permute-done((bf16[2,16,8192]{2,1,0:T(8,128)(2,1)S(1)}, bf16[2,16,8192]{2,1,0:T(8,128)(2,1)S(1)}, u32[]{:S(2)}, u32[]{:S(2)}) %collective-permute-start.1) | collective-permute-done | bytes 524320 | tf_op jit(solution)/shard_map/ppermute | solution.py:195
  83.2 0.1 convert_element_type.143
  83.3 0.2 add_bitcast_fusion.1
  83.6 0.1 copy.66
  83.7 0.1 copy.67
  83.8 0.1 copy.68
  83.9 0.1 copy.69
  84.0 0.2 maximum_reduce_fusion
  84.2 0.7 convolution_multiply_fusion
  84.9 0.1 copy.43
  85.1 0.2 slice.123
  85.2 5.3 %collective-permute-start.2 = (f32[2,4,512]{2,1,0:T(4,128)S(1)}, f32[2,4,512]{2,1,0:T(4,128)S(1)}, u32[]{:S(2)}, u32[]{:S(2)}) collective-permute-start(f32[2,4,512]{2,1,0:T(4,128)S(1)} %slice.123), channel_id=1, source_target_pairs={{128,0},{288,32},{320,64},{224,96},{384,128},{32,160},{64,192},{48... | collective-permute-start | bytes 49160 | tf_op jit(solution)/shard_map/ppermute | solution.py:198
  90.5 0.1 copy.45
  90.7 0.2 slice.127
  90.8 1.9 %collective-permute-start.3 = (f32[2,4,512]{2,1,0:T(4,128)S(1)}, f32[2,4,512]{2,1,0:T(4,128)S(1)}, u32[]{:S(2)}, u32[]{:S(2)}) collective-permute-start(f32[2,4,512]{2,1,0:T(4,128)S(1)} %slice.127), channel_id=1, source_target_pairs={{32,0},{96,32},{0,64},{64,96},{192,128},{128,160},{224,192},{160,2... | collective-permute-start | bytes 49160 | tf_op jit(solution)/shard_map/ppermute | solution.py:198
  92.8 0.1 copy.44
  92.9 0.1 broadcast_in_dim.124
  93.0 0.1 copy.46
  93.1 0.1 broadcast_in_dim.129
  93.2 0.1 copy.47
  93.3 0.1 broadcast_in_dim.133
  93.4 0.1 copy.48
  93.5 0.1 broadcast_in_dim.137
  93.7 2.8 %collective-permute-done.3 = f32[2,4,512]{2,1,0:T(4,128)S(1)} collective-permute-done((f32[2,4,512]{2,1,0:T(4,128)S(1)}, f32[2,4,512]{2,1,0:T(4,128)S(1)}, u32[]{:S(2)}, u32[]{:S(2)}) %collective-permute-start.3) | collective-permute-done | bytes 16416 | tf_op jit(solution)/shard_map/ppermute | solution.py:198
  96.5 0.7 select_select_fusion
  (24 shorter events, 0.1 us)
Async XLA Ops:
  0.6 4.7 %copy-start = (bf16[1,2,256,1535]{2,1,3,0:T(2,128)(2,1)S(1)}, bf16[1,2,256,1535]{2,1,3,0:T(2,128)(2,1)}, u32[]{:S(2)}) copy-start(bf16[1,2,256,1535]{2,1,3,0:T(2,128)(2,1)} %param.5) | copy-start | bytes 4715524
  9.9 19.4 %copy-start.8 = (s32[1,2]{1,0:T(1,128)S(1)}, s32[1,2]{1,0:T(1,128)}, u32[]{:S(2)}) copy-start(s32[1,2]{1,0:T(1,128)} %param.9) | copy-start | bytes 28
  9.9 27.7 %copy-start.9 = (f32[16]{0:T(128)S(1)}, f32[16]{0:T(128)}, u32[]{:S(2)}) copy-start(f32[16]{0:T(128)} %param.8) | copy-start | bytes 196
  11.3 51.7 %all-to-all-start = ((bf16[2,512,256]{2,0,1:T(2,128)(2,1)}), bf16[2,512,256]{2,0,1:T(2,128)(2,1)S(1)}, u32[]{:S(2)}, u32[]{:S(2)}) async-start(bf16[2,512,256]{2,0,1:T(2,128)(2,1)} %copy.33), calls=%async_computation | async-start | bytes 1048576 | tf_op jit(solution)/shard_map/all_to_all | solution.py:191
  63.6 1.6 %copy-start.3 = (f32[64,128]{1,0:T(8,128)S(1)}, f32[64,128]{1,0:T(8,128)}, u32[]{:S(2)}) copy-start(f32[64,128]{1,0:T(8,128)} %get-tuple-element.62) | copy-start | bytes 98308
  63.6 1.6 %copy-start.5 = (f32[64,128]{1,0:T(8,128)S(1)}, f32[64,128]{1,0:T(8,128)}, u32[]{:S(2)}) copy-start(f32[64,128]{1,0:T(8,128)} %get-tuple-element.63) | copy-start | bytes 98308
  63.7 1.6 %copy-start.2 = (f32[1,2,128,128]{3,2,0,1:T(8,128)S(1)}, f32[1,2,128,128]{3,2,0,1:T(8,128)}, u32[]{:S(2)}) copy-start(f32[1,2,128,128]{3,2,0,1:T(8,128)} %get-tuple-element.46) | copy-start | bytes 393220
  65.1 1.0 %copy-start.1 = (f32[16,64,128]{2,1,0:T(8,128)S(1)}, f32[16,64,128]{2,1,0:T(8,128)}, u32[]{:S(2)}) copy-start(f32[16,64,128]{2,1,0:T(8,128)} %get-tuple-element.14) | copy-start | bytes 1572868
  66.2 0.9 copy-start.4
  66.5 0.8 copy-start.6
  66.5 0.9 copy-start.7
  68.2 13.5 %collective-permute-start = (bf16[2,16,8192]{2,1,0:T(8,128)(2,1)S(1)}, bf16[2,16,8192]{2,1,0:T(8,128)(2,1)S(1)}, u32[]{:S(2)}, u32[]{:S(2)}) collective-permute-start(bf16[2,16,8192]{2,1,0:T(8,128)(2,1)S(1)} %convert_element_type.140), channel_id=1, source_target_pairs={{0,32},{32,96},{64,0},{96,64},{128,192},{160,128},{192,224},{224,1... | collective-permute-start | bytes 1572872 | tf_op jit(solution)/shard_map/ppermute | solution.py:195
  70.7 12.6 %collective-permute-start.1 = (bf16[2,16,8192]{2,1,0:T(8,128)(2,1)S(1)}, bf16[2,16,8192]{2,1,0:T(8,128)(2,1)S(1)}, u32[]{:S(2)}, u32[]{:S(2)}) collective-permute-start(bf16[2,16,8192]{2,1,0:T(8,128)(2,1)S(1)} %convert_element_type.140), channel_id=1, source_target_pairs={{0,128},{32,288},{64,320},{96,224},{128,384},{160,32},{192,64},{22... | collective-permute-start | bytes 1572872 | tf_op jit(solution)/shard_map/ppermute | solution.py:195
  85.2 8.4 %collective-permute-start.2 = (f32[2,4,512]{2,1,0:T(4,128)S(1)}, f32[2,4,512]{2,1,0:T(4,128)S(1)}, u32[]{:S(2)}, u32[]{:S(2)}) collective-permute-start(f32[2,4,512]{2,1,0:T(4,128)S(1)} %slice.123), channel_id=1, source_target_pairs={{128,0},{288,32},{320,64},{224,96},{384,128},{32,160},{64,192},{48... | collective-permute-start | bytes 49160 | tf_op jit(solution)/shard_map/ppermute | solution.py:198
  90.8 5.6 %collective-permute-start.3 = (f32[2,4,512]{2,1,0:T(4,128)S(1)}, f32[2,4,512]{2,1,0:T(4,128)S(1)}, u32[]{:S(2)}, u32[]{:S(2)}) collective-permute-start(f32[2,4,512]{2,1,0:T(4,128)S(1)} %slice.127), channel_id=1, source_target_pairs={{32,0},{96,32},{0,64},{64,96},{192,128},{128,160},{224,192},{160,2... | collective-permute-start | bytes 49160 | tf_op jit(solution)/shard_map/ppermute | solution.py:198

commit v22 on v21

--- a/solution.py
+++ b/solution.py
@@ -144,7 +144,7 @@
     lanes = jnp.arange(inner, dtype=jnp.int32)
     groups = jnp.arange(inner // LOOK_AZ, dtype=jnp.int32)
     pool = (lanes[:, None] // LOOK_AZ == groups[None, :]).astype(jnp.float32)
-    looked = jnp.einsum("nrab,bg->nrag", summed, pool, precision=lax.Precision.HIGHEST)
+    looked = jnp.einsum("nrab,bg->nrag", summed, pool, precision=lax.Precision.HIGH)
     scale = 1.0 / (LOOK_RNG * LOOK_AZ)
     return looked.reshape(count, columns // LOOK_RNG, pulse_len // LOOK_AZ) * scale
 

time: 97.7 us -> 97.5 us (level)
  no operation moved by 1% of the time
where the time goes in v22:
time: 97.5 us; the launch traced here: 97 us
  waiting for transfers between devices  35.7 us (37%)
  starting transfers between devices  29.7 us (30%)
  other arithmetic  8.55 us (9%)
  matrix products  8.28 us (8%)
  between operations  5.73 us (6%)
  local copies, waits for them, and re-layouts  5.11 us (5%)
  Pallas kernels  3.9 us (4%)
    all_to_all x1, waiting for transfers between devices, per_device(): lax.all_to_all(compressed, 'pulse', split_axis=1, concat_axis=2, tiled=True)  22.7 us
    all_to_all x1, starting transfers between devices, per_device(): lax.all_to_all(compressed, 'pulse', split_axis=1, concat_axis=2, tiled=True)  18 us
    ppermute x2, waiting for transfers between devices, per_device(): arrived = [lax.ppermute(focused, 'acq', pairs) for pairs in edge_pairs]  10.2 us
    ppermute x2, starting transfers between devices, per_device(): lax.ppermute(looked[slot], 'acq', [(dst, src) for src, dst in edge_pairs[...  7.22 us
    dot_general x1, matrix products, compress(): lax.dot_general(band, echoes, dims, preferred_element_type=jnp.float32)  4.57 us
    ppermute x2, starting transfers between devices, per_device(): arrived = [lax.ppermute(focused, 'acq', pairs) for pairs in edge_pairs]  4.51 us
    pallas_call x1, Pallas kernels, band_tables(): band = pl.pallas_call(band_kernel, out_shape=shape)(chirp_phase[None])  3.9 us
    ppermute x2, waiting for transfers between devices, per_device(): lax.ppermute(looked[slot], 'acq', [(dst, src) for src, dst in edge_pairs[...  2.8 us
  transfers between devices with their start and end apart: 5, of which 4 were waited for; matrix products, arithmetic and copies ran while one was open for 9% of the time, Pallas kernels for 0%

profile of v22, /device:TPU:34, one launch (start us, length us, event | category | flops | bytes accessed | tf_op | source)
XLA Modules:
  0.0 97.0 jit_solution(5306626737927538005)
XLA Ops:
  0.6 0.0 copy-start
  1.4 3.9 %shard_map.68 = bf16[2,2,512,1535]{3,2,1,0:T(8,128)(2,1)} custom-call(f32[1,1024]{1,0:T(1,128)} %bitcast.198), custom_call_target="tpu_custom_call" | custom-call | tf_op jit(solution)/shard_map/pallas_call | solution.py:63
  5.3 4.6 %fusion.14 = bf16[2,512,256]{2,1,0:T(8,128)(2,1)S(1)} fusion(bf16[2,256,1535,1]{1,0,2,3:T(2,128)(2,1)S(1)} %bitcast.189, bf16[2,2,512,1535]{3,2,1,0:T(8,128)(2,1)} %shard_map.68, f32[256]{0:T(256)S(1)} %compare_convert_fusion), kind=kOutput, calls=%fused_computation.11 | convolution fusion | flops 1610088448 | bytes 8384512 | tf_op jit(solution)/shard_map/dot_general | solution.py:70
  9.9 0.0 copy-start.8
  9.9 0.0 copy-start.9
  9.9 1.4 %copy.33 = bf16[2,512,256]{2,0,1:T(2,128)(2,1)} copy(bf16[2,512,256]{2,1,0:T(8,128)(2,1)S(1)} %fusion.14) | data formatting | bytes 1048576 | tf_op jit(solution)/shard_map/convert_element_type | solution.py:74
  11.3 18.0 %all-to-all-start = ((bf16[2,512,256]{2,0,1:T(2,128)(2,1)}), bf16[2,512,256]{2,0,1:T(2,128)(2,1)S(1)}, u32[]{:S(2)}, u32[]{:S(2)}) async-start(bf16[2,512,256]{2,0,1:T(2,128)(2,1)} %copy.33), calls=%async_computation | async-start | bytes 1048576 | tf_op jit(solution)/shard_map/all_to_all | solution.py:191
  29.3 0.6 fusion.82
  33.8 0.1 fusion.71
  33.9 0.8 fusion.67
  34.7 0.1 fusion.69
  34.8 0.8 fusion.68
  35.6 0.3 fusion.66
  35.9 0.3 fusion.60
  36.2 0.7 fusion.41
  36.9 0.7 fusion.34
  37.6 2.7 %multiply_sine_fusion = (f32[16,64,128]{2,1,0:T(8,128)S(1)}, f32[16,64,128]{2,1,0:T(8,128)}) fusion(f32[64,128]{1,0:T(8,128)S(1)} %fusion.57, f32[16]{0:T(128)S(1)} %broadcast_multiply_fusion), kind=kLoop, calls=%fused_computation.24 | loop fusion | flops 131072 | bytes 1081408 | tf_op jit(solution)/shard_map/sin | solution.py:88
  40.3 22.7 %all-to-all-done = bf16[2,512,256]{2,0,1:T(2,128)(2,1)S(1)} async-done(((bf16[2,512,256]{2,0,1:T(2,128)(2,1)}), bf16[2,512,256]{2,0,1:T(2,128)(2,1)S(1)}, u32[]{:S(2)}, u32[]{:S(2)}) %all-to-all-start) | async-done | bytes 524320 | tf_op jit(solution)/shard_map/all_to_all | solution.py:191
  63.0 0.3 copy.99
  63.3 0.2 all_to_all.16
  63.6 0.1 copy.65
  63.7 1.4 %convolution_bitcast_fusion.3 = f32[2,16,64,128]{3,2,1,0:T(8,128)S(1)} fusion(f32[1,2,64,64]{2,3,0,1:T(8,128)} %get-tuple-element.43, f32[1,2,64,64]{2,3,0,1:T(8,128)} %get-tuple-element.50, bf16[2,16,64,128]{3,2,1,0:T(8,128)(2,1)S(1)} %bitcast.195), kind=kOutput, calls=%fused_computation.9 | convolution fusion | flops 201342976 | bytes 1638400 | tf_op jit(solution)/shard_map/pcab,pqak->qckb/dot_general | solution.py:98
  65.2 0.1 multiply_subtract_fusion.1
  65.3 0.6 convolution_bitcast_fusion.2
  65.9 0.3 copy-done.1
  66.2 0.3 subtract_bitcast_fusion.2
  66.5 0.6 convolution_bitcast_fusion.1
  67.1 0.1 multiply_subtract_fusion
  67.2 0.1 copy-done.6
  67.3 0.0 copy-done.7
  67.3 0.6 fusion.20
  68.0 0.2 convert_element_type.140
  68.2 2.4 %collective-permute-start = (bf16[2,16,8192]{2,1,0:T(8,128)(2,1)S(1)}, bf16[2,16,8192]{2,1,0:T(8,128)(2,1)S(1)}, u32[]{:S(2)}, u32[]{:S(2)}) collective-permute-start(bf16[2,16,8192]{2,1,0:T(8,128)(2,1)S(1)} %convert_element_type.140), channel_id=1, source_target_pairs={{0,32},{32,96},{64,0},{96,64},{128,192},{160,128},{192,224},{224,1... | collective-permute-start | bytes 1572872 | tf_op jit(solution)/shard_map/ppermute | solution.py:195
  70.7 2.1 %collective-permute-start.1 = (bf16[2,16,8192]{2,1,0:T(8,128)(2,1)S(1)}, bf16[2,16,8192]{2,1,0:T(8,128)(2,1)S(1)}, u32[]{:S(2)}, u32[]{:S(2)}) collective-permute-start(bf16[2,16,8192]{2,1,0:T(8,128)(2,1)S(1)} %convert_element_type.140), channel_id=1, source_target_pairs={{0,128},{32,288},{64,320},{96,224},{128,384},{160,32},{192,64},{22... | collective-permute-start | bytes 1572872 | tf_op jit(solution)/shard_map/ppermute | solution.py:195
  72.7 0.1 convert_element_type.141
  72.8 0.1 pad_add_fusion.2
  72.9 0.1 pad_add_fusion
  73.0 8.7 %collective-permute-done = bf16[2,16,8192]{2,1,0:T(8,128)(2,1)S(1)} collective-permute-done((bf16[2,16,8192]{2,1,0:T(8,128)(2,1)S(1)}, bf16[2,16,8192]{2,1,0:T(8,128)(2,1)S(1)}, u32[]{:S(2)}, u32[]{:S(2)}) %collective-permute-start) | collective-permute-done | bytes 524320 | tf_op jit(solution)/shard_map/ppermute | solution.py:195
  81.7 0.1 convert_element_type.142
  81.8 1.5 %collective-permute-done.1 = bf16[2,16,8192]{2,1,0:T(8,128)(2,1)S(1)} collective-permute-done((bf16[2,16,8192]{2,1,0:T(8,128)(2,1)S(1)}, bf16[2,16,8192]{2,1,0:T(8,128)(2,1)S(1)}, u32[]{:S(2)}, u32[]{:S(2)}) %collective-permute-start.1) | collective-permute-done | bytes 524320 | tf_op jit(solution)/shard_map/ppermute | solution.py:195
  83.2 0.1 convert_element_type.143
  83.3 0.2 add_bitcast_fusion.1
  83.6 0.1 copy.66
  83.7 0.1 copy.67
  83.8 0.1 copy.68
  83.9 0.1 copy.69
  84.0 0.2 maximum_reduce_fusion
  84.2 0.5 convolution_multiply_fusion
  84.7 0.1 copy.43
  84.8 0.2 slice.123
  85.0 5.3 %collective-permute-start.2 = (f32[2,4,512]{2,1,0:T(4,128)S(1)}, f32[2,4,512]{2,1,0:T(4,128)S(1)}, u32[]{:S(2)}, u32[]{:S(2)}) collective-permute-start(f32[2,4,512]{2,1,0:T(4,128)S(1)} %slice.123), channel_id=1, source_target_pairs={{128,0},{288,32},{320,64},{224,96},{384,128},{32,160},{64,192},{48... | collective-permute-start | bytes 49160 | tf_op jit(solution)/shard_map/ppermute | solution.py:198
  90.3 0.1 copy.45
  90.5 0.2 slice.127
  90.6 1.9 %collective-permute-start.3 = (f32[2,4,512]{2,1,0:T(4,128)S(1)}, f32[2,4,512]{2,1,0:T(4,128)S(1)}, u32[]{:S(2)}, u32[]{:S(2)}) collective-permute-start(f32[2,4,512]{2,1,0:T(4,128)S(1)} %slice.127), channel_id=1, source_target_pairs={{32,0},{96,32},{0,64},{64,96},{192,128},{128,160},{224,192},{160,2... | collective-permute-start | bytes 49160 | tf_op jit(solution)/shard_map/ppermute | solution.py:198
  92.6 0.1 copy.44
  92.6 0.1 broadcast_in_dim.124
  92.8 0.1 copy.46
  92.9 0.1 broadcast_in_dim.129
  93.0 0.1 copy.47
  93.1 0.1 broadcast_in_dim.133
  93.2 0.1 copy.48
  93.3 0.1 broadcast_in_dim.137
  93.5 2.8 %collective-permute-done.3 = f32[2,4,512]{2,1,0:T(4,128)S(1)} collective-permute-done((f32[2,4,512]{2,1,0:T(4,128)S(1)}, f32[2,4,512]{2,1,0:T(4,128)S(1)}, u32[]{:S(2)}, u32[]{:S(2)}) %collective-permute-start.3) | collective-permute-done | bytes 16416 | tf_op jit(solution)/shard_map/ppermute | solution.py:198
  96.3 0.7 select_select_fusion
  (24 shorter events, 0.1 us)
Async XLA Ops:
  0.6 4.7 %copy-start = (bf16[1,2,256,1535]{2,1,3,0:T(2,128)(2,1)S(1)}, bf16[1,2,256,1535]{2,1,3,0:T(2,128)(2,1)}, u32[]{:S(2)}) copy-start(bf16[1,2,256,1535]{2,1,3,0:T(2,128)(2,1)} %param.5) | copy-start | bytes 4715524
  9.9 19.4 %copy-start.8 = (s32[1,2]{1,0:T(1,128)S(1)}, s32[1,2]{1,0:T(1,128)}, u32[]{:S(2)}) copy-start(s32[1,2]{1,0:T(1,128)} %param.9) | copy-start | bytes 28
  9.9 27.7 %copy-start.9 = (f32[16]{0:T(128)S(1)}, f32[16]{0:T(128)}, u32[]{:S(2)}) copy-start(f32[16]{0:T(128)} %param.8) | copy-start | bytes 196
  11.3 51.7 %all-to-all-start = ((bf16[2,512,256]{2,0,1:T(2,128)(2,1)}), bf16[2,512,256]{2,0,1:T(2,128)(2,1)S(1)}, u32[]{:S(2)}, u32[]{:S(2)}) async-start(bf16[2,512,256]{2,0,1:T(2,128)(2,1)} %copy.33), calls=%async_computation | async-start | bytes 1048576 | tf_op jit(solution)/shard_map/all_to_all | solution.py:191
  63.6 1.6 %copy-start.3 = (f32[64,128]{1,0:T(8,128)S(1)}, f32[64,128]{1,0:T(8,128)}, u32[]{:S(2)}) copy-start(f32[64,128]{1,0:T(8,128)} %get-tuple-element.62) | copy-start | bytes 98308
  63.6 1.6 %copy-start.5 = (f32[64,128]{1,0:T(8,128)S(1)}, f32[64,128]{1,0:T(8,128)}, u32[]{:S(2)}) copy-start(f32[64,128]{1,0:T(8,128)} %get-tuple-element.63) | copy-start | bytes 98308
  63.7 1.6 %copy-start.2 = (f32[1,2,128,128]{3,2,0,1:T(8,128)S(1)}, f32[1,2,128,128]{3,2,0,1:T(8,128)}, u32[]{:S(2)}) copy-start(f32[1,2,128,128]{3,2,0,1:T(8,128)} %get-tuple-element.46) | copy-start | bytes 393220
  65.1 1.0 %copy-start.1 = (f32[16,64,128]{2,1,0:T(8,128)S(1)}, f32[16,64,128]{2,1,0:T(8,128)}, u32[]{:S(2)}) copy-start(f32[16,64,128]{2,1,0:T(8,128)} %get-tuple-element.14) | copy-start | bytes 1572868
  66.2 0.9 copy-start.4
  66.5 0.8 copy-start.6
  66.5 0.9 copy-start.7
  68.2 13.5 %collective-permute-start = (bf16[2,16,8192]{2,1,0:T(8,128)(2,1)S(1)}, bf16[2,16,8192]{2,1,0:T(8,128)(2,1)S(1)}, u32[]{:S(2)}, u32[]{:S(2)}) collective-permute-start(bf16[2,16,8192]{2,1,0:T(8,128)(2,1)S(1)} %convert_element_type.140), channel_id=1, source_target_pairs={{0,32},{32,96},{64,0},{96,64},{128,192},{160,128},{192,224},{224,1... | collective-permute-start | bytes 1572872 | tf_op jit(solution)/shard_map/ppermute | solution.py:195
  70.7 12.6 %collective-permute-start.1 = (bf16[2,16,8192]{2,1,0:T(8,128)(2,1)S(1)}, bf16[2,16,8192]{2,1,0:T(8,128)(2,1)S(1)}, u32[]{:S(2)}, u32[]{:S(2)}) collective-permute-start(bf16[2,16,8192]{2,1,0:T(8,128)(2,1)S(1)} %convert_element_type.140), channel_id=1, source_target_pairs={{0,128},{32,288},{64,320},{96,224},{128,384},{160,32},{192,64},{22... | collective-permute-start | bytes 1572872 | tf_op jit(solution)/shard_map/ppermute | solution.py:195
  85.0 8.4 %collective-permute-start.2 = (f32[2,4,512]{2,1,0:T(4,128)S(1)}, f32[2,4,512]{2,1,0:T(4,128)S(1)}, u32[]{:S(2)}, u32[]{:S(2)}) collective-permute-start(f32[2,4,512]{2,1,0:T(4,128)S(1)} %slice.123), channel_id=1, source_target_pairs={{128,0},{288,32},{320,64},{224,96},{384,128},{32,160},{64,192},{48... | collective-permute-start | bytes 49160 | tf_op jit(solution)/shard_map/ppermute | solution.py:198
  90.6 5.6 %collective-permute-start.3 = (f32[2,4,512]{2,1,0:T(4,128)S(1)}, f32[2,4,512]{2,1,0:T(4,128)S(1)}, u32[]{:S(2)}, u32[]{:S(2)}) collective-permute-start(f32[2,4,512]{2,1,0:T(4,128)S(1)} %slice.127), channel_id=1, source_target_pairs={{32,0},{96,32},{0,64},{64,96},{192,128},{128,160},{224,192},{160,2... | collective-permute-start | bytes 49160 | tf_op jit(solution)/shard_map/ppermute | solution.py:198

commit v23 on v22

--- a/solution.py
+++ b/solution.py
@@ -94,10 +94,13 @@
     outer_len = 64
     inner_len = length // outer_len
     highest = lax.Precision.HIGH
-    signal = turned.astype(jnp.float32).reshape(2, columns, outer_len, inner_len)
+    signal = turned.reshape(2, columns, outer_len, inner_len)
+    table = part_tables(outer_len, False)
+    table_hi = table.astype(turned.dtype)
+    table_lo = (table - table_hi.astype(jnp.float32)).astype(turned.dtype)
     section_one = jnp.einsum(
-        "pcab,pqak->qckb", signal, part_tables(outer_len, False), precision=highest
-    )
+        "pcab,pqak->qckb", signal, table_hi, preferred_element_type=jnp.float32
+    ) + jnp.einsum("pcab,pqak->qckb", signal, table_lo, preferred_element_type=jnp.float32)
     outer_ids = jnp.arange(outer_len, dtype=jnp.int32)
     inner_ids = jnp.arange(inner_len, dtype=jnp.int32)
     twist = (

time: 97.5 us -> 96.9 us (level)
  no operation moved by 1% of the time
where the time goes in v23:
time: 96.9 us; the launch traced here: 96.4 us
  waiting for transfers between devices  35.7 us (37%)
  starting transfers between devices  29.7 us (31%)
  other arithmetic  8.55 us (9%)
  matrix products  7.57 us (8%)
  between operations  5.73 us (6%)
  local copies, waits for them, and re-layouts  5.24 us (5%)
  Pallas kernels  3.9 us (4%)
    all_to_all x1, waiting for transfers between devices, per_device(): lax.all_to_all(compressed, 'pulse', split_axis=1, concat_axis=2, tiled=True)  22.7 us
    all_to_all x1, starting transfers between devices, per_device(): lax.all_to_all(compressed, 'pulse', split_axis=1, concat_axis=2, tiled=True)  18 us
    ppermute x2, waiting for transfers between devices, per_device(): arrived = [lax.ppermute(focused, 'acq', pairs) for pairs in edge_pairs]  10.2 us
    ppermute x2, starting transfers between devices, per_device(): lax.ppermute(looked[slot], 'acq', [(dst, src) for src, dst in edge_pairs[...  7.21 us
    dot_general x1, matrix products, compress(): lax.dot_general(band, echoes, dims, preferred_element_type=jnp.float32)  4.57 us
    ppermute x2, starting transfers between devices, per_device(): arrived = [lax.ppermute(focused, 'acq', pairs) for pairs in edge_pairs]  4.5 us
    pallas_call x1, Pallas kernels, band_tables(): band = pl.pallas_call(band_kernel, out_shape=shape)(chirp_phase[None])  3.9 us
    ppermute x2, waiting for transfers between devices, per_device(): lax.ppermute(looked[slot], 'acq', [(dst, src) for src, dst in edge_pairs[...  2.8 us
  transfers between devices with their start and end apart: 5, of which 4 were waited for; matrix products, arithmetic and copies ran while one was open for 9% of the time, Pallas kernels for 0%

profile of v23, /device:TPU:34, one launch (start us, length us, event | category | flops | bytes accessed | tf_op | source)
XLA Modules:
  0.0 96.4 jit_solution(6909621303711862658)
XLA Ops:
  1.4 3.9 %shard_map.68 = bf16[2,2,512,1535]{3,2,1,0:T(8,128)(2,1)} custom-call(f32[1,1024]{1,0:T(1,128)} %bitcast.220), custom_call_target="tpu_custom_call" | custom-call | tf_op jit(solution)/shard_map/pallas_call | solution.py:63
  5.3 4.6 %fusion.16 = bf16[2,512,256]{2,1,0:T(8,128)(2,1)S(1)} fusion(bf16[2,256,1535,1]{1,0,2,3:T(2,128)(2,1)S(1)} %bitcast.210, bf16[2,2,512,1535]{3,2,1,0:T(8,128)(2,1)} %shard_map.68, f32[256]{0:T(256)S(1)} %compare_convert_fusion), kind=kOutput, calls=%fused_computation.14 | convolution fusion | flops 1610088448 | bytes 8384512 | tf_op jit(solution)/shard_map/dot_general | solution.py:70
  9.9 1.4 %copy.34 = bf16[2,512,256]{2,0,1:T(2,128)(2,1)} copy(bf16[2,512,256]{2,1,0:T(8,128)(2,1)S(1)} %fusion.16) | data formatting | bytes 1048576 | tf_op jit(solution)/shard_map/convert_element_type | solution.py:74
  11.3 18.0 %all-to-all-start = ((bf16[2,512,256]{2,0,1:T(2,128)(2,1)}), bf16[2,512,256]{2,0,1:T(2,128)(2,1)S(1)}, u32[]{:S(2)}, u32[]{:S(2)}) async-start(bf16[2,512,256]{2,0,1:T(2,128)(2,1)} %copy.34), calls=%async_computation | async-start | bytes 1048576 | tf_op jit(solution)/shard_map/all_to_all | solution.py:194
  29.3 0.6 fusion.90
  33.8 0.1 fusion.78
  33.9 0.7 fusion.74
  34.7 0.1 fusion.76
  34.8 0.8 fusion.75
  35.6 0.3 fusion.73
  35.9 0.3 fusion.67
  36.1 0.7 fusion.46
  36.8 0.7 fusion.38
  37.6 2.7 %multiply_sine_fusion = (f32[16,64,128]{2,1,0:T(8,128)S(1)}, f32[16,64,128]{2,1,0:T(8,128)}) fusion(f32[64,128]{1,0:T(8,128)S(1)} %fusion.64, f32[16]{0:T(128)S(1)} %broadcast_multiply_fusion), kind=kLoop, calls=%fused_computation.27 | loop fusion | flops 131072 | bytes 1081408 | tf_op jit(solution)/shard_map/sin | solution.py:88
  40.3 22.7 %all-to-all-done = bf16[2,512,256]{2,0,1:T(2,128)(2,1)S(1)} async-done(((bf16[2,512,256]{2,0,1:T(2,128)(2,1)}), bf16[2,512,256]{2,0,1:T(2,128)(2,1)S(1)}, u32[]{:S(2)}, u32[]{:S(2)}) %all-to-all-start) | async-done | bytes 524320 | tf_op jit(solution)/shard_map/all_to_all | solution.py:194
  63.0 0.3 copy.107
  63.3 0.2 all_to_all.16
  63.6 0.1 copy.69
  63.7 0.3 convolution_bitcast_fusion
  64.1 0.3 fusion.15
  64.4 0.0 copy-done.4
  64.5 0.1 multiply_subtract_fusion.1
  64.6 0.3 copy-done.2
  65.0 0.1 copy-done.3
  65.0 0.6 convolution_bitcast_fusion.4
  65.6 0.3 subtract_bitcast_fusion.2
  65.9 0.6 convolution_bitcast_fusion.3
  66.5 0.2 multiply_subtract_fusion
  66.7 0.0 copy-done.7
  66.8 0.0 copy-done.8
  66.8 0.6 fusion.22
  67.4 0.2 convert_element_type.151
  67.7 2.4 %collective-permute-start = (bf16[2,16,8192]{2,1,0:T(8,128)(2,1)S(1)}, bf16[2,16,8192]{2,1,0:T(8,128)(2,1)S(1)}, u32[]{:S(2)}, u32[]{:S(2)}) collective-permute-start(bf16[2,16,8192]{2,1,0:T(8,128)(2,1)S(1)} %convert_element_type.151), channel_id=1, source_target_pairs={{0,32},{32,96},{64,0},{96,64},{128,192},{160,128},{192,224},{224,1... | collective-permute-start | bytes 1572872 | tf_op jit(solution)/shard_map/ppermute | solution.py:198
  70.1 2.1 %collective-permute-start.1 = (bf16[2,16,8192]{2,1,0:T(8,128)(2,1)S(1)}, bf16[2,16,8192]{2,1,0:T(8,128)(2,1)S(1)}, u32[]{:S(2)}, u32[]{:S(2)}) collective-permute-start(bf16[2,16,8192]{2,1,0:T(8,128)(2,1)S(1)} %convert_element_type.151), channel_id=1, source_target_pairs={{0,128},{32,288},{64,320},{96,224},{128,384},{160,32},{192,64},{22... | collective-permute-start | bytes 1572872 | tf_op jit(solution)/shard_map/ppermute | solution.py:198
  72.2 0.1 convert_element_type.152
  72.3 0.1 pad_add_fusion.2
  72.3 0.1 pad_add_fusion
  72.4 8.7 %collective-permute-done = bf16[2,16,8192]{2,1,0:T(8,128)(2,1)S(1)} collective-permute-done((bf16[2,16,8192]{2,1,0:T(8,128)(2,1)S(1)}, bf16[2,16,8192]{2,1,0:T(8,128)(2,1)S(1)}, u32[]{:S(2)}, u32[]{:S(2)}) %collective-permute-start) | collective-permute-done | bytes 524320 | tf_op jit(solution)/shard_map/ppermute | solution.py:198
  81.2 0.1 convert_element_type.153
  81.2 1.5 %collective-permute-done.1 = bf16[2,16,8192]{2,1,0:T(8,128)(2,1)S(1)} collective-permute-done((bf16[2,16,8192]{2,1,0:T(8,128)(2,1)S(1)}, bf16[2,16,8192]{2,1,0:T(8,128)(2,1)S(1)}, u32[]{:S(2)}, u32[]{:S(2)}) %collective-permute-start.1) | collective-permute-done | bytes 524320 | tf_op jit(solution)/shard_map/ppermute | solution.py:198
  82.7 0.1 convert_element_type.154
  82.8 0.2 add_bitcast_fusion.1
  83.0 0.1 copy.70
  83.1 0.1 copy.71
  83.2 0.1 copy.72
  83.3 0.1 copy.73
  83.4 0.2 maximum_reduce_fusion
  83.6 0.5 convolution_multiply_fusion
  84.2 0.1 copy.45
  84.3 0.2 slice.123
  84.5 5.3 %collective-permute-start.2 = (f32[2,4,512]{2,1,0:T(4,128)S(1)}, f32[2,4,512]{2,1,0:T(4,128)S(1)}, u32[]{:S(2)}, u32[]{:S(2)}) collective-permute-start(f32[2,4,512]{2,1,0:T(4,128)S(1)} %slice.123), channel_id=1, source_target_pairs={{128,0},{288,32},{320,64},{224,96},{384,128},{32,160},{64,192},{48... | collective-permute-start | bytes 49160 | tf_op jit(solution)/shard_map/ppermute | solution.py:201
  89.8 0.1 copy.47
  89.9 0.2 slice.127
  90.1 1.9 %collective-permute-start.3 = (f32[2,4,512]{2,1,0:T(4,128)S(1)}, f32[2,4,512]{2,1,0:T(4,128)S(1)}, u32[]{:S(2)}, u32[]{:S(2)}) collective-permute-start(f32[2,4,512]{2,1,0:T(4,128)S(1)} %slice.127), channel_id=1, source_target_pairs={{32,0},{96,32},{0,64},{64,96},{192,128},{128,160},{224,192},{160,2... | collective-permute-start | bytes 49160 | tf_op jit(solution)/shard_map/ppermute | solution.py:201
  92.0 0.1 copy.46
  92.1 0.1 broadcast_in_dim.124
  92.2 0.1 copy.48
  92.3 0.1 broadcast_in_dim.129
  92.4 0.1 copy.49
  92.5 0.1 broadcast_in_dim.133
  92.7 0.1 copy.50
  92.8 0.1 broadcast_in_dim.137
  92.9 2.8 %collective-permute-done.3 = f32[2,4,512]{2,1,0:T(4,128)S(1)} collective-permute-done((f32[2,4,512]{2,1,0:T(4,128)S(1)}, f32[2,4,512]{2,1,0:T(4,128)S(1)}, u32[]{:S(2)}, u32[]{:S(2)}) %collective-permute-start.3) | collective-permute-done | bytes 16416 | tf_op jit(solution)/shard_map/ppermute | solution.py:201
  95.7 0.7 select_select_fusion
  (27 shorter events, 0.1 us)
Async XLA Ops:
  0.6 4.7 %copy-start = (bf16[1,2,256,1535]{2,1,3,0:T(2,128)(2,1)S(1)}, bf16[1,2,256,1535]{2,1,3,0:T(2,128)(2,1)}, u32[]{:S(2)}) copy-start(bf16[1,2,256,1535]{2,1,3,0:T(2,128)(2,1)} %param.5) | copy-start | bytes 4715524
  9.9 19.4 %copy-start.9 = (s32[1,2]{1,0:T(1,128)S(1)}, s32[1,2]{1,0:T(1,128)}, u32[]{:S(2)}) copy-start(s32[1,2]{1,0:T(1,128)} %param.9) | copy-start | bytes 28
  9.9 27.6 %copy-start.10 = (f32[16]{0:T(128)S(1)}, f32[16]{0:T(128)}, u32[]{:S(2)}) copy-start(f32[16]{0:T(128)} %param.8) | copy-start | bytes 196
  11.3 51.7 %all-to-all-start = ((bf16[2,512,256]{2,0,1:T(2,128)(2,1)}), bf16[2,512,256]{2,0,1:T(2,128)(2,1)S(1)}, u32[]{:S(2)}, u32[]{:S(2)}) async-start(bf16[2,512,256]{2,0,1:T(2,128)(2,1)} %copy.34), calls=%async_computation | async-start | bytes 1048576 | tf_op jit(solution)/shard_map/all_to_all | solution.py:194
  63.7 0.8 copy-start.4
  63.7 0.8 copy-start.6
  64.1 0.9 copy-start.2
  64.1 1.0 %copy-start.3 = (f32[1,2,128,128]{3,2,0,1:T(8,128)S(1)}, f32[1,2,128,128]{3,2,0,1:T(8,128)}, u32[]{:S(2)}) copy-start(f32[1,2,128,128]{3,2,0,1:T(8,128)} %get-tuple-element.46) | copy-start | bytes 393220
  64.5 1.2 %copy-start.1 = (f32[16,64,128]{2,1,0:T(8,128)S(1)}, f32[16,64,128]{2,1,0:T(8,128)}, u32[]{:S(2)}) copy-start(f32[16,64,128]{2,1,0:T(8,128)} %get-tuple-element.14) | copy-start | bytes 1572868
  65.6 0.9 copy-start.5
  65.9 0.8 copy-start.7
  65.9 0.9 copy-start.8
  67.7 13.5 %collective-permute-start = (bf16[2,16,8192]{2,1,0:T(8,128)(2,1)S(1)}, bf16[2,16,8192]{2,1,0:T(8,128)(2,1)S(1)}, u32[]{:S(2)}, u32[]{:S(2)}) collective-permute-start(bf16[2,16,8192]{2,1,0:T(8,128)(2,1)S(1)} %convert_element_type.151), channel_id=1, source_target_pairs={{0,32},{32,96},{64,0},{96,64},{128,192},{160,128},{192,224},{224,1... | collective-permute-start | bytes 1572872 | tf_op jit(solution)/shard_map/ppermute | solution.py:198
  70.1 12.6 %collective-permute-start.1 = (bf16[2,16,8192]{2,1,0:T(8,128)(2,1)S(1)}, bf16[2,16,8192]{2,1,0:T(8,128)(2,1)S(1)}, u32[]{:S(2)}, u32[]{:S(2)}) collective-permute-start(bf16[2,16,8192]{2,1,0:T(8,128)(2,1)S(1)} %convert_element_type.151), channel_id=1, source_target_pairs={{0,128},{32,288},{64,320},{96,224},{128,384},{160,32},{192,64},{22... | collective-permute-start | bytes 1572872 | tf_op jit(solution)/shard_map/ppermute | solution.py:198
  84.5 8.4 %collective-permute-start.2 = (f32[2,4,512]{2,1,0:T(4,128)S(1)}, f32[2,4,512]{2,1,0:T(4,128)S(1)}, u32[]{:S(2)}, u32[]{:S(2)}) collective-permute-start(f32[2,4,512]{2,1,0:T(4,128)S(1)} %slice.123), channel_id=1, source_target_pairs={{128,0},{288,32},{320,64},{224,96},{384,128},{32,160},{64,192},{48... | collective-permute-start | bytes 49160 | tf_op jit(solution)/shard_map/ppermute | solution.py:201
  90.1 5.6 %collective-permute-start.3 = (f32[2,4,512]{2,1,0:T(4,128)S(1)}, f32[2,4,512]{2,1,0:T(4,128)S(1)}, u32[]{:S(2)}, u32[]{:S(2)}) collective-permute-start(f32[2,4,512]{2,1,0:T(4,128)S(1)} %slice.127), channel_id=1, source_target_pairs={{32,0},{96,32},{0,64},{64,96},{192,128},{128,160},{224,192},{160,2... | collective-permute-start | bytes 49160 | tf_op jit(solution)/shard_map/ppermute | solution.py:201
